TPU v7x, 512 devices: a whole 4x4x16 slice. The times are simulated.
512 devices in a mesh: replica: 64 (over z, x), shard: 8 (over y, core).
Axes of the slice: x: 4, y: 4, z: 16, core: 2. Of those that a mesh axis runs over, the one named last changes fastest.
Arguments:
- grad_query: float32 [512, 512, 384], P(('replica', 'shard')), may hold values from -1.25 to 1.25
- grad_output: float32 [512, 384, 512], P(('replica', 'shard')), may hold values from -1.25 to 1.25
- grad_norm: float32 [512, 512], P(('replica', 'shard')), may hold values from -1.25 to 1.25
- grad_bias: float32 [512, 32, 6], P(('replica', 'shard')), may hold values from -0.3 to 0.3
- weight_query: float32 [512, 384], P('shard'), may hold values from -5.303301 to 5.303301
- weight_output: float32 [384, 512], P('shard'), may hold values from -6.1237244 to 6.1237244
- weight_norm: float32 [512], P('shard'), may hold values from 0 to 120
- weight_bias: float32 [32, 6], P('shard'), may hold values from -120 to 120
- first_query: float32 [512, 384], P('shard'), may hold values from -120 to 120
- first_output: float32 [384, 512], P('shard'), may hold values from -120 to 120
- first_norm: float32 [512], P('shard'), may hold values from -120 to 120
- first_bias: float32 [32, 6], P('shard'), may hold values from -120 to 120
- second_query: float32 [512, 384], P('shard'), may hold values from 0.05 to 2
- second_output: float32 [384, 512], P('shard'), may hold values from 0.05 to 2
- second_norm: float32 [512], P('shard'), may hold values from 0.05 to 2
- second_bias: float32 [32, 6], P('shard'), may hold values from 0.05 to 2
Outputs:
- updated_query: bfloat16 [512, 384], replicated
- updated_output: bfloat16 [384, 512], replicated
- updated_norm: bfloat16 [512], replicated
- updated_bias: bfloat16 [32, 6], replicated
- first_query_next: float32 [512, 384], P('shard')
- first_output_next: float32 [384, 512], P('shard')
- first_norm_next: float32 [512], P('shard')
- first_bias_next: float32 [32, 6], P('shard')
- second_query_next: float32 [512, 384], P('shard')
- second_output_next: float32 [384, 512], P('shard')
- second_norm_next: float32 [512], P('shard')
- second_bias_next: float32 [32, 6], P('shard')
- norm_table: float32 [2, 4], replicated
- trust_ratios: float32 [4], replicated
All inputs are finite; a program needn't handle non-finite values.
Results may differ from a plain program's by a relative error of at most 0.008.
Values may be sent and summed in bfloat16 or wider, within the bound.
No kernel may reach another device: no remote copies, remote signals or barrier semaphores. Data moves between devices by JAX's collectives and lax.ppermute only.
A program may use at most 64 MiB of HBM per device.

v0:
```python
import jax
import jax.numpy as jnp
from jax import lax
from jax.sharding import PartitionSpec as P


def step_math(summed, moment, second, weight, decay_rate):
    moment_next = 0.5 * moment + 0.5 * summed
    second_next = 0.5 * second + 0.5 * summed * summed
    update = moment_next / (jnp.sqrt(second_next) + 1e-06) + decay_rate * weight
    return (moment_next, second_next, update)


def on_device(
    grad_query,
    grad_output,
    grad_norm,
    grad_bias,
    weight_query,
    weight_output,
    weight_norm,
    weight_bias,
    first_query,
    first_output,
    first_norm,
    first_bias,
    second_query,
    second_output,
    second_norm,
    second_bias,
):
    weights = (weight_query, weight_output, weight_norm, weight_bias)
    moments = (first_query, first_output, first_norm, first_bias)
    seconds = (second_query, second_output, second_norm, second_bias)
    decay_rates = (0.01, 0.01, 0.0, 0.0)
    gradients = (grad_query[0], grad_output[0], grad_norm[0], grad_bias[0])
    totals = lax.psum(
        (gradients[0], gradients[1], gradients[2], gradients[3]), ("replica", "shard")
    )
    position = lax.axis_index("shard")
    summed_all = tuple(
        (
            lax.dynamic_slice_in_dim(entire, position * weight.shape[0], weight.shape[0], 0)
            for entire, weight in zip(totals, weights)
        )
    )
    results = [
        step_math(
            summed_all[member],
            moments[member],
            seconds[member],
            weights[member],
            decay_rates[member],
        )
        for member in range(4)
    ]
    weight_squares = [jnp.sum(weight * weight) for weight in weights]
    update_squares = [jnp.sum(result[2] * result[2]) for result in results]
    couples = [
        lax.psum((weight_squares[member], update_squares[member]), "shard") for member in range(4)
    ]
    weight_sizes = jnp.sqrt(jnp.stack([couple[0] for couple in couples]))
    update_sizes = jnp.sqrt(jnp.stack([couple[1] for couple in couples]))
    trust_ratios = weight_sizes / (update_sizes + 1e-06)
    shards = tuple(
        (
            (weights[member] - 0.01 * trust_ratios[member] * results[member][2]).astype(
                jnp.bfloat16
            )
            for member in range(4)
        )
    )
    gathered = (
        lax.all_gather(shards[0], "shard", axis=0, tiled=True),
        lax.all_gather(shards[1], "shard", axis=0, tiled=True),
        lax.all_gather(shards[2], "shard", axis=0, tiled=True),
        lax.all_gather(shards[3], "shard", axis=0, tiled=True),
    )
    norm_table = jnp.stack([weight_sizes, update_sizes])
    return (
        gathered[0],
        gathered[1],
        gathered[2],
        gathered[3],
        results[0][0],
        results[1][0],
        results[2][0],
        results[3][0],
        results[0][1],
        results[1][1],
        results[2][1],
        results[3][1],
        norm_table,
        trust_ratios,
    )


def solution(mesh):
    placed = (
        P(("replica", "shard"), None, None),
        P(("replica", "shard"), None, None),
        P(("replica", "shard"), None),
        P(("replica", "shard"), None, None),
        P("shard", None),
        P("shard", None),
        P("shard"),
        P("shard", None),
        P("shard", None),
        P("shard", None),
        P("shard"),
        P("shard", None),
        P("shard", None),
        P("shard", None),
        P("shard"),
        P("shard", None),
    )
    return jax.shard_map(
        on_device,
        mesh=mesh,
        in_specs=placed,
        out_specs=(
            P(),
            P(),
            P(),
            P(),
            P("shard", None),
            P("shard", None),
            P("shard"),
            P("shard", None),
            P("shard", None),
            P("shard", None),
            P("shard"),
            P("shard", None),
            P(),
            P(),
        ),
        check_vma=False,
    )
```

profile of v0, /device:TPU:1, one launch (start us, length us, event | category | flops | bytes accessed | tf_op | source)
XLA Modules:
  0.0 580.5 jit_solution(12802664677548248440)
XLA Ops:
  7.2 0.0 all-reduce.6.cloned.1.call-start
  7.2 0.0 copy-start.12
  7.2 0.0 copy-start.13
  7.2 0.0 copy-start.14
  7.3 0.0 copy-start.17
  7.3 0.0 copy-start.18
  7.3 0.0 copy-start.11
  7.3 0.0 copy-start.15
  7.3 0.0 copy-start.16
  7.3 0.0 copy-start.6
  7.3 0.0 copy-start.7
  7.3 0.6 all-reduce.6.cloned.1.call-update
  7.9 0.0 copy-start
  7.9 0.0 copy-done.12
  7.9 0.1 copy.32
  8.0 1.3 dynamic-slice
  9.9 0.0 copy-done.13
  10.0 111.8 %all-reduce.1 = (f32[32,6]{1,0:T(8,128)S(1)}, f32[512]{0:T(512)S(1)}) all-reduce(f32[32,6]{1,0:T(8,128)S(1)} %bitcast.30, f32[512]{0:T(512)S(1)} %bitcast.32), channel_id=1, replica_groups=mesh['replica'=64,'shard'=8] {'replica','shard'}, use_global_device_ids=true, to_apply=%region_17.0 | all-reduce | flops 704 | bytes 5632 | tf_op jit(solution)/shard_map/psum | solution.py:37
  121.8 1.2 multiply_reduce_fusion.6
  123.0 0.0 copy-done.16
  123.0 1.2 multiply_reduce_fusion.4
  124.2 366.8 %all-reduce.6.cloned.1.call-done = (f32[384,512]{1,0:T(8,128)}, f32[512,384]{1,0:T(8,128)}) async-done(((f32[384,512]{1,0:T(8,128)}, f32[512,384]{1,0:T(8,128)}), (f32[384,512]{1,0:T(8,128)}, f32[512,384]{1,0:T(8,128)})) %all-reduce.6.cloned.1.call-update) | async-done | bytes 1572880 | tf_op jit(solution)/shard_map/psum | solution.py:37
  490.9 0.0 copy-done.6
  490.9 0.0 copy-done
  491.0 0.0 copy-start.8
  491.0 0.0 copy-start.9
  491.0 1.7 multiply_reduce_fusion.1
  492.7 0.0 copy-done.1
  492.7 1.6 multiply_reduce_fusion
  494.4 14.6 %all-reduce.3 = (f32[]{:T(128)}, f32[]{:T(128)}, f32[]{:T(128)}, f32[]{:T(128)}, f32[]{:T(128)}, /*index=5*/f32[]{:T(128)}, f32[]{:T(128)}, f32[]{:T(128)}) all-reduce(f32[]{:T(128)} %get-tuple-element.70, f32[]{:T(128)} %get-tuple-element.75, f32[]{:T(128)} %get-tuple-element.45, ...), channel_id=1, replica_groups=mesh['replica'=64,'shard'=8] {'shard'}, use_global_device_ids=true, to_apply=%region_7.0 | all-reduce | flops 8 | bytes 64 | tf_op jit(solution)/shard_map/psum | solution.py:60
  508.9 5.1 fusion.5
  514.1 0.0 copy-start.10
  514.1 0.6 fusion.11
  514.7 0.0 copy-done.10
  515.3 0.0 copy-done.2
  515.3 0.0 copy-done.3
  515.3 0.1 subtract_convert_fusion.1
  515.4 14.0 %all_gather.12 = bf16[512,384]{1,0:T(8,128)(2,1)S(1)} all-gather(bf16[64,384]{1,0:T(8,128)(2,1)S(1)} %subtract_convert_fusion.1), channel_id=1, replica_groups=mesh['replica'=64,'shard'=8] {'shard'}, dimensions={0}, use_global_device_ids=true | all-gather | bytes 442368 | tf_op jit(solution)/shard_map/all_gather | solution.py:74
  530.0 0.1 subtract_convert_fusion
  530.1 13.0 %all_gather.13 = bf16[384,512]{1,0:T(8,128)(2,1)S(1)} all-gather(bf16[48,512]{1,0:T(8,128)(2,1)S(1)} %subtract_convert_fusion), channel_id=1, replica_groups=mesh['replica'=64,'shard'=8] {'shard'}, dimensions={0}, use_global_device_ids=true | all-gather | bytes 442368 | tf_op jit(solution)/shard_map/all_gather | solution.py:75
  543.7 0.2 dynamic-update-slice
  544.0 12.5 %all-reduce = bf16[512]{0:T(512)(128)(2,1)} all-reduce(bf16[512]{0:T(512)(128)(2,1)S(1)} %dynamic-update-slice), channel_id=1, replica_groups=mesh['replica'=64,'shard'=8] {'shard'}, use_global_device_ids=true, to_apply=%add | all-reduce | flops 512 | bytes 2048
  557.1 8.6 %all-gather = bf16[8,4,6]{2,1,0:T(4,128)(2,1)S(1)} all-gather(bf16[1,4,6]{2,1,0:T(4,128)(2,1)S(1)} %fusion.3), channel_id=1, replica_groups=mesh['replica'=64,'shard'=8] {'shard'}, dimensions={0}, use_global_device_ids=true | all-gather | bytes 432 | tf_op jit(solution)/shard_map/all_gather | solution.py:77
  565.7 0.7 copy.33
  566.4 5.1 maximum_sqrt_fusion.2
  571.5 0.6 pad_maximum_fusion
  572.1 0.7 copy.41
  572.9 0.7 copy.42
  (18 shorter events, 0.0 us)
Async XLA Ops:
  7.2 483.8 %all-reduce.6.cloned.1.call-start = ((), (), s32[]{:S(2)}) async-start(), calls=%async_computation | async-start | bytes 3145728 | tf_op jit(solution)/shard_map/psum | solution.py:37
  7.2 0.7 copy-start.12
  7.2 2.7 copy-start.13
  7.2 114.5 %copy-start.14 = (f32[64]{0:T(128)S(1)}, f32[64]{0:T(128)}, u32[]{:S(2)}) copy-start(f32[64]{0:T(128)} %param.22) | copy-start | bytes 772
  7.3 114.5 %copy-start.17 = (f32[64]{0:T(128)S(1)}, f32[64]{0:T(128)}, u32[]{:S(2)}) copy-start(f32[64]{0:T(128)} %param.30) | copy-start | bytes 772
  7.3 114.5 %copy-start.18 = (f32[64]{0:T(128)S(1)}, f32[64]{0:T(128)}, u32[]{:S(2)}) copy-start(f32[64]{0:T(128)} %param.26) | copy-start | bytes 772
  7.3 115.7 %copy-start.11 = (f32[4,6]{1,0:T(4,128)S(1)}, f32[4,6]{1,0:T(4,128)}, u32[]{:S(2)}) copy-start(f32[4,6]{1,0:T(4,128)} %param.23) | copy-start | bytes 292
  7.3 115.7 %copy-start.15 = (f32[4,6]{1,0:T(4,128)S(1)}, f32[4,6]{1,0:T(4,128)}, u32[]{:S(2)}) copy-start(f32[4,6]{1,0:T(4,128)} %param.31) | copy-start | bytes 292
  7.3 115.7 %copy-start.16 = (f32[4,6]{1,0:T(4,128)S(1)}, f32[4,6]{1,0:T(4,128)}, u32[]{:S(2)}) copy-start(f32[4,6]{1,0:T(4,128)} %param.27) | copy-start | bytes 292
  7.3 483.6 %copy-start.6 = (f32[64,384]{1,0:T(8,128)S(1)}, f32[64,384]{1,0:T(8,128)}, u32[]{:S(2)}) copy-start(f32[64,384]{1,0:T(8,128)} %param.28) | copy-start | bytes 294916
  7.3 483.6 %copy-start.7 = (f32[64,384]{1,0:T(8,128)S(1)}, f32[64,384]{1,0:T(8,128)}, u32[]{:S(2)}) copy-start(f32[64,384]{1,0:T(8,128)} %param.24) | copy-start | bytes 294916
  7.9 483.0 %copy-start = (f32[64,384]{1,0:T(8,128)S(1)}, f32[64,384]{1,0:T(8,128)}, u32[]{:S(2)}) copy-start(f32[64,384]{1,0:T(8,128)} %param.20) | copy-start | bytes 294916
  491.0 1.7 copy-start.1
  491.0 1.7 copy-start.8
  491.0 1.7 copy-start.9
  492.7 22.6 %copy-start.2 = (f32[64,384]{1,0:T(8,128)}, f32[64,384]{1,0:T(8,128)S(1)}, u32[]{:S(2)}) copy-start(f32[64,384]{1,0:T(8,128)S(1)} %get-tuple-element.100) | copy-start | bytes 294916
  492.7 22.6 %copy-start.3 = (f32[64,384]{1,0:T(8,128)}, f32[64,384]{1,0:T(8,128)S(1)}, u32[]{:S(2)}) copy-start(f32[64,384]{1,0:T(8,128)S(1)} %get-tuple-element.96) | copy-start | bytes 294916
  494.4 35.6 %copy-start.4 = (f32[48,512]{1,0:T(8,128)}, f32[48,512]{1,0:T(8,128)S(1)}, u32[]{:S(2)}) copy-start(f32[48,512]{1,0:T(8,128)S(1)} %get-tuple-element.101) | copy-start | bytes 294916
  494.4 35.6 %copy-start.5 = (f32[48,512]{1,0:T(8,128)}, f32[48,512]{1,0:T(8,128)S(1)}, u32[]{:S(2)}) copy-start(f32[48,512]{1,0:T(8,128)S(1)} %get-tuple-element.97) | copy-start | bytes 294916
  514.1 0.6 copy-start.10
Sparse Core Ops, SparseCore 0:
  13.4 477.5 all-reduce.5
where the time goes:
time: 581 us; the launch traced here: 580 us
  waiting for transfers between devices  367 us (63%)
  blocking collectives  174 us (30%)
  between operations  17.4 us (3%)
  other arithmetic  16.7 us (3%)
    psum x1, waiting for transfers between devices, on_device(): lax.psum((gradients[0], gradients[1], gradients[2], gradients[3]), ('repl...  367 us
    psum x1, blocking collectives, on_device(): lax.psum((gradients[0], gradients[1], gradients[2], gradients[3]), ('repl...  112 us
    psum x1, blocking collectives, on_device(): lax.psum((weight_squares[member], update_squares[member]), 'shard')  14.6 us
    all_gather x1, blocking collectives, on_device(): lax.all_gather(shards[0], 'shard', axis=0, tiled=True)  14 us
    all_gather x1, blocking collectives, on_device(): lax.all_gather(shards[1], 'shard', axis=0, tiled=True)  13 us
    unnamed x1, blocking collectives  12.5 us
  transfers between devices with their start and end apart: 1, of which 1 were waited for; matrix products, arithmetic and copies ran while one was open for 1% of the time, Pallas kernels for 0%

commit v1 on v0

v1 whole, which is shorter than its diff:
```python
import jax
import jax.numpy as jnp
from jax import lax
from jax.sharding import PartitionSpec as P

LANES = 128
SHARD_BITS = (0, 1, 2)
REPLICA_BITS = (3, 5, 4, 6, 7, 8)
AXES = ("replica", "shard")


def step_math(summed, moment, second, weight, decay_rate):
    moment_next = 0.5 * moment + 0.5 * summed
    second_next = 0.5 * second + 0.5 * summed * summed
    update = moment_next / (jnp.sqrt(second_next) + 1e-06) + decay_rate * weight
    return (moment_next, second_next, update)


def padded_width(width, multiple):
    return -(-width // multiple) * multiple


def bit_of(index, bit):
    return (index >> bit) & 1


def exchange(value, bit, devices):
    return lax.ppermute(value, AXES, [(d, d ^ (1 << bit)) for d in range(devices)])


def halve(rows, bits, devices):
    index = lax.axis_index(AXES)
    for bit in bits:
        half = rows.shape[0] // 2
        mine = bit_of(index, bit)
        keep = lax.dynamic_slice_in_dim(rows, mine * half, half, 0)
        send = lax.dynamic_slice_in_dim(rows, (1 - mine) * half, half, 0)
        rows = keep + exchange(send, bit, devices)
    return rows


def double(rows, bits, devices):
    index = lax.axis_index(AXES)
    for bit in reversed(bits):
        other = exchange(rows, bit, devices)
        first = bit_of(index, bit) == 0
        rows = jnp.concatenate([jnp.where(first, rows, other), jnp.where(first, other, rows)], axis=0)
    return rows


def on_device(
    grad_query,
    grad_output,
    grad_norm,
    grad_bias,
    weight_query,
    weight_output,
    weight_norm,
    weight_bias,
    first_query,
    first_output,
    first_norm,
    first_bias,
    second_query,
    second_output,
    second_norm,
    second_bias,
    shards,
    replicas,
):
    weights = (weight_query, weight_output, weight_norm, weight_bias)
    moments = (first_query, first_output, first_norm, first_bias)
    seconds = (second_query, second_output, second_norm, second_bias)
    decay_rates = (0.01, 0.01, 0.0, 0.0)
    gradients = (grad_query[0], grad_output[0], grad_norm[0], grad_bias[0])
    sizes = [weight.size for weight in weights]
    offsets = [sum(sizes[:member]) for member in range(4)]
    total = sum(sizes)
    devices = shards * replicas
    width = padded_width(total, LANES * replicas)
    levels = len(SHARD_BITS)
    position = [sum(((s >> SHARD_BITS[j]) & 1) << (levels - 1 - j) for j in range(levels)) for s in range(shards)]
    blocks = [gradient.reshape(shards, -1) for gradient in gradients]
    filler = jnp.zeros((width - total,), jnp.float32)
    packed = jnp.stack(
        [jnp.concatenate([block[position.index(p)] for block in blocks] + [filler]) for p in range(shards)]
    )
    chunks = packed.reshape(shards * replicas * (width // replicas // LANES), LANES)
    mine = halve(chunks, SHARD_BITS + REPLICA_BITS, devices)
    block = double(mine, REPLICA_BITS, devices)
    summed_flat = block.reshape(width)
    summed_all = [
        summed_flat[offsets[member] : offsets[member] + sizes[member]].reshape(weights[member].shape)
        for member in range(4)
    ]
    results = [
        step_math(
            summed_all[member],
            moments[member],
            seconds[member],
            weights[member],
            decay_rates[member],
        )
        for member in range(4)
    ]
    weight_squares = [jnp.sum(weight * weight) for weight in weights]
    update_squares = [jnp.sum(result[2] * result[2]) for result in results]
    squares = lax.psum(jnp.stack(weight_squares + update_squares), "shard")
    weight_sizes = jnp.sqrt(squares[:4])
    update_sizes = jnp.sqrt(squares[4:])
    trust_ratios = weight_sizes / (update_sizes + 1e-06)
    shards_out = [
        (weights[member] - 0.01 * trust_ratios[member] * results[member][2]).astype(jnp.bfloat16).reshape(-1)
        for member in range(4)
    ]
    out_width = padded_width(total, LANES)
    shards_out.append(jnp.zeros((out_width - total,), jnp.bfloat16))
    gathered = lax.all_gather(jnp.concatenate(shards_out), "shard", axis=0, tiled=False)
    full = [
        gathered[:, offsets[member] : offsets[member] + sizes[member]].reshape(
            (shards * weights[member].shape[0],) + weights[member].shape[1:]
        )
        for member in range(4)
    ]
    norm_table = jnp.stack([weight_sizes, update_sizes])
    return (
        full[0],
        full[1],
        full[2],
        full[3],
        results[0][0],
        results[1][0],
        results[2][0],
        results[3][0],
        results[0][1],
        results[1][1],
        results[2][1],
        results[3][1],
        norm_table,
        trust_ratios,
    )


def solution(mesh):
    shards = mesh.shape["shard"]
    replicas = mesh.shape["replica"]
    placed = (
        P(("replica", "shard"), None, None),
        P(("replica", "shard"), None, None),
        P(("replica", "shard"), None),
        P(("replica", "shard"), None, None),
        P("shard", None),
        P("shard", None),
        P("shard"),
        P("shard", None),
        P("shard", None),
        P("shard", None),
        P("shard"),
        P("shard", None),
        P("shard", None),
        P("shard", None),
        P("shard"),
        P("shard", None),
    )

    def body(*args):
        return on_device(*args, shards=shards, replicas=replicas)

    return jax.shard_map(
        body,
        mesh=mesh,
        in_specs=placed,
        out_specs=(
            P(),
            P(),
            P(),
            P(),
            P("shard", None),
            P("shard", None),
            P("shard"),
            P("shard", None),
            P("shard", None),
            P("shard", None),
            P("shard"),
            P("shard", None),
            P(),
            P(),
        ),
        check_vma=False,
    )
```

time: 581 us -> 206 us (0.35)
  waiting for transfers between devices: 367 us -> 63.6 us
  blocking collectives: 174 us -> 42 us
  starting transfers between devices: 0.04 us -> 57.5 us
  local copies, waits for them, and re-layouts: 4.44 us -> 31.6 us
  between operations: 17.4 us -> 4.1 us
  other arithmetic: 16.7 us -> 6.09 us
    psum x1 -> x0, waiting for transfers between devices: 367 us -> none  [on_device(): lax.psum((gradients[0], gradients[1], gradients[2], gradients[3]), ('repl...]
    psum x2 -> x1, blocking collectives: 126 us -> 26.8 us  [on_device(): squares = lax.psum(jnp.stack(weight_squares + update_squares), 'shard')]
    ppermute x0 -> x15, waiting for transfers between devices: none -> 63.6 us  [exchange(): lax.ppermute(value, AXES, [(d, d ^ 1 << bit) for d in range(devices)])]
    ppermute x0 -> x15, starting transfers between devices: none -> 57.5 us  [exchange(): lax.ppermute(value, AXES, [(d, d ^ 1 << bit) for d in range(devices)])]
    all_gather x3 -> x1, blocking collectives: 35.6 us -> 15.2 us  [on_device(): lax.all_gather(jnp.concatenate(shards_out), 'shard', axis=0, tiled=False)]
    unnamed x1 -> x0, blocking collectives: 12.5 us -> none
    concatenate x0 -> x9, local copies, waits for them, and re-layouts: none -> 10.8 us  [the longest x8 10.6 us: on_device(): jnp.concatenate([block[position.index(p)] for block in blocks] + [filler])]
    another operation x0 -> x2, local copies, waits for them, and re-layouts: none -> 9.87 us  [the longest x1 5.32 us: on_device(): squares = lax.psum(jnp.stack(weight_squares + update_squares), 'shard')]
  transfers between devices with their start and end apart: 1 -> 15, of which waited for: 1 -> 15; matrix products, arithmetic and copies ran while one was open for 1% -> 0% of each run, Pallas kernels for 0% -> 0%
where the time goes in v1:
time: 206 us; the launch traced here: 205 us
  waiting for transfers between devices  63.6 us (31%)
  starting transfers between devices  57.5 us (28%)
  blocking collectives  42 us (20%)
  local copies, waits for them, and re-layouts  31.6 us (15%)
  other arithmetic  6.09 us (3%)
  between operations  4.1 us (2%)
    ppermute x15, waiting for transfers between devices, exchange(): lax.ppermute(value, AXES, [(d, d ^ 1 << bit) for d in range(devices)])  63.6 us
    ppermute x15, starting transfers between devices, exchange(): lax.ppermute(value, AXES, [(d, d ^ 1 << bit) for d in range(devices)])  57.5 us
    psum x1, blocking collectives, on_device(): squares = lax.psum(jnp.stack(weight_squares + update_squares), 'shard')  26.8 us
    all_gather x1, blocking collectives, on_device(): lax.all_gather(jnp.concatenate(shards_out), 'shard', axis=0, tiled=False)  15.2 us
    concatenate x8, local copies, waits for them, and re-layouts, on_device(): jnp.concatenate([block[position.index(p)] for block in blocks] + [filler])  10.6 us
    another operation x1, local copies, waits for them, and re-layouts, on_device(): squares = lax.psum(jnp.stack(weight_squares + update_squares), 'shard')  5.32 us
    another operation x1, local copies, waits for them, and re-layouts, on_device(): jnp.stack([jnp.concatenate([block[position.index(p)] for block in blocks]...  4.55 us
  transfers between devices with their start and end apart: 15, of which 15 were waited for; matrix products, arithmetic and copies ran while one was open for 0% of the time, Pallas kernels for 0%

profile of v1, /device:TPU:1, one launch (start us, length us, event | category | flops | bytes accessed | tf_op | source)
XLA Modules:
  0.0 204.9 jit_solution(14163425917352322013)
XLA Ops:
  0.7 1.3 slice_bitcast_fusion
  4.2 1.0 concatenate.48
  5.1 1.0 concatenate.49
  6.2 1.0 concatenate.50
  7.2 1.0 concatenate.51
  8.2 1.0 concatenate.52
  9.2 1.0 concatenate.45
  10.2 1.0 concatenate.46
  11.2 3.6 %concatenate.47 = f32[57344]{0:T(1024)} concatenate(f32[24576]{0:T(1024)S(1)} %squeeze.108, f32[24576]{0:T(1024)S(1)} %bitcast.90, f32[64]{0:T(128)S(1)} %get-tuple-element.117, f32[24]{0:T(128)S(1)} %squeeze.111, f32[8104]{0:T(1024)S(1)} %broadcast_in_dim.6), dimensions={0} | concatenate | bytes 458752 | tf_op jit(solution)/shard_map/concatenate | solution.py:86
  14.8 4.5 %stack.75 = f32[8,57344]{1,0:T(8,128)S(1)} concatenate(f32[1,57344]{1,0:T(1,128)S(1)} %bitcast.80, f32[1,57344]{1,0:T(1,128)S(1)} %bitcast.81, f32[1,57344]{1,0:T(1,128)} %bitcast.82, f32[1,57344]{1,0:T(1,128)S(1)} %bitcast.75, f32[1,57344]{1,0:T(1,128)S(1)} %bitcast.76, f32[1,57344]{1,0:T(1,128)S(1)} %bitcast.77, f32[1,57344]{1,0:T(1,128)S(1)} %bitcast.78, f32[1,57344]{1,0:T(1,128)S(1)} %bitcast.79), dimensions={0} | concatenate | bytes 3670016 | tf_op jit(solution)/shard_map/stack | solution.py:85
  19.4 1.5 reshape.140
  20.9 1.4 constant_dynamic-slice_fusion.9
  22.3 8.8 %collective-permute-start = (f32[1792,128]{1,0:T(8,128)S(1)}, f32[1792,128]{1,0:T(8,128)}, u32[]{:S(2)}, u32[]{:S(2)}) collective-permute-start(f32[1792,128]{1,0:T(8,128)S(1)} %constant_dynamic-slice_fusion.9), channel_id=1, source_target_pairs={{0,1},{1,0},{2,3},{3,2},{4,5},{5,4},{6,7},{7,6},{8,9},{9,8},{10,11... | collective-permute-start | bytes 2752520 | tf_op jit(solution)/shard_map/ppermute | solution.py:28
  31.1 2.2 %collective-permute-done = f32[1792,128]{1,0:T(8,128)} collective-permute-done((f32[1792,128]{1,0:T(8,128)S(1)}, f32[1792,128]{1,0:T(8,128)}, u32[]{:S(2)}, u32[]{:S(2)}) %collective-permute-start) | collective-permute-done | bytes 917536 | tf_op jit(solution)/shard_map/ppermute | solution.py:28
  33.3 1.3 dynamic-slice_add_fusion
  34.6 1.9 collective-permute-start.1
  36.5 11.7 %collective-permute-done.1 = f32[896,128]{1,0:T(8,128)S(1)} collective-permute-done((f32[896,128]{1,0:T(8,128)S(1)}, f32[896,128]{1,0:T(8,128)S(1)}, u32[]{:S(2)}, u32[]{:S(2)}) %collective-permute-start.1) | collective-permute-done | bytes 458784 | tf_op jit(solution)/shard_map/ppermute | solution.py:28
  48.3 1.9 collective-permute-start.2
  50.3 7.4 %collective-permute-done.2 = f32[448,128]{1,0:T(8,128)S(1)} collective-permute-done((f32[448,128]{1,0:T(8,128)S(1)}, f32[448,128]{1,0:T(8,128)S(1)}, u32[]{:S(2)}, u32[]{:S(2)}) %collective-permute-start.2) | collective-permute-done | bytes 229408 | tf_op jit(solution)/shard_map/ppermute | solution.py:28
  57.7 1.9 collective-permute-start.3
  59.7 3.5 %collective-permute-done.3 = f32[224,128]{1,0:T(8,128)S(1)} collective-permute-done((f32[224,128]{1,0:T(8,128)S(1)}, f32[224,128]{1,0:T(8,128)S(1)}, u32[]{:S(2)}, u32[]{:S(2)}) %collective-permute-start.3) | collective-permute-done | bytes 114720 | tf_op jit(solution)/shard_map/ppermute | solution.py:28
  63.2 1.9 collective-permute-start.4
  65.2 3.0 %collective-permute-done.4 = f32[112,128]{1,0:T(8,128)S(1)} collective-permute-done((f32[112,128]{1,0:T(8,128)S(1)}, f32[112,128]{1,0:T(8,128)S(1)}, u32[]{:S(2)}, u32[]{:S(2)}) %collective-permute-start.4) | collective-permute-done | bytes 57376 | tf_op jit(solution)/shard_map/ppermute | solution.py:28
  68.2 1.9 collective-permute-start.5
  70.2 4.1 %collective-permute-done.5 = f32[56,128]{1,0:T(8,128)S(1)} collective-permute-done((f32[56,128]{1,0:T(8,128)S(1)}, f32[56,128]{1,0:T(8,128)S(1)}, u32[]{:S(2)}, u32[]{:S(2)}) %collective-permute-start.5) | collective-permute-done | bytes 28704 | tf_op jit(solution)/shard_map/ppermute | solution.py:28
  74.3 1.9 collective-permute-start.6
  76.3 3.4 %collective-permute-done.6 = f32[28,128]{1,0:T(8,128)S(1)} collective-permute-done((f32[28,128]{1,0:T(8,128)S(1)}, f32[28,128]{1,0:T(8,128)S(1)}, u32[]{:S(2)}, u32[]{:S(2)}) %collective-permute-start.6) | collective-permute-done | bytes 14368 | tf_op jit(solution)/shard_map/ppermute | solution.py:28
  79.7 4.3 %collective-permute-start.7 = (f32[14,128]{1,0:T(8,128)S(1)}, f32[14,128]{1,0:T(8,128)S(1)}, u32[]{:S(2)}, u32[]{:S(2)}) collective-permute-start(f32[14,128]{1,0:T(8,128)S(1)} %constant_dynamic-slice_fusion.2), channel_id=1, source_target_pairs={{0,128},{1,129},{2,130},{3,131},{4,132},{5,133},{6,134},{7,135},{8... | collective-permute-start | bytes 21512 | tf_op jit(solution)/shard_map/ppermute | solution.py:28
  84.0 4.0 %collective-permute-done.7 = f32[14,128]{1,0:T(8,128)S(1)} collective-permute-done((f32[14,128]{1,0:T(8,128)S(1)}, f32[14,128]{1,0:T(8,128)S(1)}, u32[]{:S(2)}, u32[]{:S(2)}) %collective-permute-start.7) | collective-permute-done | bytes 7200 | tf_op jit(solution)/shard_map/ppermute | solution.py:28
  88.1 10.1 %collective-permute-start.8 = (f32[7,128]{1,0:T(8,128)S(1)}, f32[7,128]{1,0:T(8,128)S(1)}, u32[]{:S(2)}, u32[]{:S(2)}) collective-permute-start(f32[7,128]{1,0:T(8,128)S(1)} %constant_dynamic-slice_fusion), channel_id=1, source_target_pairs={{0,256},{1,257},{2,258},{3,259},{4,260},{5,261},{6,262},{7,263},{8... | collective-permute-start | bytes 10760 | tf_op jit(solution)/shard_map/ppermute | solution.py:28
  98.2 3.0 %collective-permute-done.8 = f32[7,128]{1,0:T(8,128)S(1)} collective-permute-done((f32[7,128]{1,0:T(8,128)S(1)}, f32[7,128]{1,0:T(8,128)S(1)}, u32[]{:S(2)}, u32[]{:S(2)}) %collective-permute-start.8) | collective-permute-done | bytes 3616 | tf_op jit(solution)/shard_map/ppermute | solution.py:28
  101.1 10.1 %collective-permute-start.9 = (f32[7,128]{1,0:T(8,128)S(1)}, f32[7,128]{1,0:T(8,128)S(1)}, u32[]{:S(2)}, u32[]{:S(2)}) collective-permute-start(f32[7,128]{1,0:T(8,128)S(1)} %fusion.5), channel_id=1, source_target_pairs={{0,256},{1,257},{2,258},{3,259},{4,260},{5,261},{6,262},{7,263},{8... | collective-permute-start | bytes 10760 | tf_op jit(solution)/shard_map/ppermute | solution.py:28
  111.2 3.0 %collective-permute-done.9 = f32[7,128]{1,0:T(8,128)S(1)} collective-permute-done((f32[7,128]{1,0:T(8,128)S(1)}, f32[7,128]{1,0:T(8,128)S(1)}, u32[]{:S(2)}, u32[]{:S(2)}) %collective-permute-start.9) | collective-permute-done | bytes 3616 | tf_op jit(solution)/shard_map/ppermute | solution.py:28
  114.2 4.3 %collective-permute-start.10 = (f32[14,128]{1,0:T(8,128)S(1)}, f32[14,128]{1,0:T(8,128)S(1)}, u32[]{:S(2)}, u32[]{:S(2)}) collective-permute-start(f32[14,128]{1,0:T(8,128)S(1)} %pad_maximum_fusion.5), channel_id=1, source_target_pairs={{0,128},{1,129},{2,130},{3,131},{4,132},{5,133},{6,134},{7,135},{8... | collective-permute-start | bytes 21512 | tf_op jit(solution)/shard_map/ppermute | solution.py:28
  118.5 4.3 %collective-permute-done.10 = f32[14,128]{1,0:T(8,128)S(1)} collective-permute-done((f32[14,128]{1,0:T(8,128)S(1)}, f32[14,128]{1,0:T(8,128)S(1)}, u32[]{:S(2)}, u32[]{:S(2)}) %collective-permute-start.10) | collective-permute-done | bytes 7200 | tf_op jit(solution)/shard_map/ppermute | solution.py:28
  122.8 1.9 collective-permute-start.11
  124.8 3.4 %collective-permute-done.11 = f32[28,128]{1,0:T(8,128)S(1)} collective-permute-done((f32[28,128]{1,0:T(8,128)S(1)}, f32[28,128]{1,0:T(8,128)S(1)}, u32[]{:S(2)}, u32[]{:S(2)}) %collective-permute-start.11) | collective-permute-done | bytes 14368 | tf_op jit(solution)/shard_map/ppermute | solution.py:28
  128.2 2.6 %collective-permute-start.12 = (f32[56,128]{1,0:T(8,128)S(1)}, f32[56,128]{1,0:T(8,128)S(1)}, u32[]{:S(2)}, u32[]{:S(2)}) collective-permute-start(f32[56,128]{1,0:T(8,128)S(1)} %pad_maximum_fusion.3), channel_id=1, source_target_pairs={{0,16},{1,17},{2,18},{3,19},{4,20},{5,21},{6,22},{7,23},{8,24},{9,... | collective-permute-start | bytes 86024 | tf_op jit(solution)/shard_map/ppermute | solution.py:28
  130.9 3.5 %collective-permute-done.12 = f32[56,128]{1,0:T(8,128)S(1)} collective-permute-done((f32[56,128]{1,0:T(8,128)S(1)}, f32[56,128]{1,0:T(8,128)S(1)}, u32[]{:S(2)}, u32[]{:S(2)}) %collective-permute-start.12) | collective-permute-done | bytes 28704 | tf_op jit(solution)/shard_map/ppermute | solution.py:28
  134.4 2.0 collective-permute-start.13
  136.4 3.2 %collective-permute-done.13 = f32[112,128]{1,0:T(8,128)S(1)} collective-permute-done((f32[112,128]{1,0:T(8,128)S(1)}, f32[112,128]{1,0:T(8,128)S(1)}, u32[]{:S(2)}, u32[]{:S(2)}) %collective-permute-start.13) | collective-permute-done | bytes 57376 | tf_op jit(solution)/shard_map/ppermute | solution.py:28
  139.6 1.9 collective-permute-start.14
  141.6 3.9 %collective-permute-done.14 = f32[224,128]{1,0:T(8,128)S(1)} collective-permute-done((f32[224,128]{1,0:T(8,128)S(1)}, f32[224,128]{1,0:T(8,128)S(1)}, u32[]{:S(2)}, u32[]{:S(2)}) %collective-permute-start.14) | collective-permute-done | bytes 114720 | tf_op jit(solution)/shard_map/ppermute | solution.py:28
  145.8 1.1 multiply_reduce_fusion.6
  146.9 1.3 multiply_reduce_fusion.4
  149.6 5.3 %stack.80 = f32[8]{0:T(128)S(1)} concatenate(f32[1]{0:T(128)} %bitcast, f32[1]{0:T(128)} %bitcast.1, f32[1]{0:T(128)} %bitcast.2, f32[1]{0:T(128)} %bitcast.3, f32[1]{0:T(128)} %bitcast.20, f32[1]{0:T(128)} %bitcast.21, f32[1]{0:T(128)} %bitcast.23, f32[1]{0:T(128)} %bitcast.24), dimensions={0} | concatenate | bytes 64 | tf_op jit(solution)/shard_map/stack | solution.py:108
  154.9 26.8 %psum.7 = f32[8]{0:T(128)S(1)} all-reduce(f32[8]{0:T(128)S(1)} %stack.80), channel_id=1, replica_groups=mesh['replica'=64,'shard'=8] {'shard'}, use_global_device_ids=true, to_apply=%region_8.9 | all-reduce | flops 8 | bytes 64 | tf_op jit(solution)/shard_map/psum | solution.py:108
  185.6 15.2 %all-gather.1 = bf16[8,1,49280]{2,1,0:T(2,128)(2,1)S(1)} all-gather(bf16[1,1,49280]{2,1,0:T(2,128)(2,1)S(1)} %reshape.153), channel_id=2, replica_groups=mesh['replica'=64,'shard'=8] {'shard'}, dimensions={0}, use_global_device_ids=true | all-gather | bytes 887040 | tf_op jit(solution)/shard_map/all_gather | solution.py:118
  (135 shorter events, 9.3 us)
Async XLA Ops:
  0.6 1.5 copy-start.1
  0.7 1.5 copy-start.8
  0.7 1.8 copy-start.14
  20.9 12.4 %copy-start = (f32[3584,128]{1,0:T(8,128)S(1)}, f32[3584,128]{1,0:T(8,128)}, u32[]{:S(2)}) copy-start(f32[3584,128]{1,0:T(8,128)} %reshape.140) | copy-start | bytes 5505028
  22.3 11.0 %collective-permute-start = (f32[1792,128]{1,0:T(8,128)S(1)}, f32[1792,128]{1,0:T(8,128)}, u32[]{:S(2)}, u32[]{:S(2)}) collective-permute-start(f32[1792,128]{1,0:T(8,128)S(1)} %constant_dynamic-slice_fusion.9), channel_id=1, source_target_pairs={{0,1},{1,0},{2,3},{3,2},{4,5},{5,4},{6,7},{7,6},{8,9},{9,8},{10,11... | collective-permute-start | bytes 2752520 | tf_op jit(solution)/shard_map/ppermute | solution.py:28
  34.6 13.6 %collective-permute-start.1 = (f32[896,128]{1,0:T(8,128)S(1)}, f32[896,128]{1,0:T(8,128)S(1)}, u32[]{:S(2)}, u32[]{:S(2)}) collective-permute-start(f32[896,128]{1,0:T(8,128)S(1)} %constant_dynamic-slice_fusion.8), channel_id=1, source_target_pairs={{0,2},{1,3},{2,0},{3,1},{4,6},{5,7},{6,4},{7,5},{8,10},{9,11},{10,... | collective-permute-start | bytes 1376264 | tf_op jit(solution)/shard_map/ppermute | solution.py:28
  48.3 9.3 %collective-permute-start.2 = (f32[448,128]{1,0:T(8,128)S(1)}, f32[448,128]{1,0:T(8,128)S(1)}, u32[]{:S(2)}, u32[]{:S(2)}) collective-permute-start(f32[448,128]{1,0:T(8,128)S(1)} %constant_dynamic-slice_fusion.7), channel_id=1, source_target_pairs={{0,4},{1,5},{2,6},{3,7},{4,0},{5,1},{6,2},{7,3},{8,12},{9,13},{10,... | collective-permute-start | bytes 688136 | tf_op jit(solution)/shard_map/ppermute | solution.py:28
  57.7 5.5 %collective-permute-start.3 = (f32[224,128]{1,0:T(8,128)S(1)}, f32[224,128]{1,0:T(8,128)S(1)}, u32[]{:S(2)}, u32[]{:S(2)}) collective-permute-start(f32[224,128]{1,0:T(8,128)S(1)} %constant_dynamic-slice_fusion.6), channel_id=1, source_target_pairs={{0,8},{1,9},{2,10},{3,11},{4,12},{5,13},{6,14},{7,15},{8,0},{9,1},... | collective-permute-start | bytes 344072 | tf_op jit(solution)/shard_map/ppermute | solution.py:28
  59.6 86.2 %copy-start.18 = (f32[64]{0:T(128)S(1)}, f32[64]{0:T(128)}, u32[]{:S(2)}) copy-start(f32[64]{0:T(128)} %param.22) | copy-start | bytes 772
  59.6 86.2 %copy-start.19 = (f32[64]{0:T(128)S(1)}, f32[64]{0:T(128)}, u32[]{:S(2)}) copy-start(f32[64]{0:T(128)} %param.30) | copy-start | bytes 772
  59.6 86.2 %copy-start.20 = (f32[64]{0:T(128)S(1)}, f32[64]{0:T(128)}, u32[]{:S(2)}) copy-start(f32[64]{0:T(128)} %param.26) | copy-start | bytes 772
  59.6 87.3 %copy-start.15 = (f32[4,6]{1,0:T(4,128)S(1)}, f32[4,6]{1,0:T(4,128)}, u32[]{:S(2)}) copy-start(f32[4,6]{1,0:T(4,128)} %param.23) | copy-start | bytes 292
  59.7 87.3 %copy-start.16 = (f32[4,6]{1,0:T(4,128)S(1)}, f32[4,6]{1,0:T(4,128)}, u32[]{:S(2)}) copy-start(f32[4,6]{1,0:T(4,128)} %param.31) | copy-start | bytes 292
  59.7 87.3 %copy-start.17 = (f32[4,6]{1,0:T(4,128)S(1)}, f32[4,6]{1,0:T(4,128)}, u32[]{:S(2)}) copy-start(f32[4,6]{1,0:T(4,128)} %param.27) | copy-start | bytes 292
  59.7 88.5 %copy-start.3 = (f32[64,384]{1,0:T(8,128)S(1)}, f32[64,384]{1,0:T(8,128)}, u32[]{:S(2)}) copy-start(f32[64,384]{1,0:T(8,128)} %param.20) | copy-start | bytes 294916
  59.7 88.5 %copy-start.9 = (f32[64,384]{1,0:T(8,128)S(1)}, f32[64,384]{1,0:T(8,128)}, u32[]{:S(2)}) copy-start(f32[64,384]{1,0:T(8,128)} %param.28) | copy-start | bytes 294916
  59.7 88.5 %copy-start.10 = (f32[64,384]{1,0:T(8,128)S(1)}, f32[64,384]{1,0:T(8,128)}, u32[]{:S(2)}) copy-start(f32[64,384]{1,0:T(8,128)} %param.24) | copy-start | bytes 294916
  63.2 4.9 %collective-permute-start.4 = (f32[112,128]{1,0:T(8,128)S(1)}, f32[112,128]{1,0:T(8,128)S(1)}, u32[]{:S(2)}, u32[]{:S(2)}) collective-permute-start(f32[112,128]{1,0:T(8,128)S(1)} %constant_dynamic-slice_fusion.5), channel_id=1, source_target_pairs={{0,32},{1,33},{2,34},{3,35},{4,36},{5,37},{6,38},{7,39},{8,40},{9,... | collective-permute-start | bytes 172040 | tf_op jit(solution)/shard_map/ppermute | solution.py:28
  68.2 6.1 %collective-permute-start.5 = (f32[56,128]{1,0:T(8,128)S(1)}, f32[56,128]{1,0:T(8,128)S(1)}, u32[]{:S(2)}, u32[]{:S(2)}) collective-permute-start(f32[56,128]{1,0:T(8,128)S(1)} %constant_dynamic-slice_fusion.4), channel_id=1, source_target_pairs={{0,16},{1,17},{2,18},{3,19},{4,20},{5,21},{6,22},{7,23},{8,24},{9,... | collective-permute-start | bytes 86024 | tf_op jit(solution)/shard_map/ppermute | solution.py:28
  70.1 78.8 %copy-start.2 = (f32[48,512]{1,0:T(8,128)S(1)}, f32[48,512]{1,0:T(8,128)}, u32[]{:S(2)}) copy-start(f32[48,512]{1,0:T(8,128)} %param.21) | copy-start | bytes 294916
  70.1 78.8 %copy-start.11 = (f32[48,512]{1,0:T(8,128)S(1)}, f32[48,512]{1,0:T(8,128)}, u32[]{:S(2)}) copy-start(f32[48,512]{1,0:T(8,128)} %param.29) | copy-start | bytes 294916
  70.2 78.7 %copy-start.12 = (f32[48,512]{1,0:T(8,128)S(1)}, f32[48,512]{1,0:T(8,128)}, u32[]{:S(2)}) copy-start(f32[48,512]{1,0:T(8,128)} %param.25) | copy-start | bytes 294916
  74.3 5.4 %collective-permute-start.6 = (f32[28,128]{1,0:T(8,128)S(1)}, f32[28,128]{1,0:T(8,128)S(1)}, u32[]{:S(2)}, u32[]{:S(2)}) collective-permute-start(f32[28,128]{1,0:T(8,128)S(1)} %constant_dynamic-slice_fusion.3), channel_id=1, source_target_pairs={{0,64},{1,65},{2,66},{3,67},{4,68},{5,69},{6,70},{7,71},{8,72},{9,... | collective-permute-start | bytes 43016 | tf_op jit(solution)/shard_map/ppermute | solution.py:28
  79.7 8.3 %collective-permute-start.7 = (f32[14,128]{1,0:T(8,128)S(1)}, f32[14,128]{1,0:T(8,128)S(1)}, u32[]{:S(2)}, u32[]{:S(2)}) collective-permute-start(f32[14,128]{1,0:T(8,128)S(1)} %constant_dynamic-slice_fusion.2), channel_id=1, source_target_pairs={{0,128},{1,129},{2,130},{3,131},{4,132},{5,133},{6,134},{7,135},{8... | collective-permute-start | bytes 21512 | tf_op jit(solution)/shard_map/ppermute | solution.py:28
  88.1 13.1 %collective-permute-start.8 = (f32[7,128]{1,0:T(8,128)S(1)}, f32[7,128]{1,0:T(8,128)S(1)}, u32[]{:S(2)}, u32[]{:S(2)}) collective-permute-start(f32[7,128]{1,0:T(8,128)S(1)} %constant_dynamic-slice_fusion), channel_id=1, source_target_pairs={{0,256},{1,257},{2,258},{3,259},{4,260},{5,261},{6,262},{7,263},{8... | collective-permute-start | bytes 10760 | tf_op jit(solution)/shard_map/ppermute | solution.py:28
  101.1 13.1 %collective-permute-start.9 = (f32[7,128]{1,0:T(8,128)S(1)}, f32[7,128]{1,0:T(8,128)S(1)}, u32[]{:S(2)}, u32[]{:S(2)}) collective-permute-start(f32[7,128]{1,0:T(8,128)S(1)} %fusion.5), channel_id=1, source_target_pairs={{0,256},{1,257},{2,258},{3,259},{4,260},{5,261},{6,262},{7,263},{8... | collective-permute-start | bytes 10760 | tf_op jit(solution)/shard_map/ppermute | solution.py:28
  114.2 8.6 %collective-permute-start.10 = (f32[14,128]{1,0:T(8,128)S(1)}, f32[14,128]{1,0:T(8,128)S(1)}, u32[]{:S(2)}, u32[]{:S(2)}) collective-permute-start(f32[14,128]{1,0:T(8,128)S(1)} %pad_maximum_fusion.5), channel_id=1, source_target_pairs={{0,128},{1,129},{2,130},{3,131},{4,132},{5,133},{6,134},{7,135},{8... | collective-permute-start | bytes 21512 | tf_op jit(solution)/shard_map/ppermute | solution.py:28
  122.8 5.4 %collective-permute-start.11 = (f32[28,128]{1,0:T(8,128)S(1)}, f32[28,128]{1,0:T(8,128)S(1)}, u32[]{:S(2)}, u32[]{:S(2)}) collective-permute-start(f32[28,128]{1,0:T(8,128)S(1)} %pad_maximum_fusion.4), channel_id=1, source_target_pairs={{0,64},{1,65},{2,66},{3,67},{4,68},{5,69},{6,70},{7,71},{8,72},{9,... | collective-permute-start | bytes 43016 | tf_op jit(solution)/shard_map/ppermute | solution.py:28
  128.2 6.1 %collective-permute-start.12 = (f32[56,128]{1,0:T(8,128)S(1)}, f32[56,128]{1,0:T(8,128)S(1)}, u32[]{:S(2)}, u32[]{:S(2)}) collective-permute-start(f32[56,128]{1,0:T(8,128)S(1)} %pad_maximum_fusion.3), channel_id=1, source_target_pairs={{0,16},{1,17},{2,18},{3,19},{4,20},{5,21},{6,22},{7,23},{8,24},{9,... | collective-permute-start | bytes 86024 | tf_op jit(solution)/shard_map/ppermute | solution.py:28
  134.4 5.2 %collective-permute-start.13 = (f32[112,128]{1,0:T(8,128)S(1)}, f32[112,128]{1,0:T(8,128)S(1)}, u32[]{:S(2)}, u32[]{:S(2)}) collective-permute-start(f32[112,128]{1,0:T(8,128)S(1)} %pad_maximum_fusion.2), channel_id=1, source_target_pairs={{0,32},{1,33},{2,34},{3,35},{4,36},{5,37},{6,38},{7,39},{8,40},{9,... | collective-permute-start | bytes 172040 | tf_op jit(solution)/shard_map/ppermute | solution.py:28
  139.6 5.8 %collective-permute-start.14 = (f32[224,128]{1,0:T(8,128)S(1)}, f32[224,128]{1,0:T(8,128)S(1)}, u32[]{:S(2)}, u32[]{:S(2)}) collective-permute-start(f32[224,128]{1,0:T(8,128)S(1)} %pad_maximum_fusion.1), channel_id=1, source_target_pairs={{0,8},{1,9},{2,10},{3,11},{4,12},{5,13},{6,14},{7,15},{8,0},{9,1},... | collective-permute-start | bytes 344072 | tf_op jit(solution)/shard_map/ppermute | solution.py:28
  148.9 51.9 %copy-start.4 = (f32[64,384]{1,0:T(8,128)}, f32[64,384]{1,0:T(8,128)S(1)}, u32[]{:S(2)}) copy-start(f32[64,384]{1,0:T(8,128)S(1)} %get-tuple-element.70) | copy-start | bytes 294916
  148.9 51.9 %copy-start.5 = (f32[64,384]{1,0:T(8,128)}, f32[64,384]{1,0:T(8,128)S(1)}, u32[]{:S(2)}) copy-start(f32[64,384]{1,0:T(8,128)S(1)} %get-tuple-element.71) | copy-start | bytes 294916
  149.6 51.3 %copy-start.6 = (f32[48,512]{1,0:T(8,128)}, f32[48,512]{1,0:T(8,128)S(1)}, u32[]{:S(2)}) copy-start(f32[48,512]{1,0:T(8,128)S(1)} %get-tuple-element.68) | copy-start | bytes 294916
  149.6 51.3 %copy-start.7 = (f32[48,512]{1,0:T(8,128)}, f32[48,512]{1,0:T(8,128)S(1)}, u32[]{:S(2)}) copy-start(f32[48,512]{1,0:T(8,128)S(1)} %get-tuple-element.69) | copy-start | bytes 294916
  181.8 19.1 %copy-start.13 = (f32[4]{0:T(128)}, f32[4]{0:T(128)S(1)}, u32[]{:S(2)}) copy-start(f32[4]{0:T(128)S(1)} %get-tuple-element.123) | copy-start | bytes 52

commit v2 on v1

--- a/solution.py
+++ b/solution.py
@@ -4,8 +4,8 @@
 from jax.sharding import PartitionSpec as P
 
 LANES = 128
-SHARD_BITS = (0, 1, 2)
-REPLICA_BITS = (3, 5, 4, 6, 7, 8)
+SHARD_GROUPS = ((0,), (1, 2))
+REPLICA_GROUPS = ((3, 5), (4, 6), (7, 8))
 AXES = ("replica", "shard")
 
 
@@ -24,27 +24,52 @@
     return (index >> bit) & 1
 
 
-def exchange(value, bit, devices):
-    return lax.ppermute(value, AXES, [(d, d ^ (1 << bit)) for d in range(devices)])
-
-
-def halve(rows, bits, devices):
+def exchange(value, mask, devices):
+    return lax.ppermute(value, AXES, [(d, d ^ mask) for d in range(devices)])
+
+
+def masks_of(group):
+    width = len(group)
+    return [
+        sum(((t >> (width - 1 - j)) & 1) << group[j] for j in range(width))
+        for t in range(1 << width)
+    ]
+
+
+def part_of(index, group):
+    return sum(bit_of(index, bit) << (len(group) - 1 - j) for j, bit in enumerate(group))
+
+
+def halve(rows, groups, devices):
     index = lax.axis_index(AXES)
-    for bit in bits:
-        half = rows.shape[0] // 2
-        mine = bit_of(index, bit)
-        keep = lax.dynamic_slice_in_dim(rows, mine * half, half, 0)
-        send = lax.dynamic_slice_in_dim(rows, (1 - mine) * half, half, 0)
-        rows = keep + exchange(send, bit, devices)
+    for group in groups:
+        count = 1 << len(group)
+        size = rows.shape[0] // count
+        mine = part_of(index, group)
+        masks = masks_of(group)
+        total = lax.dynamic_slice_in_dim(rows, mine * size, size, 0)
+        for t in range(1, count):
+            part = lax.dynamic_slice_in_dim(rows, (mine ^ t) * size, size, 0)
+            total = total + exchange(part, masks[t], devices)
+        rows = total
     return rows
 
 
-def double(rows, bits, devices):
+def double(rows, groups, devices):
     index = lax.axis_index(AXES)
-    for bit in reversed(bits):
-        other = exchange(rows, bit, devices)
-        first = bit_of(index, bit) == 0
-        rows = jnp.concatenate([jnp.where(first, rows, other), jnp.where(first, other, rows)], axis=0)
+    for group in reversed(groups):
+        count = 1 << len(group)
+        mine = part_of(index, group)
+        masks = masks_of(group)
+        got = [rows] + [exchange(rows, masks[t], devices) for t in range(1, count)]
+        ordered = []
+        for j in range(count):
+            owner = mine ^ j
+            pick = got[0]
+            for t in range(1, count):
+                pick = jnp.where(owner == t, got[t], pick)
+            ordered.append(pick)
+        rows = jnp.concatenate(ordered, axis=0)
     return rows
 
 
@@ -78,16 +103,15 @@
     total = sum(sizes)
     devices = shards * replicas
     width = padded_width(total, LANES * replicas)
-    levels = len(SHARD_BITS)
-    position = [sum(((s >> SHARD_BITS[j]) & 1) << (levels - 1 - j) for j in range(levels)) for s in range(shards)]
-    blocks = [gradient.reshape(shards, -1) for gradient in gradients]
-    filler = jnp.zeros((width - total,), jnp.float32)
-    packed = jnp.stack(
-        [jnp.concatenate([block[position.index(p)] for block in blocks] + [filler]) for p in range(shards)]
-    )
+    rows = [gradient.reshape(shards, -1) for gradient in gradients]
+    rows.append(jnp.zeros((shards, width - total), jnp.float32))
+    packed = jnp.concatenate(rows, axis=1)
+    levels = shards.bit_length() - 1
+    packed = packed.reshape((2,) * levels + (width,))
+    packed = packed.transpose(tuple(reversed(range(levels))) + (levels,))
     chunks = packed.reshape(shards * replicas * (width // replicas // LANES), LANES)
-    mine = halve(chunks, SHARD_BITS + REPLICA_BITS, devices)
-    block = double(mine, REPLICA_BITS, devices)
+    mine = halve(chunks, SHARD_GROUPS + REPLICA_GROUPS, devices)
+    block = double(mine, REPLICA_GROUPS, devices)
     summed_flat = block.reshape(width)
     summed_all = [
         summed_flat[offsets[member] : offsets[member] + sizes[member]].reshape(weights[member].shape)

time: 206 us -> 198 us (0.961)
  waiting for transfers between devices: 63.6 us -> 29.2 us
  starting transfers between devices: 57.5 us -> 91.5 us
  local copies, waits for them, and re-layouts: 31.6 us -> 26.5 us
  blocking collectives: 42 us -> 38.5 us
    ppermute x15 -> x22, waiting for transfers between devices: 63.6 us -> 29.2 us  [exchange(): return lax.ppermute(value, AXES, [(d, d ^ mask) for d in range(devices)])]
    ppermute x15 -> x22, starting transfers between devices: 57.5 us -> 91.5 us  [exchange(): return lax.ppermute(value, AXES, [(d, d ^ mask) for d in range(devices)])]
    another operation x1 -> x0, local copies, waits for them, and re-layouts: 4.55 us -> none  [on_device(): jnp.stack([jnp.concatenate([block[position.index(p)] for block in blocks]...]
    concatenate x8 -> x5, local copies, waits for them, and re-layouts: 10.6 us -> 6.29 us  [on_device(): packed = jnp.concatenate(rows, axis=1)]
    psum x1, blocking collectives: 26.8 us -> 23.3 us  [on_device(): squares = lax.psum(jnp.stack(weight_squares + update_squares), 'shard')]
    transpose x0 -> x1, local copies, waits for them, and re-layouts: none -> 2.92 us  [on_device(): packed = packed.transpose(tuple(reversed(range(levels))) + (levels,))]
  transfers between devices with their start and end apart: 15 -> 22, of which waited for: 15 -> 11; matrix products, arithmetic and copies ran while one was open for 0% -> 0% of each run, Pallas kernels for 0% -> 0%
where the time goes in v2:
time: 198 us; the launch traced here: 197 us
  starting transfers between devices  91.5 us (46%)
  blocking collectives  38.5 us (19%)
  waiting for transfers between devices  29.2 us (15%)
  local copies, waits for them, and re-layouts  26.5 us (13%)
  other arithmetic  6.74 us (3%)
  between operations  4.2 us (2%)
    ppermute x22, starting transfers between devices, exchange(): return lax.ppermute(value, AXES, [(d, d ^ mask) for d in range(devices)])  91.5 us
    ppermute x22, waiting for transfers between devices, exchange(): return lax.ppermute(value, AXES, [(d, d ^ mask) for d in range(devices)])  29.2 us
    psum x1, blocking collectives, on_device(): squares = lax.psum(jnp.stack(weight_squares + update_squares), 'shard')  23.3 us
    all_gather x1, blocking collectives, on_device(): lax.all_gather(jnp.concatenate(shards_out), 'shard', axis=0, tiled=False)  15.2 us
    concatenate x5, local copies, waits for them, and re-layouts, on_device(): packed = jnp.concatenate(rows, axis=1)  6.29 us
    another operation x1, local copies, waits for them, and re-layouts, on_device(): squares = lax.psum(jnp.stack(weight_squares + update_squares), 'shard')  5.26 us
  transfers between devices with their start and end apart: 22, of which 11 were waited for; matrix products, arithmetic and copies ran while one was open for 0% of the time, Pallas kernels for 0%

profile of v2, /device:TPU:1, one launch (start us, length us, event | category | flops | bytes accessed | tf_op | source)
XLA Modules:
  0.0 196.7 jit_solution(4432313228246713614)
XLA Ops:
  0.7 1.7 concatenate.30
  4.9 0.7 dynamic-update-slice.3
  5.7 3.8 %dynamic-update-slice.4 = f32[2,2,2,57344]{3,2,1,0:T(2,128)S(1)} dynamic-update-slice(f32[2,2,2,57344]{3,2,1,0:T(2,128)S(1)} %dynamic-update-slice.3, f32[2,2,2,8104]{3,2,1,0:T(2,128)S(1)} %broadcast_in_dim.6, s32[]{} %constant.79, s32[]{} %constant.79, s32[]{} %constant.79, s32[]{} %constant.83) | dynamic-update-slice | bytes 518660 | tf_op jit(solution)/shard_map/concatenate | solution.py:108
  9.5 1.3 copy-done.1
  10.7 2.9 %copy.38 = f32[2,2,2,57344]{3,2,1,0:T(2,128)S(1)} copy(f32[2,2,2,57344]{3,0,1,2:T(2,128)} %bitcast.25) | data formatting | bytes 3670016 | tf_op jit(solution)/shard_map/transpose | solution.py:111
  13.6 2.8 %reshape.86 = f32[3584,128]{1,0:T(8,128)} reshape(f32[2,2,2,57344]{3,2,1,0:T(2,128)S(1)} %copy.38) | data formatting | bytes 3670016 | tf_op jit(solution)/shard_map/reshape | solution.py:112
  16.4 1.4 constant_dynamic-slice_fusion.13
  17.8 8.8 %collective-permute-start = (f32[1792,128]{1,0:T(8,128)S(1)}, f32[1792,128]{1,0:T(8,128)}, u32[]{:S(2)}, u32[]{:S(2)}) collective-permute-start(f32[1792,128]{1,0:T(8,128)S(1)} %constant_dynamic-slice_fusion.13), channel_id=1, source_target_pairs={{0,1},{1,0},{2,3},{3,2},{4,5},{5,4},{6,7},{7,6},{8,9},{9,8},{10,11... | collective-permute-start | bytes 2752520 | tf_op jit(solution)/shard_map/ppermute | solution.py:28
  26.6 2.2 %collective-permute-done = f32[1792,128]{1,0:T(8,128)} collective-permute-done((f32[1792,128]{1,0:T(8,128)S(1)}, f32[1792,128]{1,0:T(8,128)}, u32[]{:S(2)}, u32[]{:S(2)}) %collective-permute-start) | collective-permute-done | bytes 917536 | tf_op jit(solution)/shard_map/ppermute | solution.py:28
  28.8 1.3 dynamic-slice_add_fusion
  30.1 1.9 collective-permute-start.3
  32.1 1.9 collective-permute-start.2
  34.0 5.7 %collective-permute-start.1 = (f32[448,128]{1,0:T(8,128)S(1)}, f32[448,128]{1,0:T(8,128)S(1)}, u32[]{:S(2)}, u32[]{:S(2)}) collective-permute-start(f32[448,128]{1,0:T(8,128)S(1)} %get-tuple-element.72), channel_id=1, source_target_pairs={{0,4},{1,5},{2,6},{3,7},{4,0},{5,1},{6,2},{7,3},{8,12},{9,13},{10,... | collective-permute-start | bytes 688136 | tf_op jit(solution)/shard_map/ppermute | solution.py:28
  40.1 0.7 collective-permute-done.2
  40.8 7.0 %collective-permute-done.1 = f32[448,128]{1,0:T(8,128)S(1)} collective-permute-done((f32[448,128]{1,0:T(8,128)S(1)}, f32[448,128]{1,0:T(8,128)S(1)}, u32[]{:S(2)}, u32[]{:S(2)}) %collective-permute-start.1) | collective-permute-done | bytes 229408 | tf_op jit(solution)/shard_map/ppermute | solution.py:28
  47.9 2.1 %collective-permute-start.6 = (f32[112,128]{1,0:T(8,128)S(1)}, f32[112,128]{1,0:T(8,128)S(1)}, u32[]{:S(2)}, u32[]{:S(2)}) collective-permute-start(f32[112,128]{1,0:T(8,128)S(1)} %get-tuple-element.82), channel_id=1, source_target_pairs={{0,40},{1,41},{2,42},{3,43},{4,44},{5,45},{6,46},{7,47},{8,32},{9,... | collective-permute-start | bytes 172040 | tf_op jit(solution)/shard_map/ppermute | solution.py:28
  50.0 1.9 collective-permute-start.5
  51.9 4.5 %collective-permute-start.4 = (f32[112,128]{1,0:T(8,128)S(1)}, f32[112,128]{1,0:T(8,128)S(1)}, u32[]{:S(2)}, u32[]{:S(2)}) collective-permute-start(f32[112,128]{1,0:T(8,128)S(1)} %get-tuple-element.81), channel_id=1, source_target_pairs={{0,32},{1,33},{2,34},{3,35},{4,36},{5,37},{6,38},{7,39},{8,40},{9,... | collective-permute-start | bytes 172040 | tf_op jit(solution)/shard_map/ppermute | solution.py:28
  56.5 1.5 collective-permute-done.4
  58.1 3.9 %collective-permute-start.9 = (f32[28,128]{1,0:T(8,128)S(1)}, f32[28,128]{1,0:T(8,128)S(1)}, u32[]{:S(2)}, u32[]{:S(2)}) collective-permute-start(f32[28,128]{1,0:T(8,128)S(1)} %get-tuple-element.91), channel_id=1, source_target_pairs={{0,80},{1,81},{2,82},{3,83},{4,84},{5,85},{6,86},{7,87},{8,88},{9,... | collective-permute-start | bytes 43016 | tf_op jit(solution)/shard_map/ppermute | solution.py:28
  62.0 2.4 %collective-permute-start.8 = (f32[28,128]{1,0:T(8,128)S(1)}, f32[28,128]{1,0:T(8,128)S(1)}, u32[]{:S(2)}, u32[]{:S(2)}) collective-permute-start(f32[28,128]{1,0:T(8,128)S(1)} %get-tuple-element.92), channel_id=1, source_target_pairs={{0,16},{1,17},{2,18},{3,19},{4,20},{5,21},{6,22},{7,23},{8,24},{9,... | collective-permute-start | bytes 43016 | tf_op jit(solution)/shard_map/ppermute | solution.py:28
  64.4 4.6 %collective-permute-start.7 = (f32[28,128]{1,0:T(8,128)S(1)}, f32[28,128]{1,0:T(8,128)S(1)}, u32[]{:S(2)}, u32[]{:S(2)}) collective-permute-start(f32[28,128]{1,0:T(8,128)S(1)} %get-tuple-element.90), channel_id=1, source_target_pairs={{0,64},{1,65},{2,66},{3,67},{4,68},{5,69},{6,70},{7,71},{8,72},{9,... | collective-permute-start | bytes 43016 | tf_op jit(solution)/shard_map/ppermute | solution.py:28
  69.1 1.1 collective-permute-done.7
  70.2 9.4 %collective-permute-start.12 = (f32[7,128]{1,0:T(8,128)S(1)}, f32[7,128]{1,0:T(8,128)S(1)}, u32[]{:S(2)}, u32[]{:S(2)}) collective-permute-start(f32[7,128]{1,0:T(8,128)S(1)} %get-tuple-element.98), channel_id=1, source_target_pairs={{0,384},{1,385},{2,386},{3,387},{4,388},{5,389},{6,390},{7,391},{8... | collective-permute-start | bytes 10760 | tf_op jit(solution)/shard_map/ppermute | solution.py:28
  79.6 5.2 %collective-permute-start.11 = (f32[7,128]{1,0:T(8,128)S(1)}, f32[7,128]{1,0:T(8,128)S(1)}, u32[]{:S(2)}, u32[]{:S(2)}) collective-permute-start(f32[7,128]{1,0:T(8,128)S(1)} %get-tuple-element.99), channel_id=1, source_target_pairs={{0,128},{1,129},{2,130},{3,131},{4,132},{5,133},{6,134},{7,135},{8... | collective-permute-start | bytes 10760 | tf_op jit(solution)/shard_map/ppermute | solution.py:28
  84.8 3.7 %collective-permute-start.10 = (f32[7,128]{1,0:T(8,128)S(1)}, f32[7,128]{1,0:T(8,128)S(1)}, u32[]{:S(2)}, u32[]{:S(2)}) collective-permute-start(f32[7,128]{1,0:T(8,128)S(1)} %get-tuple-element.97), channel_id=1, source_target_pairs={{0,256},{1,257},{2,258},{3,259},{4,260},{5,261},{6,262},{7,263},{8... | collective-permute-start | bytes 10760 | tf_op jit(solution)/shard_map/ppermute | solution.py:28
  88.6 9.3 %collective-permute-done.10 = f32[7,128]{1,0:T(8,128)S(1)} collective-permute-done((f32[7,128]{1,0:T(8,128)S(1)}, f32[7,128]{1,0:T(8,128)S(1)}, u32[]{:S(2)}, u32[]{:S(2)}) %collective-permute-start.10) | collective-permute-done | bytes 3616 | tf_op jit(solution)/shard_map/ppermute | solution.py:28
  97.9 3.1 %collective-permute-start.13 = (f32[7,128]{1,0:T(8,128)S(1)}, f32[7,128]{1,0:T(8,128)S(1)}, u32[]{:S(2)}, u32[]{:S(2)}) collective-permute-start(f32[7,128]{1,0:T(8,128)S(1)} %fusion.5), channel_id=1, source_target_pairs={{0,384},{1,385},{2,386},{3,387},{4,388},{5,389},{6,390},{7,391},{8... | collective-permute-start | bytes 10760 | tf_op jit(solution)/shard_map/ppermute | solution.py:28
  101.0 2.9 %collective-permute-start.14 = (f32[7,128]{1,0:T(8,128)S(1)}, f32[7,128]{1,0:T(8,128)S(1)}, u32[]{:S(2)}, u32[]{:S(2)}) collective-permute-start(f32[7,128]{1,0:T(8,128)S(1)} %fusion.5), channel_id=1, source_target_pairs={{0,128},{1,129},{2,130},{3,131},{4,132},{5,133},{6,134},{7,135},{8... | collective-permute-start | bytes 10760 | tf_op jit(solution)/shard_map/ppermute | solution.py:28
  103.8 10.3 %collective-permute-start.15 = (f32[7,128]{1,0:T(8,128)S(1)}, f32[7,128]{1,0:T(8,128)S(1)}, u32[]{:S(2)}, u32[]{:S(2)}) collective-permute-start(f32[7,128]{1,0:T(8,128)S(1)} %fusion.5), channel_id=1, source_target_pairs={{0,256},{1,257},{2,258},{3,259},{4,260},{5,261},{6,262},{7,263},{8... | collective-permute-start | bytes 10760 | tf_op jit(solution)/shard_map/ppermute | solution.py:28
  114.2 2.7 %collective-permute-done.15 = f32[7,128]{1,0:T(8,128)S(1)} collective-permute-done((f32[7,128]{1,0:T(8,128)S(1)}, f32[7,128]{1,0:T(8,128)S(1)}, u32[]{:S(2)}, u32[]{:S(2)}) %collective-permute-start.15) | collective-permute-done | bytes 3616 | tf_op jit(solution)/shard_map/ppermute | solution.py:28
  116.9 5.4 %collective-permute-start.16 = (f32[28,128]{1,0:T(8,128)S(1)}, f32[28,128]{1,0:T(8,128)S(1)}, u32[]{:S(2)}, u32[]{:S(2)}) collective-permute-start(f32[28,128]{1,0:T(8,128)S(1)} %pad_maximum_fusion.4), channel_id=1, source_target_pairs={{0,80},{1,81},{2,82},{3,83},{4,84},{5,85},{6,86},{7,87},{8,88},{9,... | collective-permute-start | bytes 43016 | tf_op jit(solution)/shard_map/ppermute | solution.py:28
  122.3 2.3 %collective-permute-start.17 = (f32[28,128]{1,0:T(8,128)S(1)}, f32[28,128]{1,0:T(8,128)S(1)}, u32[]{:S(2)}, u32[]{:S(2)}) collective-permute-start(f32[28,128]{1,0:T(8,128)S(1)} %pad_maximum_fusion.4), channel_id=1, source_target_pairs={{0,16},{1,17},{2,18},{3,19},{4,20},{5,21},{6,22},{7,23},{8,24},{9,... | collective-permute-start | bytes 43016 | tf_op jit(solution)/shard_map/ppermute | solution.py:28
  124.6 3.1 %collective-permute-start.18 = (f32[28,128]{1,0:T(8,128)S(1)}, f32[28,128]{1,0:T(8,128)S(1)}, u32[]{:S(2)}, u32[]{:S(2)}) collective-permute-start(f32[28,128]{1,0:T(8,128)S(1)} %pad_maximum_fusion.4), channel_id=1, source_target_pairs={{0,64},{1,65},{2,66},{3,67},{4,68},{5,69},{6,70},{7,71},{8,72},{9,... | collective-permute-start | bytes 43016 | tf_op jit(solution)/shard_map/ppermute | solution.py:28
  128.3 1.7 collective-permute-done.18
  130.1 3.3 %collective-permute-start.19 = (f32[112,128]{1,0:T(8,128)S(1)}, f32[112,128]{1,0:T(8,128)S(1)}, u32[]{:S(2)}, u32[]{:S(2)}) collective-permute-start(f32[112,128]{1,0:T(8,128)S(1)} %pad_maximum_fusion.3), channel_id=1, source_target_pairs={{0,40},{1,41},{2,42},{3,43},{4,44},{5,45},{6,46},{7,47},{8,32},{9,... | collective-permute-start | bytes 172040 | tf_op jit(solution)/shard_map/ppermute | solution.py:28
  133.4 2.5 %collective-permute-start.20 = (f32[112,128]{1,0:T(8,128)S(1)}, f32[112,128]{1,0:T(8,128)S(1)}, u32[]{:S(2)}, u32[]{:S(2)}) collective-permute-start(f32[112,128]{1,0:T(8,128)S(1)} %pad_maximum_fusion.3), channel_id=1, source_target_pairs={{0,8},{1,9},{2,10},{3,11},{4,12},{5,13},{6,14},{7,15},{8,0},{9,1},... | collective-permute-start | bytes 172040 | tf_op jit(solution)/shard_map/ppermute | solution.py:28
  135.8 2.6 %collective-permute-start.21 = (f32[112,128]{1,0:T(8,128)S(1)}, f32[112,128]{1,0:T(8,128)S(1)}, u32[]{:S(2)}, u32[]{:S(2)}) collective-permute-start(f32[112,128]{1,0:T(8,128)S(1)} %pad_maximum_fusion.3), channel_id=1, source_target_pairs={{0,32},{1,33},{2,34},{3,35},{4,36},{5,37},{6,38},{7,39},{8,40},{9,... | collective-permute-start | bytes 172040 | tf_op jit(solution)/shard_map/ppermute | solution.py:28
  138.5 2.2 %collective-permute-done.21 = f32[112,128]{1,0:T(8,128)S(1)} collective-permute-done((f32[112,128]{1,0:T(8,128)S(1)}, f32[112,128]{1,0:T(8,128)S(1)}, u32[]{:S(2)}, u32[]{:S(2)}) %collective-permute-start.21) | collective-permute-done | bytes 57376 | tf_op jit(solution)/shard_map/ppermute | solution.py:28
  141.1 1.1 multiply_reduce_fusion.6
  142.2 0.7 multiply_reduce_fusion.1
  142.9 0.7 multiply_reduce_fusion
  143.6 1.3 multiply_reduce_fusion.4
  144.9 5.3 %stack.44 = f32[8]{0:T(128)S(1)} concatenate(f32[1]{0:T(128)} %bitcast, f32[1]{0:T(128)} %bitcast.1, f32[1]{0:T(128)} %bitcast.2, f32[1]{0:T(128)} %bitcast.3, f32[1]{0:T(128)} %bitcast.5, f32[1]{0:T(128)} %bitcast.6, f32[1]{0:T(128)} %bitcast.8, f32[1]{0:T(128)} %bitcast.9), dimensions={0} | concatenate | bytes 64 | tf_op jit(solution)/shard_map/stack | solution.py:132
  150.2 23.3 %psum.7 = f32[8]{0:T(128)S(1)} all-reduce(f32[8]{0:T(128)S(1)} %stack.44), channel_id=1, replica_groups=mesh['replica'=64,'shard'=8] {'shard'}, use_global_device_ids=true, to_apply=%region_8.9 | all-reduce | flops 8 | bytes 64 | tf_op jit(solution)/shard_map/psum | solution.py:132
  177.3 15.2 %all-gather.1 = bf16[8,1,49280]{2,1,0:T(2,128)(2,1)S(1)} all-gather(bf16[1,1,49280]{2,1,0:T(2,128)(2,1)S(1)} %reshape.99), channel_id=2, replica_groups=mesh['replica'=64,'shard'=8] {'shard'}, dimensions={0}, use_global_device_ids=true | all-gather | bytes 887040 | tf_op jit(solution)/shard_map/all_gather | solution.py:142
  192.8 0.9 reshape.94
  193.8 0.9 reshape.95
  (106 shorter events, 7.4 us)
Async XLA Ops:
  0.6 1.8 copy-start.2
  2.4 1.3 copy-start.18
  2.4 2.0 %copy-start.15 = (f32[1,32,6]{1,0,2:T(1,128)S(1)}, f32[1,32,6]{1,0,2:T(1,128)}, u32[]{:S(2)}) copy-start(f32[1,32,6]{1,0,2:T(1,128)} %param.19) | copy-start | bytes 2308
  9.5 1.3 copy-start.1
  16.4 12.4 %copy-start = (f32[3584,128]{1,0:T(8,128)S(1)}, f32[3584,128]{1,0:T(8,128)}, u32[]{:S(2)}) copy-start(f32[3584,128]{1,0:T(8,128)} %reshape.86) | copy-start | bytes 5505028
  17.8 11.0 %collective-permute-start = (f32[1792,128]{1,0:T(8,128)S(1)}, f32[1792,128]{1,0:T(8,128)}, u32[]{:S(2)}, u32[]{:S(2)}) collective-permute-start(f32[1792,128]{1,0:T(8,128)S(1)} %constant_dynamic-slice_fusion.13), channel_id=1, source_target_pairs={{0,1},{1,0},{2,3},{3,2},{4,5},{5,4},{6,7},{7,6},{8,9},{9,8},{10,11... | collective-permute-start | bytes 2752520 | tf_op jit(solution)/shard_map/ppermute | solution.py:28
  30.1 9.9 %collective-permute-start.3 = (f32[448,128]{1,0:T(8,128)S(1)}, f32[448,128]{1,0:T(8,128)S(1)}, u32[]{:S(2)}, u32[]{:S(2)}) collective-permute-start(f32[448,128]{1,0:T(8,128)S(1)} %get-tuple-element.73), channel_id=1, source_target_pairs={{0,6},{1,7},{2,4},{3,5},{4,2},{5,3},{6,0},{7,1},{8,14},{9,15},{10,... | collective-permute-start | bytes 688136 | tf_op jit(solution)/shard_map/ppermute | solution.py:28
  32.1 8.7 %collective-permute-start.2 = (f32[448,128]{1,0:T(8,128)S(1)}, f32[448,128]{1,0:T(8,128)S(1)}, u32[]{:S(2)}, u32[]{:S(2)}) collective-permute-start(f32[448,128]{1,0:T(8,128)S(1)} %get-tuple-element.74), channel_id=1, source_target_pairs={{0,2},{1,3},{2,0},{3,1},{4,6},{5,7},{6,4},{7,5},{8,10},{9,11},{10,... | collective-permute-start | bytes 688136 | tf_op jit(solution)/shard_map/ppermute | solution.py:28
  34.0 13.8 %collective-permute-start.1 = (f32[448,128]{1,0:T(8,128)S(1)}, f32[448,128]{1,0:T(8,128)S(1)}, u32[]{:S(2)}, u32[]{:S(2)}) collective-permute-start(f32[448,128]{1,0:T(8,128)S(1)} %get-tuple-element.72), channel_id=1, source_target_pairs={{0,4},{1,5},{2,6},{3,7},{4,0},{5,1},{6,2},{7,3},{8,12},{9,13},{10,... | collective-permute-start | bytes 688136 | tf_op jit(solution)/shard_map/ppermute | solution.py:28
  47.8 93.2 %copy-start.19 = (f32[64]{0:T(128)S(1)}, f32[64]{0:T(128)}, u32[]{:S(2)}) copy-start(f32[64]{0:T(128)} %param.22) | copy-start | bytes 772
  47.8 93.2 %copy-start.20 = (f32[64]{0:T(128)S(1)}, f32[64]{0:T(128)}, u32[]{:S(2)}) copy-start(f32[64]{0:T(128)} %param.30) | copy-start | bytes 772
  47.8 93.2 %copy-start.21 = (f32[64]{0:T(128)S(1)}, f32[64]{0:T(128)}, u32[]{:S(2)}) copy-start(f32[64]{0:T(128)} %param.26) | copy-start | bytes 772
  47.8 94.3 %copy-start.3 = (f32[64,384]{1,0:T(8,128)S(1)}, f32[64,384]{1,0:T(8,128)}, u32[]{:S(2)}) copy-start(f32[64,384]{1,0:T(8,128)} %param.20) | copy-start | bytes 294916
  47.9 94.3 %copy-start.9 = (f32[64,384]{1,0:T(8,128)S(1)}, f32[64,384]{1,0:T(8,128)}, u32[]{:S(2)}) copy-start(f32[64,384]{1,0:T(8,128)} %param.28) | copy-start | bytes 294916
  47.9 94.3 %copy-start.10 = (f32[64,384]{1,0:T(8,128)S(1)}, f32[64,384]{1,0:T(8,128)}, u32[]{:S(2)}) copy-start(f32[64,384]{1,0:T(8,128)} %param.24) | copy-start | bytes 294916
  47.9 95.0 %copy-start.4 = (f32[48,512]{1,0:T(8,128)S(1)}, f32[48,512]{1,0:T(8,128)}, u32[]{:S(2)}) copy-start(f32[48,512]{1,0:T(8,128)} %param.21) | copy-start | bytes 294916
  47.9 95.0 %copy-start.11 = (f32[48,512]{1,0:T(8,128)S(1)}, f32[48,512]{1,0:T(8,128)}, u32[]{:S(2)}) copy-start(f32[48,512]{1,0:T(8,128)} %param.29) | copy-start | bytes 294916
  47.9 95.0 %copy-start.12 = (f32[48,512]{1,0:T(8,128)S(1)}, f32[48,512]{1,0:T(8,128)}, u32[]{:S(2)}) copy-start(f32[48,512]{1,0:T(8,128)} %param.25) | copy-start | bytes 294916
  47.9 8.6 %collective-permute-start.6 = (f32[112,128]{1,0:T(8,128)S(1)}, f32[112,128]{1,0:T(8,128)S(1)}, u32[]{:S(2)}, u32[]{:S(2)}) collective-permute-start(f32[112,128]{1,0:T(8,128)S(1)} %get-tuple-element.82), channel_id=1, source_target_pairs={{0,40},{1,41},{2,42},{3,43},{4,44},{5,45},{6,46},{7,47},{8,32},{9,... | collective-permute-start | bytes 172040 | tf_op jit(solution)/shard_map/ppermute | solution.py:28
  50.0 6.5 %collective-permute-start.5 = (f32[112,128]{1,0:T(8,128)S(1)}, f32[112,128]{1,0:T(8,128)S(1)}, u32[]{:S(2)}, u32[]{:S(2)}) collective-permute-start(f32[112,128]{1,0:T(8,128)S(1)} %get-tuple-element.83), channel_id=1, source_target_pairs={{0,8},{1,9},{2,10},{3,11},{4,12},{5,13},{6,14},{7,15},{8,0},{9,1},... | collective-permute-start | bytes 172040 | tf_op jit(solution)/shard_map/ppermute | solution.py:28
  51.9 6.1 %collective-permute-start.4 = (f32[112,128]{1,0:T(8,128)S(1)}, f32[112,128]{1,0:T(8,128)S(1)}, u32[]{:S(2)}, u32[]{:S(2)}) collective-permute-start(f32[112,128]{1,0:T(8,128)S(1)} %get-tuple-element.81), channel_id=1, source_target_pairs={{0,32},{1,33},{2,34},{3,35},{4,36},{5,37},{6,38},{7,39},{8,40},{9,... | collective-permute-start | bytes 172040 | tf_op jit(solution)/shard_map/ppermute | solution.py:28
  58.1 85.5 %copy-start.14 = (f32[4,6]{1,0:T(4,128)S(1)}, f32[4,6]{1,0:T(4,128)}, u32[]{:S(2)}) copy-start(f32[4,6]{1,0:T(4,128)} %param.23) | copy-start | bytes 292
  58.1 85.5 %copy-start.16 = (f32[4,6]{1,0:T(4,128)S(1)}, f32[4,6]{1,0:T(4,128)}, u32[]{:S(2)}) copy-start(f32[4,6]{1,0:T(4,128)} %param.31) | copy-start | bytes 292
  58.1 85.5 %copy-start.17 = (f32[4,6]{1,0:T(4,128)S(1)}, f32[4,6]{1,0:T(4,128)}, u32[]{:S(2)}) copy-start(f32[4,6]{1,0:T(4,128)} %param.27) | copy-start | bytes 292
  58.1 11.0 %collective-permute-start.9 = (f32[28,128]{1,0:T(8,128)S(1)}, f32[28,128]{1,0:T(8,128)S(1)}, u32[]{:S(2)}, u32[]{:S(2)}) collective-permute-start(f32[28,128]{1,0:T(8,128)S(1)} %get-tuple-element.91), channel_id=1, source_target_pairs={{0,80},{1,81},{2,82},{3,83},{4,84},{5,85},{6,86},{7,87},{8,88},{9,... | collective-permute-start | bytes 43016 | tf_op jit(solution)/shard_map/ppermute | solution.py:28
  62.0 7.1 %collective-permute-start.8 = (f32[28,128]{1,0:T(8,128)S(1)}, f32[28,128]{1,0:T(8,128)S(1)}, u32[]{:S(2)}, u32[]{:S(2)}) collective-permute-start(f32[28,128]{1,0:T(8,128)S(1)} %get-tuple-element.92), channel_id=1, source_target_pairs={{0,16},{1,17},{2,18},{3,19},{4,20},{5,21},{6,22},{7,23},{8,24},{9,... | collective-permute-start | bytes 43016 | tf_op jit(solution)/shard_map/ppermute | solution.py:28
  64.4 5.7 %collective-permute-start.7 = (f32[28,128]{1,0:T(8,128)S(1)}, f32[28,128]{1,0:T(8,128)S(1)}, u32[]{:S(2)}, u32[]{:S(2)}) collective-permute-start(f32[28,128]{1,0:T(8,128)S(1)} %get-tuple-element.90), channel_id=1, source_target_pairs={{0,64},{1,65},{2,66},{3,67},{4,68},{5,69},{6,70},{7,71},{8,72},{9,... | collective-permute-start | bytes 43016 | tf_op jit(solution)/shard_map/ppermute | solution.py:28
  70.2 18.4 %collective-permute-start.12 = (f32[7,128]{1,0:T(8,128)S(1)}, f32[7,128]{1,0:T(8,128)S(1)}, u32[]{:S(2)}, u32[]{:S(2)}) collective-permute-start(f32[7,128]{1,0:T(8,128)S(1)} %get-tuple-element.98), channel_id=1, source_target_pairs={{0,384},{1,385},{2,386},{3,387},{4,388},{5,389},{6,390},{7,391},{8... | collective-permute-start | bytes 10760 | tf_op jit(solution)/shard_map/ppermute | solution.py:28
  79.6 9.0 %collective-permute-start.11 = (f32[7,128]{1,0:T(8,128)S(1)}, f32[7,128]{1,0:T(8,128)S(1)}, u32[]{:S(2)}, u32[]{:S(2)}) collective-permute-start(f32[7,128]{1,0:T(8,128)S(1)} %get-tuple-element.99), channel_id=1, source_target_pairs={{0,128},{1,129},{2,130},{3,131},{4,132},{5,133},{6,134},{7,135},{8... | collective-permute-start | bytes 10760 | tf_op jit(solution)/shard_map/ppermute | solution.py:28
  84.8 13.1 %collective-permute-start.10 = (f32[7,128]{1,0:T(8,128)S(1)}, f32[7,128]{1,0:T(8,128)S(1)}, u32[]{:S(2)}, u32[]{:S(2)}) collective-permute-start(f32[7,128]{1,0:T(8,128)S(1)} %get-tuple-element.97), channel_id=1, source_target_pairs={{0,256},{1,257},{2,258},{3,259},{4,260},{5,261},{6,262},{7,263},{8... | collective-permute-start | bytes 10760 | tf_op jit(solution)/shard_map/ppermute | solution.py:28
  97.9 16.2 %collective-permute-start.13 = (f32[7,128]{1,0:T(8,128)S(1)}, f32[7,128]{1,0:T(8,128)S(1)}, u32[]{:S(2)}, u32[]{:S(2)}) collective-permute-start(f32[7,128]{1,0:T(8,128)S(1)} %fusion.5), channel_id=1, source_target_pairs={{0,384},{1,385},{2,386},{3,387},{4,388},{5,389},{6,390},{7,391},{8... | collective-permute-start | bytes 10760 | tf_op jit(solution)/shard_map/ppermute | solution.py:28
  101.0 13.2 %collective-permute-start.14 = (f32[7,128]{1,0:T(8,128)S(1)}, f32[7,128]{1,0:T(8,128)S(1)}, u32[]{:S(2)}, u32[]{:S(2)}) collective-permute-start(f32[7,128]{1,0:T(8,128)S(1)} %fusion.5), channel_id=1, source_target_pairs={{0,128},{1,129},{2,130},{3,131},{4,132},{5,133},{6,134},{7,135},{8... | collective-permute-start | bytes 10760 | tf_op jit(solution)/shard_map/ppermute | solution.py:28
  103.8 13.1 %collective-permute-start.15 = (f32[7,128]{1,0:T(8,128)S(1)}, f32[7,128]{1,0:T(8,128)S(1)}, u32[]{:S(2)}, u32[]{:S(2)}) collective-permute-start(f32[7,128]{1,0:T(8,128)S(1)} %fusion.5), channel_id=1, source_target_pairs={{0,256},{1,257},{2,258},{3,259},{4,260},{5,261},{6,262},{7,263},{8... | collective-permute-start | bytes 10760 | tf_op jit(solution)/shard_map/ppermute | solution.py:28
  116.9 10.8 %collective-permute-start.16 = (f32[28,128]{1,0:T(8,128)S(1)}, f32[28,128]{1,0:T(8,128)S(1)}, u32[]{:S(2)}, u32[]{:S(2)}) collective-permute-start(f32[28,128]{1,0:T(8,128)S(1)} %pad_maximum_fusion.4), channel_id=1, source_target_pairs={{0,80},{1,81},{2,82},{3,83},{4,84},{5,85},{6,86},{7,87},{8,88},{9,... | collective-permute-start | bytes 43016 | tf_op jit(solution)/shard_map/ppermute | solution.py:28
  122.3 6.0 %collective-permute-start.17 = (f32[28,128]{1,0:T(8,128)S(1)}, f32[28,128]{1,0:T(8,128)S(1)}, u32[]{:S(2)}, u32[]{:S(2)}) collective-permute-start(f32[28,128]{1,0:T(8,128)S(1)} %pad_maximum_fusion.4), channel_id=1, source_target_pairs={{0,16},{1,17},{2,18},{3,19},{4,20},{5,21},{6,22},{7,23},{8,24},{9,... | collective-permute-start | bytes 43016 | tf_op jit(solution)/shard_map/ppermute | solution.py:28
  124.6 5.4 %collective-permute-start.18 = (f32[28,128]{1,0:T(8,128)S(1)}, f32[28,128]{1,0:T(8,128)S(1)}, u32[]{:S(2)}, u32[]{:S(2)}) collective-permute-start(f32[28,128]{1,0:T(8,128)S(1)} %pad_maximum_fusion.4), channel_id=1, source_target_pairs={{0,64},{1,65},{2,66},{3,67},{4,68},{5,69},{6,70},{7,71},{8,72},{9,... | collective-permute-start | bytes 43016 | tf_op jit(solution)/shard_map/ppermute | solution.py:28
  130.1 8.4 %collective-permute-start.19 = (f32[112,128]{1,0:T(8,128)S(1)}, f32[112,128]{1,0:T(8,128)S(1)}, u32[]{:S(2)}, u32[]{:S(2)}) collective-permute-start(f32[112,128]{1,0:T(8,128)S(1)} %pad_maximum_fusion.3), channel_id=1, source_target_pairs={{0,40},{1,41},{2,42},{3,43},{4,44},{5,45},{6,46},{7,47},{8,32},{9,... | collective-permute-start | bytes 172040 | tf_op jit(solution)/shard_map/ppermute | solution.py:28
  133.4 5.2 %collective-permute-start.20 = (f32[112,128]{1,0:T(8,128)S(1)}, f32[112,128]{1,0:T(8,128)S(1)}, u32[]{:S(2)}, u32[]{:S(2)}) collective-permute-start(f32[112,128]{1,0:T(8,128)S(1)} %pad_maximum_fusion.3), channel_id=1, source_target_pairs={{0,8},{1,9},{2,10},{3,11},{4,12},{5,13},{6,14},{7,15},{8,0},{9,1},... | collective-permute-start | bytes 172040 | tf_op jit(solution)/shard_map/ppermute | solution.py:28
  135.8 4.9 %collective-permute-start.21 = (f32[112,128]{1,0:T(8,128)S(1)}, f32[112,128]{1,0:T(8,128)S(1)}, u32[]{:S(2)}, u32[]{:S(2)}) collective-permute-start(f32[112,128]{1,0:T(8,128)S(1)} %pad_maximum_fusion.3), channel_id=1, source_target_pairs={{0,32},{1,33},{2,34},{3,35},{4,36},{5,37},{6,38},{7,39},{8,40},{9,... | collective-permute-start | bytes 172040 | tf_op jit(solution)/shard_map/ppermute | solution.py:28
  142.9 49.7 %copy-start.5 = (f32[64,384]{1,0:T(8,128)}, f32[64,384]{1,0:T(8,128)S(1)}, u32[]{:S(2)}) copy-start(f32[64,384]{1,0:T(8,128)S(1)} %get-tuple-element.70) | copy-start | bytes 294916
  142.9 49.7 %copy-start.6 = (f32[64,384]{1,0:T(8,128)}, f32[64,384]{1,0:T(8,128)S(1)}, u32[]{:S(2)}) copy-start(f32[64,384]{1,0:T(8,128)S(1)} %get-tuple-element.71) | copy-start | bytes 294916
  143.6 49.1 %copy-start.7 = (f32[48,512]{1,0:T(8,128)}, f32[48,512]{1,0:T(8,128)S(1)}, u32[]{:S(2)}) copy-start(f32[48,512]{1,0:T(8,128)S(1)} %get-tuple-element.68) | copy-start | bytes 294916
  143.6 49.1 %copy-start.8 = (f32[48,512]{1,0:T(8,128)}, f32[48,512]{1,0:T(8,128)S(1)}, u32[]{:S(2)}) copy-start(f32[48,512]{1,0:T(8,128)S(1)} %get-tuple-element.69) | copy-start | bytes 294916
  173.6 19.1 %copy-start.13 = (f32[4]{0:T(128)}, f32[4]{0:T(128)S(1)}, u32[]{:S(2)}) copy-start(f32[4]{0:T(128)S(1)} %get-tuple-element.103) | copy-start | bytes 52

commit v3 on v1

--- a/solution.py
+++ b/solution.py
@@ -4,7 +4,8 @@
 from jax.sharding import PartitionSpec as P
 
 LANES = 128
-SHARD_BITS = (0, 1, 2)
+CORE_BIT = 0
+Y_GROUP = (2, 1)
 REPLICA_BITS = (3, 5, 4, 6, 7, 8)
 AXES = ("replica", "shard")
 
@@ -24,28 +25,39 @@
     return (index >> bit) & 1
 
 
-def exchange(value, bit, devices):
-    return lax.ppermute(value, AXES, [(d, d ^ (1 << bit)) for d in range(devices)])
-
-
-def halve(rows, bits, devices):
+def exchange(value, mask, devices):
+    return lax.ppermute(value, AXES, [(d, d ^ mask) for d in range(devices)])
+
+
+def masks_of(group):
+    width = len(group)
+    return [
+        sum(((t >> (width - 1 - j)) & 1) << group[j] for j in range(width))
+        for t in range(1 << width)
+    ]
+
+
+def part_of(index, group):
+    return sum(bit_of(index, bit) << (len(group) - 1 - j) for j, bit in enumerate(group))
+
+
+def reduce_blocks(packed, devices):
     index = lax.axis_index(AXES)
-    for bit in bits:
-        half = rows.shape[0] // 2
-        mine = bit_of(index, bit)
-        keep = lax.dynamic_slice_in_dim(rows, mine * half, half, 0)
-        send = lax.dynamic_slice_in_dim(rows, (1 - mine) * half, half, 0)
-        rows = keep + exchange(send, bit, devices)
-    return rows
-
-
-def double(rows, bits, devices):
-    index = lax.axis_index(AXES)
-    for bit in reversed(bits):
-        other = exchange(rows, bit, devices)
-        first = bit_of(index, bit) == 0
-        rows = jnp.concatenate([jnp.where(first, rows, other), jnp.where(first, other, rows)], axis=0)
-    return rows
+    shards = packed.shape[0]
+    pairs = packed.reshape((shards // 2, 2) + packed.shape[1:])
+    mine = bit_of(index, CORE_BIT)
+    keep = lax.dynamic_index_in_dim(pairs, mine, 1, keepdims=False)
+    send = lax.dynamic_index_in_dim(pairs, 1 - mine, 1, keepdims=False)
+    blocks = keep + exchange(send, 1 << CORE_BIT, devices)
+    mine = part_of(index, Y_GROUP)
+    masks = masks_of(Y_GROUP)
+    total = lax.dynamic_index_in_dim(blocks, mine, 0, keepdims=False)
+    for t in range(1, len(masks)):
+        part = lax.dynamic_index_in_dim(blocks, mine ^ t, 0, keepdims=False)
+        total = total + exchange(part, masks[t], devices)
+    for bit in REPLICA_BITS:
+        total = total + exchange(total, 1 << bit, devices)
+    return total
 
 
 def on_device(
@@ -77,21 +89,29 @@
     offsets = [sum(sizes[:member]) for member in range(4)]
     total = sum(sizes)
     devices = shards * replicas
-    width = padded_width(total, LANES * replicas)
-    levels = len(SHARD_BITS)
-    position = [sum(((s >> SHARD_BITS[j]) & 1) << (levels - 1 - j) for j in range(levels)) for s in range(shards)]
-    blocks = [gradient.reshape(shards, -1) for gradient in gradients]
-    filler = jnp.zeros((width - total,), jnp.float32)
-    packed = jnp.stack(
-        [jnp.concatenate([block[position.index(p)] for block in blocks] + [filler]) for p in range(shards)]
-    )
-    chunks = packed.reshape(shards * replicas * (width // replicas // LANES), LANES)
-    mine = halve(chunks, SHARD_BITS + REPLICA_BITS, devices)
-    block = double(mine, REPLICA_BITS, devices)
-    summed_flat = block.reshape(width)
+    query_rows, lanes = weight_query.shape
+    output_rows = weight_output.size // lanes
+    small = jnp.concatenate(
+        [grad_norm[0].reshape(shards, -1), grad_bias[0].reshape(shards, -1)], axis=1
+    )
+    small_width = small.shape[1]
+    small = jnp.pad(small, ((0, 0), (0, lanes - small_width))).reshape(shards, 1, lanes)
+    small = jnp.pad(small, ((0, 0), (0, 7), (0, 0)))
+    packed = jnp.concatenate(
+        [
+            grad_query[0].reshape(shards, query_rows, lanes),
+            grad_output[0].reshape(shards, output_rows, lanes),
+            small,
+        ],
+        axis=1,
+    )
+    block = reduce_blocks(packed, devices)
+    summed_rest = block[query_rows + output_rows, :small_width]
     summed_all = [
-        summed_flat[offsets[member] : offsets[member] + sizes[member]].reshape(weights[member].shape)
-        for member in range(4)
+        block[:query_rows],
+        block[query_rows : query_rows + output_rows].reshape(weight_output.shape),
+        summed_rest[: weight_norm.size].reshape(weight_norm.shape),
+        summed_rest[weight_norm.size :].reshape(weight_bias.shape),
     ]
     results = [
         step_math(
@@ -105,9 +125,9 @@
     ]
     weight_squares = [jnp.sum(weight * weight) for weight in weights]
     update_squares = [jnp.sum(result[2] * result[2]) for result in results]
-    squares = lax.psum(jnp.stack(weight_squares + update_squares), "shard")
-    weight_sizes = jnp.sqrt(squares[:4])
-    update_sizes = jnp.sqrt(squares[4:])
+    squares = lax.psum(tuple(weight_squares + update_squares), "shard")
+    weight_sizes = jnp.sqrt(jnp.stack(squares[:4]))
+    update_sizes = jnp.sqrt(jnp.stack(squares[4:]))
     trust_ratios = weight_sizes / (update_sizes + 1e-06)
     shards_out = [
         (weights[member] - 0.01 * trust_ratios[member] * results[member][2]).astype(jnp.bfloat16).reshape(-1)

time: 206 us -> 177 us (0.86)
  local copies, waits for them, and re-layouts: 31.6 us -> 7.71 us
  blocking collectives: 42 us -> 28.2 us
  other arithmetic: 6.09 us -> 16.7 us
  starting transfers between devices: 57.5 us -> 53.7 us
  waiting for transfers between devices: 63.6 us -> 66.8 us
    psum x1, blocking collectives: 26.8 us -> 13 us  [on_device(): squares = lax.psum(tuple(weight_squares + update_squares), 'shard')]
    another operation x2, local copies, waits for them, and re-layouts: 9.87 us -> 0.15 us  [the longest x1 0.08 us: on_device(): grad_norm[0].reshape(shards, -1)]
    concatenate x8 -> x1, local copies, waits for them, and re-layouts: 10.6 us -> 1.4 us  [on_device(): jnp.concatenate([grad_query[0].reshape(shards, query_rows, lanes), grad_o...]
    div x0 -> x1, other arithmetic: none -> 5.16 us  [on_device(): trust_ratios = weight_sizes / (update_sizes + 1e-06)]
    sqrt x0 -> x1, other arithmetic: none -> 5.16 us  [on_device(): weight_sizes = jnp.sqrt(jnp.stack(squares[:4]))]
    ppermute x15 -> x10, starting transfers between devices: 57.5 us -> 53.7 us  [exchange(): return lax.ppermute(value, AXES, [(d, d ^ mask) for d in range(devices)])]
    ppermute x15 -> x10, waiting for transfers between devices: 63.6 us -> 66.8 us  [exchange(): return lax.ppermute(value, AXES, [(d, d ^ mask) for d in range(devices)])]
  transfers between devices with their start and end apart: 15 -> 10, of which waited for: 15 -> 9; matrix products, arithmetic and copies ran while one was open for 0% -> 0% of each run, Pallas kernels for 0% -> 0%
where the time goes in v3:
time: 177 us
  waiting for transfers between devices  66.8 us (38%)
  starting transfers between devices  53.7 us (30%)
  blocking collectives  28.2 us (16%)
  other arithmetic  16.7 us (9%)
  local copies, waits for them, and re-layouts  7.71 us (4%)
  between operations  3.67 us (2%)
    ppermute x10, waiting for transfers between devices, exchange(): return lax.ppermute(value, AXES, [(d, d ^ mask) for d in range(devices)])  66.8 us
    ppermute x10, starting transfers between devices, exchange(): return lax.ppermute(value, AXES, [(d, d ^ mask) for d in range(devices)])  53.7 us
    all_gather x1, blocking collectives, on_device(): lax.all_gather(jnp.concatenate(shards_out), 'shard', axis=0, tiled=False)  15.2 us
    psum x1, blocking collectives, on_device(): squares = lax.psum(tuple(weight_squares + update_squares), 'shard')  13 us
    div x1, other arithmetic, on_device(): trust_ratios = weight_sizes / (update_sizes + 1e-06)  5.16 us
    sqrt x1, other arithmetic, on_device(): weight_sizes = jnp.sqrt(jnp.stack(squares[:4]))  5.16 us
    reduce_sum x4, other arithmetic, on_device(): update_squares = [jnp.sum(result[2] * result[2]) for result in results]  3.74 us
  transfers between devices with their start and end apart: 10, of which 9 were waited for; matrix products, arithmetic and copies ran while one was open for 0% of the time, Pallas kernels for 0%

profile of v3, /device:TPU:1, one launch (start us, length us, event | category | flops | bytes accessed | tf_op | source)
XLA Modules:
  0.0 176.8 jit_solution(17017878952638217309)
XLA Ops:
  0.7 1.4 concatenate.31
  2.1 0.8 copy.37
  2.9 0.5 broadcast.55
  3.4 1.3 reduce.7
  4.8 0.1 reshape_squeeze.8
  4.8 0.1 fusion.5
  5.0 0.1 pad_maximum_fusion
  5.2 8.8 %collective-permute-start = (f32[4,136,384]{2,1,0:T(8,128)S(1)}, f32[4,136,384]{2,1,0:T(8,128)S(1)}, u32[]{:S(2)}, u32[]{:S(2)}) collective-permute-start(f32[4,136,384]{2,1,0:T(8,128)S(1)} %dynamic-slice_bitcast_fusion), channel_id=1, source_target_pairs={{0,1},{1,0},{2,3},{3,2},{4,5},{5,4},{6,7},{7,6},{8,9},{9,8},{10,11... | collective-permute-start | bytes 2506760 | tf_op jit(solution)/shard_map/ppermute | solution.py:29
  14.0 1.9 %collective-permute-done = f32[4,136,384]{2,1,0:T(8,128)S(1)} collective-permute-done((f32[4,136,384]{2,1,0:T(8,128)S(1)}, f32[4,136,384]{2,1,0:T(8,128)S(1)}, u32[]{:S(2)}, u32[]{:S(2)}) %collective-permute-start) | collective-permute-done | bytes 835616 | tf_op jit(solution)/shard_map/ppermute | solution.py:29
  15.9 0.1 bitcast_add_fusion
  16.1 1.9 %collective-permute-start.1 = (f32[136,384]{1,0:T(8,128)S(1)}, f32[136,384]{1,0:T(8,128)S(1)}, u32[]{:S(2)}, u32[]{:S(2)}) collective-permute-start(f32[136,384]{1,0:T(8,128)S(1)} %get-tuple-element.80), channel_id=1, source_target_pairs={{0,2},{1,3},{2,0},{3,1},{4,6},{5,7},{6,4},{7,5},{8,10},{9,11},{10,... | collective-permute-start | bytes 626696 | tf_op jit(solution)/shard_map/ppermute | solution.py:29
  18.0 1.9 %collective-permute-start.2 = (f32[136,384]{1,0:T(8,128)S(1)}, f32[136,384]{1,0:T(8,128)S(1)}, u32[]{:S(2)}, u32[]{:S(2)}) collective-permute-start(f32[136,384]{1,0:T(8,128)S(1)} %get-tuple-element.82), channel_id=1, source_target_pairs={{0,4},{1,5},{2,6},{3,7},{4,0},{5,1},{6,2},{7,3},{8,12},{9,13},{10,... | collective-permute-start | bytes 626696 | tf_op jit(solution)/shard_map/ppermute | solution.py:29
  20.0 5.7 %collective-permute-start.3 = (f32[136,384]{1,0:T(8,128)S(1)}, f32[136,384]{1,0:T(8,128)S(1)}, u32[]{:S(2)}, u32[]{:S(2)}) collective-permute-start(f32[136,384]{1,0:T(8,128)S(1)} %get-tuple-element.81), channel_id=1, source_target_pairs={{0,6},{1,7},{2,4},{3,5},{4,2},{5,3},{6,0},{7,1},{8,14},{9,15},{10,... | collective-permute-start | bytes 626696 | tf_op jit(solution)/shard_map/ppermute | solution.py:29
  25.7 2.1 %collective-permute-done.2 = f32[136,384]{1,0:T(8,128)S(1)} collective-permute-done((f32[136,384]{1,0:T(8,128)S(1)}, f32[136,384]{1,0:T(8,128)S(1)}, u32[]{:S(2)}, u32[]{:S(2)}) %collective-permute-start.2) | collective-permute-done | bytes 208928 | tf_op jit(solution)/shard_map/ppermute | solution.py:29
  27.8 5.2 %collective-permute-done.3 = f32[136,384]{1,0:T(8,128)S(1)} collective-permute-done((f32[136,384]{1,0:T(8,128)S(1)}, f32[136,384]{1,0:T(8,128)S(1)}, u32[]{:S(2)}, u32[]{:S(2)}) %collective-permute-start.3) | collective-permute-done | bytes 208928 | tf_op jit(solution)/shard_map/ppermute | solution.py:29
  33.1 1.9 %collective-permute-start.4 = (f32[136,384]{1,0:T(8,128)S(1)}, f32[136,384]{1,0:T(8,128)S(1)}, u32[]{:S(2)}, u32[]{:S(2)}) collective-permute-start(f32[136,384]{1,0:T(8,128)S(1)} %fusion.1), channel_id=1, source_target_pairs={{0,8},{1,9},{2,10},{3,11},{4,12},{5,13},{6,14},{7,15},{8,0},{9,1},... | collective-permute-start | bytes 626696 | tf_op jit(solution)/shard_map/ppermute | solution.py:29
  35.0 6.2 %collective-permute-done.4 = f32[136,384]{1,0:T(8,128)S(1)} collective-permute-done((f32[136,384]{1,0:T(8,128)S(1)}, f32[136,384]{1,0:T(8,128)S(1)}, u32[]{:S(2)}, u32[]{:S(2)}) %collective-permute-start.4) | collective-permute-done | bytes 208928 | tf_op jit(solution)/shard_map/ppermute | solution.py:29
  41.3 2.1 %collective-permute-start.5 = (f32[136,384]{1,0:T(8,128)S(1)}, f32[136,384]{1,0:T(8,128)S(1)}, u32[]{:S(2)}, u32[]{:S(2)}) collective-permute-start(f32[136,384]{1,0:T(8,128)S(1)} %add.149), channel_id=1, source_target_pairs={{0,32},{1,33},{2,34},{3,35},{4,36},{5,37},{6,38},{7,39},{8,40},{9,... | collective-permute-start | bytes 626696 | tf_op jit(solution)/shard_map/ppermute | solution.py:29
  43.3 5.3 %collective-permute-done.5 = f32[136,384]{1,0:T(8,128)S(1)} collective-permute-done((f32[136,384]{1,0:T(8,128)S(1)}, f32[136,384]{1,0:T(8,128)S(1)}, u32[]{:S(2)}, u32[]{:S(2)}) %collective-permute-start.5) | collective-permute-done | bytes 208928 | tf_op jit(solution)/shard_map/ppermute | solution.py:29
  48.7 3.2 %collective-permute-start.6 = (f32[136,384]{1,0:T(8,128)S(1)}, f32[136,384]{1,0:T(8,128)S(1)}, u32[]{:S(2)}, u32[]{:S(2)}) collective-permute-start(f32[136,384]{1,0:T(8,128)S(1)} %add.150), channel_id=1, source_target_pairs={{0,16},{1,17},{2,18},{3,19},{4,20},{5,21},{6,22},{7,23},{8,24},{9,... | collective-permute-start | bytes 626696 | tf_op jit(solution)/shard_map/ppermute | solution.py:29
  52.0 4.9 %collective-permute-done.6 = f32[136,384]{1,0:T(8,128)S(1)} collective-permute-done((f32[136,384]{1,0:T(8,128)S(1)}, f32[136,384]{1,0:T(8,128)S(1)}, u32[]{:S(2)}, u32[]{:S(2)}) %collective-permute-start.6) | collective-permute-done | bytes 208928 | tf_op jit(solution)/shard_map/ppermute | solution.py:29
  57.0 3.5 %collective-permute-start.7 = (f32[136,384]{1,0:T(8,128)S(1)}, f32[136,384]{1,0:T(8,128)S(1)}, u32[]{:S(2)}, u32[]{:S(2)}) collective-permute-start(f32[136,384]{1,0:T(8,128)S(1)} %add.151), channel_id=1, source_target_pairs={{0,64},{1,65},{2,66},{3,67},{4,68},{5,69},{6,70},{7,71},{8,72},{9,... | collective-permute-start | bytes 626696 | tf_op jit(solution)/shard_map/ppermute | solution.py:29
  60.5 9.5 %collective-permute-done.7 = f32[136,384]{1,0:T(8,128)S(1)} collective-permute-done((f32[136,384]{1,0:T(8,128)S(1)}, f32[136,384]{1,0:T(8,128)S(1)}, u32[]{:S(2)}, u32[]{:S(2)}) %collective-permute-start.7) | collective-permute-done | bytes 208928 | tf_op jit(solution)/shard_map/ppermute | solution.py:29
  70.0 8.3 %collective-permute-start.8 = (f32[136,384]{1,0:T(8,128)S(1)}, f32[136,384]{1,0:T(8,128)S(1)}, u32[]{:S(2)}, u32[]{:S(2)}) collective-permute-start(f32[136,384]{1,0:T(8,128)S(1)} %add.152), channel_id=1, source_target_pairs={{0,128},{1,129},{2,130},{3,131},{4,132},{5,133},{6,134},{7,135},{8... | collective-permute-start | bytes 626696 | tf_op jit(solution)/shard_map/ppermute | solution.py:29
  78.3 18.0 %collective-permute-done.8 = f32[136,384]{1,0:T(8,128)S(1)} collective-permute-done((f32[136,384]{1,0:T(8,128)S(1)}, f32[136,384]{1,0:T(8,128)S(1)}, u32[]{:S(2)}, u32[]{:S(2)}) %collective-permute-start.8) | collective-permute-done | bytes 208928 | tf_op jit(solution)/shard_map/ppermute | solution.py:29
  96.3 16.3 %collective-permute-start.9 = (f32[136,384]{1,0:T(8,128)S(1)}, f32[136,384]{1,0:T(8,128)S(1)}, u32[]{:S(2)}, u32[]{:S(2)}) collective-permute-start(f32[136,384]{1,0:T(8,128)S(1)} %add.153), channel_id=1, source_target_pairs={{0,256},{1,257},{2,258},{3,259},{4,260},{5,261},{6,262},{7,263},{8... | collective-permute-start | bytes 626696 | tf_op jit(solution)/shard_map/ppermute | solution.py:29
  112.7 13.7 %collective-permute-done.9 = f32[136,384]{1,0:T(8,128)S(1)} collective-permute-done((f32[136,384]{1,0:T(8,128)S(1)}, f32[136,384]{1,0:T(8,128)S(1)}, u32[]{:S(2)}, u32[]{:S(2)}) %collective-permute-start.9) | collective-permute-done | bytes 208928 | tf_op jit(solution)/shard_map/ppermute | solution.py:29
  126.4 0.1 slice_reduce_fusion
  126.5 0.7 multiply_reduce_fusion.1
  127.2 0.1 reshape.195
  127.3 1.1 multiply_reduce_fusion.6
  128.4 0.7 multiply_reduce_fusion
  129.2 1.2 multiply_reduce_fusion.4
  130.4 13.0 %all-reduce.2 = (f32[]{:T(128)}, f32[]{:T(128)}, f32[]{:T(128)}, f32[]{:T(128)}, f32[]{:T(128)}, /*index=5*/f32[]{:T(128)}, f32[]{:T(128)}, f32[]{:T(128)}) all-reduce(f32[]{:T(128)} %get-tuple-element.86, f32[]{:T(128)} %get-tuple-element.91, f32[]{:T(128)} %get-tuple-element.59, ...), channel_id=1, replica_groups=mesh['replica'=64,'shard'=8] {'shard'}, use_global_device_ids=true, to_apply=%region_7.8 | all-reduce | flops 8 | bytes 64 | tf_op jit(solution)/shard_map/psum | solution.py:128
  143.3 5.2 %fusion.8 = f32[4]{0:T(128)S(1)} fusion(f32[1]{0:T(128)} %bitcast.3, f32[1]{0:T(128)} %bitcast.2, f32[1]{0:T(128)} %bitcast.1, f32[1]{0:T(128)} %bitcast, f32[1]{0:T(128)} %bitcast.17, f32[1]{0:T(128)} %bitcast.16, f32[1]{0:T(128)} %bitcast.14, f32[1]{0:T(128)} %bitcast.13), kind=kLoop, calls=%fused_computation.42 | loop fusion | flops 32 | bytes 48 | tf_op jit(solution)/shard_map/div | solution.py:131
  148.5 0.6 fusion.15
  149.8 0.1 reshape.198
  152.0 0.1 concatenate.35
  152.2 0.1 reshape.204
  152.3 15.2 %all-gather.1 = bf16[8,1,49280]{2,1,0:T(2,128)(2,1)S(1)} all-gather(bf16[1,1,49280]{2,1,0:T(2,128)(2,1)S(1)} %reshape.204), channel_id=2, replica_groups=mesh['replica'=64,'shard'=8] {'shard'}, dimensions={0}, use_global_device_ids=true | all-gather | bytes 887040 | tf_op jit(solution)/shard_map/all_gather | solution.py:138
  167.5 0.1 copy.45
  167.8 0.9 reshape.199
  168.7 0.9 reshape.200
  169.6 0.1 reshape.202
  169.7 0.7 copy.39
  170.4 0.6 reshape.201
  171.0 5.2 %maximum_sqrt_fusion.2 = (f32[1,4]{1,0:T(1,128)S(1)}, f32[1,4]{1,0:T(1,128)S(1)}) fusion(f32[1,1]{1,0:T(1,128)} %bitcast.25, f32[1,1]{1,0:T(1,128)} %bitcast.24, f32[1,1]{1,0:T(1,128)} %bitcast.23, f32[1,1]{1,0:T(1,128)} %bitcast.22, f32[1,1]{1,0:T(1,128)} %bitcast.29, f32[1,1]{1,0:T(1,128)} %bitcast.28, f32[1,1]{1,0:T(1,128)} %bitcast.27, f32[1,1]{1,0:T(1,128)} %bitcast.26), kind=kLoop, calls=%fused_computation.45 | loop fusion | flops 24 | bytes 64 | tf_op jit(solution)/shard_map/sqrt | solution.py:129
  176.2 0.6 pad_maximum_fusion.1
  (60 shorter events, 0.9 us)
Async XLA Ops:
  0.6 4.3 %copy-start = (f32[1,512,384]{2,1,0:T(8,128)S(1)}, f32[1,512,384]{2,1,0:T(8,128)}, u32[]{:S(2)}) copy-start(f32[1,512,384]{2,1,0:T(8,128)} %param.16) | copy-start | bytes 2359300
  5.2 10.8 %collective-permute-start = (f32[4,136,384]{2,1,0:T(8,128)S(1)}, f32[4,136,384]{2,1,0:T(8,128)S(1)}, u32[]{:S(2)}, u32[]{:S(2)}) collective-permute-start(f32[4,136,384]{2,1,0:T(8,128)S(1)} %dynamic-slice_bitcast_fusion), channel_id=1, source_target_pairs={{0,1},{1,0},{2,3},{3,2},{4,5},{5,4},{6,7},{7,6},{8,9},{9,8},{10,11... | collective-permute-start | bytes 2506760 | tf_op jit(solution)/shard_map/ppermute | solution.py:29
  16.1 9.6 %collective-permute-start.1 = (f32[136,384]{1,0:T(8,128)S(1)}, f32[136,384]{1,0:T(8,128)S(1)}, u32[]{:S(2)}, u32[]{:S(2)}) collective-permute-start(f32[136,384]{1,0:T(8,128)S(1)} %get-tuple-element.80), channel_id=1, source_target_pairs={{0,2},{1,3},{2,0},{3,1},{4,6},{5,7},{6,4},{7,5},{8,10},{9,11},{10,... | collective-permute-start | bytes 626696 | tf_op jit(solution)/shard_map/ppermute | solution.py:29
  18.0 9.8 %collective-permute-start.2 = (f32[136,384]{1,0:T(8,128)S(1)}, f32[136,384]{1,0:T(8,128)S(1)}, u32[]{:S(2)}, u32[]{:S(2)}) collective-permute-start(f32[136,384]{1,0:T(8,128)S(1)} %get-tuple-element.82), channel_id=1, source_target_pairs={{0,4},{1,5},{2,6},{3,7},{4,0},{5,1},{6,2},{7,3},{8,12},{9,13},{10,... | collective-permute-start | bytes 626696 | tf_op jit(solution)/shard_map/ppermute | solution.py:29
  20.0 13.1 %collective-permute-start.3 = (f32[136,384]{1,0:T(8,128)S(1)}, f32[136,384]{1,0:T(8,128)S(1)}, u32[]{:S(2)}, u32[]{:S(2)}) collective-permute-start(f32[136,384]{1,0:T(8,128)S(1)} %get-tuple-element.81), channel_id=1, source_target_pairs={{0,6},{1,7},{2,4},{3,5},{4,2},{5,3},{6,0},{7,1},{8,14},{9,15},{10,... | collective-permute-start | bytes 626696 | tf_op jit(solution)/shard_map/ppermute | solution.py:29
  33.1 8.1 %collective-permute-start.4 = (f32[136,384]{1,0:T(8,128)S(1)}, f32[136,384]{1,0:T(8,128)S(1)}, u32[]{:S(2)}, u32[]{:S(2)}) collective-permute-start(f32[136,384]{1,0:T(8,128)S(1)} %fusion.1), channel_id=1, source_target_pairs={{0,8},{1,9},{2,10},{3,11},{4,12},{5,13},{6,14},{7,15},{8,0},{9,1},... | collective-permute-start | bytes 626696 | tf_op jit(solution)/shard_map/ppermute | solution.py:29
  41.2 85.2 %copy-start.2 = (f32[64,384]{1,0:T(8,128)S(1)}, f32[64,384]{1,0:T(8,128)}, u32[]{:S(2)}) copy-start(f32[64,384]{1,0:T(8,128)} %param.20) | copy-start | bytes 294916
  41.3 85.2 %copy-start.7 = (f32[64,384]{1,0:T(8,128)S(1)}, f32[64,384]{1,0:T(8,128)}, u32[]{:S(2)}) copy-start(f32[64,384]{1,0:T(8,128)} %param.28) | copy-start | bytes 294916
  41.3 85.2 %copy-start.8 = (f32[64,384]{1,0:T(8,128)S(1)}, f32[64,384]{1,0:T(8,128)}, u32[]{:S(2)}) copy-start(f32[64,384]{1,0:T(8,128)} %param.24) | copy-start | bytes 294916
  41.3 7.3 %collective-permute-start.5 = (f32[136,384]{1,0:T(8,128)S(1)}, f32[136,384]{1,0:T(8,128)S(1)}, u32[]{:S(2)}, u32[]{:S(2)}) collective-permute-start(f32[136,384]{1,0:T(8,128)S(1)} %add.149), channel_id=1, source_target_pairs={{0,32},{1,33},{2,34},{3,35},{4,36},{5,37},{6,38},{7,39},{8,40},{9,... | collective-permute-start | bytes 626696 | tf_op jit(solution)/shard_map/ppermute | solution.py:29
  48.7 78.6 %copy-start.15 = (f32[64]{0:T(128)S(1)}, f32[64]{0:T(128)}, u32[]{:S(2)}) copy-start(f32[64]{0:T(128)} %param.22) | copy-start | bytes 772
  48.7 78.6 %copy-start.16 = (f32[64]{0:T(128)S(1)}, f32[64]{0:T(128)}, u32[]{:S(2)}) copy-start(f32[64]{0:T(128)} %param.30) | copy-start | bytes 772
  48.7 78.6 %copy-start.17 = (f32[64]{0:T(128)S(1)}, f32[64]{0:T(128)}, u32[]{:S(2)}) copy-start(f32[64]{0:T(128)} %param.26) | copy-start | bytes 772
  48.7 79.7 %copy-start.1 = (f32[48,512]{1,0:T(8,128)S(1)}, f32[48,512]{1,0:T(8,128)}, u32[]{:S(2)}) copy-start(f32[48,512]{1,0:T(8,128)} %param.21) | copy-start | bytes 294916
  48.7 79.7 %copy-start.9 = (f32[48,512]{1,0:T(8,128)S(1)}, f32[48,512]{1,0:T(8,128)}, u32[]{:S(2)}) copy-start(f32[48,512]{1,0:T(8,128)} %param.29) | copy-start | bytes 294916
  48.7 79.7 %copy-start.10 = (f32[48,512]{1,0:T(8,128)S(1)}, f32[48,512]{1,0:T(8,128)}, u32[]{:S(2)}) copy-start(f32[48,512]{1,0:T(8,128)} %param.25) | copy-start | bytes 294916
  48.7 8.2 %collective-permute-start.6 = (f32[136,384]{1,0:T(8,128)S(1)}, f32[136,384]{1,0:T(8,128)S(1)}, u32[]{:S(2)}, u32[]{:S(2)}) collective-permute-start(f32[136,384]{1,0:T(8,128)S(1)} %add.150), channel_id=1, source_target_pairs={{0,16},{1,17},{2,18},{3,19},{4,20},{5,21},{6,22},{7,23},{8,24},{9,... | collective-permute-start | bytes 626696 | tf_op jit(solution)/shard_map/ppermute | solution.py:29
  56.9 72.2 %copy-start.12 = (f32[4,6]{1,0:T(4,128)S(1)}, f32[4,6]{1,0:T(4,128)}, u32[]{:S(2)}) copy-start(f32[4,6]{1,0:T(4,128)} %param.23) | copy-start | bytes 292
  57.0 72.2 %copy-start.13 = (f32[4,6]{1,0:T(4,128)S(1)}, f32[4,6]{1,0:T(4,128)}, u32[]{:S(2)}) copy-start(f32[4,6]{1,0:T(4,128)} %param.31) | copy-start | bytes 292
  57.0 72.2 %copy-start.14 = (f32[4,6]{1,0:T(4,128)S(1)}, f32[4,6]{1,0:T(4,128)}, u32[]{:S(2)}) copy-start(f32[4,6]{1,0:T(4,128)} %param.27) | copy-start | bytes 292
  57.0 13.0 %collective-permute-start.7 = (f32[136,384]{1,0:T(8,128)S(1)}, f32[136,384]{1,0:T(8,128)S(1)}, u32[]{:S(2)}, u32[]{:S(2)}) collective-permute-start(f32[136,384]{1,0:T(8,128)S(1)} %add.151), channel_id=1, source_target_pairs={{0,64},{1,65},{2,66},{3,67},{4,68},{5,69},{6,70},{7,71},{8,72},{9,... | collective-permute-start | bytes 626696 | tf_op jit(solution)/shard_map/ppermute | solution.py:29
  70.0 26.3 %collective-permute-start.8 = (f32[136,384]{1,0:T(8,128)S(1)}, f32[136,384]{1,0:T(8,128)S(1)}, u32[]{:S(2)}, u32[]{:S(2)}) collective-permute-start(f32[136,384]{1,0:T(8,128)S(1)} %add.152), channel_id=1, source_target_pairs={{0,128},{1,129},{2,130},{3,131},{4,132},{5,133},{6,134},{7,135},{8... | collective-permute-start | bytes 626696 | tf_op jit(solution)/shard_map/ppermute | solution.py:29
  96.3 30.0 %collective-permute-start.9 = (f32[136,384]{1,0:T(8,128)S(1)}, f32[136,384]{1,0:T(8,128)S(1)}, u32[]{:S(2)}, u32[]{:S(2)}) collective-permute-start(f32[136,384]{1,0:T(8,128)S(1)} %add.153), channel_id=1, source_target_pairs={{0,256},{1,257},{2,258},{3,259},{4,260},{5,261},{6,262},{7,263},{8... | collective-permute-start | bytes 626696 | tf_op jit(solution)/shard_map/ppermute | solution.py:29
  127.2 40.3 %copy-start.3 = (f32[64,384]{1,0:T(8,128)}, f32[64,384]{1,0:T(8,128)S(1)}, u32[]{:S(2)}) copy-start(f32[64,384]{1,0:T(8,128)S(1)} %get-tuple-element.76) | copy-start | bytes 294916
  127.2 40.3 %copy-start.4 = (f32[64,384]{1,0:T(8,128)}, f32[64,384]{1,0:T(8,128)S(1)}, u32[]{:S(2)}) copy-start(f32[64,384]{1,0:T(8,128)S(1)} %get-tuple-element.77) | copy-start | bytes 294916
  129.1 38.5 %copy-start.5 = (f32[48,512]{1,0:T(8,128)}, f32[48,512]{1,0:T(8,128)S(1)}, u32[]{:S(2)}) copy-start(f32[48,512]{1,0:T(8,128)S(1)} %get-tuple-element.78) | copy-start | bytes 294916
  129.1 38.5 %copy-start.6 = (f32[48,512]{1,0:T(8,128)}, f32[48,512]{1,0:T(8,128)S(1)}, u32[]{:S(2)}) copy-start(f32[48,512]{1,0:T(8,128)S(1)} %get-tuple-element.79) | copy-start | bytes 294916
  148.5 19.1 %copy-start.11 = (f32[4]{0:T(128)}, f32[4]{0:T(128)S(1)}, u32[]{:S(2)}) copy-start(f32[4]{0:T(128)S(1)} %fusion.8) | copy-start | bytes 52

commit v4 on v3

--- a/solution.py
+++ b/solution.py
@@ -6,7 +6,9 @@
 LANES = 128
 CORE_BIT = 0
 Y_GROUP = (2, 1)
-REPLICA_BITS = (3, 5, 4, 6, 7, 8)
+REPLICA_SPLIT_BITS = (3, 5)
+REPLICA_BUTTERFLY_BITS = (4, 6, 7, 8)
+ROW_TILE = 8
 AXES = ("replica", "shard")
 
 
@@ -55,9 +57,22 @@
     for t in range(1, len(masks)):
         part = lax.dynamic_index_in_dim(blocks, mine ^ t, 0, keepdims=False)
         total = total + exchange(part, masks[t], devices)
-    for bit in REPLICA_BITS:
+    rows, lanes = total.shape
+    multiple = ROW_TILE << len(REPLICA_SPLIT_BITS)
+    total = jnp.pad(total, ((0, padded_width(rows, multiple) - rows), (0, 0)))
+    for bit in REPLICA_SPLIT_BITS:
+        halves = total.reshape((2, total.shape[0] // 2, lanes))
+        mine = bit_of(index, bit)
+        keep = lax.dynamic_index_in_dim(halves, mine, 0, keepdims=False)
+        send = lax.dynamic_index_in_dim(halves, 1 - mine, 0, keepdims=False)
+        total = keep + exchange(send, 1 << bit, devices)
+    for bit in REPLICA_BUTTERFLY_BITS:
         total = total + exchange(total, 1 << bit, devices)
-    return total
+    for bit in reversed(REPLICA_SPLIT_BITS):
+        other = exchange(total, 1 << bit, devices)
+        first = bit_of(index, bit) == 0
+        total = jnp.concatenate([jnp.where(first, total, other), jnp.where(first, other, total)], axis=0)
+    return total[:rows]
 
 
 def on_device(

time: 177 us -> 154 us (0.87)
  waiting for transfers between devices: 66.8 us -> 32.9 us
  blocking collectives: 28.2 us -> 36.3 us
  starting transfers between devices: 53.7 us -> 56.2 us
    ppermute x10 -> x12, waiting for transfers between devices: 66.8 us -> 32.9 us  [exchange(): return lax.ppermute(value, AXES, [(d, d ^ mask) for d in range(devices)])]
    psum x1, blocking collectives: 13 us -> 21 us  [on_device(): squares = lax.psum(tuple(weight_squares + update_squares), 'shard')]
    ppermute x10 -> x12, starting transfers between devices: 53.7 us -> 56.2 us  [exchange(): return lax.ppermute(value, AXES, [(d, d ^ mask) for d in range(devices)])]
  transfers between devices with their start and end apart: 10 -> 12, of which waited for: 9 -> 11; matrix products, arithmetic and copies ran while one was open for 0% -> 0% of each run, Pallas kernels for 0% -> 0%
where the time goes in v4:
time: 154 us; the launch traced here: 153 us
  starting transfers between devices  56.2 us (36%)
  blocking collectives  36.3 us (24%)
  waiting for transfers between devices  32.9 us (21%)
  other arithmetic  16.4 us (11%)
  local copies, waits for them, and re-layouts  7.77 us (5%)
  between operations  3.75 us (2%)
    ppermute x12, starting transfers between devices, exchange(): return lax.ppermute(value, AXES, [(d, d ^ mask) for d in range(devices)])  56.2 us
    ppermute x12, waiting for transfers between devices, exchange(): return lax.ppermute(value, AXES, [(d, d ^ mask) for d in range(devices)])  32.9 us
    psum x1, blocking collectives, on_device(): squares = lax.psum(tuple(weight_squares + update_squares), 'shard')  21 us
    all_gather x1, blocking collectives, on_device(): lax.all_gather(jnp.concatenate(shards_out), 'shard', axis=0, tiled=False)  15.2 us
    div x1, other arithmetic, on_device(): trust_ratios = weight_sizes / (update_sizes + 1e-06)  5.06 us
    sqrt x1, other arithmetic, on_device(): weight_sizes = jnp.sqrt(jnp.stack(squares[:4]))  5.05 us
    reduce_sum x4, other arithmetic, on_device(): update_squares = [jnp.sum(result[2] * result[2]) for result in results]  3.8 us
  transfers between devices with their start and end apart: 12, of which 11 were waited for; matrix products, arithmetic and copies ran while one was open for 0% of the time, Pallas kernels for 0%

profile of v4, /device:TPU:1, one launch (start us, length us, event | category | flops | bytes accessed | tf_op | source)
XLA Modules:
  0.0 153.4 jit_solution(1165165575015432689)
XLA Ops:
  0.7 1.4 concatenate.37
  2.1 0.8 copy.37
  2.9 0.5 broadcast.57
  3.4 1.3 reduce.7
  5.0 0.1 pad_maximum_fusion
  5.2 8.8 %collective-permute-start = (f32[4,136,384]{2,1,0:T(8,128)S(1)}, f32[4,136,384]{2,1,0:T(8,128)S(1)}, u32[]{:S(2)}, u32[]{:S(2)}) collective-permute-start(f32[4,136,384]{2,1,0:T(8,128)S(1)} %dynamic-slice_bitcast_fusion), channel_id=1, source_target_pairs={{0,1},{1,0},{2,3},{3,2},{4,5},{5,4},{6,7},{7,6},{8,9},{9,8},{10,11... | collective-permute-start | bytes 2506760 | tf_op jit(solution)/shard_map/ppermute | solution.py:31
  14.0 1.9 %collective-permute-done = f32[4,136,384]{2,1,0:T(8,128)S(1)} collective-permute-done((f32[4,136,384]{2,1,0:T(8,128)S(1)}, f32[4,136,384]{2,1,0:T(8,128)S(1)}, u32[]{:S(2)}, u32[]{:S(2)}) %collective-permute-start) | collective-permute-done | bytes 835616 | tf_op jit(solution)/shard_map/ppermute | solution.py:31
  15.9 0.1 bitcast_add_fusion
  16.1 1.9 %collective-permute-start.1 = (f32[136,384]{1,0:T(8,128)S(1)}, f32[136,384]{1,0:T(8,128)S(1)}, u32[]{:S(2)}, u32[]{:S(2)}) collective-permute-start(f32[136,384]{1,0:T(8,128)S(1)} %get-tuple-element.80), channel_id=1, source_target_pairs={{0,2},{1,3},{2,0},{3,1},{4,6},{5,7},{6,4},{7,5},{8,10},{9,11},{10,... | collective-permute-start | bytes 626696 | tf_op jit(solution)/shard_map/ppermute | solution.py:31
  18.0 1.9 %collective-permute-start.2 = (f32[136,384]{1,0:T(8,128)S(1)}, f32[136,384]{1,0:T(8,128)S(1)}, u32[]{:S(2)}, u32[]{:S(2)}) collective-permute-start(f32[136,384]{1,0:T(8,128)S(1)} %get-tuple-element.82), channel_id=1, source_target_pairs={{0,4},{1,5},{2,6},{3,7},{4,0},{5,1},{6,2},{7,3},{8,12},{9,13},{10,... | collective-permute-start | bytes 626696 | tf_op jit(solution)/shard_map/ppermute | solution.py:31
  20.0 5.7 %collective-permute-start.3 = (f32[136,384]{1,0:T(8,128)S(1)}, f32[136,384]{1,0:T(8,128)S(1)}, u32[]{:S(2)}, u32[]{:S(2)}) collective-permute-start(f32[136,384]{1,0:T(8,128)S(1)} %get-tuple-element.81), channel_id=1, source_target_pairs={{0,6},{1,7},{2,4},{3,5},{4,2},{5,3},{6,0},{7,1},{8,14},{9,15},{10,... | collective-permute-start | bytes 626696 | tf_op jit(solution)/shard_map/ppermute | solution.py:31
  25.7 2.1 %collective-permute-done.2 = f32[136,384]{1,0:T(8,128)S(1)} collective-permute-done((f32[136,384]{1,0:T(8,128)S(1)}, f32[136,384]{1,0:T(8,128)S(1)}, u32[]{:S(2)}, u32[]{:S(2)}) %collective-permute-start.2) | collective-permute-done | bytes 208928 | tf_op jit(solution)/shard_map/ppermute | solution.py:31
  27.8 5.2 %collective-permute-done.3 = f32[136,384]{1,0:T(8,128)S(1)} collective-permute-done((f32[136,384]{1,0:T(8,128)S(1)}, f32[136,384]{1,0:T(8,128)S(1)}, u32[]{:S(2)}, u32[]{:S(2)}) %collective-permute-start.3) | collective-permute-done | bytes 208928 | tf_op jit(solution)/shard_map/ppermute | solution.py:31
  33.2 2.1 %collective-permute-start.4 = (f32[80,384]{1,0:T(8,128)S(1)}, f32[80,384]{1,0:T(8,128)S(1)}, u32[]{:S(2)}, u32[]{:S(2)}) collective-permute-start(f32[80,384]{1,0:T(8,128)S(1)} %dynamic-slice_bitcast_fusion.4), channel_id=1, source_target_pairs={{0,8},{1,9},{2,10},{3,11},{4,12},{5,13},{6,14},{7,15},{8,0},{9,1},... | collective-permute-start | bytes 368648 | tf_op jit(solution)/shard_map/ppermute | solution.py:31
  35.2 4.4 %collective-permute-done.4 = f32[80,384]{1,0:T(8,128)S(1)} collective-permute-done((f32[80,384]{1,0:T(8,128)S(1)}, f32[80,384]{1,0:T(8,128)S(1)}, u32[]{:S(2)}, u32[]{:S(2)}) %collective-permute-start.4) | collective-permute-done | bytes 122912 | tf_op jit(solution)/shard_map/ppermute | solution.py:31
  39.7 2.1 %collective-permute-start.5 = (f32[40,384]{1,0:T(8,128)S(1)}, f32[40,384]{1,0:T(8,128)S(1)}, u32[]{:S(2)}, u32[]{:S(2)}) collective-permute-start(f32[40,384]{1,0:T(8,128)S(1)} %dynamic-slice_bitcast_fusion.5), channel_id=1, source_target_pairs={{0,32},{1,33},{2,34},{3,35},{4,36},{5,37},{6,38},{7,39},{8,40},{9,... | collective-permute-start | bytes 184328 | tf_op jit(solution)/shard_map/ppermute | solution.py:31
  41.8 3.0 %collective-permute-done.5 = f32[40,384]{1,0:T(8,128)S(1)} collective-permute-done((f32[40,384]{1,0:T(8,128)S(1)}, f32[40,384]{1,0:T(8,128)S(1)}, u32[]{:S(2)}, u32[]{:S(2)}) %collective-permute-start.5) | collective-permute-done | bytes 61472 | tf_op jit(solution)/shard_map/ppermute | solution.py:31
  44.8 2.9 %collective-permute-start.6 = (f32[40,384]{1,0:T(8,128)S(1)}, f32[40,384]{1,0:T(8,128)S(1)}, u32[]{:S(2)}, u32[]{:S(2)}) collective-permute-start(f32[40,384]{1,0:T(8,128)S(1)} %bitcast_add_fusion.3), channel_id=1, source_target_pairs={{0,16},{1,17},{2,18},{3,19},{4,20},{5,21},{6,22},{7,23},{8,24},{9,... | collective-permute-start | bytes 184328 | tf_op jit(solution)/shard_map/ppermute | solution.py:31
  47.8 3.5 %collective-permute-done.6 = f32[40,384]{1,0:T(8,128)S(1)} collective-permute-done((f32[40,384]{1,0:T(8,128)S(1)}, f32[40,384]{1,0:T(8,128)S(1)}, u32[]{:S(2)}, u32[]{:S(2)}) %collective-permute-start.6) | collective-permute-done | bytes 61472 | tf_op jit(solution)/shard_map/ppermute | solution.py:31
  51.3 3.3 %collective-permute-start.7 = (f32[40,384]{1,0:T(8,128)S(1)}, f32[40,384]{1,0:T(8,128)S(1)}, u32[]{:S(2)}, u32[]{:S(2)}) collective-permute-start(f32[40,384]{1,0:T(8,128)S(1)} %add.173), channel_id=1, source_target_pairs={{0,64},{1,65},{2,66},{3,67},{4,68},{5,69},{6,70},{7,71},{8,72},{9,... | collective-permute-start | bytes 184328 | tf_op jit(solution)/shard_map/ppermute | solution.py:31
  54.7 3.3 %collective-permute-done.7 = f32[40,384]{1,0:T(8,128)S(1)} collective-permute-done((f32[40,384]{1,0:T(8,128)S(1)}, f32[40,384]{1,0:T(8,128)S(1)}, u32[]{:S(2)}, u32[]{:S(2)}) %collective-permute-start.7) | collective-permute-done | bytes 61472 | tf_op jit(solution)/shard_map/ppermute | solution.py:31
  58.0 7.1 %collective-permute-start.8 = (f32[40,384]{1,0:T(8,128)S(1)}, f32[40,384]{1,0:T(8,128)S(1)}, u32[]{:S(2)}, u32[]{:S(2)}) collective-permute-start(f32[40,384]{1,0:T(8,128)S(1)} %add.174), channel_id=1, source_target_pairs={{0,128},{1,129},{2,130},{3,131},{4,132},{5,133},{6,134},{7,135},{8... | collective-permute-start | bytes 184328 | tf_op jit(solution)/shard_map/ppermute | solution.py:31
  65.1 1.8 %collective-permute-done.8 = f32[40,384]{1,0:T(8,128)S(1)} collective-permute-done((f32[40,384]{1,0:T(8,128)S(1)}, f32[40,384]{1,0:T(8,128)S(1)}, u32[]{:S(2)}, u32[]{:S(2)}) %collective-permute-start.8) | collective-permute-done | bytes 61472 | tf_op jit(solution)/shard_map/ppermute | solution.py:31
  66.9 15.4 %collective-permute-start.9 = (f32[40,384]{1,0:T(8,128)S(1)}, f32[40,384]{1,0:T(8,128)S(1)}, u32[]{:S(2)}, u32[]{:S(2)}) collective-permute-start(f32[40,384]{1,0:T(8,128)S(1)} %add.175), channel_id=1, source_target_pairs={{0,256},{1,257},{2,258},{3,259},{4,260},{5,261},{6,262},{7,263},{8... | collective-permute-start | bytes 184328 | tf_op jit(solution)/shard_map/ppermute | solution.py:31
  82.3 1.6 %collective-permute-done.9 = f32[40,384]{1,0:T(8,128)S(1)} collective-permute-done((f32[40,384]{1,0:T(8,128)S(1)}, f32[40,384]{1,0:T(8,128)S(1)}, u32[]{:S(2)}, u32[]{:S(2)}) %collective-permute-start.9) | collective-permute-done | bytes 61472 | tf_op jit(solution)/shard_map/ppermute | solution.py:31
  83.9 1.9 %collective-permute-start.10 = (f32[40,384]{1,0:T(8,128)S(1)}, f32[40,384]{1,0:T(8,128)S(1)}, u32[]{:S(2)}, u32[]{:S(2)}) collective-permute-start(f32[40,384]{1,0:T(8,128)S(1)} %add.176), channel_id=1, source_target_pairs={{0,32},{1,33},{2,34},{3,35},{4,36},{5,37},{6,38},{7,39},{8,40},{9,... | collective-permute-start | bytes 184328 | tf_op jit(solution)/shard_map/ppermute | solution.py:31
  85.9 3.6 %collective-permute-done.10 = f32[40,384]{1,0:T(8,128)S(1)} collective-permute-done((f32[40,384]{1,0:T(8,128)S(1)}, f32[40,384]{1,0:T(8,128)S(1)}, u32[]{:S(2)}, u32[]{:S(2)}) %collective-permute-start.10) | collective-permute-done | bytes 61472 | tf_op jit(solution)/shard_map/ppermute | solution.py:31
  89.5 3.1 %collective-permute-start.11 = (f32[80,384]{1,0:T(8,128)S(1)}, f32[80,384]{1,0:T(8,128)S(1)}, u32[]{:S(2)}, u32[]{:S(2)}) collective-permute-start(f32[80,384]{1,0:T(8,128)S(1)} %pad_maximum_fusion.1), channel_id=1, source_target_pairs={{0,8},{1,9},{2,10},{3,11},{4,12},{5,13},{6,14},{7,15},{8,0},{9,1},... | collective-permute-start | bytes 368648 | tf_op jit(solution)/shard_map/ppermute | solution.py:31
  92.6 2.5 %collective-permute-done.11 = f32[80,384]{1,0:T(8,128)S(1)} collective-permute-done((f32[80,384]{1,0:T(8,128)S(1)}, f32[80,384]{1,0:T(8,128)S(1)}, u32[]{:S(2)}, u32[]{:S(2)}) %collective-permute-start.11) | collective-permute-done | bytes 122912 | tf_op jit(solution)/shard_map/ppermute | solution.py:31
  95.1 0.1 slice_reduce_fusion
  95.2 0.7 multiply_reduce_fusion.1
  96.0 1.1 multiply_reduce_fusion.6
  97.1 0.8 multiply_reduce_fusion
  97.9 1.2 multiply_reduce_fusion.4
  99.2 21.0 %all-reduce.3 = (f32[]{:T(128)}, f32[]{:T(128)}, f32[]{:T(128)}, f32[]{:T(128)}, f32[]{:T(128)}, /*index=5*/f32[]{:T(128)}, f32[]{:T(128)}, f32[]{:T(128)}) all-reduce(f32[]{:T(128)} %get-tuple-element.90, f32[]{:T(128)} %get-tuple-element.95, f32[]{:T(128)} %get-tuple-element.59, ...), channel_id=1, replica_groups=mesh['replica'=64,'shard'=8] {'shard'}, use_global_device_ids=true, to_apply=%region_7.8 | all-reduce | flops 8 | bytes 64 | tf_op jit(solution)/shard_map/psum | solution.py:143
  120.2 5.1 %fusion.8 = f32[4]{0:T(128)S(1)} fusion(f32[1]{0:T(128)} %bitcast.3, f32[1]{0:T(128)} %bitcast.2, f32[1]{0:T(128)} %bitcast.1, f32[1]{0:T(128)} %bitcast, f32[1]{0:T(128)} %bitcast.23, f32[1]{0:T(128)} %bitcast.22, f32[1]{0:T(128)} %bitcast.20, f32[1]{0:T(128)} %bitcast.19), kind=kLoop, calls=%fused_computation.52 | loop fusion | flops 32 | bytes 48 | tf_op jit(solution)/shard_map/div | solution.py:146
  125.3 0.6 fusion.15
  126.5 0.1 reshape.206
  128.8 0.1 concatenate.43
  128.9 0.1 reshape.212
  129.0 15.2 %all-gather.1 = bf16[8,1,49280]{2,1,0:T(2,128)(2,1)S(1)} all-gather(bf16[1,1,49280]{2,1,0:T(2,128)(2,1)S(1)} %reshape.212), channel_id=2, replica_groups=mesh['replica'=64,'shard'=8] {'shard'}, dimensions={0}, use_global_device_ids=true | all-gather | bytes 887040 | tf_op jit(solution)/shard_map/all_gather | solution.py:153
  144.3 0.1 copy.45
  144.5 0.9 reshape.207
  145.4 0.9 reshape.208
  146.5 0.7 copy.39
  147.1 0.6 reshape.209
  147.8 5.1 %maximum_sqrt_fusion.2 = (f32[1,4]{1,0:T(1,128)S(1)}, f32[1,4]{1,0:T(1,128)S(1)}) fusion(f32[1,1]{1,0:T(1,128)} %bitcast.31, f32[1,1]{1,0:T(1,128)} %bitcast.30, f32[1,1]{1,0:T(1,128)} %bitcast.29, f32[1,1]{1,0:T(1,128)} %bitcast.28, f32[1,1]{1,0:T(1,128)} %bitcast.35, f32[1,1]{1,0:T(1,128)} %bitcast.34, f32[1,1]{1,0:T(1,128)} %bitcast.33, f32[1,1]{1,0:T(1,128)} %bitcast.32), kind=kLoop, calls=%fused_computation.55 | loop fusion | flops 24 | bytes 64 | tf_op jit(solution)/shard_map/sqrt | solution.py:144
  152.8 0.6 pad_maximum_fusion.3
  (70 shorter events, 1.2 us)
Async XLA Ops:
  0.6 4.3 %copy-start = (f32[1,512,384]{2,1,0:T(8,128)S(1)}, f32[1,512,384]{2,1,0:T(8,128)}, u32[]{:S(2)}) copy-start(f32[1,512,384]{2,1,0:T(8,128)} %param.16) | copy-start | bytes 2359300
  5.2 10.8 %collective-permute-start = (f32[4,136,384]{2,1,0:T(8,128)S(1)}, f32[4,136,384]{2,1,0:T(8,128)S(1)}, u32[]{:S(2)}, u32[]{:S(2)}) collective-permute-start(f32[4,136,384]{2,1,0:T(8,128)S(1)} %dynamic-slice_bitcast_fusion), channel_id=1, source_target_pairs={{0,1},{1,0},{2,3},{3,2},{4,5},{5,4},{6,7},{7,6},{8,9},{9,8},{10,11... | collective-permute-start | bytes 2506760 | tf_op jit(solution)/shard_map/ppermute | solution.py:31
  16.1 9.6 %collective-permute-start.1 = (f32[136,384]{1,0:T(8,128)S(1)}, f32[136,384]{1,0:T(8,128)S(1)}, u32[]{:S(2)}, u32[]{:S(2)}) collective-permute-start(f32[136,384]{1,0:T(8,128)S(1)} %get-tuple-element.80), channel_id=1, source_target_pairs={{0,2},{1,3},{2,0},{3,1},{4,6},{5,7},{6,4},{7,5},{8,10},{9,11},{10,... | collective-permute-start | bytes 626696 | tf_op jit(solution)/shard_map/ppermute | solution.py:31
  18.0 9.8 %collective-permute-start.2 = (f32[136,384]{1,0:T(8,128)S(1)}, f32[136,384]{1,0:T(8,128)S(1)}, u32[]{:S(2)}, u32[]{:S(2)}) collective-permute-start(f32[136,384]{1,0:T(8,128)S(1)} %get-tuple-element.82), channel_id=1, source_target_pairs={{0,4},{1,5},{2,6},{3,7},{4,0},{5,1},{6,2},{7,3},{8,12},{9,13},{10,... | collective-permute-start | bytes 626696 | tf_op jit(solution)/shard_map/ppermute | solution.py:31
  20.0 13.1 %collective-permute-start.3 = (f32[136,384]{1,0:T(8,128)S(1)}, f32[136,384]{1,0:T(8,128)S(1)}, u32[]{:S(2)}, u32[]{:S(2)}) collective-permute-start(f32[136,384]{1,0:T(8,128)S(1)} %get-tuple-element.81), channel_id=1, source_target_pairs={{0,6},{1,7},{2,4},{3,5},{4,2},{5,3},{6,0},{7,1},{8,14},{9,15},{10,... | collective-permute-start | bytes 626696 | tf_op jit(solution)/shard_map/ppermute | solution.py:31
  33.1 62.1 %copy-start.4 = (f32[64,384]{1,0:T(8,128)S(1)}, f32[64,384]{1,0:T(8,128)}, u32[]{:S(2)}) copy-start(f32[64,384]{1,0:T(8,128)} %param.20) | copy-start | bytes 294916
  33.1 62.1 %copy-start.9 = (f32[64,384]{1,0:T(8,128)S(1)}, f32[64,384]{1,0:T(8,128)}, u32[]{:S(2)}) copy-start(f32[64,384]{1,0:T(8,128)} %param.28) | copy-start | bytes 294916
  33.1 62.1 %copy-start.10 = (f32[64,384]{1,0:T(8,128)S(1)}, f32[64,384]{1,0:T(8,128)}, u32[]{:S(2)}) copy-start(f32[64,384]{1,0:T(8,128)} %param.24) | copy-start | bytes 294916
  33.2 6.4 %collective-permute-start.4 = (f32[80,384]{1,0:T(8,128)S(1)}, f32[80,384]{1,0:T(8,128)S(1)}, u32[]{:S(2)}, u32[]{:S(2)}) collective-permute-start(f32[80,384]{1,0:T(8,128)S(1)} %dynamic-slice_bitcast_fusion.4), channel_id=1, source_target_pairs={{0,8},{1,9},{2,10},{3,11},{4,12},{5,13},{6,14},{7,15},{8,0},{9,1},... | collective-permute-start | bytes 368648 | tf_op jit(solution)/shard_map/ppermute | solution.py:31
  39.6 56.4 %copy-start.15 = (f32[64]{0:T(128)S(1)}, f32[64]{0:T(128)}, u32[]{:S(2)}) copy-start(f32[64]{0:T(128)} %param.22) | copy-start | bytes 772
  39.6 56.4 %copy-start.16 = (f32[64]{0:T(128)S(1)}, f32[64]{0:T(128)}, u32[]{:S(2)}) copy-start(f32[64]{0:T(128)} %param.30) | copy-start | bytes 772
  39.6 56.4 %copy-start.17 = (f32[64]{0:T(128)S(1)}, f32[64]{0:T(128)}, u32[]{:S(2)}) copy-start(f32[64]{0:T(128)} %param.26) | copy-start | bytes 772
  39.6 57.5 %copy-start.1 = (f32[48,512]{1,0:T(8,128)S(1)}, f32[48,512]{1,0:T(8,128)}, u32[]{:S(2)}) copy-start(f32[48,512]{1,0:T(8,128)} %param.21) | copy-start | bytes 294916
  39.7 57.5 %copy-start.7 = (f32[48,512]{1,0:T(8,128)S(1)}, f32[48,512]{1,0:T(8,128)}, u32[]{:S(2)}) copy-start(f32[48,512]{1,0:T(8,128)} %param.29) | copy-start | bytes 294916
  39.7 57.5 %copy-start.8 = (f32[48,512]{1,0:T(8,128)S(1)}, f32[48,512]{1,0:T(8,128)}, u32[]{:S(2)}) copy-start(f32[48,512]{1,0:T(8,128)} %param.25) | copy-start | bytes 294916
  39.7 5.1 %collective-permute-start.5 = (f32[40,384]{1,0:T(8,128)S(1)}, f32[40,384]{1,0:T(8,128)S(1)}, u32[]{:S(2)}, u32[]{:S(2)}) collective-permute-start(f32[40,384]{1,0:T(8,128)S(1)} %dynamic-slice_bitcast_fusion.5), channel_id=1, source_target_pairs={{0,32},{1,33},{2,34},{3,35},{4,36},{5,37},{6,38},{7,39},{8,40},{9,... | collective-permute-start | bytes 184328 | tf_op jit(solution)/shard_map/ppermute | solution.py:31
  44.8 6.5 %collective-permute-start.6 = (f32[40,384]{1,0:T(8,128)S(1)}, f32[40,384]{1,0:T(8,128)S(1)}, u32[]{:S(2)}, u32[]{:S(2)}) collective-permute-start(f32[40,384]{1,0:T(8,128)S(1)} %bitcast_add_fusion.3), channel_id=1, source_target_pairs={{0,16},{1,17},{2,18},{3,19},{4,20},{5,21},{6,22},{7,23},{8,24},{9,... | collective-permute-start | bytes 184328 | tf_op jit(solution)/shard_map/ppermute | solution.py:31
  51.3 46.6 %copy-start.12 = (f32[4,6]{1,0:T(4,128)S(1)}, f32[4,6]{1,0:T(4,128)}, u32[]{:S(2)}) copy-start(f32[4,6]{1,0:T(4,128)} %param.23) | copy-start | bytes 292
  51.3 46.6 %copy-start.13 = (f32[4,6]{1,0:T(4,128)S(1)}, f32[4,6]{1,0:T(4,128)}, u32[]{:S(2)}) copy-start(f32[4,6]{1,0:T(4,128)} %param.31) | copy-start | bytes 292
  51.3 46.6 %copy-start.14 = (f32[4,6]{1,0:T(4,128)S(1)}, f32[4,6]{1,0:T(4,128)}, u32[]{:S(2)}) copy-start(f32[4,6]{1,0:T(4,128)} %param.27) | copy-start | bytes 292
  51.3 6.7 %collective-permute-start.7 = (f32[40,384]{1,0:T(8,128)S(1)}, f32[40,384]{1,0:T(8,128)S(1)}, u32[]{:S(2)}, u32[]{:S(2)}) collective-permute-start(f32[40,384]{1,0:T(8,128)S(1)} %add.173), channel_id=1, source_target_pairs={{0,64},{1,65},{2,66},{3,67},{4,68},{5,69},{6,70},{7,71},{8,72},{9,... | collective-permute-start | bytes 184328 | tf_op jit(solution)/shard_map/ppermute | solution.py:31
  58.0 8.9 %collective-permute-start.8 = (f32[40,384]{1,0:T(8,128)S(1)}, f32[40,384]{1,0:T(8,128)S(1)}, u32[]{:S(2)}, u32[]{:S(2)}) collective-permute-start(f32[40,384]{1,0:T(8,128)S(1)} %add.174), channel_id=1, source_target_pairs={{0,128},{1,129},{2,130},{3,131},{4,132},{5,133},{6,134},{7,135},{8... | collective-permute-start | bytes 184328 | tf_op jit(solution)/shard_map/ppermute | solution.py:31
  66.9 17.0 %collective-permute-start.9 = (f32[40,384]{1,0:T(8,128)S(1)}, f32[40,384]{1,0:T(8,128)S(1)}, u32[]{:S(2)}, u32[]{:S(2)}) collective-permute-start(f32[40,384]{1,0:T(8,128)S(1)} %add.175), channel_id=1, source_target_pairs={{0,256},{1,257},{2,258},{3,259},{4,260},{5,261},{6,262},{7,263},{8... | collective-permute-start | bytes 184328 | tf_op jit(solution)/shard_map/ppermute | solution.py:31
  83.9 5.5 %collective-permute-start.10 = (f32[40,384]{1,0:T(8,128)S(1)}, f32[40,384]{1,0:T(8,128)S(1)}, u32[]{:S(2)}, u32[]{:S(2)}) collective-permute-start(f32[40,384]{1,0:T(8,128)S(1)} %add.176), channel_id=1, source_target_pairs={{0,32},{1,33},{2,34},{3,35},{4,36},{5,37},{6,38},{7,39},{8,40},{9,... | collective-permute-start | bytes 184328 | tf_op jit(solution)/shard_map/ppermute | solution.py:31
  89.5 5.6 %collective-permute-start.11 = (f32[80,384]{1,0:T(8,128)S(1)}, f32[80,384]{1,0:T(8,128)S(1)}, u32[]{:S(2)}, u32[]{:S(2)}) collective-permute-start(f32[80,384]{1,0:T(8,128)S(1)} %pad_maximum_fusion.1), channel_id=1, source_target_pairs={{0,8},{1,9},{2,10},{3,11},{4,12},{5,13},{6,14},{7,15},{8,0},{9,1},... | collective-permute-start | bytes 368648 | tf_op jit(solution)/shard_map/ppermute | solution.py:31
  95.9 48.4 %copy-start.5 = (f32[64,384]{1,0:T(8,128)}, f32[64,384]{1,0:T(8,128)S(1)}, u32[]{:S(2)}) copy-start(f32[64,384]{1,0:T(8,128)S(1)} %get-tuple-element.76) | copy-start | bytes 294916
  95.9 48.4 %copy-start.6 = (f32[64,384]{1,0:T(8,128)}, f32[64,384]{1,0:T(8,128)S(1)}, u32[]{:S(2)}) copy-start(f32[64,384]{1,0:T(8,128)S(1)} %get-tuple-element.77) | copy-start | bytes 294916
  97.9 46.4 %copy-start.2 = (f32[48,512]{1,0:T(8,128)}, f32[48,512]{1,0:T(8,128)S(1)}, u32[]{:S(2)}) copy-start(f32[48,512]{1,0:T(8,128)S(1)} %get-tuple-element.78) | copy-start | bytes 294916
  97.9 46.4 %copy-start.3 = (f32[48,512]{1,0:T(8,128)}, f32[48,512]{1,0:T(8,128)S(1)}, u32[]{:S(2)}) copy-start(f32[48,512]{1,0:T(8,128)S(1)} %get-tuple-element.79) | copy-start | bytes 294916
  125.3 19.1 %copy-start.11 = (f32[4]{0:T(128)}, f32[4]{0:T(128)S(1)}, u32[]{:S(2)}) copy-start(f32[4]{0:T(128)S(1)} %fusion.8) | copy-start | bytes 52

commit v5 on v4

--- a/solution.py
+++ b/solution.py
@@ -73,6 +73,15 @@
         first = bit_of(index, bit) == 0
         total = jnp.concatenate([jnp.where(first, total, other), jnp.where(first, other, total)], axis=0)
     return total[:rows]
+
+
+def as_tile(value, rows, lanes):
+    if value.size == rows * lanes:
+        return value.reshape(rows, lanes)
+    flat = value.reshape(1, -1)
+    flat = jnp.pad(flat, ((0, 0), (0, lanes * (-(-flat.shape[1] // lanes)) - flat.shape[1])))
+    flat = flat.reshape(-1, lanes)
+    return jnp.pad(flat, ((0, rows - flat.shape[0]), (0, 0)))
 
 
 def on_device(
@@ -138,11 +147,12 @@
         )
         for member in range(4)
     ]
-    weight_squares = [jnp.sum(weight * weight) for weight in weights]
-    update_squares = [jnp.sum(result[2] * result[2]) for result in results]
-    squares = lax.psum(tuple(weight_squares + update_squares), "shard")
-    weight_sizes = jnp.sqrt(jnp.stack(squares[:4]))
-    update_sizes = jnp.sqrt(jnp.stack(squares[4:]))
+    terms = [as_tile(weight, query_rows, lanes) for weight in weights]
+    terms += [as_tile(result[2], query_rows, lanes) for result in results]
+    stacked = jnp.stack(terms)
+    squares = lax.psum(jnp.sum(stacked * stacked, axis=(1, 2)), "shard")
+    weight_sizes = jnp.sqrt(squares[:4])
+    update_sizes = jnp.sqrt(squares[4:])
     trust_ratios = weight_sizes / (update_sizes + 1e-06)
     shards_out = [
         (weights[member] - 0.01 * trust_ratios[member] * results[member][2]).astype(jnp.bfloat16).reshape(-1)

time: 154 us -> 142 us (0.922)
  other arithmetic: 16.4 us -> 4.63 us
    div x1 -> x0, other arithmetic: 5.06 us -> none  [on_device(): trust_ratios = weight_sizes / (update_sizes + 1e-06)]
    sqrt x1 -> x0, other arithmetic: 5.05 us -> none  [on_device(): weight_sizes = jnp.sqrt(jnp.stack(squares[:4]))]
    reduce_sum x4 -> x1, other arithmetic: 3.8 us -> 0.17 us  [on_device(): squares = lax.psum(jnp.sum(stacked * stacked, axis=(1, 2)), 'shard')]
    add x0 -> x3, other arithmetic: none -> 1.83 us  [step_math(): update = moment_next / (jnp.sqrt(second_next) + 1e-06) + decay_rate * weight]
where the time goes in v5:
time: 142 us; the launch traced here: 141 us
  starting transfers between devices  56.2 us (40%)
  blocking collectives  35.5 us (25%)
  waiting for transfers between devices  32.7 us (23%)
  local copies, waits for them, and re-layouts  8.05 us (6%)
  other arithmetic  4.63 us (3%)
  between operations  3.85 us (3%)
    ppermute x12, starting transfers between devices, exchange(): return lax.ppermute(value, AXES, [(d, d ^ mask) for d in range(devices)])  56.2 us
    ppermute x12, waiting for transfers between devices, exchange(): return lax.ppermute(value, AXES, [(d, d ^ mask) for d in range(devices)])  32.7 us
    psum x1, blocking collectives, on_device(): squares = lax.psum(jnp.sum(stacked * stacked, axis=(1, 2)), 'shard')  20.3 us
    all_gather x1, blocking collectives, on_device(): lax.all_gather(jnp.concatenate(shards_out), 'shard', axis=0, tiled=False)  15.2 us
  transfers between devices with their start and end apart: 12, of which 11 were waited for; matrix products, arithmetic and copies ran while one was open for 0% of the time, Pallas kernels for 0%

profile of v5, /device:TPU:1, one launch (start us, length us, event | category | flops | bytes accessed | tf_op | source)
XLA Modules:
  0.0 141.0 jit_solution(514536368523868865)
XLA Ops:
  0.7 1.4 concatenate.23
  2.1 0.8 copy.37
  2.9 0.5 broadcast.73
  3.4 1.3 reduce.7
  5.0 0.1 pad_maximum_fusion
  5.2 8.8 %collective-permute-start = (f32[4,136,384]{2,1,0:T(8,128)S(1)}, f32[4,136,384]{2,1,0:T(8,128)S(1)}, u32[]{:S(2)}, u32[]{:S(2)}) collective-permute-start(f32[4,136,384]{2,1,0:T(8,128)S(1)} %dynamic-slice_bitcast_fusion), channel_id=1, source_target_pairs={{0,1},{1,0},{2,3},{3,2},{4,5},{5,4},{6,7},{7,6},{8,9},{9,8},{10,11... | collective-permute-start | bytes 2506760 | tf_op jit(solution)/shard_map/ppermute | solution.py:31
  14.0 1.9 %collective-permute-done = f32[4,136,384]{2,1,0:T(8,128)S(1)} collective-permute-done((f32[4,136,384]{2,1,0:T(8,128)S(1)}, f32[4,136,384]{2,1,0:T(8,128)S(1)}, u32[]{:S(2)}, u32[]{:S(2)}) %collective-permute-start) | collective-permute-done | bytes 835616 | tf_op jit(solution)/shard_map/ppermute | solution.py:31
  15.9 0.1 bitcast_add_fusion
  16.1 2.1 %collective-permute-start.1 = (f32[136,384]{1,0:T(8,128)S(1)}, f32[136,384]{1,0:T(8,128)S(1)}, u32[]{:S(2)}, u32[]{:S(2)}) collective-permute-start(f32[136,384]{1,0:T(8,128)S(1)} %get-tuple-element.68), channel_id=1, source_target_pairs={{0,2},{1,3},{2,0},{3,1},{4,6},{5,7},{6,4},{7,5},{8,10},{9,11},{10,... | collective-permute-start | bytes 626696 | tf_op jit(solution)/shard_map/ppermute | solution.py:31
  18.2 1.9 %collective-permute-start.2 = (f32[136,384]{1,0:T(8,128)S(1)}, f32[136,384]{1,0:T(8,128)S(1)}, u32[]{:S(2)}, u32[]{:S(2)}) collective-permute-start(f32[136,384]{1,0:T(8,128)S(1)} %get-tuple-element.70), channel_id=1, source_target_pairs={{0,4},{1,5},{2,6},{3,7},{4,0},{5,1},{6,2},{7,3},{8,12},{9,13},{10,... | collective-permute-start | bytes 626696 | tf_op jit(solution)/shard_map/ppermute | solution.py:31
  20.1 5.7 %collective-permute-start.3 = (f32[136,384]{1,0:T(8,128)S(1)}, f32[136,384]{1,0:T(8,128)S(1)}, u32[]{:S(2)}, u32[]{:S(2)}) collective-permute-start(f32[136,384]{1,0:T(8,128)S(1)} %get-tuple-element.69), channel_id=1, source_target_pairs={{0,6},{1,7},{2,4},{3,5},{4,2},{5,3},{6,0},{7,1},{8,14},{9,15},{10,... | collective-permute-start | bytes 626696 | tf_op jit(solution)/shard_map/ppermute | solution.py:31
  25.9 2.1 %collective-permute-done.2 = f32[136,384]{1,0:T(8,128)S(1)} collective-permute-done((f32[136,384]{1,0:T(8,128)S(1)}, f32[136,384]{1,0:T(8,128)S(1)}, u32[]{:S(2)}, u32[]{:S(2)}) %collective-permute-start.2) | collective-permute-done | bytes 208928 | tf_op jit(solution)/shard_map/ppermute | solution.py:31
  28.0 5.2 %collective-permute-done.3 = f32[136,384]{1,0:T(8,128)S(1)} collective-permute-done((f32[136,384]{1,0:T(8,128)S(1)}, f32[136,384]{1,0:T(8,128)S(1)}, u32[]{:S(2)}, u32[]{:S(2)}) %collective-permute-start.3) | collective-permute-done | bytes 208928 | tf_op jit(solution)/shard_map/ppermute | solution.py:31
  33.3 1.9 %collective-permute-start.4 = (f32[80,384]{1,0:T(8,128)S(1)}, f32[80,384]{1,0:T(8,128)S(1)}, u32[]{:S(2)}, u32[]{:S(2)}) collective-permute-start(f32[80,384]{1,0:T(8,128)S(1)} %dynamic-slice_bitcast_fusion.4), channel_id=1, source_target_pairs={{0,8},{1,9},{2,10},{3,11},{4,12},{5,13},{6,14},{7,15},{8,0},{9,1},... | collective-permute-start | bytes 368648 | tf_op jit(solution)/shard_map/ppermute | solution.py:31
  35.2 4.4 %collective-permute-done.4 = f32[80,384]{1,0:T(8,128)S(1)} collective-permute-done((f32[80,384]{1,0:T(8,128)S(1)}, f32[80,384]{1,0:T(8,128)S(1)}, u32[]{:S(2)}, u32[]{:S(2)}) %collective-permute-start.4) | collective-permute-done | bytes 122912 | tf_op jit(solution)/shard_map/ppermute | solution.py:31
  39.7 2.1 %collective-permute-start.5 = (f32[40,384]{1,0:T(8,128)S(1)}, f32[40,384]{1,0:T(8,128)S(1)}, u32[]{:S(2)}, u32[]{:S(2)}) collective-permute-start(f32[40,384]{1,0:T(8,128)S(1)} %dynamic-slice_bitcast_fusion.5), channel_id=1, source_target_pairs={{0,32},{1,33},{2,34},{3,35},{4,36},{5,37},{6,38},{7,39},{8,40},{9,... | collective-permute-start | bytes 184328 | tf_op jit(solution)/shard_map/ppermute | solution.py:31
  41.7 3.0 %collective-permute-done.5 = f32[40,384]{1,0:T(8,128)S(1)} collective-permute-done((f32[40,384]{1,0:T(8,128)S(1)}, f32[40,384]{1,0:T(8,128)S(1)}, u32[]{:S(2)}, u32[]{:S(2)}) %collective-permute-start.5) | collective-permute-done | bytes 61472 | tf_op jit(solution)/shard_map/ppermute | solution.py:31
  44.8 2.9 %collective-permute-start.6 = (f32[40,384]{1,0:T(8,128)S(1)}, f32[40,384]{1,0:T(8,128)S(1)}, u32[]{:S(2)}, u32[]{:S(2)}) collective-permute-start(f32[40,384]{1,0:T(8,128)S(1)} %bitcast_add_fusion.3), channel_id=1, source_target_pairs={{0,16},{1,17},{2,18},{3,19},{4,20},{5,21},{6,22},{7,23},{8,24},{9,... | collective-permute-start | bytes 184328 | tf_op jit(solution)/shard_map/ppermute | solution.py:31
  47.7 3.5 %collective-permute-done.6 = f32[40,384]{1,0:T(8,128)S(1)} collective-permute-done((f32[40,384]{1,0:T(8,128)S(1)}, f32[40,384]{1,0:T(8,128)S(1)}, u32[]{:S(2)}, u32[]{:S(2)}) %collective-permute-start.6) | collective-permute-done | bytes 61472 | tf_op jit(solution)/shard_map/ppermute | solution.py:31
  51.3 3.2 %collective-permute-start.7 = (f32[40,384]{1,0:T(8,128)S(1)}, f32[40,384]{1,0:T(8,128)S(1)}, u32[]{:S(2)}, u32[]{:S(2)}) collective-permute-start(f32[40,384]{1,0:T(8,128)S(1)} %add.175), channel_id=1, source_target_pairs={{0,64},{1,65},{2,66},{3,67},{4,68},{5,69},{6,70},{7,71},{8,72},{9,... | collective-permute-start | bytes 184328 | tf_op jit(solution)/shard_map/ppermute | solution.py:31
  54.4 3.3 %collective-permute-done.7 = f32[40,384]{1,0:T(8,128)S(1)} collective-permute-done((f32[40,384]{1,0:T(8,128)S(1)}, f32[40,384]{1,0:T(8,128)S(1)}, u32[]{:S(2)}, u32[]{:S(2)}) %collective-permute-start.7) | collective-permute-done | bytes 61472 | tf_op jit(solution)/shard_map/ppermute | solution.py:31
  57.8 7.1 %collective-permute-start.8 = (f32[40,384]{1,0:T(8,128)S(1)}, f32[40,384]{1,0:T(8,128)S(1)}, u32[]{:S(2)}, u32[]{:S(2)}) collective-permute-start(f32[40,384]{1,0:T(8,128)S(1)} %add.176), channel_id=1, source_target_pairs={{0,128},{1,129},{2,130},{3,131},{4,132},{5,133},{6,134},{7,135},{8... | collective-permute-start | bytes 184328 | tf_op jit(solution)/shard_map/ppermute | solution.py:31
  64.9 1.8 %collective-permute-done.8 = f32[40,384]{1,0:T(8,128)S(1)} collective-permute-done((f32[40,384]{1,0:T(8,128)S(1)}, f32[40,384]{1,0:T(8,128)S(1)}, u32[]{:S(2)}, u32[]{:S(2)}) %collective-permute-start.8) | collective-permute-done | bytes 61472 | tf_op jit(solution)/shard_map/ppermute | solution.py:31
  66.7 15.5 %collective-permute-start.9 = (f32[40,384]{1,0:T(8,128)S(1)}, f32[40,384]{1,0:T(8,128)S(1)}, u32[]{:S(2)}, u32[]{:S(2)}) collective-permute-start(f32[40,384]{1,0:T(8,128)S(1)} %add.177), channel_id=1, source_target_pairs={{0,256},{1,257},{2,258},{3,259},{4,260},{5,261},{6,262},{7,263},{8... | collective-permute-start | bytes 184328 | tf_op jit(solution)/shard_map/ppermute | solution.py:31
  82.3 1.5 %collective-permute-done.9 = f32[40,384]{1,0:T(8,128)S(1)} collective-permute-done((f32[40,384]{1,0:T(8,128)S(1)}, f32[40,384]{1,0:T(8,128)S(1)}, u32[]{:S(2)}, u32[]{:S(2)}) %collective-permute-start.9) | collective-permute-done | bytes 61472 | tf_op jit(solution)/shard_map/ppermute | solution.py:31
  83.9 1.9 %collective-permute-start.10 = (f32[40,384]{1,0:T(8,128)S(1)}, f32[40,384]{1,0:T(8,128)S(1)}, u32[]{:S(2)}, u32[]{:S(2)}) collective-permute-start(f32[40,384]{1,0:T(8,128)S(1)} %add.178), channel_id=1, source_target_pairs={{0,32},{1,33},{2,34},{3,35},{4,36},{5,37},{6,38},{7,39},{8,40},{9,... | collective-permute-start | bytes 184328 | tf_op jit(solution)/shard_map/ppermute | solution.py:31
  85.8 3.6 %collective-permute-done.10 = f32[40,384]{1,0:T(8,128)S(1)} collective-permute-done((f32[40,384]{1,0:T(8,128)S(1)}, f32[40,384]{1,0:T(8,128)S(1)}, u32[]{:S(2)}, u32[]{:S(2)}) %collective-permute-start.10) | collective-permute-done | bytes 61472 | tf_op jit(solution)/shard_map/ppermute | solution.py:31
  89.5 3.1 %collective-permute-start.11 = (f32[80,384]{1,0:T(8,128)S(1)}, f32[80,384]{1,0:T(8,128)S(1)}, u32[]{:S(2)}, u32[]{:S(2)}) collective-permute-start(f32[80,384]{1,0:T(8,128)S(1)} %pad_maximum_fusion.1), channel_id=1, source_target_pairs={{0,8},{1,9},{2,10},{3,11},{4,12},{5,13},{6,14},{7,15},{8,0},{9,1},... | collective-permute-start | bytes 368648 | tf_op jit(solution)/shard_map/ppermute | solution.py:31
  92.6 0.1 reshape.94
  92.7 2.4 %collective-permute-done.11 = f32[80,384]{1,0:T(8,128)S(1)} collective-permute-done((f32[80,384]{1,0:T(8,128)S(1)}, f32[80,384]{1,0:T(8,128)S(1)}, u32[]{:S(2)}, u32[]{:S(2)}) %collective-permute-start.11) | collective-permute-done | bytes 122912 | tf_op jit(solution)/shard_map/ppermute | solution.py:31
  95.1 0.1 slice_reduce_fusion
  95.3 0.7 multiply_add_fusion.2
  96.0 0.1 reshape.100
  96.1 0.6 multiply_add_fusion.5
  96.9 0.5 multiply_add_fusion.7
  97.5 0.2 multiply_reduce_fusion
  97.6 20.3 %psum.7 = f32[8]{0:T(128)S(1)} all-reduce(f32[8]{0:T(128)S(1)} %multiply_reduce_fusion), channel_id=1, replica_groups=mesh['replica'=64,'shard'=8] {'shard'}, use_global_device_ids=true, to_apply=%region_1.2 | all-reduce | flops 8 | bytes 64 | tf_op jit(solution)/shard_map/psum | solution.py:153
  118.0 0.6 fusion.19
  119.3 0.1 reshape.104
  121.5 0.1 concatenate.29
  121.6 0.1 reshape.110
  121.7 15.2 %all-gather.1 = bf16[8,1,49280]{2,1,0:T(2,128)(2,1)S(1)} all-gather(bf16[1,1,49280]{2,1,0:T(2,128)(2,1)S(1)} %reshape.110), channel_id=2, replica_groups=mesh['replica'=64,'shard'=8] {'shard'}, dimensions={0}, use_global_device_ids=true | all-gather | bytes 887040 | tf_op jit(solution)/shard_map/all_gather | solution.py:163
  137.0 0.1 copy.45
  137.2 0.9 reshape.105
  138.1 0.9 reshape.106
  139.1 0.7 copy.39
  139.8 0.6 reshape.107
  140.5 0.6 pad_maximum_fusion.3
  (78 shorter events, 1.4 us)
Async XLA Ops:
  0.6 4.3 %copy-start.2 = (f32[1,512,384]{2,1,0:T(8,128)S(1)}, f32[1,512,384]{2,1,0:T(8,128)}, u32[]{:S(2)}) copy-start(f32[1,512,384]{2,1,0:T(8,128)} %param.16) | copy-start | bytes 2359300
  5.2 10.8 %collective-permute-start = (f32[4,136,384]{2,1,0:T(8,128)S(1)}, f32[4,136,384]{2,1,0:T(8,128)S(1)}, u32[]{:S(2)}, u32[]{:S(2)}) collective-permute-start(f32[4,136,384]{2,1,0:T(8,128)S(1)} %dynamic-slice_bitcast_fusion), channel_id=1, source_target_pairs={{0,1},{1,0},{2,3},{3,2},{4,5},{5,4},{6,7},{7,6},{8,9},{9,8},{10,11... | collective-permute-start | bytes 2506760 | tf_op jit(solution)/shard_map/ppermute | solution.py:31
  16.1 66.2 %copy-start.1 = (f32[64,384]{1,0:T(8,128)S(1)}, f32[64,384]{1,0:T(8,128)}, u32[]{:S(2)}) copy-start(f32[64,384]{1,0:T(8,128)} %param.20) | copy-start | bytes 294916
  16.1 66.2 %copy-start = (f32[48,512]{1,0:T(8,128)S(1)}, f32[48,512]{1,0:T(8,128)}, u32[]{:S(2)}) copy-start(f32[48,512]{1,0:T(8,128)} %param.21) | copy-start | bytes 294916
  16.1 9.7 %collective-permute-start.1 = (f32[136,384]{1,0:T(8,128)S(1)}, f32[136,384]{1,0:T(8,128)S(1)}, u32[]{:S(2)}, u32[]{:S(2)}) collective-permute-start(f32[136,384]{1,0:T(8,128)S(1)} %get-tuple-element.68), channel_id=1, source_target_pairs={{0,2},{1,3},{2,0},{3,1},{4,6},{5,7},{6,4},{7,5},{8,10},{9,11},{10,... | collective-permute-start | bytes 626696 | tf_op jit(solution)/shard_map/ppermute | solution.py:31
  18.2 9.8 %collective-permute-start.2 = (f32[136,384]{1,0:T(8,128)S(1)}, f32[136,384]{1,0:T(8,128)S(1)}, u32[]{:S(2)}, u32[]{:S(2)}) collective-permute-start(f32[136,384]{1,0:T(8,128)S(1)} %get-tuple-element.70), channel_id=1, source_target_pairs={{0,4},{1,5},{2,6},{3,7},{4,0},{5,1},{6,2},{7,3},{8,12},{9,13},{10,... | collective-permute-start | bytes 626696 | tf_op jit(solution)/shard_map/ppermute | solution.py:31
  20.1 13.1 %collective-permute-start.3 = (f32[136,384]{1,0:T(8,128)S(1)}, f32[136,384]{1,0:T(8,128)S(1)}, u32[]{:S(2)}, u32[]{:S(2)}) collective-permute-start(f32[136,384]{1,0:T(8,128)S(1)} %get-tuple-element.69), channel_id=1, source_target_pairs={{0,6},{1,7},{2,4},{3,5},{4,2},{5,3},{6,0},{7,1},{8,14},{9,15},{10,... | collective-permute-start | bytes 626696 | tf_op jit(solution)/shard_map/ppermute | solution.py:31
  33.2 59.4 %copy-start.11 = (f32[64]{0:T(128)S(1)}, f32[64]{0:T(128)}, u32[]{:S(2)}) copy-start(f32[64]{0:T(128)} %param.22) | copy-start | bytes 772
  33.2 59.4 %copy-start.9 = (f32[4,6]{1,0:T(4,128)S(1)}, f32[4,6]{1,0:T(4,128)}, u32[]{:S(2)}) copy-start(f32[4,6]{1,0:T(4,128)} %param.23) | copy-start | bytes 292
  33.3 6.3 %collective-permute-start.4 = (f32[80,384]{1,0:T(8,128)S(1)}, f32[80,384]{1,0:T(8,128)S(1)}, u32[]{:S(2)}, u32[]{:S(2)}) collective-permute-start(f32[80,384]{1,0:T(8,128)S(1)} %dynamic-slice_bitcast_fusion.4), channel_id=1, source_target_pairs={{0,8},{1,9},{2,10},{3,11},{4,12},{5,13},{6,14},{7,15},{8,0},{9,1},... | collective-permute-start | bytes 368648 | tf_op jit(solution)/shard_map/ppermute | solution.py:31
  39.6 55.6 %copy-start.5 = (f32[48,512]{1,0:T(8,128)S(1)}, f32[48,512]{1,0:T(8,128)}, u32[]{:S(2)}) copy-start(f32[48,512]{1,0:T(8,128)} %param.29) | copy-start | bytes 294916
  39.6 55.6 %copy-start.6 = (f32[48,512]{1,0:T(8,128)S(1)}, f32[48,512]{1,0:T(8,128)}, u32[]{:S(2)}) copy-start(f32[48,512]{1,0:T(8,128)} %param.25) | copy-start | bytes 294916
  39.7 5.1 %collective-permute-start.5 = (f32[40,384]{1,0:T(8,128)S(1)}, f32[40,384]{1,0:T(8,128)S(1)}, u32[]{:S(2)}, u32[]{:S(2)}) collective-permute-start(f32[40,384]{1,0:T(8,128)S(1)} %dynamic-slice_bitcast_fusion.5), channel_id=1, source_target_pairs={{0,32},{1,33},{2,34},{3,35},{4,36},{5,37},{6,38},{7,39},{8,40},{9,... | collective-permute-start | bytes 184328 | tf_op jit(solution)/shard_map/ppermute | solution.py:31
  44.8 6.5 %collective-permute-start.6 = (f32[40,384]{1,0:T(8,128)S(1)}, f32[40,384]{1,0:T(8,128)S(1)}, u32[]{:S(2)}, u32[]{:S(2)}) collective-permute-start(f32[40,384]{1,0:T(8,128)S(1)} %bitcast_add_fusion.3), channel_id=1, source_target_pairs={{0,16},{1,17},{2,18},{3,19},{4,20},{5,21},{6,22},{7,23},{8,24},{9,... | collective-permute-start | bytes 184328 | tf_op jit(solution)/shard_map/ppermute | solution.py:31
  51.3 6.5 %collective-permute-start.7 = (f32[40,384]{1,0:T(8,128)S(1)}, f32[40,384]{1,0:T(8,128)S(1)}, u32[]{:S(2)}, u32[]{:S(2)}) collective-permute-start(f32[40,384]{1,0:T(8,128)S(1)} %add.175), channel_id=1, source_target_pairs={{0,64},{1,65},{2,66},{3,67},{4,68},{5,69},{6,70},{7,71},{8,72},{9,... | collective-permute-start | bytes 184328 | tf_op jit(solution)/shard_map/ppermute | solution.py:31
  57.8 8.9 %collective-permute-start.8 = (f32[40,384]{1,0:T(8,128)S(1)}, f32[40,384]{1,0:T(8,128)S(1)}, u32[]{:S(2)}, u32[]{:S(2)}) collective-permute-start(f32[40,384]{1,0:T(8,128)S(1)} %add.176), channel_id=1, source_target_pairs={{0,128},{1,129},{2,130},{3,131},{4,132},{5,133},{6,134},{7,135},{8... | collective-permute-start | bytes 184328 | tf_op jit(solution)/shard_map/ppermute | solution.py:31
  66.7 29.4 %copy-start.12 = (f32[4,6]{1,0:T(4,128)S(1)}, f32[4,6]{1,0:T(4,128)}, u32[]{:S(2)}) copy-start(f32[4,6]{1,0:T(4,128)} %param.31) | copy-start | bytes 292
  66.7 29.4 %copy-start.13 = (f32[4,6]{1,0:T(4,128)S(1)}, f32[4,6]{1,0:T(4,128)}, u32[]{:S(2)}) copy-start(f32[4,6]{1,0:T(4,128)} %param.27) | copy-start | bytes 292
  66.7 30.1 %copy-start.7 = (f32[64,384]{1,0:T(8,128)S(1)}, f32[64,384]{1,0:T(8,128)}, u32[]{:S(2)}) copy-start(f32[64,384]{1,0:T(8,128)} %param.28) | copy-start | bytes 294916
  66.7 30.1 %copy-start.8 = (f32[64,384]{1,0:T(8,128)S(1)}, f32[64,384]{1,0:T(8,128)}, u32[]{:S(2)}) copy-start(f32[64,384]{1,0:T(8,128)} %param.24) | copy-start | bytes 294916
  66.7 17.1 %collective-permute-start.9 = (f32[40,384]{1,0:T(8,128)S(1)}, f32[40,384]{1,0:T(8,128)S(1)}, u32[]{:S(2)}, u32[]{:S(2)}) collective-permute-start(f32[40,384]{1,0:T(8,128)S(1)} %add.177), channel_id=1, source_target_pairs={{0,256},{1,257},{2,258},{3,259},{4,260},{5,261},{6,262},{7,263},{8... | collective-permute-start | bytes 184328 | tf_op jit(solution)/shard_map/ppermute | solution.py:31
  83.9 5.5 %collective-permute-start.10 = (f32[40,384]{1,0:T(8,128)S(1)}, f32[40,384]{1,0:T(8,128)S(1)}, u32[]{:S(2)}, u32[]{:S(2)}) collective-permute-start(f32[40,384]{1,0:T(8,128)S(1)} %add.178), channel_id=1, source_target_pairs={{0,32},{1,33},{2,34},{3,35},{4,36},{5,37},{6,38},{7,39},{8,40},{9,... | collective-permute-start | bytes 184328 | tf_op jit(solution)/shard_map/ppermute | solution.py:31
  89.4 7.5 %copy-start.14 = (f32[64]{0:T(128)S(1)}, f32[64]{0:T(128)}, u32[]{:S(2)}) copy-start(f32[64]{0:T(128)} %param.30) | copy-start | bytes 772
  89.4 7.5 %copy-start.15 = (f32[64]{0:T(128)S(1)}, f32[64]{0:T(128)}, u32[]{:S(2)}) copy-start(f32[64]{0:T(128)} %param.26) | copy-start | bytes 772
  89.5 5.6 %collective-permute-start.11 = (f32[80,384]{1,0:T(8,128)S(1)}, f32[80,384]{1,0:T(8,128)S(1)}, u32[]{:S(2)}, u32[]{:S(2)}) collective-permute-start(f32[80,384]{1,0:T(8,128)S(1)} %pad_maximum_fusion.1), channel_id=1, source_target_pairs={{0,8},{1,9},{2,10},{3,11},{4,12},{5,13},{6,14},{7,15},{8,0},{9,1},... | collective-permute-start | bytes 368648 | tf_op jit(solution)/shard_map/ppermute | solution.py:31
  96.9 40.1 %copy-start.3 = (f32[64,384]{1,0:T(8,128)}, f32[64,384]{1,0:T(8,128)S(1)}, u32[]{:S(2)}) copy-start(f32[64,384]{1,0:T(8,128)S(1)} %get-tuple-element.66) | copy-start | bytes 294916
  96.9 40.1 %copy-start.4 = (f32[64,384]{1,0:T(8,128)}, f32[64,384]{1,0:T(8,128)S(1)}, u32[]{:S(2)}) copy-start(f32[64,384]{1,0:T(8,128)S(1)} %get-tuple-element.67) | copy-start | bytes 294916
  118.0 19.1 %copy-start.10 = (f32[4]{0:T(128)}, f32[4]{0:T(128)S(1)}, u32[]{:S(2)}) copy-start(f32[4]{0:T(128)S(1)} %get-tuple-element.79) | copy-start | bytes 52

commit v6 on v5

--- a/solution.py
+++ b/solution.py
@@ -6,8 +6,8 @@
 LANES = 128
 CORE_BIT = 0
 Y_GROUP = (2, 1)
-REPLICA_SPLIT_BITS = (3, 5)
-REPLICA_BUTTERFLY_BITS = (4, 6, 7, 8)
+REPLICA_SPLITS = ((0b11 << 3, 4), (1 << 5, 5))
+REPLICA_BUTTERFLY = (1 << 3, 1 << 6, 1 << 7, 0b11 << 7)
 ROW_TILE = 8
 AXES = ("replica", "shard")
 
@@ -58,18 +58,18 @@
         part = lax.dynamic_index_in_dim(blocks, mine ^ t, 0, keepdims=False)
         total = total + exchange(part, masks[t], devices)
     rows, lanes = total.shape
-    multiple = ROW_TILE << len(REPLICA_SPLIT_BITS)
+    multiple = ROW_TILE << len(REPLICA_SPLITS)
     total = jnp.pad(total, ((0, padded_width(rows, multiple) - rows), (0, 0)))
-    for bit in REPLICA_SPLIT_BITS:
+    for mask, bit in REPLICA_SPLITS:
         halves = total.reshape((2, total.shape[0] // 2, lanes))
         mine = bit_of(index, bit)
         keep = lax.dynamic_index_in_dim(halves, mine, 0, keepdims=False)
         send = lax.dynamic_index_in_dim(halves, 1 - mine, 0, keepdims=False)
-        total = keep + exchange(send, 1 << bit, devices)
-    for bit in REPLICA_BUTTERFLY_BITS:
-        total = total + exchange(total, 1 << bit, devices)
-    for bit in reversed(REPLICA_SPLIT_BITS):
-        other = exchange(total, 1 << bit, devices)
+        total = keep + exchange(send, mask, devices)
+    for mask in REPLICA_BUTTERFLY:
+        total = total + exchange(total, mask, devices)
+    for mask, bit in reversed(REPLICA_SPLITS):
+        other = exchange(total, mask, devices)
         first = bit_of(index, bit) == 0
         total = jnp.concatenate([jnp.where(first, total, other), jnp.where(first, other, total)], axis=0)
     return total[:rows]

time: 142 us -> 138 us (0.972)
  starting transfers between devices: 56.2 us -> 52.2 us
    ppermute x12, starting transfers between devices: 56.2 us -> 52.2 us  [exchange(): return lax.ppermute(value, AXES, [(d, d ^ mask) for d in range(devices)])]
where the time goes in v6:
time: 138 us; the launch traced here: 137 us
  starting transfers between devices  52.2 us (38%)
  blocking collectives  34.9 us (25%)
  waiting for transfers between devices  33.7 us (24%)
  local copies, waits for them, and re-layouts  8.05 us (6%)
  other arithmetic  4.63 us (3%)
  between operations  3.85 us (3%)
    ppermute x12, starting transfers between devices, exchange(): return lax.ppermute(value, AXES, [(d, d ^ mask) for d in range(devices)])  52.2 us
    ppermute x12, waiting for transfers between devices, exchange(): return lax.ppermute(value, AXES, [(d, d ^ mask) for d in range(devices)])  33.7 us
    psum x1, blocking collectives, on_device(): squares = lax.psum(jnp.sum(stacked * stacked, axis=(1, 2)), 'shard')  19.7 us
    all_gather x1, blocking collectives, on_device(): lax.all_gather(jnp.concatenate(shards_out), 'shard', axis=0, tiled=False)  15.2 us
  transfers between devices with their start and end apart: 12, of which 11 were waited for; matrix products, arithmetic and copies ran while one was open for 0% of the time, Pallas kernels for 0%

profile of v6, /device:TPU:1, one launch (start us, length us, event | category | flops | bytes accessed | tf_op | source)
XLA Modules:
  0.0 137.3 jit_solution(12768179573907499547)
XLA Ops:
  0.7 1.4 %concatenate.23 = f32[4,2,64,384]{3,2,1,0:T(8,128)S(1)} reshape(f32[1,384,512]{2,1,0:T(8,128)} %param.17) | data formatting | bytes 1572864 | tf_op jit(solution)/shard_map/concatenate | solution.py:124
  2.1 0.8 copy.37
  2.9 0.5 broadcast.73
  3.4 1.3 reduce.7
  5.0 0.1 pad_maximum_fusion
  5.2 8.8 %collective-permute-start = (f32[4,136,384]{2,1,0:T(8,128)S(1)}, f32[4,136,384]{2,1,0:T(8,128)S(1)}, u32[]{:S(2)}, u32[]{:S(2)}) collective-permute-start(f32[4,136,384]{2,1,0:T(8,128)S(1)} %dynamic-slice_bitcast_fusion), channel_id=1, source_target_pairs={{0,1},{1,0},{2,3},{3,2},{4,5},{5,4},{6,7},{7,6},{8,9},{9,8},{10,11... | collective-permute-start | bytes 2506760 | tf_op jit(solution)/shard_map/ppermute | solution.py:31
  14.0 1.9 %collective-permute-done = f32[4,136,384]{2,1,0:T(8,128)S(1)} collective-permute-done((f32[4,136,384]{2,1,0:T(8,128)S(1)}, f32[4,136,384]{2,1,0:T(8,128)S(1)}, u32[]{:S(2)}, u32[]{:S(2)}) %collective-permute-start) | collective-permute-done | bytes 835616 | tf_op jit(solution)/shard_map/ppermute | solution.py:31
  15.9 0.1 bitcast_add_fusion
  16.1 2.1 %collective-permute-start.1 = (f32[136,384]{1,0:T(8,128)S(1)}, f32[136,384]{1,0:T(8,128)S(1)}, u32[]{:S(2)}, u32[]{:S(2)}) collective-permute-start(f32[136,384]{1,0:T(8,128)S(1)} %get-tuple-element.68), channel_id=1, source_target_pairs={{0,2},{1,3},{2,0},{3,1},{4,6},{5,7},{6,4},{7,5},{8,10},{9,11},{10,... | collective-permute-start | bytes 626696 | tf_op jit(solution)/shard_map/ppermute | solution.py:31
  18.2 1.9 %collective-permute-start.2 = (f32[136,384]{1,0:T(8,128)S(1)}, f32[136,384]{1,0:T(8,128)S(1)}, u32[]{:S(2)}, u32[]{:S(2)}) collective-permute-start(f32[136,384]{1,0:T(8,128)S(1)} %get-tuple-element.70), channel_id=1, source_target_pairs={{0,4},{1,5},{2,6},{3,7},{4,0},{5,1},{6,2},{7,3},{8,12},{9,13},{10,... | collective-permute-start | bytes 626696 | tf_op jit(solution)/shard_map/ppermute | solution.py:31
  20.1 5.7 %collective-permute-start.3 = (f32[136,384]{1,0:T(8,128)S(1)}, f32[136,384]{1,0:T(8,128)S(1)}, u32[]{:S(2)}, u32[]{:S(2)}) collective-permute-start(f32[136,384]{1,0:T(8,128)S(1)} %get-tuple-element.69), channel_id=1, source_target_pairs={{0,6},{1,7},{2,4},{3,5},{4,2},{5,3},{6,0},{7,1},{8,14},{9,15},{10,... | collective-permute-start | bytes 626696 | tf_op jit(solution)/shard_map/ppermute | solution.py:31
  25.9 2.1 %collective-permute-done.2 = f32[136,384]{1,0:T(8,128)S(1)} collective-permute-done((f32[136,384]{1,0:T(8,128)S(1)}, f32[136,384]{1,0:T(8,128)S(1)}, u32[]{:S(2)}, u32[]{:S(2)}) %collective-permute-start.2) | collective-permute-done | bytes 208928 | tf_op jit(solution)/shard_map/ppermute | solution.py:31
  28.0 5.2 %collective-permute-done.3 = f32[136,384]{1,0:T(8,128)S(1)} collective-permute-done((f32[136,384]{1,0:T(8,128)S(1)}, f32[136,384]{1,0:T(8,128)S(1)}, u32[]{:S(2)}, u32[]{:S(2)}) %collective-permute-start.3) | collective-permute-done | bytes 208928 | tf_op jit(solution)/shard_map/ppermute | solution.py:31
  33.3 2.5 %collective-permute-start.4 = (f32[80,384]{1,0:T(8,128)S(1)}, f32[80,384]{1,0:T(8,128)S(1)}, u32[]{:S(2)}, u32[]{:S(2)}) collective-permute-start(f32[80,384]{1,0:T(8,128)S(1)} %dynamic-slice_bitcast_fusion.4), channel_id=1, source_target_pairs={{0,24},{1,25},{2,26},{3,27},{4,28},{5,29},{6,30},{7,31},{8,16},{9,... | collective-permute-start | bytes 368648 | tf_op jit(solution)/shard_map/ppermute | solution.py:31
  35.8 5.0 %collective-permute-done.4 = f32[80,384]{1,0:T(8,128)S(1)} collective-permute-done((f32[80,384]{1,0:T(8,128)S(1)}, f32[80,384]{1,0:T(8,128)S(1)}, u32[]{:S(2)}, u32[]{:S(2)}) %collective-permute-start.4) | collective-permute-done | bytes 122912 | tf_op jit(solution)/shard_map/ppermute | solution.py:31
  40.9 2.1 %collective-permute-start.5 = (f32[40,384]{1,0:T(8,128)S(1)}, f32[40,384]{1,0:T(8,128)S(1)}, u32[]{:S(2)}, u32[]{:S(2)}) collective-permute-start(f32[40,384]{1,0:T(8,128)S(1)} %dynamic-slice_bitcast_fusion.5), channel_id=1, source_target_pairs={{0,32},{1,33},{2,34},{3,35},{4,36},{5,37},{6,38},{7,39},{8,40},{9,... | collective-permute-start | bytes 184328 | tf_op jit(solution)/shard_map/ppermute | solution.py:31
  42.9 3.0 %collective-permute-done.5 = f32[40,384]{1,0:T(8,128)S(1)} collective-permute-done((f32[40,384]{1,0:T(8,128)S(1)}, f32[40,384]{1,0:T(8,128)S(1)}, u32[]{:S(2)}, u32[]{:S(2)}) %collective-permute-start.5) | collective-permute-done | bytes 61472 | tf_op jit(solution)/shard_map/ppermute | solution.py:31
  46.0 1.9 %collective-permute-start.6 = (f32[40,384]{1,0:T(8,128)S(1)}, f32[40,384]{1,0:T(8,128)S(1)}, u32[]{:S(2)}, u32[]{:S(2)}) collective-permute-start(f32[40,384]{1,0:T(8,128)S(1)} %bitcast_add_fusion.3), channel_id=1, source_target_pairs={{0,8},{1,9},{2,10},{3,11},{4,12},{5,13},{6,14},{7,15},{8,0},{9,1},... | collective-permute-start | bytes 184328 | tf_op jit(solution)/shard_map/ppermute | solution.py:31
  47.9 3.0 %collective-permute-done.6 = f32[40,384]{1,0:T(8,128)S(1)} collective-permute-done((f32[40,384]{1,0:T(8,128)S(1)}, f32[40,384]{1,0:T(8,128)S(1)}, u32[]{:S(2)}, u32[]{:S(2)}) %collective-permute-start.6) | collective-permute-done | bytes 61472 | tf_op jit(solution)/shard_map/ppermute | solution.py:31
  51.0 3.2 %collective-permute-start.7 = (f32[40,384]{1,0:T(8,128)S(1)}, f32[40,384]{1,0:T(8,128)S(1)}, u32[]{:S(2)}, u32[]{:S(2)}) collective-permute-start(f32[40,384]{1,0:T(8,128)S(1)} %add.175), channel_id=1, source_target_pairs={{0,64},{1,65},{2,66},{3,67},{4,68},{5,69},{6,70},{7,71},{8,72},{9,... | collective-permute-start | bytes 184328 | tf_op jit(solution)/shard_map/ppermute | solution.py:31
  54.1 3.3 %collective-permute-done.7 = f32[40,384]{1,0:T(8,128)S(1)} collective-permute-done((f32[40,384]{1,0:T(8,128)S(1)}, f32[40,384]{1,0:T(8,128)S(1)}, u32[]{:S(2)}, u32[]{:S(2)}) %collective-permute-start.7) | collective-permute-done | bytes 61472 | tf_op jit(solution)/shard_map/ppermute | solution.py:31
  57.5 7.1 %collective-permute-start.8 = (f32[40,384]{1,0:T(8,128)S(1)}, f32[40,384]{1,0:T(8,128)S(1)}, u32[]{:S(2)}, u32[]{:S(2)}) collective-permute-start(f32[40,384]{1,0:T(8,128)S(1)} %add.176), channel_id=1, source_target_pairs={{0,128},{1,129},{2,130},{3,131},{4,132},{5,133},{6,134},{7,135},{8... | collective-permute-start | bytes 184328 | tf_op jit(solution)/shard_map/ppermute | solution.py:31
  64.6 1.8 %collective-permute-done.8 = f32[40,384]{1,0:T(8,128)S(1)} collective-permute-done((f32[40,384]{1,0:T(8,128)S(1)}, f32[40,384]{1,0:T(8,128)S(1)}, u32[]{:S(2)}, u32[]{:S(2)}) %collective-permute-start.8) | collective-permute-done | bytes 61472 | tf_op jit(solution)/shard_map/ppermute | solution.py:31
  66.4 10.7 %collective-permute-start.9 = (f32[40,384]{1,0:T(8,128)S(1)}, f32[40,384]{1,0:T(8,128)S(1)}, u32[]{:S(2)}, u32[]{:S(2)}) collective-permute-start(f32[40,384]{1,0:T(8,128)S(1)} %add.177), channel_id=1, source_target_pairs={{0,384},{1,385},{2,386},{3,387},{4,388},{5,389},{6,390},{7,391},{8... | collective-permute-start | bytes 184328 | tf_op jit(solution)/shard_map/ppermute | solution.py:31
  77.2 2.8 %collective-permute-done.9 = f32[40,384]{1,0:T(8,128)S(1)} collective-permute-done((f32[40,384]{1,0:T(8,128)S(1)}, f32[40,384]{1,0:T(8,128)S(1)}, u32[]{:S(2)}, u32[]{:S(2)}) %collective-permute-start.9) | collective-permute-done | bytes 61472 | tf_op jit(solution)/shard_map/ppermute | solution.py:31
  80.0 1.9 %collective-permute-start.10 = (f32[40,384]{1,0:T(8,128)S(1)}, f32[40,384]{1,0:T(8,128)S(1)}, u32[]{:S(2)}, u32[]{:S(2)}) collective-permute-start(f32[40,384]{1,0:T(8,128)S(1)} %add.178), channel_id=1, source_target_pairs={{0,32},{1,33},{2,34},{3,35},{4,36},{5,37},{6,38},{7,39},{8,40},{9,... | collective-permute-start | bytes 184328 | tf_op jit(solution)/shard_map/ppermute | solution.py:31
  81.9 3.2 %collective-permute-done.10 = f32[40,384]{1,0:T(8,128)S(1)} collective-permute-done((f32[40,384]{1,0:T(8,128)S(1)}, f32[40,384]{1,0:T(8,128)S(1)}, u32[]{:S(2)}, u32[]{:S(2)}) %collective-permute-start.10) | collective-permute-done | bytes 61472 | tf_op jit(solution)/shard_map/ppermute | solution.py:31
  85.2 4.4 %collective-permute-start.11 = (f32[80,384]{1,0:T(8,128)S(1)}, f32[80,384]{1,0:T(8,128)S(1)}, u32[]{:S(2)}, u32[]{:S(2)}) collective-permute-start(f32[80,384]{1,0:T(8,128)S(1)} %pad_maximum_fusion.1), channel_id=1, source_target_pairs={{0,24},{1,25},{2,26},{3,27},{4,28},{5,29},{6,30},{7,31},{8,16},{9,... | collective-permute-start | bytes 368648 | tf_op jit(solution)/shard_map/ppermute | solution.py:31
  89.6 0.1 reshape.94
  89.7 2.3 %collective-permute-done.11 = f32[80,384]{1,0:T(8,128)S(1)} collective-permute-done((f32[80,384]{1,0:T(8,128)S(1)}, f32[80,384]{1,0:T(8,128)S(1)}, u32[]{:S(2)}, u32[]{:S(2)}) %collective-permute-start.11) | collective-permute-done | bytes 122912 | tf_op jit(solution)/shard_map/ppermute | solution.py:31
  92.0 0.1 slice_reduce_fusion
  92.2 0.7 multiply_add_fusion.2
  93.0 0.6 multiply_add_fusion.5
  93.6 0.1 reshape.101
  93.8 0.5 multiply_add_fusion.7
  94.4 0.2 multiply_reduce_fusion
  94.6 19.7 %psum.7 = f32[8]{0:T(128)S(1)} all-reduce(f32[8]{0:T(128)S(1)} %multiply_reduce_fusion), channel_id=1, replica_groups=mesh['replica'=64,'shard'=8] {'shard'}, use_global_device_ids=true, to_apply=%region_1.2 | all-reduce | flops 8 | bytes 64 | tf_op jit(solution)/shard_map/psum | solution.py:153
  114.3 0.6 fusion.19
  115.6 0.1 reshape.104
  117.8 0.1 concatenate.29
  117.9 0.1 reshape.110
  118.0 15.2 %all-gather.1 = bf16[8,1,49280]{2,1,0:T(2,128)(2,1)S(1)} all-gather(bf16[1,1,49280]{2,1,0:T(2,128)(2,1)S(1)} %reshape.110), channel_id=2, replica_groups=mesh['replica'=64,'shard'=8] {'shard'}, dimensions={0}, use_global_device_ids=true | all-gather | bytes 887040 | tf_op jit(solution)/shard_map/all_gather | solution.py:163
  133.2 0.1 copy.45
  133.5 0.9 reshape.105
  134.4 0.9 reshape.106
  135.4 0.7 copy.39
  136.1 0.6 reshape.107
  136.7 0.6 pad_maximum_fusion.3
  (78 shorter events, 1.4 us)
Async XLA Ops:
  0.6 4.3 %copy-start.2 = (f32[1,512,384]{2,1,0:T(8,128)S(1)}, f32[1,512,384]{2,1,0:T(8,128)}, u32[]{:S(2)}) copy-start(f32[1,512,384]{2,1,0:T(8,128)} %param.16) | copy-start | bytes 2359300
  5.2 10.8 %collective-permute-start = (f32[4,136,384]{2,1,0:T(8,128)S(1)}, f32[4,136,384]{2,1,0:T(8,128)S(1)}, u32[]{:S(2)}, u32[]{:S(2)}) collective-permute-start(f32[4,136,384]{2,1,0:T(8,128)S(1)} %dynamic-slice_bitcast_fusion), channel_id=1, source_target_pairs={{0,1},{1,0},{2,3},{3,2},{4,5},{5,4},{6,7},{7,6},{8,9},{9,8},{10,11... | collective-permute-start | bytes 2506760 | tf_op jit(solution)/shard_map/ppermute | solution.py:31
  16.1 61.0 %copy-start.1 = (f32[64,384]{1,0:T(8,128)S(1)}, f32[64,384]{1,0:T(8,128)}, u32[]{:S(2)}) copy-start(f32[64,384]{1,0:T(8,128)} %param.20) | copy-start | bytes 294916
  16.1 61.0 %copy-start = (f32[48,512]{1,0:T(8,128)S(1)}, f32[48,512]{1,0:T(8,128)}, u32[]{:S(2)}) copy-start(f32[48,512]{1,0:T(8,128)} %param.21) | copy-start | bytes 294916
  16.1 9.7 %collective-permute-start.1 = (f32[136,384]{1,0:T(8,128)S(1)}, f32[136,384]{1,0:T(8,128)S(1)}, u32[]{:S(2)}, u32[]{:S(2)}) collective-permute-start(f32[136,384]{1,0:T(8,128)S(1)} %get-tuple-element.68), channel_id=1, source_target_pairs={{0,2},{1,3},{2,0},{3,1},{4,6},{5,7},{6,4},{7,5},{8,10},{9,11},{10,... | collective-permute-start | bytes 626696 | tf_op jit(solution)/shard_map/ppermute | solution.py:31
  18.2 9.8 %collective-permute-start.2 = (f32[136,384]{1,0:T(8,128)S(1)}, f32[136,384]{1,0:T(8,128)S(1)}, u32[]{:S(2)}, u32[]{:S(2)}) collective-permute-start(f32[136,384]{1,0:T(8,128)S(1)} %get-tuple-element.70), channel_id=1, source_target_pairs={{0,4},{1,5},{2,6},{3,7},{4,0},{5,1},{6,2},{7,3},{8,12},{9,13},{10,... | collective-permute-start | bytes 626696 | tf_op jit(solution)/shard_map/ppermute | solution.py:31
  20.1 13.1 %collective-permute-start.3 = (f32[136,384]{1,0:T(8,128)S(1)}, f32[136,384]{1,0:T(8,128)S(1)}, u32[]{:S(2)}, u32[]{:S(2)}) collective-permute-start(f32[136,384]{1,0:T(8,128)S(1)} %get-tuple-element.69), channel_id=1, source_target_pairs={{0,6},{1,7},{2,4},{3,5},{4,2},{5,3},{6,0},{7,1},{8,14},{9,15},{10,... | collective-permute-start | bytes 626696 | tf_op jit(solution)/shard_map/ppermute | solution.py:31
  33.2 56.4 %copy-start.11 = (f32[64]{0:T(128)S(1)}, f32[64]{0:T(128)}, u32[]{:S(2)}) copy-start(f32[64]{0:T(128)} %param.22) | copy-start | bytes 772
  33.2 56.4 %copy-start.9 = (f32[4,6]{1,0:T(4,128)S(1)}, f32[4,6]{1,0:T(4,128)}, u32[]{:S(2)}) copy-start(f32[4,6]{1,0:T(4,128)} %param.23) | copy-start | bytes 292
  33.3 7.5 %collective-permute-start.4 = (f32[80,384]{1,0:T(8,128)S(1)}, f32[80,384]{1,0:T(8,128)S(1)}, u32[]{:S(2)}, u32[]{:S(2)}) collective-permute-start(f32[80,384]{1,0:T(8,128)S(1)} %dynamic-slice_bitcast_fusion.4), channel_id=1, source_target_pairs={{0,24},{1,25},{2,26},{3,27},{4,28},{5,29},{6,30},{7,31},{8,16},{9,... | collective-permute-start | bytes 368648 | tf_op jit(solution)/shard_map/ppermute | solution.py:31
  40.8 51.3 %copy-start.5 = (f32[48,512]{1,0:T(8,128)S(1)}, f32[48,512]{1,0:T(8,128)}, u32[]{:S(2)}) copy-start(f32[48,512]{1,0:T(8,128)} %param.29) | copy-start | bytes 294916
  40.8 51.3 %copy-start.6 = (f32[48,512]{1,0:T(8,128)S(1)}, f32[48,512]{1,0:T(8,128)}, u32[]{:S(2)}) copy-start(f32[48,512]{1,0:T(8,128)} %param.25) | copy-start | bytes 294916
  40.9 5.1 %collective-permute-start.5 = (f32[40,384]{1,0:T(8,128)S(1)}, f32[40,384]{1,0:T(8,128)S(1)}, u32[]{:S(2)}, u32[]{:S(2)}) collective-permute-start(f32[40,384]{1,0:T(8,128)S(1)} %dynamic-slice_bitcast_fusion.5), channel_id=1, source_target_pairs={{0,32},{1,33},{2,34},{3,35},{4,36},{5,37},{6,38},{7,39},{8,40},{9,... | collective-permute-start | bytes 184328 | tf_op jit(solution)/shard_map/ppermute | solution.py:31
  46.0 5.0 %collective-permute-start.6 = (f32[40,384]{1,0:T(8,128)S(1)}, f32[40,384]{1,0:T(8,128)S(1)}, u32[]{:S(2)}, u32[]{:S(2)}) collective-permute-start(f32[40,384]{1,0:T(8,128)S(1)} %bitcast_add_fusion.3), channel_id=1, source_target_pairs={{0,8},{1,9},{2,10},{3,11},{4,12},{5,13},{6,14},{7,15},{8,0},{9,1},... | collective-permute-start | bytes 184328 | tf_op jit(solution)/shard_map/ppermute | solution.py:31
  51.0 6.5 %collective-permute-start.7 = (f32[40,384]{1,0:T(8,128)S(1)}, f32[40,384]{1,0:T(8,128)S(1)}, u32[]{:S(2)}, u32[]{:S(2)}) collective-permute-start(f32[40,384]{1,0:T(8,128)S(1)} %add.175), channel_id=1, source_target_pairs={{0,64},{1,65},{2,66},{3,67},{4,68},{5,69},{6,70},{7,71},{8,72},{9,... | collective-permute-start | bytes 184328 | tf_op jit(solution)/shard_map/ppermute | solution.py:31
  57.5 8.9 %collective-permute-start.8 = (f32[40,384]{1,0:T(8,128)S(1)}, f32[40,384]{1,0:T(8,128)S(1)}, u32[]{:S(2)}, u32[]{:S(2)}) collective-permute-start(f32[40,384]{1,0:T(8,128)S(1)} %add.176), channel_id=1, source_target_pairs={{0,128},{1,129},{2,130},{3,131},{4,132},{5,133},{6,134},{7,135},{8... | collective-permute-start | bytes 184328 | tf_op jit(solution)/shard_map/ppermute | solution.py:31
  66.4 26.6 %copy-start.12 = (f32[4,6]{1,0:T(4,128)S(1)}, f32[4,6]{1,0:T(4,128)}, u32[]{:S(2)}) copy-start(f32[4,6]{1,0:T(4,128)} %param.31) | copy-start | bytes 292
  66.4 26.6 %copy-start.13 = (f32[4,6]{1,0:T(4,128)S(1)}, f32[4,6]{1,0:T(4,128)}, u32[]{:S(2)}) copy-start(f32[4,6]{1,0:T(4,128)} %param.27) | copy-start | bytes 292
  66.4 27.3 %copy-start.7 = (f32[64,384]{1,0:T(8,128)S(1)}, f32[64,384]{1,0:T(8,128)}, u32[]{:S(2)}) copy-start(f32[64,384]{1,0:T(8,128)} %param.28) | copy-start | bytes 294916
  66.4 27.3 %copy-start.8 = (f32[64,384]{1,0:T(8,128)S(1)}, f32[64,384]{1,0:T(8,128)}, u32[]{:S(2)}) copy-start(f32[64,384]{1,0:T(8,128)} %param.24) | copy-start | bytes 294916
  66.4 13.5 %collective-permute-start.9 = (f32[40,384]{1,0:T(8,128)S(1)}, f32[40,384]{1,0:T(8,128)S(1)}, u32[]{:S(2)}, u32[]{:S(2)}) collective-permute-start(f32[40,384]{1,0:T(8,128)S(1)} %add.177), channel_id=1, source_target_pairs={{0,384},{1,385},{2,386},{3,387},{4,388},{5,389},{6,390},{7,391},{8... | collective-permute-start | bytes 184328 | tf_op jit(solution)/shard_map/ppermute | solution.py:31
  80.0 5.1 %collective-permute-start.10 = (f32[40,384]{1,0:T(8,128)S(1)}, f32[40,384]{1,0:T(8,128)S(1)}, u32[]{:S(2)}, u32[]{:S(2)}) collective-permute-start(f32[40,384]{1,0:T(8,128)S(1)} %add.178), channel_id=1, source_target_pairs={{0,32},{1,33},{2,34},{3,35},{4,36},{5,37},{6,38},{7,39},{8,40},{9,... | collective-permute-start | bytes 184328 | tf_op jit(solution)/shard_map/ppermute | solution.py:31
  85.1 8.7 %copy-start.14 = (f32[64]{0:T(128)S(1)}, f32[64]{0:T(128)}, u32[]{:S(2)}) copy-start(f32[64]{0:T(128)} %param.30) | copy-start | bytes 772
  85.2 8.7 %copy-start.15 = (f32[64]{0:T(128)S(1)}, f32[64]{0:T(128)}, u32[]{:S(2)}) copy-start(f32[64]{0:T(128)} %param.26) | copy-start | bytes 772
  85.2 6.8 %collective-permute-start.11 = (f32[80,384]{1,0:T(8,128)S(1)}, f32[80,384]{1,0:T(8,128)S(1)}, u32[]{:S(2)}, u32[]{:S(2)}) collective-permute-start(f32[80,384]{1,0:T(8,128)S(1)} %pad_maximum_fusion.1), channel_id=1, source_target_pairs={{0,24},{1,25},{2,26},{3,27},{4,28},{5,29},{6,30},{7,31},{8,16},{9,... | collective-permute-start | bytes 368648 | tf_op jit(solution)/shard_map/ppermute | solution.py:31
  93.8 39.5 %copy-start.3 = (f32[64,384]{1,0:T(8,128)}, f32[64,384]{1,0:T(8,128)S(1)}, u32[]{:S(2)}) copy-start(f32[64,384]{1,0:T(8,128)S(1)} %get-tuple-element.66) | copy-start | bytes 294916
  93.8 39.4 %copy-start.4 = (f32[64,384]{1,0:T(8,128)}, f32[64,384]{1,0:T(8,128)S(1)}, u32[]{:S(2)}) copy-start(f32[64,384]{1,0:T(8,128)S(1)} %get-tuple-element.67) | copy-start | bytes 294916
  114.3 19.1 %copy-start.10 = (f32[4]{0:T(128)}, f32[4]{0:T(128)S(1)}, u32[]{:S(2)}) copy-start(f32[4]{0:T(128)S(1)} %get-tuple-element.79) | copy-start | bytes 52

commit v7 on v6

--- a/solution.py
+++ b/solution.py
@@ -75,13 +75,27 @@
     return total[:rows]
 
 
-def as_tile(value, rows, lanes):
-    if value.size == rows * lanes:
-        return value.reshape(rows, lanes)
-    flat = value.reshape(1, -1)
-    flat = jnp.pad(flat, ((0, 0), (0, lanes * (-(-flat.shape[1] // lanes)) - flat.shape[1])))
-    flat = flat.reshape(-1, lanes)
-    return jnp.pad(flat, ((0, rows - flat.shape[0]), (0, 0)))
+def pack(query, output, norm, bias, rows, pad_rows):
+    lanes = query.shape[-1]
+    rest = jnp.concatenate([norm.reshape(-1), bias.reshape(-1)])
+    rest = jnp.pad(rest, (0, lanes - rest.shape[0])).reshape(1, lanes)
+    block = jnp.concatenate([query, output.reshape(-1, lanes), rest], axis=0)
+    return jnp.pad(block, ((0, pad_rows - block.shape[0]), (0, 0)))
+
+
+def unpack(block, shapes):
+    query_shape, output_shape, norm_shape, bias_shape = shapes
+    query_rows, lanes = query_shape
+    output_rows = (output_shape[0] * output_shape[1]) // lanes
+    norm_size = norm_shape[0]
+    bias_size = bias_shape[0] * bias_shape[1]
+    rest = block[..., query_rows + output_rows, :]
+    return (
+        block[..., :query_rows, :],
+        block[..., query_rows : query_rows + output_rows, :],
+        rest[..., :norm_size],
+        rest[..., norm_size : norm_size + bias_size],
+    )
 
 
 def on_device(
@@ -104,83 +118,92 @@
     shards,
     replicas,
 ):
-    weights = (weight_query, weight_output, weight_norm, weight_bias)
-    moments = (first_query, first_output, first_norm, first_bias)
-    seconds = (second_query, second_output, second_norm, second_bias)
-    decay_rates = (0.01, 0.01, 0.0, 0.0)
-    gradients = (grad_query[0], grad_output[0], grad_norm[0], grad_bias[0])
-    sizes = [weight.size for weight in weights]
-    offsets = [sum(sizes[:member]) for member in range(4)]
-    total = sum(sizes)
     devices = shards * replicas
+    shapes = (weight_query.shape, weight_output.shape, weight_norm.shape, weight_bias.shape)
     query_rows, lanes = weight_query.shape
     output_rows = weight_output.size // lanes
-    small = jnp.concatenate(
-        [grad_norm[0].reshape(shards, -1), grad_bias[0].reshape(shards, -1)], axis=1
-    )
-    small_width = small.shape[1]
-    small = jnp.pad(small, ((0, 0), (0, lanes - small_width))).reshape(shards, 1, lanes)
-    small = jnp.pad(small, ((0, 0), (0, 7), (0, 0)))
-    packed = jnp.concatenate(
+    block_rows = padded_width(query_rows + output_rows + 1, ROW_TILE)
+    packed = jax.vmap(lambda q, o, n, b: pack(q, o, n, b, query_rows + output_rows + 1, block_rows))(
+        grad_query[0].reshape(shards, query_rows, lanes),
+        grad_output[0].reshape(shards, -1, weight_output.shape[1]),
+        grad_norm[0].reshape(shards, -1),
+        grad_bias[0].reshape(shards, -1),
+    )
+    summed = reduce_blocks(packed, devices)
+    weight = pack(weight_query, weight_output, weight_norm, weight_bias, block_rows, block_rows)
+    moment = pack(first_query, first_output, first_norm, first_bias, block_rows, block_rows)
+    second = pack(second_query, second_output, second_norm, second_bias, block_rows, block_rows)
+    row = lax.broadcasted_iota(jnp.int32, (block_rows, lanes), 0)
+    lane = lax.broadcasted_iota(jnp.int32, (block_rows, lanes), 1)
+    norm_size = weight_norm.size
+    bias_size = weight_bias.size
+    member = jnp.where(
+        row < query_rows,
+        0,
+        jnp.where(
+            row < query_rows + output_rows,
+            1,
+            jnp.where(
+                row == query_rows + output_rows,
+                jnp.where(lane < norm_size, 2, jnp.where(lane < norm_size + bias_size, 3, 4)),
+                4,
+            ),
+        ),
+    )
+    decay_rate = jnp.where(member < 2, 0.01, 0.0).astype(jnp.float32)
+    moment_next, second_next, update = step_math(summed, moment, second, weight, decay_rate)
+    members = jnp.arange(4, dtype=jnp.int32).reshape(4, 1, 1)
+    chosen = member[None] == members
+    squares = jnp.stack(
         [
-            grad_query[0].reshape(shards, query_rows, lanes),
-            grad_output[0].reshape(shards, output_rows, lanes),
-            small,
-        ],
-        axis=1,
-    )
-    block = reduce_blocks(packed, devices)
-    summed_rest = block[query_rows + output_rows, :small_width]
-    summed_all = [
-        block[:query_rows],
-        block[query_rows : query_rows + output_rows].reshape(weight_output.shape),
-        summed_rest[: weight_norm.size].reshape(weight_norm.shape),
-        summed_rest[weight_norm.size :].reshape(weight_bias.shape),
-    ]
-    results = [
-        step_math(
-            summed_all[member],
-            moments[member],
-            seconds[member],
-            weights[member],
-            decay_rates[member],
+            jnp.sum(jnp.where(chosen, (weight * weight)[None], 0.0), axis=(1, 2)),
+            jnp.sum(jnp.where(chosen, (update * update)[None], 0.0), axis=(1, 2)),
+        ]
+    )
+    squares = lax.psum(squares, "shard")
+    weight_sizes = jnp.sqrt(squares[0])
+    update_sizes = jnp.sqrt(squares[1])
+    trust_ratios = weight_sizes / (update_sizes + 1e-06)
+    ratio = jnp.where(
+        member == 0,
+        trust_ratios[0],
+        jnp.where(member == 1, trust_ratios[1], jnp.where(member == 2, trust_ratios[2], trust_ratios[3])),
+    )
+    updated = (weight - 0.01 * ratio * update).astype(jnp.bfloat16)
+    gather_rows = padded_width(block_rows, 2 * ROW_TILE)
+    updated = jnp.pad(updated, ((0, gather_rows - block_rows), (0, 0)))
+    gathered = lax.all_gather(updated, "shard", axis=0, tiled=False)
+    full_query, full_output, full_norm, full_bias = unpack(gathered, shapes)
+    firsts = unpack(moment_next, shapes)
+    seconds = unpack(second_next, shapes)
+
+    def natural(parts, count):
+        query, output, norm, bias = parts
+        lead = (count,) if count else ()
+        return (
+            query.reshape(lead + shapes[0]).reshape((-1,) + shapes[0][1:]),
+            output.reshape(lead + shapes[1]).reshape((-1,) + shapes[1][1:]),
+            norm.reshape(-1),
+            bias.reshape(lead + shapes[3]).reshape((-1,) + shapes[3][1:]),
         )
-        for member in range(4)
-    ]
-    terms = [as_tile(weight, query_rows, lanes) for weight in weights]
-    terms += [as_tile(result[2], query_rows, lanes) for result in results]
-    stacked = jnp.stack(terms)
-    squares = lax.psum(jnp.sum(stacked * stacked, axis=(1, 2)), "shard")
-    weight_sizes = jnp.sqrt(squares[:4])
-    update_sizes = jnp.sqrt(squares[4:])
-    trust_ratios = weight_sizes / (update_sizes + 1e-06)
-    shards_out = [
-        (weights[member] - 0.01 * trust_ratios[member] * results[member][2]).astype(jnp.bfloat16).reshape(-1)
-        for member in range(4)
-    ]
-    out_width = padded_width(total, LANES)
-    shards_out.append(jnp.zeros((out_width - total,), jnp.bfloat16))
-    gathered = lax.all_gather(jnp.concatenate(shards_out), "shard", axis=0, tiled=False)
-    full = [
-        gathered[:, offsets[member] : offsets[member] + sizes[member]].reshape(
-            (shards * weights[member].shape[0],) + weights[member].shape[1:]
-        )
-        for member in range(4)
-    ]
+
+    full = natural((full_query, full_output, full_norm, full_bias), shards)
+    firsts = natural(firsts, 0)
+    seconds = natural(seconds, 0)
     norm_table = jnp.stack([weight_sizes, update_sizes])
     return (
         full[0],
         full[1],
         full[2],
         full[3],
-        results[0][0],
-        results[1][0],
-        results[2][0],
-        results[3][0],
-        results[0][1],
-        results[1][1],
-        results[2][1],
-        results[3][1],
+        firsts[0],
+        firsts[1],
+        firsts[2],
+        firsts[3],
+        seconds[0],
+        seconds[1],
+        seconds[2],
+        seconds[3],
         norm_table,
         trust_ratios,
     )

time: 138 us -> 138 us (level)
  local copies, waits for them, and re-layouts: 8.05 us -> 11.4 us
  between operations: 3.85 us -> 1.17 us
  blocking collectives: 34.9 us -> 33.4 us
  other arithmetic: 4.63 us -> 6.06 us
    convert_element_type x3 -> x1, other arithmetic: 0.07 us -> 2.75 us  [on_device(): updated = (weight - 0.01 * ratio * update).astype(jnp.bfloat16)]
    another operation x3, local copies, waits for them, and re-layouts: 0.06 us -> 2.54 us  [the longest x1 1.4 us: pack(): block = jnp.concatenate([query, output.reshape(-1, lanes), rest], axis=0)]
    slice x5 -> x8, local copies, waits for them, and re-layouts: 0.82 us -> 2.85 us  [the longest x2 1.57 us: unpack(): block[..., query_rows:query_rows + output_rows, :]]
    add x3 -> x0, other arithmetic: 1.83 us -> none  [step_math(): update = moment_next / (jnp.sqrt(second_next) + 1e-06) + decay_rate * weight]
    concatenate x2 -> x0, local copies, waits for them, and re-layouts: 1.52 us -> none  [the longest x1 1.4 us: on_device(): jnp.concatenate([grad_query[0].reshape(shards, query_rows, lanes), grad_o...]
    reshape x10 -> x15, local copies, waits for them, and re-layouts: 2.97 us -> 3.65 us  [the longest x2 1.33 us: natural(): output.reshape(lead + shapes[1]).reshape((-1,) + shapes[1][1:])]
  transfers between devices with their start and end apart: 12 -> 12, of which waited for: 11 -> 11; matrix products, arithmetic and copies ran while one was open for 0% -> 1% of each run, Pallas kernels for 0% -> 0%
where the time goes in v7:
time: 138 us
  starting transfers between devices  52.1 us (38%)
  waiting for transfers between devices  33.4 us (24%)
  blocking collectives  33.4 us (24%)
  local copies, waits for them, and re-layouts  11.4 us (8%)
  other arithmetic  6.06 us (4%)
    ppermute x12, starting transfers between devices, exchange(): return lax.ppermute(value, AXES, [(d, d ^ mask) for d in range(devices)])  52.1 us
    ppermute x12, waiting for transfers between devices, exchange(): return lax.ppermute(value, AXES, [(d, d ^ mask) for d in range(devices)])  33.4 us
    psum x1, blocking collectives, on_device(): squares = lax.psum(squares, 'shard')  19.4 us
    all_gather x1, blocking collectives, on_device(): gathered = lax.all_gather(updated, 'shard', axis=0, tiled=False)  14.1 us
  transfers between devices with their start and end apart: 12, of which 11 were waited for; matrix products, arithmetic and copies ran while one was open for 1% of the time, Pallas kernels for 0%

profile of v7, /device:TPU:1, one launch (start us, length us, event | category | flops | bytes accessed | tf_op | source)
XLA Modules:
  0.0 137.5 jit_solution(4126545290809529729)
XLA Ops:
  0.7 1.4 %reshape_reshape_squeeze.3 = f32[8,64,384]{2,1,0:T(8,128)S(1)} reshape(f32[1,384,512]{2,1,0:T(8,128)} %param.17) | data formatting | bytes 1572864 | tf_op jit(solution)/shard_map/vmap()/reshape;reshape;squeeze | solution.py:82
  2.1 0.8 copy.37
  2.9 0.5 broadcast.203
  3.4 1.3 reduce.11
  5.0 0.1 select_maximum_fusion
  5.1 8.8 %collective-permute-start = (f32[4,136,384]{2,1,0:T(8,128)S(1)}, f32[4,136,384]{2,1,0:T(8,128)S(1)}, u32[]{:S(2)}, u32[]{:S(2)}) collective-permute-start(f32[4,136,384]{2,1,0:T(8,128)S(1)} %dynamic-slice_bitcast_fusion), channel_id=1, source_target_pairs={{0,1},{1,0},{2,3},{3,2},{4,5},{5,4},{6,7},{7,6},{8,9},{9,8},{10,11... | collective-permute-start | bytes 2506760 | tf_op jit(solution)/shard_map/ppermute | solution.py:31
  14.0 1.9 %collective-permute-done = f32[4,136,384]{2,1,0:T(8,128)S(1)} collective-permute-done((f32[4,136,384]{2,1,0:T(8,128)S(1)}, f32[4,136,384]{2,1,0:T(8,128)S(1)}, u32[]{:S(2)}, u32[]{:S(2)}) %collective-permute-start) | collective-permute-done | bytes 835616 | tf_op jit(solution)/shard_map/ppermute | solution.py:31
  15.9 0.1 bitcast_add_fusion
  16.2 2.1 %collective-permute-start.1 = (f32[136,384]{1,0:T(8,128)S(1)}, f32[136,384]{1,0:T(8,128)S(1)}, u32[]{:S(2)}, u32[]{:S(2)}) collective-permute-start(f32[136,384]{1,0:T(8,128)S(1)} %get-tuple-element.64), channel_id=1, source_target_pairs={{0,2},{1,3},{2,0},{3,1},{4,6},{5,7},{6,4},{7,5},{8,10},{9,11},{10,... | collective-permute-start | bytes 626696 | tf_op jit(solution)/shard_map/ppermute | solution.py:31
  18.2 1.9 %collective-permute-start.2 = (f32[136,384]{1,0:T(8,128)S(1)}, f32[136,384]{1,0:T(8,128)S(1)}, u32[]{:S(2)}, u32[]{:S(2)}) collective-permute-start(f32[136,384]{1,0:T(8,128)S(1)} %get-tuple-element.66), channel_id=1, source_target_pairs={{0,4},{1,5},{2,6},{3,7},{4,0},{5,1},{6,2},{7,3},{8,12},{9,13},{10,... | collective-permute-start | bytes 626696 | tf_op jit(solution)/shard_map/ppermute | solution.py:31
  20.2 5.7 %collective-permute-start.3 = (f32[136,384]{1,0:T(8,128)S(1)}, f32[136,384]{1,0:T(8,128)S(1)}, u32[]{:S(2)}, u32[]{:S(2)}) collective-permute-start(f32[136,384]{1,0:T(8,128)S(1)} %get-tuple-element.65), channel_id=1, source_target_pairs={{0,6},{1,7},{2,4},{3,5},{4,2},{5,3},{6,0},{7,1},{8,14},{9,15},{10,... | collective-permute-start | bytes 626696 | tf_op jit(solution)/shard_map/ppermute | solution.py:31
  26.0 2.0 %collective-permute-done.2 = f32[136,384]{1,0:T(8,128)S(1)} collective-permute-done((f32[136,384]{1,0:T(8,128)S(1)}, f32[136,384]{1,0:T(8,128)S(1)}, u32[]{:S(2)}, u32[]{:S(2)}) %collective-permute-start.2) | collective-permute-done | bytes 208928 | tf_op jit(solution)/shard_map/ppermute | solution.py:31
  28.0 5.2 %collective-permute-done.3 = f32[136,384]{1,0:T(8,128)S(1)} collective-permute-done((f32[136,384]{1,0:T(8,128)S(1)}, f32[136,384]{1,0:T(8,128)S(1)}, u32[]{:S(2)}, u32[]{:S(2)}) %collective-permute-start.3) | collective-permute-done | bytes 208928 | tf_op jit(solution)/shard_map/ppermute | solution.py:31
  33.4 2.6 %collective-permute-start.4 = (f32[80,384]{1,0:T(8,128)S(1)}, f32[80,384]{1,0:T(8,128)S(1)}, u32[]{:S(2)}, u32[]{:S(2)}) collective-permute-start(f32[80,384]{1,0:T(8,128)S(1)} %dynamic-slice_bitcast_fusion.4), channel_id=1, source_target_pairs={{0,24},{1,25},{2,26},{3,27},{4,28},{5,29},{6,30},{7,31},{8,16},{9,... | collective-permute-start | bytes 368648 | tf_op jit(solution)/shard_map/ppermute | solution.py:31
  36.5 4.5 %collective-permute-done.4 = f32[80,384]{1,0:T(8,128)S(1)} collective-permute-done((f32[80,384]{1,0:T(8,128)S(1)}, f32[80,384]{1,0:T(8,128)S(1)}, u32[]{:S(2)}, u32[]{:S(2)}) %collective-permute-start.4) | collective-permute-done | bytes 122912 | tf_op jit(solution)/shard_map/ppermute | solution.py:31
  41.1 1.9 %collective-permute-start.5 = (f32[40,384]{1,0:T(8,128)S(1)}, f32[40,384]{1,0:T(8,128)S(1)}, u32[]{:S(2)}, u32[]{:S(2)}) collective-permute-start(f32[40,384]{1,0:T(8,128)S(1)} %dynamic-slice_bitcast_fusion.5), channel_id=1, source_target_pairs={{0,32},{1,33},{2,34},{3,35},{4,36},{5,37},{6,38},{7,39},{8,40},{9,... | collective-permute-start | bytes 184328 | tf_op jit(solution)/shard_map/ppermute | solution.py:31
  43.1 2.9 %collective-permute-done.5 = f32[40,384]{1,0:T(8,128)S(1)} collective-permute-done((f32[40,384]{1,0:T(8,128)S(1)}, f32[40,384]{1,0:T(8,128)S(1)}, u32[]{:S(2)}, u32[]{:S(2)}) %collective-permute-start.5) | collective-permute-done | bytes 61472 | tf_op jit(solution)/shard_map/ppermute | solution.py:31
  46.0 1.9 %collective-permute-start.6 = (f32[40,384]{1,0:T(8,128)S(1)}, f32[40,384]{1,0:T(8,128)S(1)}, u32[]{:S(2)}, u32[]{:S(2)}) collective-permute-start(f32[40,384]{1,0:T(8,128)S(1)} %bitcast_add_fusion.3), channel_id=1, source_target_pairs={{0,8},{1,9},{2,10},{3,11},{4,12},{5,13},{6,14},{7,15},{8,0},{9,1},... | collective-permute-start | bytes 184328 | tf_op jit(solution)/shard_map/ppermute | solution.py:31
  48.0 3.0 %collective-permute-done.6 = f32[40,384]{1,0:T(8,128)S(1)} collective-permute-done((f32[40,384]{1,0:T(8,128)S(1)}, f32[40,384]{1,0:T(8,128)S(1)}, u32[]{:S(2)}, u32[]{:S(2)}) %collective-permute-start.6) | collective-permute-done | bytes 61472 | tf_op jit(solution)/shard_map/ppermute | solution.py:31
  51.0 3.2 %collective-permute-start.7 = (f32[40,384]{1,0:T(8,128)S(1)}, f32[40,384]{1,0:T(8,128)S(1)}, u32[]{:S(2)}, u32[]{:S(2)}) collective-permute-start(f32[40,384]{1,0:T(8,128)S(1)} %add.132), channel_id=1, source_target_pairs={{0,64},{1,65},{2,66},{3,67},{4,68},{5,69},{6,70},{7,71},{8,72},{9,... | collective-permute-start | bytes 184328 | tf_op jit(solution)/shard_map/ppermute | solution.py:31
  54.2 3.3 %collective-permute-done.7 = f32[40,384]{1,0:T(8,128)S(1)} collective-permute-done((f32[40,384]{1,0:T(8,128)S(1)}, f32[40,384]{1,0:T(8,128)S(1)}, u32[]{:S(2)}, u32[]{:S(2)}) %collective-permute-start.7) | collective-permute-done | bytes 61472 | tf_op jit(solution)/shard_map/ppermute | solution.py:31
  57.5 7.1 %collective-permute-start.8 = (f32[40,384]{1,0:T(8,128)S(1)}, f32[40,384]{1,0:T(8,128)S(1)}, u32[]{:S(2)}, u32[]{:S(2)}) collective-permute-start(f32[40,384]{1,0:T(8,128)S(1)} %add.133), channel_id=1, source_target_pairs={{0,128},{1,129},{2,130},{3,131},{4,132},{5,133},{6,134},{7,135},{8... | collective-permute-start | bytes 184328 | tf_op jit(solution)/shard_map/ppermute | solution.py:31
  64.6 1.8 %collective-permute-done.8 = f32[40,384]{1,0:T(8,128)S(1)} collective-permute-done((f32[40,384]{1,0:T(8,128)S(1)}, f32[40,384]{1,0:T(8,128)S(1)}, u32[]{:S(2)}, u32[]{:S(2)}) %collective-permute-start.8) | collective-permute-done | bytes 61472 | tf_op jit(solution)/shard_map/ppermute | solution.py:31
  66.4 10.6 %collective-permute-start.9 = (f32[40,384]{1,0:T(8,128)S(1)}, f32[40,384]{1,0:T(8,128)S(1)}, u32[]{:S(2)}, u32[]{:S(2)}) collective-permute-start(f32[40,384]{1,0:T(8,128)S(1)} %add.134), channel_id=1, source_target_pairs={{0,384},{1,385},{2,386},{3,387},{4,388},{5,389},{6,390},{7,391},{8... | collective-permute-start | bytes 184328 | tf_op jit(solution)/shard_map/ppermute | solution.py:31
  77.0 3.0 %collective-permute-done.9 = f32[40,384]{1,0:T(8,128)S(1)} collective-permute-done((f32[40,384]{1,0:T(8,128)S(1)}, f32[40,384]{1,0:T(8,128)S(1)}, u32[]{:S(2)}, u32[]{:S(2)}) %collective-permute-start.9) | collective-permute-done | bytes 61472 | tf_op jit(solution)/shard_map/ppermute | solution.py:31
  80.0 1.9 %collective-permute-start.10 = (f32[40,384]{1,0:T(8,128)S(1)}, f32[40,384]{1,0:T(8,128)S(1)}, u32[]{:S(2)}, u32[]{:S(2)}) collective-permute-start(f32[40,384]{1,0:T(8,128)S(1)} %add.135), channel_id=1, source_target_pairs={{0,32},{1,33},{2,34},{3,35},{4,36},{5,37},{6,38},{7,39},{8,40},{9,... | collective-permute-start | bytes 184328 | tf_op jit(solution)/shard_map/ppermute | solution.py:31
  82.0 3.3 %collective-permute-done.10 = f32[40,384]{1,0:T(8,128)S(1)} collective-permute-done((f32[40,384]{1,0:T(8,128)S(1)}, f32[40,384]{1,0:T(8,128)S(1)}, u32[]{:S(2)}, u32[]{:S(2)}) %collective-permute-start.10) | collective-permute-done | bytes 61472 | tf_op jit(solution)/shard_map/ppermute | solution.py:31
  85.3 4.4 %collective-permute-start.11 = (f32[80,384]{1,0:T(8,128)S(1)}, f32[80,384]{1,0:T(8,128)S(1)}, u32[]{:S(2)}, u32[]{:S(2)}) collective-permute-start(f32[80,384]{1,0:T(8,128)S(1)} %pad_maximum_fusion.1), channel_id=1, source_target_pairs={{0,24},{1,25},{2,26},{3,27},{4,28},{5,29},{6,30},{7,31},{8,16},{9,... | collective-permute-start | bytes 368648 | tf_op jit(solution)/shard_map/ppermute | solution.py:31
  89.7 0.1 select_select_fusion
  89.9 2.3 %collective-permute-done.11 = f32[80,384]{1,0:T(8,128)S(1)} collective-permute-done((f32[80,384]{1,0:T(8,128)S(1)}, f32[80,384]{1,0:T(8,128)S(1)}, u32[]{:S(2)}, u32[]{:S(2)}) %collective-permute-start.11) | collective-permute-done | bytes 122912 | tf_op jit(solution)/shard_map/ppermute | solution.py:31
  92.2 0.2 fusion.12
  92.4 0.5 slice_bitcast_fusion
  93.0 0.7 fusion.15
  93.7 0.3 select_reduce_fusion.1
  94.0 0.1 slice_reduce_fusion
  94.1 19.4 %psum.7 = f32[2,4]{1,0:T(2,128)S(1)} all-reduce(f32[2,4]{1,0:T(2,128)S(1)} %pad_maximum_fusion.2), channel_id=1, replica_groups=mesh['replica'=64,'shard'=8] {'shard'}, use_global_device_ids=true, to_apply=%region_2.3 | all-reduce | flops 8 | bytes 64 | tf_op jit(solution)/shard_map/psum | solution.py:163
  113.5 0.6 fusion.17
  114.1 2.8 %subtract_convert_fusion = bf16[136,384]{1,0:T(8,128)(2,1)S(1)} fusion(f32[136,384]{1,0:T(8,128)S(1)} %get-tuple-element.59, f32[]{:T(128)} %bitcast.20, f32[]{:T(128)} %bitcast.19, f32[]{:T(128)} %bitcast.18, f32[]{:T(128)} %bitcast.17, s32[384]{0:T(512)S(1)} %fusion.10, pred[136]{0:T(512)(128)(4,1)S(1)} %iota_compare_fusion.7, ...), kind=kLoop, calls=%fused_computation.24 | loop fusion | flops 1044480 | bytes 513832 | tf_op jit(solution)/shard_map/convert_element_type | solution.py:172
  116.8 14.1 %all-gather = bf16[1152,384]{1,0:T(8,128)(2,1)S(1)} all-gather(bf16[144,384]{1,0:T(8,128)(2,1)S(1)} %pad.45), channel_id=2, replica_groups=mesh['replica'=64,'shard'=8] {'shard'}, dimensions={0}, use_global_device_ids=true | all-gather | bytes 995328 | tf_op jit(solution)/shard_map/all_gather | solution.py:175
  130.9 0.9 fusion.14
  131.9 0.7 reshape.180
  132.5 0.7 reshape.182
  133.2 0.7 reshape.179
  133.8 0.7 reshape.181
  134.5 1.1 reshape_reshape.6
  135.6 0.7 copy.39
  136.3 0.6 reshape.178
  137.0 0.6 pad_maximum_fusion.3
  (73 shorter events, 1.5 us)
Async XLA Ops:
  0.6 4.3 %copy-start = (f32[1,512,384]{2,1,0:T(8,128)S(1)}, f32[1,512,384]{2,1,0:T(8,128)}, u32[]{:S(2)}) copy-start(f32[1,512,384]{2,1,0:T(8,128)} %param.16) | copy-start | bytes 2359300
  5.1 10.8 %collective-permute-start = (f32[4,136,384]{2,1,0:T(8,128)S(1)}, f32[4,136,384]{2,1,0:T(8,128)S(1)}, u32[]{:S(2)}, u32[]{:S(2)}) collective-permute-start(f32[4,136,384]{2,1,0:T(8,128)S(1)} %dynamic-slice_bitcast_fusion), channel_id=1, source_target_pairs={{0,1},{1,0},{2,3},{3,2},{4,5},{5,4},{6,7},{7,6},{8,9},{9,8},{10,11... | collective-permute-start | bytes 2506760 | tf_op jit(solution)/shard_map/ppermute | solution.py:31
  14.0 12.0 %copy-start.8 = (f32[4,6]{1,0:T(4,128)S(1)}, f32[4,6]{1,0:T(4,128)}, u32[]{:S(2)}) copy-start(f32[4,6]{1,0:T(4,128)} %param.23) | copy-start | bytes 292
  16.0 20.0 %copy-start.11 = (f32[64]{0:T(128)S(1)}, f32[64]{0:T(128)}, u32[]{:S(2)}) copy-start(f32[64]{0:T(128)} %param.22) | copy-start | bytes 772
  16.0 20.1 %copy-start.4 = (f32[48,512]{1,0:T(8,128)S(1)}, f32[48,512]{1,0:T(8,128)}, u32[]{:S(2)}) copy-start(f32[48,512]{1,0:T(8,128)} %param.21) | copy-start | bytes 294916
  16.0 20.1 %copy-start.5 = (f32[48,512]{1,0:T(8,128)S(1)}, f32[48,512]{1,0:T(8,128)}, u32[]{:S(2)}) copy-start(f32[48,512]{1,0:T(8,128)} %param.25) | copy-start | bytes 294916
  16.1 20.1 %copy-start.6 = (f32[48,512]{1,0:T(8,128)S(1)}, f32[48,512]{1,0:T(8,128)}, u32[]{:S(2)}) copy-start(f32[48,512]{1,0:T(8,128)} %param.29) | copy-start | bytes 294916
  16.1 20.2 %copy-start.9 = (f32[4,6]{1,0:T(4,128)S(1)}, f32[4,6]{1,0:T(4,128)}, u32[]{:S(2)}) copy-start(f32[4,6]{1,0:T(4,128)} %param.27) | copy-start | bytes 292
  16.1 20.2 %copy-start.12 = (f32[64]{0:T(128)S(1)}, f32[64]{0:T(128)}, u32[]{:S(2)}) copy-start(f32[64]{0:T(128)} %param.26) | copy-start | bytes 772
  16.1 20.3 %copy-start.10 = (f32[4,6]{1,0:T(4,128)S(1)}, f32[4,6]{1,0:T(4,128)}, u32[]{:S(2)}) copy-start(f32[4,6]{1,0:T(4,128)} %param.31) | copy-start | bytes 292
  16.2 26.8 %copy-start.13 = (f32[64]{0:T(128)S(1)}, f32[64]{0:T(128)}, u32[]{:S(2)}) copy-start(f32[64]{0:T(128)} %param.30) | copy-start | bytes 772
  16.2 9.8 %collective-permute-start.1 = (f32[136,384]{1,0:T(8,128)S(1)}, f32[136,384]{1,0:T(8,128)S(1)}, u32[]{:S(2)}, u32[]{:S(2)}) collective-permute-start(f32[136,384]{1,0:T(8,128)S(1)} %get-tuple-element.64), channel_id=1, source_target_pairs={{0,2},{1,3},{2,0},{3,1},{4,6},{5,7},{6,4},{7,5},{8,10},{9,11},{10,... | collective-permute-start | bytes 626696 | tf_op jit(solution)/shard_map/ppermute | solution.py:31
  18.2 9.8 %collective-permute-start.2 = (f32[136,384]{1,0:T(8,128)S(1)}, f32[136,384]{1,0:T(8,128)S(1)}, u32[]{:S(2)}, u32[]{:S(2)}) collective-permute-start(f32[136,384]{1,0:T(8,128)S(1)} %get-tuple-element.66), channel_id=1, source_target_pairs={{0,4},{1,5},{2,6},{3,7},{4,0},{5,1},{6,2},{7,3},{8,12},{9,13},{10,... | collective-permute-start | bytes 626696 | tf_op jit(solution)/shard_map/ppermute | solution.py:31
  20.2 13.1 %collective-permute-start.3 = (f32[136,384]{1,0:T(8,128)S(1)}, f32[136,384]{1,0:T(8,128)S(1)}, u32[]{:S(2)}, u32[]{:S(2)}) collective-permute-start(f32[136,384]{1,0:T(8,128)S(1)} %get-tuple-element.65), channel_id=1, source_target_pairs={{0,6},{1,7},{2,4},{3,5},{4,2},{5,3},{6,0},{7,1},{8,14},{9,15},{10,... | collective-permute-start | bytes 626696 | tf_op jit(solution)/shard_map/ppermute | solution.py:31
  33.3 58.9 %copy-start.1 = (f32[64,384]{1,0:T(8,128)S(1)}, f32[64,384]{1,0:T(8,128)}, u32[]{:S(2)}) copy-start(f32[64,384]{1,0:T(8,128)} %param.20) | copy-start | bytes 294916
  33.4 58.8 %copy-start.2 = (f32[64,384]{1,0:T(8,128)S(1)}, f32[64,384]{1,0:T(8,128)}, u32[]{:S(2)}) copy-start(f32[64,384]{1,0:T(8,128)} %param.28) | copy-start | bytes 294916
  33.4 58.8 %copy-start.3 = (f32[64,384]{1,0:T(8,128)S(1)}, f32[64,384]{1,0:T(8,128)}, u32[]{:S(2)}) copy-start(f32[64,384]{1,0:T(8,128)} %param.24) | copy-start | bytes 294916
  33.4 7.6 %collective-permute-start.4 = (f32[80,384]{1,0:T(8,128)S(1)}, f32[80,384]{1,0:T(8,128)S(1)}, u32[]{:S(2)}, u32[]{:S(2)}) collective-permute-start(f32[80,384]{1,0:T(8,128)S(1)} %dynamic-slice_bitcast_fusion.4), channel_id=1, source_target_pairs={{0,24},{1,25},{2,26},{3,27},{4,28},{5,29},{6,30},{7,31},{8,16},{9,... | collective-permute-start | bytes 368648 | tf_op jit(solution)/shard_map/ppermute | solution.py:31
  41.1 5.0 %collective-permute-start.5 = (f32[40,384]{1,0:T(8,128)S(1)}, f32[40,384]{1,0:T(8,128)S(1)}, u32[]{:S(2)}, u32[]{:S(2)}) collective-permute-start(f32[40,384]{1,0:T(8,128)S(1)} %dynamic-slice_bitcast_fusion.5), channel_id=1, source_target_pairs={{0,32},{1,33},{2,34},{3,35},{4,36},{5,37},{6,38},{7,39},{8,40},{9,... | collective-permute-start | bytes 184328 | tf_op jit(solution)/shard_map/ppermute | solution.py:31
  46.0 5.0 %collective-permute-start.6 = (f32[40,384]{1,0:T(8,128)S(1)}, f32[40,384]{1,0:T(8,128)S(1)}, u32[]{:S(2)}, u32[]{:S(2)}) collective-permute-start(f32[40,384]{1,0:T(8,128)S(1)} %bitcast_add_fusion.3), channel_id=1, source_target_pairs={{0,8},{1,9},{2,10},{3,11},{4,12},{5,13},{6,14},{7,15},{8,0},{9,1},... | collective-permute-start | bytes 184328 | tf_op jit(solution)/shard_map/ppermute | solution.py:31
  51.0 6.5 %collective-permute-start.7 = (f32[40,384]{1,0:T(8,128)S(1)}, f32[40,384]{1,0:T(8,128)S(1)}, u32[]{:S(2)}, u32[]{:S(2)}) collective-permute-start(f32[40,384]{1,0:T(8,128)S(1)} %add.132), channel_id=1, source_target_pairs={{0,64},{1,65},{2,66},{3,67},{4,68},{5,69},{6,70},{7,71},{8,72},{9,... | collective-permute-start | bytes 184328 | tf_op jit(solution)/shard_map/ppermute | solution.py:31
  57.5 8.9 %collective-permute-start.8 = (f32[40,384]{1,0:T(8,128)S(1)}, f32[40,384]{1,0:T(8,128)S(1)}, u32[]{:S(2)}, u32[]{:S(2)}) collective-permute-start(f32[40,384]{1,0:T(8,128)S(1)} %add.133), channel_id=1, source_target_pairs={{0,128},{1,129},{2,130},{3,131},{4,132},{5,133},{6,134},{7,135},{8... | collective-permute-start | bytes 184328 | tf_op jit(solution)/shard_map/ppermute | solution.py:31
  66.4 13.6 %collective-permute-start.9 = (f32[40,384]{1,0:T(8,128)S(1)}, f32[40,384]{1,0:T(8,128)S(1)}, u32[]{:S(2)}, u32[]{:S(2)}) collective-permute-start(f32[40,384]{1,0:T(8,128)S(1)} %add.134), channel_id=1, source_target_pairs={{0,384},{1,385},{2,386},{3,387},{4,388},{5,389},{6,390},{7,391},{8... | collective-permute-start | bytes 184328 | tf_op jit(solution)/shard_map/ppermute | solution.py:31
  80.0 5.3 %collective-permute-start.10 = (f32[40,384]{1,0:T(8,128)S(1)}, f32[40,384]{1,0:T(8,128)S(1)}, u32[]{:S(2)}, u32[]{:S(2)}) collective-permute-start(f32[40,384]{1,0:T(8,128)S(1)} %add.135), channel_id=1, source_target_pairs={{0,32},{1,33},{2,34},{3,35},{4,36},{5,37},{6,38},{7,39},{8,40},{9,... | collective-permute-start | bytes 184328 | tf_op jit(solution)/shard_map/ppermute | solution.py:31
  85.3 6.8 %collective-permute-start.11 = (f32[80,384]{1,0:T(8,128)S(1)}, f32[80,384]{1,0:T(8,128)S(1)}, u32[]{:S(2)}, u32[]{:S(2)}) collective-permute-start(f32[80,384]{1,0:T(8,128)S(1)} %pad_maximum_fusion.1), channel_id=1, source_target_pairs={{0,24},{1,25},{2,26},{3,27},{4,28},{5,29},{6,30},{7,31},{8,16},{9,... | collective-permute-start | bytes 368648 | tf_op jit(solution)/shard_map/ppermute | solution.py:31
  113.5 18.3 %copy-start.7 = (f32[1,4]{1,0:T(1,128)}, f32[1,4]{1,0:T(1,128)S(1)}, u32[]{:S(2)}) copy-start(f32[1,4]{1,0:T(1,128)S(1)} %get-tuple-element.77) | copy-start | bytes 52

commit v8 on v6

--- a/solution.py
+++ b/solution.py
@@ -9,6 +9,7 @@
 REPLICA_SPLITS = ((0b11 << 3, 4), (1 << 5, 5))
 REPLICA_BUTTERFLY = (1 << 3, 1 << 6, 1 << 7, 0b11 << 7)
 ROW_TILE = 8
+SHARD_BUTTERFLY = (1, 0b01 << 1, 0b11 << 1)
 AXES = ("replica", "shard")
 
 
@@ -150,7 +151,9 @@
     terms = [as_tile(weight, query_rows, lanes) for weight in weights]
     terms += [as_tile(result[2], query_rows, lanes) for result in results]
     stacked = jnp.stack(terms)
-    squares = lax.psum(jnp.sum(stacked * stacked, axis=(1, 2)), "shard")
+    squares = jnp.sum(stacked * stacked, axis=(1, 2))
+    for mask in SHARD_BUTTERFLY:
+        squares = squares + exchange(squares, mask, shards * replicas)
     weight_sizes = jnp.sqrt(squares[:4])
     update_sizes = jnp.sqrt(squares[4:])
     trust_ratios = weight_sizes / (update_sizes + 1e-06)

time: 138 us -> 141 us (1.022)
  blocking collectives: 34.9 us -> 17.3 us
  starting transfers between devices: 52.2 us -> 66.8 us
  waiting for transfers between devices: 33.7 us -> 39.5 us
    psum x1 -> x0, blocking collectives: 19.7 us -> none  [on_device(): squares = lax.psum(jnp.sum(stacked * stacked, axis=(1, 2)), 'shard')]
    ppermute x12 -> x15, starting transfers between devices: 52.2 us -> 66.8 us  [exchange(): return lax.ppermute(value, AXES, [(d, d ^ mask) for d in range(devices)])]
    ppermute x12 -> x15, waiting for transfers between devices: 33.7 us -> 39.5 us  [exchange(): return lax.ppermute(value, AXES, [(d, d ^ mask) for d in range(devices)])]
    all_gather x1, blocking collectives: 15.2 us -> 17.3 us  [on_device(): lax.all_gather(jnp.concatenate(shards_out), 'shard', axis=0, tiled=False)]
  transfers between devices with their start and end apart: 12 -> 15, of which waited for: 11 -> 14; matrix products, arithmetic and copies ran while one was open for 0% -> 0% of each run, Pallas kernels for 0% -> 0%
where the time goes in v8:
time: 141 us; the launch traced here: 140 us
  starting transfers between devices  66.8 us (47%)
  waiting for transfers between devices  39.5 us (28%)
  blocking collectives  17.3 us (12%)
  local copies, waits for them, and re-layouts  8.05 us (6%)
  other arithmetic  4.64 us (3%)
  between operations  3.87 us (3%)
    ppermute x15, starting transfers between devices, exchange(): return lax.ppermute(value, AXES, [(d, d ^ mask) for d in range(devices)])  66.8 us
    ppermute x15, waiting for transfers between devices, exchange(): return lax.ppermute(value, AXES, [(d, d ^ mask) for d in range(devices)])  39.5 us
    all_gather x1, blocking collectives, on_device(): lax.all_gather(jnp.concatenate(shards_out), 'shard', axis=0, tiled=False)  17.3 us
  transfers between devices with their start and end apart: 15, of which 14 were waited for; matrix products, arithmetic and copies ran while one was open for 0% of the time, Pallas kernels for 0%

profile of v8, /device:TPU:1, one launch (start us, length us, event | category | flops | bytes accessed | tf_op | source)
XLA Modules:
  0.0 140.1 jit_solution(12028756179296875575)
XLA Ops:
  0.7 1.4 %concatenate.23 = f32[4,2,64,384]{3,2,1,0:T(8,128)S(1)} reshape(f32[1,384,512]{2,1,0:T(8,128)} %param.17) | data formatting | bytes 1572864 | tf_op jit(solution)/shard_map/concatenate | solution.py:125
  2.1 0.8 copy.37
  2.9 0.5 broadcast.73
  3.4 1.3 reduce.7
  5.0 0.1 pad_maximum_fusion
  5.2 8.8 %collective-permute-start = (f32[4,136,384]{2,1,0:T(8,128)S(1)}, f32[4,136,384]{2,1,0:T(8,128)S(1)}, u32[]{:S(2)}, u32[]{:S(2)}) collective-permute-start(f32[4,136,384]{2,1,0:T(8,128)S(1)} %dynamic-slice_bitcast_fusion), channel_id=1, source_target_pairs={{0,1},{1,0},{2,3},{3,2},{4,5},{5,4},{6,7},{7,6},{8,9},{9,8},{10,11... | collective-permute-start | bytes 2506760 | tf_op jit(solution)/shard_map/ppermute | solution.py:32
  14.0 1.9 %collective-permute-done = f32[4,136,384]{2,1,0:T(8,128)S(1)} collective-permute-done((f32[4,136,384]{2,1,0:T(8,128)S(1)}, f32[4,136,384]{2,1,0:T(8,128)S(1)}, u32[]{:S(2)}, u32[]{:S(2)}) %collective-permute-start) | collective-permute-done | bytes 835616 | tf_op jit(solution)/shard_map/ppermute | solution.py:32
  15.9 0.1 bitcast_add_fusion
  16.1 2.1 %collective-permute-start.1 = (f32[136,384]{1,0:T(8,128)S(1)}, f32[136,384]{1,0:T(8,128)S(1)}, u32[]{:S(2)}, u32[]{:S(2)}) collective-permute-start(f32[136,384]{1,0:T(8,128)S(1)} %get-tuple-element.68), channel_id=1, source_target_pairs={{0,2},{1,3},{2,0},{3,1},{4,6},{5,7},{6,4},{7,5},{8,10},{9,11},{10,... | collective-permute-start | bytes 626696 | tf_op jit(solution)/shard_map/ppermute | solution.py:32
  18.2 1.9 %collective-permute-start.2 = (f32[136,384]{1,0:T(8,128)S(1)}, f32[136,384]{1,0:T(8,128)S(1)}, u32[]{:S(2)}, u32[]{:S(2)}) collective-permute-start(f32[136,384]{1,0:T(8,128)S(1)} %get-tuple-element.70), channel_id=1, source_target_pairs={{0,4},{1,5},{2,6},{3,7},{4,0},{5,1},{6,2},{7,3},{8,12},{9,13},{10,... | collective-permute-start | bytes 626696 | tf_op jit(solution)/shard_map/ppermute | solution.py:32
  20.1 5.7 %collective-permute-start.3 = (f32[136,384]{1,0:T(8,128)S(1)}, f32[136,384]{1,0:T(8,128)S(1)}, u32[]{:S(2)}, u32[]{:S(2)}) collective-permute-start(f32[136,384]{1,0:T(8,128)S(1)} %get-tuple-element.69), channel_id=1, source_target_pairs={{0,6},{1,7},{2,4},{3,5},{4,2},{5,3},{6,0},{7,1},{8,14},{9,15},{10,... | collective-permute-start | bytes 626696 | tf_op jit(solution)/shard_map/ppermute | solution.py:32
  25.9 2.1 %collective-permute-done.2 = f32[136,384]{1,0:T(8,128)S(1)} collective-permute-done((f32[136,384]{1,0:T(8,128)S(1)}, f32[136,384]{1,0:T(8,128)S(1)}, u32[]{:S(2)}, u32[]{:S(2)}) %collective-permute-start.2) | collective-permute-done | bytes 208928 | tf_op jit(solution)/shard_map/ppermute | solution.py:32
  28.0 5.2 %collective-permute-done.3 = f32[136,384]{1,0:T(8,128)S(1)} collective-permute-done((f32[136,384]{1,0:T(8,128)S(1)}, f32[136,384]{1,0:T(8,128)S(1)}, u32[]{:S(2)}, u32[]{:S(2)}) %collective-permute-start.3) | collective-permute-done | bytes 208928 | tf_op jit(solution)/shard_map/ppermute | solution.py:32
  33.3 2.5 %collective-permute-start.4 = (f32[80,384]{1,0:T(8,128)S(1)}, f32[80,384]{1,0:T(8,128)S(1)}, u32[]{:S(2)}, u32[]{:S(2)}) collective-permute-start(f32[80,384]{1,0:T(8,128)S(1)} %dynamic-slice_bitcast_fusion.4), channel_id=1, source_target_pairs={{0,24},{1,25},{2,26},{3,27},{4,28},{5,29},{6,30},{7,31},{8,16},{9,... | collective-permute-start | bytes 368648 | tf_op jit(solution)/shard_map/ppermute | solution.py:32
  35.8 5.0 %collective-permute-done.4 = f32[80,384]{1,0:T(8,128)S(1)} collective-permute-done((f32[80,384]{1,0:T(8,128)S(1)}, f32[80,384]{1,0:T(8,128)S(1)}, u32[]{:S(2)}, u32[]{:S(2)}) %collective-permute-start.4) | collective-permute-done | bytes 122912 | tf_op jit(solution)/shard_map/ppermute | solution.py:32
  40.9 2.1 %collective-permute-start.5 = (f32[40,384]{1,0:T(8,128)S(1)}, f32[40,384]{1,0:T(8,128)S(1)}, u32[]{:S(2)}, u32[]{:S(2)}) collective-permute-start(f32[40,384]{1,0:T(8,128)S(1)} %dynamic-slice_bitcast_fusion.5), channel_id=1, source_target_pairs={{0,32},{1,33},{2,34},{3,35},{4,36},{5,37},{6,38},{7,39},{8,40},{9,... | collective-permute-start | bytes 184328 | tf_op jit(solution)/shard_map/ppermute | solution.py:32
  42.9 3.0 %collective-permute-done.5 = f32[40,384]{1,0:T(8,128)S(1)} collective-permute-done((f32[40,384]{1,0:T(8,128)S(1)}, f32[40,384]{1,0:T(8,128)S(1)}, u32[]{:S(2)}, u32[]{:S(2)}) %collective-permute-start.5) | collective-permute-done | bytes 61472 | tf_op jit(solution)/shard_map/ppermute | solution.py:32
  46.0 1.9 %collective-permute-start.6 = (f32[40,384]{1,0:T(8,128)S(1)}, f32[40,384]{1,0:T(8,128)S(1)}, u32[]{:S(2)}, u32[]{:S(2)}) collective-permute-start(f32[40,384]{1,0:T(8,128)S(1)} %bitcast_add_fusion.3), channel_id=1, source_target_pairs={{0,8},{1,9},{2,10},{3,11},{4,12},{5,13},{6,14},{7,15},{8,0},{9,1},... | collective-permute-start | bytes 184328 | tf_op jit(solution)/shard_map/ppermute | solution.py:32
  47.9 3.0 %collective-permute-done.6 = f32[40,384]{1,0:T(8,128)S(1)} collective-permute-done((f32[40,384]{1,0:T(8,128)S(1)}, f32[40,384]{1,0:T(8,128)S(1)}, u32[]{:S(2)}, u32[]{:S(2)}) %collective-permute-start.6) | collective-permute-done | bytes 61472 | tf_op jit(solution)/shard_map/ppermute | solution.py:32
  51.0 3.2 %collective-permute-start.7 = (f32[40,384]{1,0:T(8,128)S(1)}, f32[40,384]{1,0:T(8,128)S(1)}, u32[]{:S(2)}, u32[]{:S(2)}) collective-permute-start(f32[40,384]{1,0:T(8,128)S(1)} %add.182), channel_id=1, source_target_pairs={{0,64},{1,65},{2,66},{3,67},{4,68},{5,69},{6,70},{7,71},{8,72},{9,... | collective-permute-start | bytes 184328 | tf_op jit(solution)/shard_map/ppermute | solution.py:32
  54.1 3.3 %collective-permute-done.7 = f32[40,384]{1,0:T(8,128)S(1)} collective-permute-done((f32[40,384]{1,0:T(8,128)S(1)}, f32[40,384]{1,0:T(8,128)S(1)}, u32[]{:S(2)}, u32[]{:S(2)}) %collective-permute-start.7) | collective-permute-done | bytes 61472 | tf_op jit(solution)/shard_map/ppermute | solution.py:32
  57.5 7.1 %collective-permute-start.8 = (f32[40,384]{1,0:T(8,128)S(1)}, f32[40,384]{1,0:T(8,128)S(1)}, u32[]{:S(2)}, u32[]{:S(2)}) collective-permute-start(f32[40,384]{1,0:T(8,128)S(1)} %add.183), channel_id=1, source_target_pairs={{0,128},{1,129},{2,130},{3,131},{4,132},{5,133},{6,134},{7,135},{8... | collective-permute-start | bytes 184328 | tf_op jit(solution)/shard_map/ppermute | solution.py:32
  64.6 1.8 %collective-permute-done.8 = f32[40,384]{1,0:T(8,128)S(1)} collective-permute-done((f32[40,384]{1,0:T(8,128)S(1)}, f32[40,384]{1,0:T(8,128)S(1)}, u32[]{:S(2)}, u32[]{:S(2)}) %collective-permute-start.8) | collective-permute-done | bytes 61472 | tf_op jit(solution)/shard_map/ppermute | solution.py:32
  66.4 10.7 %collective-permute-start.9 = (f32[40,384]{1,0:T(8,128)S(1)}, f32[40,384]{1,0:T(8,128)S(1)}, u32[]{:S(2)}, u32[]{:S(2)}) collective-permute-start(f32[40,384]{1,0:T(8,128)S(1)} %add.184), channel_id=1, source_target_pairs={{0,384},{1,385},{2,386},{3,387},{4,388},{5,389},{6,390},{7,391},{8... | collective-permute-start | bytes 184328 | tf_op jit(solution)/shard_map/ppermute | solution.py:32
  77.2 2.8 %collective-permute-done.9 = f32[40,384]{1,0:T(8,128)S(1)} collective-permute-done((f32[40,384]{1,0:T(8,128)S(1)}, f32[40,384]{1,0:T(8,128)S(1)}, u32[]{:S(2)}, u32[]{:S(2)}) %collective-permute-start.9) | collective-permute-done | bytes 61472 | tf_op jit(solution)/shard_map/ppermute | solution.py:32
  80.0 1.9 %collective-permute-start.10 = (f32[40,384]{1,0:T(8,128)S(1)}, f32[40,384]{1,0:T(8,128)S(1)}, u32[]{:S(2)}, u32[]{:S(2)}) collective-permute-start(f32[40,384]{1,0:T(8,128)S(1)} %add.185), channel_id=1, source_target_pairs={{0,32},{1,33},{2,34},{3,35},{4,36},{5,37},{6,38},{7,39},{8,40},{9,... | collective-permute-start | bytes 184328 | tf_op jit(solution)/shard_map/ppermute | solution.py:32
  81.9 3.2 %collective-permute-done.10 = f32[40,384]{1,0:T(8,128)S(1)} collective-permute-done((f32[40,384]{1,0:T(8,128)S(1)}, f32[40,384]{1,0:T(8,128)S(1)}, u32[]{:S(2)}, u32[]{:S(2)}) %collective-permute-start.10) | collective-permute-done | bytes 61472 | tf_op jit(solution)/shard_map/ppermute | solution.py:32
  85.2 4.4 %collective-permute-start.11 = (f32[80,384]{1,0:T(8,128)S(1)}, f32[80,384]{1,0:T(8,128)S(1)}, u32[]{:S(2)}, u32[]{:S(2)}) collective-permute-start(f32[80,384]{1,0:T(8,128)S(1)} %pad_maximum_fusion.1), channel_id=1, source_target_pairs={{0,24},{1,25},{2,26},{3,27},{4,28},{5,29},{6,30},{7,31},{8,16},{9,... | collective-permute-start | bytes 368648 | tf_op jit(solution)/shard_map/ppermute | solution.py:32
  89.7 2.3 %collective-permute-done.11 = f32[80,384]{1,0:T(8,128)S(1)} collective-permute-done((f32[80,384]{1,0:T(8,128)S(1)}, f32[80,384]{1,0:T(8,128)S(1)}, u32[]{:S(2)}, u32[]{:S(2)}) %collective-permute-start.11) | collective-permute-done | bytes 122912 | tf_op jit(solution)/shard_map/ppermute | solution.py:32
  92.2 0.7 multiply_add_fusion.2
  93.0 0.6 multiply_add_fusion.5
  93.8 0.5 multiply_add_fusion.7
  94.4 0.2 multiply_reduce_fusion
  94.6 9.8 %collective-permute-start.12 = (f32[8]{0:T(128)S(1)}, f32[8]{0:T(128)S(1)}, u32[]{:S(2)}, u32[]{:S(2)}) collective-permute-start(f32[8]{0:T(128)S(1)} %multiply_reduce_fusion), channel_id=1, source_target_pairs={{0,1},{1,0},{2,3},{3,2},{4,5},{5,4},{6,7},{7,6},{8,9},{9,8},{10,11... | collective-permute-start | bytes 104 | tf_op jit(solution)/shard_map/ppermute | solution.py:32
  104.4 0.8 collective-permute-done.12
  105.2 1.9 %collective-permute-start.13 = (f32[8]{0:T(128)S(1)}, f32[8]{0:T(128)S(1)}, u32[]{:S(2)}, u32[]{:S(2)}) collective-permute-start(f32[8]{0:T(128)S(1)} %add.205), channel_id=1, source_target_pairs={{0,2},{1,3},{2,0},{3,1},{4,6},{5,7},{6,4},{7,5},{8,10},{9,11},{10,... | collective-permute-start | bytes 104 | tf_op jit(solution)/shard_map/ppermute | solution.py:32
  107.1 2.4 %collective-permute-done.13 = f32[8]{0:T(128)S(1)} collective-permute-done((f32[8]{0:T(128)S(1)}, f32[8]{0:T(128)S(1)}, u32[]{:S(2)}, u32[]{:S(2)}) %collective-permute-start.13) | collective-permute-done | bytes 64 | tf_op jit(solution)/shard_map/ppermute | solution.py:32
  109.4 2.8 %collective-permute-start.14 = (f32[8]{0:T(128)S(1)}, f32[8]{0:T(128)S(1)}, u32[]{:S(2)}, u32[]{:S(2)}) collective-permute-start(f32[8]{0:T(128)S(1)} %add.206), channel_id=1, source_target_pairs={{0,6},{1,7},{2,4},{3,5},{4,2},{5,3},{6,0},{7,1},{8,14},{9,15},{10,... | collective-permute-start | bytes 104 | tf_op jit(solution)/shard_map/ppermute | solution.py:32
  112.3 2.6 %collective-permute-done.14 = f32[8]{0:T(128)S(1)} collective-permute-done((f32[8]{0:T(128)S(1)}, f32[8]{0:T(128)S(1)}, u32[]{:S(2)}, u32[]{:S(2)}) %collective-permute-start.14) | collective-permute-done | bytes 64 | tf_op jit(solution)/shard_map/ppermute | solution.py:32
  115.0 0.6 fusion.19
  118.5 0.1 concatenate.29
  118.6 0.1 reshape.110
  118.7 17.3 %all-gather.1 = bf16[8,1,49280]{2,1,0:T(2,128)(2,1)S(1)} all-gather(bf16[1,1,49280]{2,1,0:T(2,128)(2,1)S(1)} %reshape.110), channel_id=2, replica_groups=mesh['replica'=64,'shard'=8] {'shard'}, dimensions={0}, use_global_device_ids=true | all-gather | bytes 887040 | tf_op jit(solution)/shard_map/all_gather | solution.py:166
  136.2 0.9 reshape.105
  137.2 0.9 reshape.106
  138.2 0.7 copy.39
  138.9 0.6 reshape.107
  139.5 0.6 pad_maximum_fusion.3
  (86 shorter events, 1.9 us)
Async XLA Ops:
  0.6 4.3 %copy-start.2 = (f32[1,512,384]{2,1,0:T(8,128)S(1)}, f32[1,512,384]{2,1,0:T(8,128)}, u32[]{:S(2)}) copy-start(f32[1,512,384]{2,1,0:T(8,128)} %param.16) | copy-start | bytes 2359300
  5.2 10.8 %collective-permute-start = (f32[4,136,384]{2,1,0:T(8,128)S(1)}, f32[4,136,384]{2,1,0:T(8,128)S(1)}, u32[]{:S(2)}, u32[]{:S(2)}) collective-permute-start(f32[4,136,384]{2,1,0:T(8,128)S(1)} %dynamic-slice_bitcast_fusion), channel_id=1, source_target_pairs={{0,1},{1,0},{2,3},{3,2},{4,5},{5,4},{6,7},{7,6},{8,9},{9,8},{10,11... | collective-permute-start | bytes 2506760 | tf_op jit(solution)/shard_map/ppermute | solution.py:32
  16.1 61.0 %copy-start.1 = (f32[64,384]{1,0:T(8,128)S(1)}, f32[64,384]{1,0:T(8,128)}, u32[]{:S(2)}) copy-start(f32[64,384]{1,0:T(8,128)} %param.20) | copy-start | bytes 294916
  16.1 61.0 %copy-start = (f32[48,512]{1,0:T(8,128)S(1)}, f32[48,512]{1,0:T(8,128)}, u32[]{:S(2)}) copy-start(f32[48,512]{1,0:T(8,128)} %param.21) | copy-start | bytes 294916
  16.1 9.7 %collective-permute-start.1 = (f32[136,384]{1,0:T(8,128)S(1)}, f32[136,384]{1,0:T(8,128)S(1)}, u32[]{:S(2)}, u32[]{:S(2)}) collective-permute-start(f32[136,384]{1,0:T(8,128)S(1)} %get-tuple-element.68), channel_id=1, source_target_pairs={{0,2},{1,3},{2,0},{3,1},{4,6},{5,7},{6,4},{7,5},{8,10},{9,11},{10,... | collective-permute-start | bytes 626696 | tf_op jit(solution)/shard_map/ppermute | solution.py:32
  18.2 9.8 %collective-permute-start.2 = (f32[136,384]{1,0:T(8,128)S(1)}, f32[136,384]{1,0:T(8,128)S(1)}, u32[]{:S(2)}, u32[]{:S(2)}) collective-permute-start(f32[136,384]{1,0:T(8,128)S(1)} %get-tuple-element.70), channel_id=1, source_target_pairs={{0,4},{1,5},{2,6},{3,7},{4,0},{5,1},{6,2},{7,3},{8,12},{9,13},{10,... | collective-permute-start | bytes 626696 | tf_op jit(solution)/shard_map/ppermute | solution.py:32
  20.1 13.1 %collective-permute-start.3 = (f32[136,384]{1,0:T(8,128)S(1)}, f32[136,384]{1,0:T(8,128)S(1)}, u32[]{:S(2)}, u32[]{:S(2)}) collective-permute-start(f32[136,384]{1,0:T(8,128)S(1)} %get-tuple-element.69), channel_id=1, source_target_pairs={{0,6},{1,7},{2,4},{3,5},{4,2},{5,3},{6,0},{7,1},{8,14},{9,15},{10,... | collective-permute-start | bytes 626696 | tf_op jit(solution)/shard_map/ppermute | solution.py:32
  33.2 56.4 %copy-start.11 = (f32[64]{0:T(128)S(1)}, f32[64]{0:T(128)}, u32[]{:S(2)}) copy-start(f32[64]{0:T(128)} %param.22) | copy-start | bytes 772
  33.2 56.4 %copy-start.9 = (f32[4,6]{1,0:T(4,128)S(1)}, f32[4,6]{1,0:T(4,128)}, u32[]{:S(2)}) copy-start(f32[4,6]{1,0:T(4,128)} %param.23) | copy-start | bytes 292
  33.3 7.5 %collective-permute-start.4 = (f32[80,384]{1,0:T(8,128)S(1)}, f32[80,384]{1,0:T(8,128)S(1)}, u32[]{:S(2)}, u32[]{:S(2)}) collective-permute-start(f32[80,384]{1,0:T(8,128)S(1)} %dynamic-slice_bitcast_fusion.4), channel_id=1, source_target_pairs={{0,24},{1,25},{2,26},{3,27},{4,28},{5,29},{6,30},{7,31},{8,16},{9,... | collective-permute-start | bytes 368648 | tf_op jit(solution)/shard_map/ppermute | solution.py:32
  40.8 51.3 %copy-start.5 = (f32[48,512]{1,0:T(8,128)S(1)}, f32[48,512]{1,0:T(8,128)}, u32[]{:S(2)}) copy-start(f32[48,512]{1,0:T(8,128)} %param.29) | copy-start | bytes 294916
  40.8 51.3 %copy-start.6 = (f32[48,512]{1,0:T(8,128)S(1)}, f32[48,512]{1,0:T(8,128)}, u32[]{:S(2)}) copy-start(f32[48,512]{1,0:T(8,128)} %param.25) | copy-start | bytes 294916
  40.9 5.1 %collective-permute-start.5 = (f32[40,384]{1,0:T(8,128)S(1)}, f32[40,384]{1,0:T(8,128)S(1)}, u32[]{:S(2)}, u32[]{:S(2)}) collective-permute-start(f32[40,384]{1,0:T(8,128)S(1)} %dynamic-slice_bitcast_fusion.5), channel_id=1, source_target_pairs={{0,32},{1,33},{2,34},{3,35},{4,36},{5,37},{6,38},{7,39},{8,40},{9,... | collective-permute-start | bytes 184328 | tf_op jit(solution)/shard_map/ppermute | solution.py:32
  46.0 5.0 %collective-permute-start.6 = (f32[40,384]{1,0:T(8,128)S(1)}, f32[40,384]{1,0:T(8,128)S(1)}, u32[]{:S(2)}, u32[]{:S(2)}) collective-permute-start(f32[40,384]{1,0:T(8,128)S(1)} %bitcast_add_fusion.3), channel_id=1, source_target_pairs={{0,8},{1,9},{2,10},{3,11},{4,12},{5,13},{6,14},{7,15},{8,0},{9,1},... | collective-permute-start | bytes 184328 | tf_op jit(solution)/shard_map/ppermute | solution.py:32
  51.0 6.5 %collective-permute-start.7 = (f32[40,384]{1,0:T(8,128)S(1)}, f32[40,384]{1,0:T(8,128)S(1)}, u32[]{:S(2)}, u32[]{:S(2)}) collective-permute-start(f32[40,384]{1,0:T(8,128)S(1)} %add.182), channel_id=1, source_target_pairs={{0,64},{1,65},{2,66},{3,67},{4,68},{5,69},{6,70},{7,71},{8,72},{9,... | collective-permute-start | bytes 184328 | tf_op jit(solution)/shard_map/ppermute | solution.py:32
  57.5 8.9 %collective-permute-start.8 = (f32[40,384]{1,0:T(8,128)S(1)}, f32[40,384]{1,0:T(8,128)S(1)}, u32[]{:S(2)}, u32[]{:S(2)}) collective-permute-start(f32[40,384]{1,0:T(8,128)S(1)} %add.183), channel_id=1, source_target_pairs={{0,128},{1,129},{2,130},{3,131},{4,132},{5,133},{6,134},{7,135},{8... | collective-permute-start | bytes 184328 | tf_op jit(solution)/shard_map/ppermute | solution.py:32
  66.4 26.6 %copy-start.12 = (f32[4,6]{1,0:T(4,128)S(1)}, f32[4,6]{1,0:T(4,128)}, u32[]{:S(2)}) copy-start(f32[4,6]{1,0:T(4,128)} %param.31) | copy-start | bytes 292
  66.4 26.6 %copy-start.13 = (f32[4,6]{1,0:T(4,128)S(1)}, f32[4,6]{1,0:T(4,128)}, u32[]{:S(2)}) copy-start(f32[4,6]{1,0:T(4,128)} %param.27) | copy-start | bytes 292
  66.4 27.3 %copy-start.7 = (f32[64,384]{1,0:T(8,128)S(1)}, f32[64,384]{1,0:T(8,128)}, u32[]{:S(2)}) copy-start(f32[64,384]{1,0:T(8,128)} %param.28) | copy-start | bytes 294916
  66.4 27.3 %copy-start.8 = (f32[64,384]{1,0:T(8,128)S(1)}, f32[64,384]{1,0:T(8,128)}, u32[]{:S(2)}) copy-start(f32[64,384]{1,0:T(8,128)} %param.24) | copy-start | bytes 294916
  66.4 13.5 %collective-permute-start.9 = (f32[40,384]{1,0:T(8,128)S(1)}, f32[40,384]{1,0:T(8,128)S(1)}, u32[]{:S(2)}, u32[]{:S(2)}) collective-permute-start(f32[40,384]{1,0:T(8,128)S(1)} %add.184), channel_id=1, source_target_pairs={{0,384},{1,385},{2,386},{3,387},{4,388},{5,389},{6,390},{7,391},{8... | collective-permute-start | bytes 184328 | tf_op jit(solution)/shard_map/ppermute | solution.py:32
  80.0 5.1 %collective-permute-start.10 = (f32[40,384]{1,0:T(8,128)S(1)}, f32[40,384]{1,0:T(8,128)S(1)}, u32[]{:S(2)}, u32[]{:S(2)}) collective-permute-start(f32[40,384]{1,0:T(8,128)S(1)} %add.185), channel_id=1, source_target_pairs={{0,32},{1,33},{2,34},{3,35},{4,36},{5,37},{6,38},{7,39},{8,40},{9,... | collective-permute-start | bytes 184328 | tf_op jit(solution)/shard_map/ppermute | solution.py:32
  85.1 8.7 %copy-start.14 = (f32[64]{0:T(128)S(1)}, f32[64]{0:T(128)}, u32[]{:S(2)}) copy-start(f32[64]{0:T(128)} %param.30) | copy-start | bytes 772
  85.2 8.7 %copy-start.15 = (f32[64]{0:T(128)S(1)}, f32[64]{0:T(128)}, u32[]{:S(2)}) copy-start(f32[64]{0:T(128)} %param.26) | copy-start | bytes 772
  85.2 6.8 %collective-permute-start.11 = (f32[80,384]{1,0:T(8,128)S(1)}, f32[80,384]{1,0:T(8,128)S(1)}, u32[]{:S(2)}, u32[]{:S(2)}) collective-permute-start(f32[80,384]{1,0:T(8,128)S(1)} %pad_maximum_fusion.1), channel_id=1, source_target_pairs={{0,24},{1,25},{2,26},{3,27},{4,28},{5,29},{6,30},{7,31},{8,16},{9,... | collective-permute-start | bytes 368648 | tf_op jit(solution)/shard_map/ppermute | solution.py:32
  93.8 42.2 %copy-start.3 = (f32[64,384]{1,0:T(8,128)}, f32[64,384]{1,0:T(8,128)S(1)}, u32[]{:S(2)}) copy-start(f32[64,384]{1,0:T(8,128)S(1)} %get-tuple-element.66) | copy-start | bytes 294916
  93.8 42.2 %copy-start.4 = (f32[64,384]{1,0:T(8,128)}, f32[64,384]{1,0:T(8,128)S(1)}, u32[]{:S(2)}) copy-start(f32[64,384]{1,0:T(8,128)S(1)} %get-tuple-element.67) | copy-start | bytes 294916
  94.6 10.6 %collective-permute-start.12 = (f32[8]{0:T(128)S(1)}, f32[8]{0:T(128)S(1)}, u32[]{:S(2)}, u32[]{:S(2)}) collective-permute-start(f32[8]{0:T(128)S(1)} %multiply_reduce_fusion), channel_id=1, source_target_pairs={{0,1},{1,0},{2,3},{3,2},{4,5},{5,4},{6,7},{7,6},{8,9},{9,8},{10,11... | collective-permute-start | bytes 104 | tf_op jit(solution)/shard_map/ppermute | solution.py:32
  105.2 4.3 %collective-permute-start.13 = (f32[8]{0:T(128)S(1)}, f32[8]{0:T(128)S(1)}, u32[]{:S(2)}, u32[]{:S(2)}) collective-permute-start(f32[8]{0:T(128)S(1)} %add.205), channel_id=1, source_target_pairs={{0,2},{1,3},{2,0},{3,1},{4,6},{5,7},{6,4},{7,5},{8,10},{9,11},{10,... | collective-permute-start | bytes 104 | tf_op jit(solution)/shard_map/ppermute | solution.py:32
  109.4 5.5 %collective-permute-start.14 = (f32[8]{0:T(128)S(1)}, f32[8]{0:T(128)S(1)}, u32[]{:S(2)}, u32[]{:S(2)}) collective-permute-start(f32[8]{0:T(128)S(1)} %add.206), channel_id=1, source_target_pairs={{0,6},{1,7},{2,4},{3,5},{4,2},{5,3},{6,0},{7,1},{8,14},{9,15},{10,... | collective-permute-start | bytes 104 | tf_op jit(solution)/shard_map/ppermute | solution.py:32
  115.0 21.1 %copy-start.10 = (f32[4]{0:T(128)}, f32[4]{0:T(128)S(1)}, u32[]{:S(2)}) copy-start(f32[4]{0:T(128)S(1)} %get-tuple-element.79) | copy-start | bytes 52

commit v9 on v6

--- a/solution.py
+++ b/solution.py
@@ -6,8 +6,8 @@
 LANES = 128
 CORE_BIT = 0
 Y_GROUP = (2, 1)
-REPLICA_SPLITS = ((0b11 << 3, 4), (1 << 5, 5))
-REPLICA_BUTTERFLY = (1 << 3, 1 << 6, 1 << 7, 0b11 << 7)
+REPLICA_SPLITS = ((0b11 << 3, 4), (1 << 5, 5), (1 << 3, 3))
+REPLICA_BUTTERFLY = (1 << 6, 1 << 7, 0b11 << 7)
 ROW_TILE = 8
 AXES = ("replica", "shard")
 
@@ -58,7 +58,7 @@
         part = lax.dynamic_index_in_dim(blocks, mine ^ t, 0, keepdims=False)
         total = total + exchange(part, masks[t], devices)
     rows, lanes = total.shape
-    multiple = ROW_TILE << len(REPLICA_SPLITS)
+    multiple = ROW_TILE << (len(REPLICA_SPLITS) - 1)
     total = jnp.pad(total, ((0, padded_width(rows, multiple) - rows), (0, 0)))
     for mask, bit in REPLICA_SPLITS:
         halves = total.reshape((2, total.shape[0] // 2, lanes))

time: 138 us -> 142 us (1.029)
  blocking collectives: 34.9 us -> 36.9 us
  starting transfers between devices: 52.2 us -> 54.2 us
    psum x1, blocking collectives: 19.7 us -> 21.7 us  [on_device(): squares = lax.psum(jnp.sum(stacked * stacked, axis=(1, 2)), 'shard')]
    ppermute x12 -> x13, starting transfers between devices: 52.2 us -> 54.2 us  [exchange(): return lax.ppermute(value, AXES, [(d, d ^ mask) for d in range(devices)])]
    ppermute x12 -> x13, waiting for transfers between devices: 33.7 us -> 33.3 us  [exchange(): return lax.ppermute(value, AXES, [(d, d ^ mask) for d in range(devices)])]
  transfers between devices with their start and end apart: 12 -> 13, of which waited for: 11 -> 12; matrix products, arithmetic and copies ran while one was open for 0% -> 0% of each run, Pallas kernels for 0% -> 0%
where the time goes in v9:
time: 142 us; the launch traced here: 141 us
  starting transfers between devices  54.2 us (38%)
  blocking collectives  36.9 us (26%)
  waiting for transfers between devices  33.3 us (23%)
  local copies, waits for them, and re-layouts  8.07 us (6%)
  other arithmetic  4.63 us (3%)
  between operations  3.88 us (3%)
    ppermute x13, starting transfers between devices, exchange(): return lax.ppermute(value, AXES, [(d, d ^ mask) for d in range(devices)])  54.2 us
    ppermute x13, waiting for transfers between devices, exchange(): return lax.ppermute(value, AXES, [(d, d ^ mask) for d in range(devices)])  33.3 us
    psum x1, blocking collectives, on_device(): squares = lax.psum(jnp.sum(stacked * stacked, axis=(1, 2)), 'shard')  21.7 us
    all_gather x1, blocking collectives, on_device(): lax.all_gather(jnp.concatenate(shards_out), 'shard', axis=0, tiled=False)  15.2 us
  transfers between devices with their start and end apart: 13, of which 12 were waited for; matrix products, arithmetic and copies ran while one was open for 0% of the time, Pallas kernels for 0%

profile of v9, /device:TPU:1, one launch (start us, length us, event | category | flops | bytes accessed | tf_op | source)
XLA Modules:
  0.0 141.0 jit_solution(5566538040112533008)
XLA Ops:
  0.7 1.4 concatenate.26
  2.1 0.8 copy.37
  2.9 0.5 broadcast.73
  3.4 1.3 reduce.7
  5.0 0.1 pad_maximum_fusion
  5.2 8.8 %collective-permute-start = (f32[4,136,384]{2,1,0:T(8,128)S(1)}, f32[4,136,384]{2,1,0:T(8,128)S(1)}, u32[]{:S(2)}, u32[]{:S(2)}) collective-permute-start(f32[4,136,384]{2,1,0:T(8,128)S(1)} %dynamic-slice_bitcast_fusion), channel_id=1, source_target_pairs={{0,1},{1,0},{2,3},{3,2},{4,5},{5,4},{6,7},{7,6},{8,9},{9,8},{10,11... | collective-permute-start | bytes 2506760 | tf_op jit(solution)/shard_map/ppermute | solution.py:31
  14.0 1.9 %collective-permute-done = f32[4,136,384]{2,1,0:T(8,128)S(1)} collective-permute-done((f32[4,136,384]{2,1,0:T(8,128)S(1)}, f32[4,136,384]{2,1,0:T(8,128)S(1)}, u32[]{:S(2)}, u32[]{:S(2)}) %collective-permute-start) | collective-permute-done | bytes 835616 | tf_op jit(solution)/shard_map/ppermute | solution.py:31
  15.9 0.1 bitcast_add_fusion
  16.1 2.1 %collective-permute-start.1 = (f32[136,384]{1,0:T(8,128)S(1)}, f32[136,384]{1,0:T(8,128)S(1)}, u32[]{:S(2)}, u32[]{:S(2)}) collective-permute-start(f32[136,384]{1,0:T(8,128)S(1)} %get-tuple-element.68), channel_id=1, source_target_pairs={{0,2},{1,3},{2,0},{3,1},{4,6},{5,7},{6,4},{7,5},{8,10},{9,11},{10,... | collective-permute-start | bytes 626696 | tf_op jit(solution)/shard_map/ppermute | solution.py:31
  18.2 2.1 %collective-permute-start.2 = (f32[136,384]{1,0:T(8,128)S(1)}, f32[136,384]{1,0:T(8,128)S(1)}, u32[]{:S(2)}, u32[]{:S(2)}) collective-permute-start(f32[136,384]{1,0:T(8,128)S(1)} %get-tuple-element.70), channel_id=1, source_target_pairs={{0,4},{1,5},{2,6},{3,7},{4,0},{5,1},{6,2},{7,3},{8,12},{9,13},{10,... | collective-permute-start | bytes 626696 | tf_op jit(solution)/shard_map/ppermute | solution.py:31
  20.2 5.7 %collective-permute-start.3 = (f32[136,384]{1,0:T(8,128)S(1)}, f32[136,384]{1,0:T(8,128)S(1)}, u32[]{:S(2)}, u32[]{:S(2)}) collective-permute-start(f32[136,384]{1,0:T(8,128)S(1)} %get-tuple-element.69), channel_id=1, source_target_pairs={{0,6},{1,7},{2,4},{3,5},{4,2},{5,3},{6,0},{7,1},{8,14},{9,15},{10,... | collective-permute-start | bytes 626696 | tf_op jit(solution)/shard_map/ppermute | solution.py:31
  26.0 2.1 %collective-permute-done.2 = f32[136,384]{1,0:T(8,128)S(1)} collective-permute-done((f32[136,384]{1,0:T(8,128)S(1)}, f32[136,384]{1,0:T(8,128)S(1)}, u32[]{:S(2)}, u32[]{:S(2)}) %collective-permute-start.2) | collective-permute-done | bytes 208928 | tf_op jit(solution)/shard_map/ppermute | solution.py:31
  28.1 5.2 %collective-permute-done.3 = f32[136,384]{1,0:T(8,128)S(1)} collective-permute-done((f32[136,384]{1,0:T(8,128)S(1)}, f32[136,384]{1,0:T(8,128)S(1)}, u32[]{:S(2)}, u32[]{:S(2)}) %collective-permute-start.3) | collective-permute-done | bytes 208928 | tf_op jit(solution)/shard_map/ppermute | solution.py:31
  33.4 2.4 %collective-permute-start.4 = (f32[80,384]{1,0:T(8,128)S(1)}, f32[80,384]{1,0:T(8,128)S(1)}, u32[]{:S(2)}, u32[]{:S(2)}) collective-permute-start(f32[80,384]{1,0:T(8,128)S(1)} %dynamic-slice_bitcast_fusion.4), channel_id=1, source_target_pairs={{0,24},{1,25},{2,26},{3,27},{4,28},{5,29},{6,30},{7,31},{8,16},{9,... | collective-permute-start | bytes 368648 | tf_op jit(solution)/shard_map/ppermute | solution.py:31
  35.8 5.1 %collective-permute-done.4 = f32[80,384]{1,0:T(8,128)S(1)} collective-permute-done((f32[80,384]{1,0:T(8,128)S(1)}, f32[80,384]{1,0:T(8,128)S(1)}, u32[]{:S(2)}, u32[]{:S(2)}) %collective-permute-start.4) | collective-permute-done | bytes 122912 | tf_op jit(solution)/shard_map/ppermute | solution.py:31
  41.0 1.9 %collective-permute-start.5 = (f32[40,384]{1,0:T(8,128)S(1)}, f32[40,384]{1,0:T(8,128)S(1)}, u32[]{:S(2)}, u32[]{:S(2)}) collective-permute-start(f32[40,384]{1,0:T(8,128)S(1)} %dynamic-slice_bitcast_fusion.5), channel_id=1, source_target_pairs={{0,32},{1,33},{2,34},{3,35},{4,36},{5,37},{6,38},{7,39},{8,40},{9,... | collective-permute-start | bytes 184328 | tf_op jit(solution)/shard_map/ppermute | solution.py:31
  42.9 3.0 %collective-permute-done.5 = f32[40,384]{1,0:T(8,128)S(1)} collective-permute-done((f32[40,384]{1,0:T(8,128)S(1)}, f32[40,384]{1,0:T(8,128)S(1)}, u32[]{:S(2)}, u32[]{:S(2)}) %collective-permute-start.5) | collective-permute-done | bytes 61472 | tf_op jit(solution)/shard_map/ppermute | solution.py:31
  46.0 2.1 %collective-permute-start.6 = (f32[20,384]{1,0:T(8,128)S(1)}, f32[20,384]{1,0:T(8,128)S(1)}, u32[]{:S(2)}, u32[]{:S(2)}) collective-permute-start(f32[20,384]{1,0:T(8,128)S(1)} %dynamic-slice_bitcast_fusion.6), channel_id=1, source_target_pairs={{0,8},{1,9},{2,10},{3,11},{4,12},{5,13},{6,14},{7,15},{8,0},{9,1},... | collective-permute-start | bytes 92168 | tf_op jit(solution)/shard_map/ppermute | solution.py:31
  48.1 2.8 %collective-permute-done.6 = f32[20,384]{1,0:T(8,128)S(1)} collective-permute-done((f32[20,384]{1,0:T(8,128)S(1)}, f32[20,384]{1,0:T(8,128)S(1)}, u32[]{:S(2)}, u32[]{:S(2)}) %collective-permute-start.6) | collective-permute-done | bytes 30752 | tf_op jit(solution)/shard_map/ppermute | solution.py:31
  50.8 3.0 %collective-permute-start.7 = (f32[20,384]{1,0:T(8,128)S(1)}, f32[20,384]{1,0:T(8,128)S(1)}, u32[]{:S(2)}, u32[]{:S(2)}) collective-permute-start(f32[20,384]{1,0:T(8,128)S(1)} %bitcast_add_fusion.4), channel_id=1, source_target_pairs={{0,64},{1,65},{2,66},{3,67},{4,68},{5,69},{6,70},{7,71},{8,72},{9,... | collective-permute-start | bytes 92168 | tf_op jit(solution)/shard_map/ppermute | solution.py:31
  53.9 2.9 %collective-permute-done.7 = f32[20,384]{1,0:T(8,128)S(1)} collective-permute-done((f32[20,384]{1,0:T(8,128)S(1)}, f32[20,384]{1,0:T(8,128)S(1)}, u32[]{:S(2)}, u32[]{:S(2)}) %collective-permute-start.7) | collective-permute-done | bytes 30752 | tf_op jit(solution)/shard_map/ppermute | solution.py:31
  56.8 7.2 %collective-permute-start.8 = (f32[20,384]{1,0:T(8,128)S(1)}, f32[20,384]{1,0:T(8,128)S(1)}, u32[]{:S(2)}, u32[]{:S(2)}) collective-permute-start(f32[20,384]{1,0:T(8,128)S(1)} %add.186), channel_id=1, source_target_pairs={{0,128},{1,129},{2,130},{3,131},{4,132},{5,133},{6,134},{7,135},{8... | collective-permute-start | bytes 92168 | tf_op jit(solution)/shard_map/ppermute | solution.py:31
  64.0 1.3 collective-permute-done.8
  65.4 10.1 %collective-permute-start.9 = (f32[20,384]{1,0:T(8,128)S(1)}, f32[20,384]{1,0:T(8,128)S(1)}, u32[]{:S(2)}, u32[]{:S(2)}) collective-permute-start(f32[20,384]{1,0:T(8,128)S(1)} %add.187), channel_id=1, source_target_pairs={{0,384},{1,385},{2,386},{3,387},{4,388},{5,389},{6,390},{7,391},{8... | collective-permute-start | bytes 92168 | tf_op jit(solution)/shard_map/ppermute | solution.py:31
  75.5 1.3 collective-permute-done.9
  76.8 1.9 %collective-permute-start.10 = (f32[20,384]{1,0:T(8,128)S(1)}, f32[20,384]{1,0:T(8,128)S(1)}, u32[]{:S(2)}, u32[]{:S(2)}) collective-permute-start(f32[20,384]{1,0:T(8,128)S(1)} %add.188), channel_id=1, source_target_pairs={{0,8},{1,9},{2,10},{3,11},{4,12},{5,13},{6,14},{7,15},{8,0},{9,1},... | collective-permute-start | bytes 92168 | tf_op jit(solution)/shard_map/ppermute | solution.py:31
  78.9 2.9 %collective-permute-done.10 = f32[20,384]{1,0:T(8,128)S(1)} collective-permute-done((f32[20,384]{1,0:T(8,128)S(1)}, f32[20,384]{1,0:T(8,128)S(1)}, u32[]{:S(2)}, u32[]{:S(2)}) %collective-permute-start.10) | collective-permute-done | bytes 30752 | tf_op jit(solution)/shard_map/ppermute | solution.py:31
  81.8 2.6 %collective-permute-start.11 = (f32[40,384]{1,0:T(8,128)S(1)}, f32[40,384]{1,0:T(8,128)S(1)}, u32[]{:S(2)}, u32[]{:S(2)}) collective-permute-start(f32[40,384]{1,0:T(8,128)S(1)} %pad_maximum_fusion.3), channel_id=1, source_target_pairs={{0,32},{1,33},{2,34},{3,35},{4,36},{5,37},{6,38},{7,39},{8,40},{9,... | collective-permute-start | bytes 184328 | tf_op jit(solution)/shard_map/ppermute | solution.py:31
  84.5 2.3 %collective-permute-done.11 = f32[40,384]{1,0:T(8,128)S(1)} collective-permute-done((f32[40,384]{1,0:T(8,128)S(1)}, f32[40,384]{1,0:T(8,128)S(1)}, u32[]{:S(2)}, u32[]{:S(2)}) %collective-permute-start.11) | collective-permute-done | bytes 61472 | tf_op jit(solution)/shard_map/ppermute | solution.py:31
  86.9 4.4 %collective-permute-start.12 = (f32[80,384]{1,0:T(8,128)S(1)}, f32[80,384]{1,0:T(8,128)S(1)}, u32[]{:S(2)}, u32[]{:S(2)}) collective-permute-start(f32[80,384]{1,0:T(8,128)S(1)} %pad_maximum_fusion.1), channel_id=1, source_target_pairs={{0,24},{1,25},{2,26},{3,27},{4,28},{5,29},{6,30},{7,31},{8,16},{9,... | collective-permute-start | bytes 368648 | tf_op jit(solution)/shard_map/ppermute | solution.py:31
  91.4 2.3 %collective-permute-done.12 = f32[80,384]{1,0:T(8,128)S(1)} collective-permute-done((f32[80,384]{1,0:T(8,128)S(1)}, f32[80,384]{1,0:T(8,128)S(1)}, u32[]{:S(2)}, u32[]{:S(2)}) %collective-permute-start.12) | collective-permute-done | bytes 122912 | tf_op jit(solution)/shard_map/ppermute | solution.py:31
  93.7 0.1 slice_reduce_fusion
  93.9 0.7 multiply_add_fusion.2
  94.7 0.6 multiply_add_fusion.5
  95.5 0.5 multiply_add_fusion.7
  96.1 0.2 multiply_reduce_fusion
  96.2 21.7 %psum.7 = f32[8]{0:T(128)S(1)} all-reduce(f32[8]{0:T(128)S(1)} %multiply_reduce_fusion), channel_id=1, replica_groups=mesh['replica'=64,'shard'=8] {'shard'}, use_global_device_ids=true, to_apply=%region_1.2 | all-reduce | flops 8 | bytes 64 | tf_op jit(solution)/shard_map/psum | solution.py:153
  118.0 0.6 fusion.19
  119.3 0.1 reshape.108
  121.5 0.1 concatenate.33
  121.6 0.1 reshape.114
  121.8 15.2 %all-gather.1 = bf16[8,1,49280]{2,1,0:T(2,128)(2,1)S(1)} all-gather(bf16[1,1,49280]{2,1,0:T(2,128)(2,1)S(1)} %reshape.114), channel_id=2, replica_groups=mesh['replica'=64,'shard'=8] {'shard'}, dimensions={0}, use_global_device_ids=true | all-gather | bytes 887040 | tf_op jit(solution)/shard_map/all_gather | solution.py:163
  137.0 0.1 copy.45
  137.2 0.9 reshape.109
  138.1 0.9 reshape.110
  139.2 0.7 copy.39
  139.8 0.6 reshape.111
  140.5 0.6 pad_maximum_fusion.4
  (84 shorter events, 1.6 us)
Async XLA Ops:
  0.6 4.3 %copy-start.2 = (f32[1,512,384]{2,1,0:T(8,128)S(1)}, f32[1,512,384]{2,1,0:T(8,128)}, u32[]{:S(2)}) copy-start(f32[1,512,384]{2,1,0:T(8,128)} %param.16) | copy-start | bytes 2359300
  5.2 10.8 %collective-permute-start = (f32[4,136,384]{2,1,0:T(8,128)S(1)}, f32[4,136,384]{2,1,0:T(8,128)S(1)}, u32[]{:S(2)}, u32[]{:S(2)}) collective-permute-start(f32[4,136,384]{2,1,0:T(8,128)S(1)} %dynamic-slice_bitcast_fusion), channel_id=1, source_target_pairs={{0,1},{1,0},{2,3},{3,2},{4,5},{5,4},{6,7},{7,6},{8,9},{9,8},{10,11... | collective-permute-start | bytes 2506760 | tf_op jit(solution)/shard_map/ppermute | solution.py:31
  16.1 62.6 %copy-start.1 = (f32[64,384]{1,0:T(8,128)S(1)}, f32[64,384]{1,0:T(8,128)}, u32[]{:S(2)}) copy-start(f32[64,384]{1,0:T(8,128)} %param.20) | copy-start | bytes 294916
  16.1 9.9 %collective-permute-start.1 = (f32[136,384]{1,0:T(8,128)S(1)}, f32[136,384]{1,0:T(8,128)S(1)}, u32[]{:S(2)}, u32[]{:S(2)}) collective-permute-start(f32[136,384]{1,0:T(8,128)S(1)} %get-tuple-element.68), channel_id=1, source_target_pairs={{0,2},{1,3},{2,0},{3,1},{4,6},{5,7},{6,4},{7,5},{8,10},{9,11},{10,... | collective-permute-start | bytes 626696 | tf_op jit(solution)/shard_map/ppermute | solution.py:31
  18.2 60.7 %copy-start = (f32[48,512]{1,0:T(8,128)S(1)}, f32[48,512]{1,0:T(8,128)}, u32[]{:S(2)}) copy-start(f32[48,512]{1,0:T(8,128)} %param.21) | copy-start | bytes 294916
  18.2 9.9 %collective-permute-start.2 = (f32[136,384]{1,0:T(8,128)S(1)}, f32[136,384]{1,0:T(8,128)S(1)}, u32[]{:S(2)}, u32[]{:S(2)}) collective-permute-start(f32[136,384]{1,0:T(8,128)S(1)} %get-tuple-element.70), channel_id=1, source_target_pairs={{0,4},{1,5},{2,6},{3,7},{4,0},{5,1},{6,2},{7,3},{8,12},{9,13},{10,... | collective-permute-start | bytes 626696 | tf_op jit(solution)/shard_map/ppermute | solution.py:31
  20.2 13.0 %collective-permute-start.3 = (f32[136,384]{1,0:T(8,128)S(1)}, f32[136,384]{1,0:T(8,128)S(1)}, u32[]{:S(2)}, u32[]{:S(2)}) collective-permute-start(f32[136,384]{1,0:T(8,128)S(1)} %get-tuple-element.69), channel_id=1, source_target_pairs={{0,6},{1,7},{2,4},{3,5},{4,2},{5,3},{6,0},{7,1},{8,14},{9,15},{10,... | collective-permute-start | bytes 626696 | tf_op jit(solution)/shard_map/ppermute | solution.py:31
  33.3 57.9 %copy-start.11 = (f32[64]{0:T(128)S(1)}, f32[64]{0:T(128)}, u32[]{:S(2)}) copy-start(f32[64]{0:T(128)} %param.22) | copy-start | bytes 772
  33.3 57.9 %copy-start.9 = (f32[4,6]{1,0:T(4,128)S(1)}, f32[4,6]{1,0:T(4,128)}, u32[]{:S(2)}) copy-start(f32[4,6]{1,0:T(4,128)} %param.23) | copy-start | bytes 292
  33.4 7.5 %collective-permute-start.4 = (f32[80,384]{1,0:T(8,128)S(1)}, f32[80,384]{1,0:T(8,128)S(1)}, u32[]{:S(2)}, u32[]{:S(2)}) collective-permute-start(f32[80,384]{1,0:T(8,128)S(1)} %dynamic-slice_bitcast_fusion.4), channel_id=1, source_target_pairs={{0,24},{1,25},{2,26},{3,27},{4,28},{5,29},{6,30},{7,31},{8,16},{9,... | collective-permute-start | bytes 368648 | tf_op jit(solution)/shard_map/ppermute | solution.py:31
  41.0 5.0 %collective-permute-start.5 = (f32[40,384]{1,0:T(8,128)S(1)}, f32[40,384]{1,0:T(8,128)S(1)}, u32[]{:S(2)}, u32[]{:S(2)}) collective-permute-start(f32[40,384]{1,0:T(8,128)S(1)} %dynamic-slice_bitcast_fusion.5), channel_id=1, source_target_pairs={{0,32},{1,33},{2,34},{3,35},{4,36},{5,37},{6,38},{7,39},{8,40},{9,... | collective-permute-start | bytes 184328 | tf_op jit(solution)/shard_map/ppermute | solution.py:31
  45.9 47.9 %copy-start.5 = (f32[48,512]{1,0:T(8,128)S(1)}, f32[48,512]{1,0:T(8,128)}, u32[]{:S(2)}) copy-start(f32[48,512]{1,0:T(8,128)} %param.29) | copy-start | bytes 294916
  45.9 47.9 %copy-start.6 = (f32[48,512]{1,0:T(8,128)S(1)}, f32[48,512]{1,0:T(8,128)}, u32[]{:S(2)}) copy-start(f32[48,512]{1,0:T(8,128)} %param.25) | copy-start | bytes 294916
  46.0 4.8 %collective-permute-start.6 = (f32[20,384]{1,0:T(8,128)S(1)}, f32[20,384]{1,0:T(8,128)S(1)}, u32[]{:S(2)}, u32[]{:S(2)}) collective-permute-start(f32[20,384]{1,0:T(8,128)S(1)} %dynamic-slice_bitcast_fusion.6), channel_id=1, source_target_pairs={{0,8},{1,9},{2,10},{3,11},{4,12},{5,13},{6,14},{7,15},{8,0},{9,1},... | collective-permute-start | bytes 92168 | tf_op jit(solution)/shard_map/ppermute | solution.py:31
  50.8 6.0 %collective-permute-start.7 = (f32[20,384]{1,0:T(8,128)S(1)}, f32[20,384]{1,0:T(8,128)S(1)}, u32[]{:S(2)}, u32[]{:S(2)}) collective-permute-start(f32[20,384]{1,0:T(8,128)S(1)} %bitcast_add_fusion.4), channel_id=1, source_target_pairs={{0,64},{1,65},{2,66},{3,67},{4,68},{5,69},{6,70},{7,71},{8,72},{9,... | collective-permute-start | bytes 92168 | tf_op jit(solution)/shard_map/ppermute | solution.py:31
  56.8 8.6 %collective-permute-start.8 = (f32[20,384]{1,0:T(8,128)S(1)}, f32[20,384]{1,0:T(8,128)S(1)}, u32[]{:S(2)}, u32[]{:S(2)}) collective-permute-start(f32[20,384]{1,0:T(8,128)S(1)} %add.186), channel_id=1, source_target_pairs={{0,128},{1,129},{2,130},{3,131},{4,132},{5,133},{6,134},{7,135},{8... | collective-permute-start | bytes 92168 | tf_op jit(solution)/shard_map/ppermute | solution.py:31
  65.4 11.4 %collective-permute-start.9 = (f32[20,384]{1,0:T(8,128)S(1)}, f32[20,384]{1,0:T(8,128)S(1)}, u32[]{:S(2)}, u32[]{:S(2)}) collective-permute-start(f32[20,384]{1,0:T(8,128)S(1)} %add.187), channel_id=1, source_target_pairs={{0,384},{1,385},{2,386},{3,387},{4,388},{5,389},{6,390},{7,391},{8... | collective-permute-start | bytes 92168 | tf_op jit(solution)/shard_map/ppermute | solution.py:31
  76.8 5.0 %collective-permute-start.10 = (f32[20,384]{1,0:T(8,128)S(1)}, f32[20,384]{1,0:T(8,128)S(1)}, u32[]{:S(2)}, u32[]{:S(2)}) collective-permute-start(f32[20,384]{1,0:T(8,128)S(1)} %add.188), channel_id=1, source_target_pairs={{0,8},{1,9},{2,10},{3,11},{4,12},{5,13},{6,14},{7,15},{8,0},{9,1},... | collective-permute-start | bytes 92168 | tf_op jit(solution)/shard_map/ppermute | solution.py:31
  78.8 15.9 %copy-start.12 = (f32[4,6]{1,0:T(4,128)S(1)}, f32[4,6]{1,0:T(4,128)}, u32[]{:S(2)}) copy-start(f32[4,6]{1,0:T(4,128)} %param.31) | copy-start | bytes 292
  78.8 15.9 %copy-start.13 = (f32[4,6]{1,0:T(4,128)S(1)}, f32[4,6]{1,0:T(4,128)}, u32[]{:S(2)}) copy-start(f32[4,6]{1,0:T(4,128)} %param.27) | copy-start | bytes 292
  78.8 16.6 %copy-start.7 = (f32[64,384]{1,0:T(8,128)S(1)}, f32[64,384]{1,0:T(8,128)}, u32[]{:S(2)}) copy-start(f32[64,384]{1,0:T(8,128)} %param.28) | copy-start | bytes 294916
  78.8 16.6 %copy-start.8 = (f32[64,384]{1,0:T(8,128)S(1)}, f32[64,384]{1,0:T(8,128)}, u32[]{:S(2)}) copy-start(f32[64,384]{1,0:T(8,128)} %param.24) | copy-start | bytes 294916
  81.8 5.0 %collective-permute-start.11 = (f32[40,384]{1,0:T(8,128)S(1)}, f32[40,384]{1,0:T(8,128)S(1)}, u32[]{:S(2)}, u32[]{:S(2)}) collective-permute-start(f32[40,384]{1,0:T(8,128)S(1)} %pad_maximum_fusion.3), channel_id=1, source_target_pairs={{0,32},{1,33},{2,34},{3,35},{4,36},{5,37},{6,38},{7,39},{8,40},{9,... | collective-permute-start | bytes 184328 | tf_op jit(solution)/shard_map/ppermute | solution.py:31
  86.8 8.7 %copy-start.14 = (f32[64]{0:T(128)S(1)}, f32[64]{0:T(128)}, u32[]{:S(2)}) copy-start(f32[64]{0:T(128)} %param.30) | copy-start | bytes 772
  86.8 8.7 %copy-start.15 = (f32[64]{0:T(128)S(1)}, f32[64]{0:T(128)}, u32[]{:S(2)}) copy-start(f32[64]{0:T(128)} %param.26) | copy-start | bytes 772
  86.9 6.8 %collective-permute-start.12 = (f32[80,384]{1,0:T(8,128)S(1)}, f32[80,384]{1,0:T(8,128)S(1)}, u32[]{:S(2)}, u32[]{:S(2)}) collective-permute-start(f32[80,384]{1,0:T(8,128)S(1)} %pad_maximum_fusion.1), channel_id=1, source_target_pairs={{0,24},{1,25},{2,26},{3,27},{4,28},{5,29},{6,30},{7,31},{8,16},{9,... | collective-permute-start | bytes 368648 | tf_op jit(solution)/shard_map/ppermute | solution.py:31
  95.5 41.5 %copy-start.3 = (f32[64,384]{1,0:T(8,128)}, f32[64,384]{1,0:T(8,128)S(1)}, u32[]{:S(2)}) copy-start(f32[64,384]{1,0:T(8,128)S(1)} %get-tuple-element.66) | copy-start | bytes 294916
  95.5 41.5 %copy-start.4 = (f32[64,384]{1,0:T(8,128)}, f32[64,384]{1,0:T(8,128)S(1)}, u32[]{:S(2)}) copy-start(f32[64,384]{1,0:T(8,128)S(1)} %get-tuple-element.67) | copy-start | bytes 294916
  118.0 19.1 %copy-start.10 = (f32[4]{0:T(128)}, f32[4]{0:T(128)S(1)}, u32[]{:S(2)}) copy-start(f32[4]{0:T(128)S(1)} %get-tuple-element.81) | copy-start | bytes 52

commit v10 on v6

--- a/solution.py
+++ b/solution.py
@@ -154,18 +154,27 @@
     weight_sizes = jnp.sqrt(squares[:4])
     update_sizes = jnp.sqrt(squares[4:])
     trust_ratios = weight_sizes / (update_sizes + 1e-06)
-    shards_out = [
-        (weights[member] - 0.01 * trust_ratios[member] * results[member][2]).astype(jnp.bfloat16).reshape(-1)
+    updated = [
+        (weights[member] - 0.01 * trust_ratios[member] * results[member][2]).astype(jnp.bfloat16)
         for member in range(4)
     ]
-    out_width = padded_width(total, LANES)
-    shards_out.append(jnp.zeros((out_width - total,), jnp.bfloat16))
-    gathered = lax.all_gather(jnp.concatenate(shards_out), "shard", axis=0, tiled=False)
+    rest = jnp.concatenate([updated[2].reshape(-1), updated[3].reshape(-1)])
+    rest = jnp.pad(rest, (0, lanes - rest.shape[0])).reshape(1, lanes)
+    payload = jnp.concatenate([updated[0], updated[1].reshape(-1, lanes), rest], axis=0)
+    gather_rows = padded_width(payload.shape[0], 2 * ROW_TILE)
+    payload = jnp.pad(payload, ((0, gather_rows - payload.shape[0]), (0, 0)))
+    gathered = lax.all_gather(payload, "shard", axis=0, tiled=False)
+    gathered_rest = gathered[:, query_rows + output_rows]
+    norm_size = weight_norm.size
     full = [
-        gathered[:, offsets[member] : offsets[member] + sizes[member]].reshape(
-            (shards * weights[member].shape[0],) + weights[member].shape[1:]
-        )
-        for member in range(4)
+        gathered[:, :query_rows].reshape(-1, lanes),
+        gathered[:, query_rows : query_rows + output_rows]
+        .reshape((shards,) + weight_output.shape)
+        .reshape((-1,) + weight_output.shape[1:]),
+        gathered_rest[:, :norm_size].reshape(-1),
+        gathered_rest[:, norm_size : norm_size + weight_bias.size]
+        .reshape((shards,) + weight_bias.shape)
+        .reshape((-1,) + weight_bias.shape[1:]),
     ]
     norm_table = jnp.stack([weight_sizes, update_sizes])
     return (

time: 138 us -> 137 us (level)
    reshape x6 -> x4, local copies, waits for them, and re-layouts: 2.69 us -> 0.79 us  [the longest x1 0.64 us: on_device(): gathered_rest[:, :norm_size].reshape(-1)]
where the time goes in v10:
time: 137 us; the launch traced here: 136 us
  starting transfers between devices  52.2 us (38%)
  waiting for transfers between devices  33.7 us (25%)
  blocking collectives  33.7 us (25%)
  local copies, waits for them, and re-layouts  7.77 us (6%)
  other arithmetic  4.72 us (3%)
  between operations  3.8 us (3%)
    ppermute x12, starting transfers between devices, exchange(): return lax.ppermute(value, AXES, [(d, d ^ mask) for d in range(devices)])  52.2 us
    ppermute x12, waiting for transfers between devices, exchange(): return lax.ppermute(value, AXES, [(d, d ^ mask) for d in range(devices)])  33.7 us
    psum x1, blocking collectives, on_device(): squares = lax.psum(jnp.sum(stacked * stacked, axis=(1, 2)), 'shard')  19.7 us
    all_gather x1, blocking collectives, on_device(): gathered = lax.all_gather(payload, 'shard', axis=0, tiled=False)  14.1 us
  transfers between devices with their start and end apart: 12, of which 11 were waited for; matrix products, arithmetic and copies ran while one was open for 0% of the time, Pallas kernels for 0%

profile of v10, /device:TPU:1, one launch (start us, length us, event | category | flops | bytes accessed | tf_op | source)
XLA Modules:
  0.0 135.9 jit_solution(5275749954850225047)
XLA Ops:
  0.7 1.4 %concatenate.26 = f32[4,2,64,384]{3,2,1,0:T(8,128)S(1)} reshape(f32[1,384,512]{2,1,0:T(8,128)} %param.17) | data formatting | bytes 1572864 | tf_op jit(solution)/shard_map/concatenate | solution.py:124
  2.1 0.8 copy.31
  2.9 0.5 broadcast.91
  3.4 1.3 reduce.7
  4.8 0.1 reshape_squeeze.8
  5.0 0.1 pad_maximum_fusion
  5.2 8.8 %collective-permute-start = (f32[4,136,384]{2,1,0:T(8,128)S(1)}, f32[4,136,384]{2,1,0:T(8,128)S(1)}, u32[]{:S(2)}, u32[]{:S(2)}) collective-permute-start(f32[4,136,384]{2,1,0:T(8,128)S(1)} %dynamic-slice_bitcast_fusion), channel_id=1, source_target_pairs={{0,1},{1,0},{2,3},{3,2},{4,5},{5,4},{6,7},{7,6},{8,9},{9,8},{10,11... | collective-permute-start | bytes 2506760 | tf_op jit(solution)/shard_map/ppermute | solution.py:31
  14.0 1.9 %collective-permute-done = f32[4,136,384]{2,1,0:T(8,128)S(1)} collective-permute-done((f32[4,136,384]{2,1,0:T(8,128)S(1)}, f32[4,136,384]{2,1,0:T(8,128)S(1)}, u32[]{:S(2)}, u32[]{:S(2)}) %collective-permute-start) | collective-permute-done | bytes 835616 | tf_op jit(solution)/shard_map/ppermute | solution.py:31
  15.9 0.1 bitcast_add_fusion
  16.1 2.1 %collective-permute-start.1 = (f32[136,384]{1,0:T(8,128)S(1)}, f32[136,384]{1,0:T(8,128)S(1)}, u32[]{:S(2)}, u32[]{:S(2)}) collective-permute-start(f32[136,384]{1,0:T(8,128)S(1)} %get-tuple-element.42), channel_id=1, source_target_pairs={{0,2},{1,3},{2,0},{3,1},{4,6},{5,7},{6,4},{7,5},{8,10},{9,11},{10,... | collective-permute-start | bytes 626696 | tf_op jit(solution)/shard_map/ppermute | solution.py:31
  18.2 1.9 %collective-permute-start.2 = (f32[136,384]{1,0:T(8,128)S(1)}, f32[136,384]{1,0:T(8,128)S(1)}, u32[]{:S(2)}, u32[]{:S(2)}) collective-permute-start(f32[136,384]{1,0:T(8,128)S(1)} %get-tuple-element.44), channel_id=1, source_target_pairs={{0,4},{1,5},{2,6},{3,7},{4,0},{5,1},{6,2},{7,3},{8,12},{9,13},{10,... | collective-permute-start | bytes 626696 | tf_op jit(solution)/shard_map/ppermute | solution.py:31
  20.1 5.7 %collective-permute-start.3 = (f32[136,384]{1,0:T(8,128)S(1)}, f32[136,384]{1,0:T(8,128)S(1)}, u32[]{:S(2)}, u32[]{:S(2)}) collective-permute-start(f32[136,384]{1,0:T(8,128)S(1)} %get-tuple-element.43), channel_id=1, source_target_pairs={{0,6},{1,7},{2,4},{3,5},{4,2},{5,3},{6,0},{7,1},{8,14},{9,15},{10,... | collective-permute-start | bytes 626696 | tf_op jit(solution)/shard_map/ppermute | solution.py:31
  25.9 2.1 %collective-permute-done.2 = f32[136,384]{1,0:T(8,128)S(1)} collective-permute-done((f32[136,384]{1,0:T(8,128)S(1)}, f32[136,384]{1,0:T(8,128)S(1)}, u32[]{:S(2)}, u32[]{:S(2)}) %collective-permute-start.2) | collective-permute-done | bytes 208928 | tf_op jit(solution)/shard_map/ppermute | solution.py:31
  28.0 5.2 %collective-permute-done.3 = f32[136,384]{1,0:T(8,128)S(1)} collective-permute-done((f32[136,384]{1,0:T(8,128)S(1)}, f32[136,384]{1,0:T(8,128)S(1)}, u32[]{:S(2)}, u32[]{:S(2)}) %collective-permute-start.3) | collective-permute-done | bytes 208928 | tf_op jit(solution)/shard_map/ppermute | solution.py:31
  33.3 2.5 %collective-permute-start.4 = (f32[80,384]{1,0:T(8,128)S(1)}, f32[80,384]{1,0:T(8,128)S(1)}, u32[]{:S(2)}, u32[]{:S(2)}) collective-permute-start(f32[80,384]{1,0:T(8,128)S(1)} %dynamic-slice_bitcast_fusion.4), channel_id=1, source_target_pairs={{0,24},{1,25},{2,26},{3,27},{4,28},{5,29},{6,30},{7,31},{8,16},{9,... | collective-permute-start | bytes 368648 | tf_op jit(solution)/shard_map/ppermute | solution.py:31
  35.8 5.0 %collective-permute-done.4 = f32[80,384]{1,0:T(8,128)S(1)} collective-permute-done((f32[80,384]{1,0:T(8,128)S(1)}, f32[80,384]{1,0:T(8,128)S(1)}, u32[]{:S(2)}, u32[]{:S(2)}) %collective-permute-start.4) | collective-permute-done | bytes 122912 | tf_op jit(solution)/shard_map/ppermute | solution.py:31
  40.9 2.1 %collective-permute-start.5 = (f32[40,384]{1,0:T(8,128)S(1)}, f32[40,384]{1,0:T(8,128)S(1)}, u32[]{:S(2)}, u32[]{:S(2)}) collective-permute-start(f32[40,384]{1,0:T(8,128)S(1)} %dynamic-slice_bitcast_fusion.5), channel_id=1, source_target_pairs={{0,32},{1,33},{2,34},{3,35},{4,36},{5,37},{6,38},{7,39},{8,40},{9,... | collective-permute-start | bytes 184328 | tf_op jit(solution)/shard_map/ppermute | solution.py:31
  42.9 3.0 %collective-permute-done.5 = f32[40,384]{1,0:T(8,128)S(1)} collective-permute-done((f32[40,384]{1,0:T(8,128)S(1)}, f32[40,384]{1,0:T(8,128)S(1)}, u32[]{:S(2)}, u32[]{:S(2)}) %collective-permute-start.5) | collective-permute-done | bytes 61472 | tf_op jit(solution)/shard_map/ppermute | solution.py:31
  46.0 1.9 %collective-permute-start.6 = (f32[40,384]{1,0:T(8,128)S(1)}, f32[40,384]{1,0:T(8,128)S(1)}, u32[]{:S(2)}, u32[]{:S(2)}) collective-permute-start(f32[40,384]{1,0:T(8,128)S(1)} %bitcast_add_fusion.3), channel_id=1, source_target_pairs={{0,8},{1,9},{2,10},{3,11},{4,12},{5,13},{6,14},{7,15},{8,0},{9,1},... | collective-permute-start | bytes 184328 | tf_op jit(solution)/shard_map/ppermute | solution.py:31
  47.9 3.0 %collective-permute-done.6 = f32[40,384]{1,0:T(8,128)S(1)} collective-permute-done((f32[40,384]{1,0:T(8,128)S(1)}, f32[40,384]{1,0:T(8,128)S(1)}, u32[]{:S(2)}, u32[]{:S(2)}) %collective-permute-start.6) | collective-permute-done | bytes 61472 | tf_op jit(solution)/shard_map/ppermute | solution.py:31
  51.0 3.2 %collective-permute-start.7 = (f32[40,384]{1,0:T(8,128)S(1)}, f32[40,384]{1,0:T(8,128)S(1)}, u32[]{:S(2)}, u32[]{:S(2)}) collective-permute-start(f32[40,384]{1,0:T(8,128)S(1)} %add.179), channel_id=1, source_target_pairs={{0,64},{1,65},{2,66},{3,67},{4,68},{5,69},{6,70},{7,71},{8,72},{9,... | collective-permute-start | bytes 184328 | tf_op jit(solution)/shard_map/ppermute | solution.py:31
  54.1 3.3 %collective-permute-done.7 = f32[40,384]{1,0:T(8,128)S(1)} collective-permute-done((f32[40,384]{1,0:T(8,128)S(1)}, f32[40,384]{1,0:T(8,128)S(1)}, u32[]{:S(2)}, u32[]{:S(2)}) %collective-permute-start.7) | collective-permute-done | bytes 61472 | tf_op jit(solution)/shard_map/ppermute | solution.py:31
  57.5 7.1 %collective-permute-start.8 = (f32[40,384]{1,0:T(8,128)S(1)}, f32[40,384]{1,0:T(8,128)S(1)}, u32[]{:S(2)}, u32[]{:S(2)}) collective-permute-start(f32[40,384]{1,0:T(8,128)S(1)} %add.180), channel_id=1, source_target_pairs={{0,128},{1,129},{2,130},{3,131},{4,132},{5,133},{6,134},{7,135},{8... | collective-permute-start | bytes 184328 | tf_op jit(solution)/shard_map/ppermute | solution.py:31
  64.6 1.8 %collective-permute-done.8 = f32[40,384]{1,0:T(8,128)S(1)} collective-permute-done((f32[40,384]{1,0:T(8,128)S(1)}, f32[40,384]{1,0:T(8,128)S(1)}, u32[]{:S(2)}, u32[]{:S(2)}) %collective-permute-start.8) | collective-permute-done | bytes 61472 | tf_op jit(solution)/shard_map/ppermute | solution.py:31
  66.4 10.7 %collective-permute-start.9 = (f32[40,384]{1,0:T(8,128)S(1)}, f32[40,384]{1,0:T(8,128)S(1)}, u32[]{:S(2)}, u32[]{:S(2)}) collective-permute-start(f32[40,384]{1,0:T(8,128)S(1)} %add.181), channel_id=1, source_target_pairs={{0,384},{1,385},{2,386},{3,387},{4,388},{5,389},{6,390},{7,391},{8... | collective-permute-start | bytes 184328 | tf_op jit(solution)/shard_map/ppermute | solution.py:31
  77.2 2.8 %collective-permute-done.9 = f32[40,384]{1,0:T(8,128)S(1)} collective-permute-done((f32[40,384]{1,0:T(8,128)S(1)}, f32[40,384]{1,0:T(8,128)S(1)}, u32[]{:S(2)}, u32[]{:S(2)}) %collective-permute-start.9) | collective-permute-done | bytes 61472 | tf_op jit(solution)/shard_map/ppermute | solution.py:31
  80.0 1.9 %collective-permute-start.10 = (f32[40,384]{1,0:T(8,128)S(1)}, f32[40,384]{1,0:T(8,128)S(1)}, u32[]{:S(2)}, u32[]{:S(2)}) collective-permute-start(f32[40,384]{1,0:T(8,128)S(1)} %add.182), channel_id=1, source_target_pairs={{0,32},{1,33},{2,34},{3,35},{4,36},{5,37},{6,38},{7,39},{8,40},{9,... | collective-permute-start | bytes 184328 | tf_op jit(solution)/shard_map/ppermute | solution.py:31
  81.9 3.2 %collective-permute-done.10 = f32[40,384]{1,0:T(8,128)S(1)} collective-permute-done((f32[40,384]{1,0:T(8,128)S(1)}, f32[40,384]{1,0:T(8,128)S(1)}, u32[]{:S(2)}, u32[]{:S(2)}) %collective-permute-start.10) | collective-permute-done | bytes 61472 | tf_op jit(solution)/shard_map/ppermute | solution.py:31
  85.2 4.4 %collective-permute-start.11 = (f32[80,384]{1,0:T(8,128)S(1)}, f32[80,384]{1,0:T(8,128)S(1)}, u32[]{:S(2)}, u32[]{:S(2)}) collective-permute-start(f32[80,384]{1,0:T(8,128)S(1)} %pad_maximum_fusion.1), channel_id=1, source_target_pairs={{0,24},{1,25},{2,26},{3,27},{4,28},{5,29},{6,30},{7,31},{8,16},{9,... | collective-permute-start | bytes 368648 | tf_op jit(solution)/shard_map/ppermute | solution.py:31
  89.6 0.1 reshape.88
  89.7 2.3 %collective-permute-done.11 = f32[80,384]{1,0:T(8,128)S(1)} collective-permute-done((f32[80,384]{1,0:T(8,128)S(1)}, f32[80,384]{1,0:T(8,128)S(1)}, u32[]{:S(2)}, u32[]{:S(2)}) %collective-permute-start.11) | collective-permute-done | bytes 122912 | tf_op jit(solution)/shard_map/ppermute | solution.py:31
  92.0 0.1 slice_reduce_fusion
  92.2 0.7 multiply_add_fusion.2
  92.9 0.1 reshape.94
  93.0 0.6 multiply_add_fusion.5
  93.6 0.1 reshape.95
  93.8 0.5 multiply_add_fusion.7
  94.4 0.2 multiply_reduce_fusion
  94.6 19.7 %psum.7 = f32[8]{0:T(128)S(1)} all-reduce(f32[8]{0:T(128)S(1)} %multiply_reduce_fusion), channel_id=1, replica_groups=mesh['replica'=64,'shard'=8] {'shard'}, use_global_device_ids=true, to_apply=%region_1.2 | all-reduce | flops 8 | bytes 64 | tf_op jit(solution)/shard_map/psum | solution.py:153
  114.3 0.6 fusion.26
  117.6 0.1 reshape.97
  117.7 0.1 fusion.17
  117.9 14.1 %all-gather = bf16[1152,384]{1,0:T(8,128)(2,1)S(1)} all-gather(bf16[144,384]{1,0:T(8,128)(2,1)S(1)} %fusion.6), channel_id=2, replica_groups=mesh['replica'=64,'shard'=8] {'shard'}, dimensions={0}, use_global_device_ids=true | all-gather | bytes 995328 | tf_op jit(solution)/shard_map/all_gather | solution.py:166
  131.9 0.9 fusion.25
  132.9 1.1 reshape_reshape.6
  134.0 0.7 copy.34
  134.7 0.6 reshape.100
  135.3 0.6 pad_maximum_fusion.3
  (77 shorter events, 1.3 us)
Async XLA Ops:
  0.6 4.3 %copy-start.2 = (f32[1,512,384]{2,1,0:T(8,128)S(1)}, f32[1,512,384]{2,1,0:T(8,128)}, u32[]{:S(2)}) copy-start(f32[1,512,384]{2,1,0:T(8,128)} %param.16) | copy-start | bytes 2359300
  5.2 10.8 %collective-permute-start = (f32[4,136,384]{2,1,0:T(8,128)S(1)}, f32[4,136,384]{2,1,0:T(8,128)S(1)}, u32[]{:S(2)}, u32[]{:S(2)}) collective-permute-start(f32[4,136,384]{2,1,0:T(8,128)S(1)} %dynamic-slice_bitcast_fusion), channel_id=1, source_target_pairs={{0,1},{1,0},{2,3},{3,2},{4,5},{5,4},{6,7},{7,6},{8,9},{9,8},{10,11... | collective-permute-start | bytes 2506760 | tf_op jit(solution)/shard_map/ppermute | solution.py:31
  16.1 61.0 %copy-start.1 = (f32[64,384]{1,0:T(8,128)S(1)}, f32[64,384]{1,0:T(8,128)}, u32[]{:S(2)}) copy-start(f32[64,384]{1,0:T(8,128)} %param.20) | copy-start | bytes 294916
  16.1 61.0 %copy-start = (f32[48,512]{1,0:T(8,128)S(1)}, f32[48,512]{1,0:T(8,128)}, u32[]{:S(2)}) copy-start(f32[48,512]{1,0:T(8,128)} %param.21) | copy-start | bytes 294916
  16.1 9.7 %collective-permute-start.1 = (f32[136,384]{1,0:T(8,128)S(1)}, f32[136,384]{1,0:T(8,128)S(1)}, u32[]{:S(2)}, u32[]{:S(2)}) collective-permute-start(f32[136,384]{1,0:T(8,128)S(1)} %get-tuple-element.42), channel_id=1, source_target_pairs={{0,2},{1,3},{2,0},{3,1},{4,6},{5,7},{6,4},{7,5},{8,10},{9,11},{10,... | collective-permute-start | bytes 626696 | tf_op jit(solution)/shard_map/ppermute | solution.py:31
  18.2 9.8 %collective-permute-start.2 = (f32[136,384]{1,0:T(8,128)S(1)}, f32[136,384]{1,0:T(8,128)S(1)}, u32[]{:S(2)}, u32[]{:S(2)}) collective-permute-start(f32[136,384]{1,0:T(8,128)S(1)} %get-tuple-element.44), channel_id=1, source_target_pairs={{0,4},{1,5},{2,6},{3,7},{4,0},{5,1},{6,2},{7,3},{8,12},{9,13},{10,... | collective-permute-start | bytes 626696 | tf_op jit(solution)/shard_map/ppermute | solution.py:31
  20.1 13.1 %collective-permute-start.3 = (f32[136,384]{1,0:T(8,128)S(1)}, f32[136,384]{1,0:T(8,128)S(1)}, u32[]{:S(2)}, u32[]{:S(2)}) collective-permute-start(f32[136,384]{1,0:T(8,128)S(1)} %get-tuple-element.43), channel_id=1, source_target_pairs={{0,6},{1,7},{2,4},{3,5},{4,2},{5,3},{6,0},{7,1},{8,14},{9,15},{10,... | collective-permute-start | bytes 626696 | tf_op jit(solution)/shard_map/ppermute | solution.py:31
  33.2 56.4 %copy-start.11 = (f32[64]{0:T(128)S(1)}, f32[64]{0:T(128)}, u32[]{:S(2)}) copy-start(f32[64]{0:T(128)} %param.22) | copy-start | bytes 772
  33.2 56.4 %copy-start.9 = (f32[4,6]{1,0:T(4,128)S(1)}, f32[4,6]{1,0:T(4,128)}, u32[]{:S(2)}) copy-start(f32[4,6]{1,0:T(4,128)} %param.23) | copy-start | bytes 292
  33.3 7.5 %collective-permute-start.4 = (f32[80,384]{1,0:T(8,128)S(1)}, f32[80,384]{1,0:T(8,128)S(1)}, u32[]{:S(2)}, u32[]{:S(2)}) collective-permute-start(f32[80,384]{1,0:T(8,128)S(1)} %dynamic-slice_bitcast_fusion.4), channel_id=1, source_target_pairs={{0,24},{1,25},{2,26},{3,27},{4,28},{5,29},{6,30},{7,31},{8,16},{9,... | collective-permute-start | bytes 368648 | tf_op jit(solution)/shard_map/ppermute | solution.py:31
  40.8 51.3 %copy-start.5 = (f32[48,512]{1,0:T(8,128)S(1)}, f32[48,512]{1,0:T(8,128)}, u32[]{:S(2)}) copy-start(f32[48,512]{1,0:T(8,128)} %param.29) | copy-start | bytes 294916
  40.8 51.3 %copy-start.6 = (f32[48,512]{1,0:T(8,128)S(1)}, f32[48,512]{1,0:T(8,128)}, u32[]{:S(2)}) copy-start(f32[48,512]{1,0:T(8,128)} %param.25) | copy-start | bytes 294916
  40.9 5.1 %collective-permute-start.5 = (f32[40,384]{1,0:T(8,128)S(1)}, f32[40,384]{1,0:T(8,128)S(1)}, u32[]{:S(2)}, u32[]{:S(2)}) collective-permute-start(f32[40,384]{1,0:T(8,128)S(1)} %dynamic-slice_bitcast_fusion.5), channel_id=1, source_target_pairs={{0,32},{1,33},{2,34},{3,35},{4,36},{5,37},{6,38},{7,39},{8,40},{9,... | collective-permute-start | bytes 184328 | tf_op jit(solution)/shard_map/ppermute | solution.py:31
  46.0 5.0 %collective-permute-start.6 = (f32[40,384]{1,0:T(8,128)S(1)}, f32[40,384]{1,0:T(8,128)S(1)}, u32[]{:S(2)}, u32[]{:S(2)}) collective-permute-start(f32[40,384]{1,0:T(8,128)S(1)} %bitcast_add_fusion.3), channel_id=1, source_target_pairs={{0,8},{1,9},{2,10},{3,11},{4,12},{5,13},{6,14},{7,15},{8,0},{9,1},... | collective-permute-start | bytes 184328 | tf_op jit(solution)/shard_map/ppermute | solution.py:31
  51.0 6.5 %collective-permute-start.7 = (f32[40,384]{1,0:T(8,128)S(1)}, f32[40,384]{1,0:T(8,128)S(1)}, u32[]{:S(2)}, u32[]{:S(2)}) collective-permute-start(f32[40,384]{1,0:T(8,128)S(1)} %add.179), channel_id=1, source_target_pairs={{0,64},{1,65},{2,66},{3,67},{4,68},{5,69},{6,70},{7,71},{8,72},{9,... | collective-permute-start | bytes 184328 | tf_op jit(solution)/shard_map/ppermute | solution.py:31
  57.5 8.9 %collective-permute-start.8 = (f32[40,384]{1,0:T(8,128)S(1)}, f32[40,384]{1,0:T(8,128)S(1)}, u32[]{:S(2)}, u32[]{:S(2)}) collective-permute-start(f32[40,384]{1,0:T(8,128)S(1)} %add.180), channel_id=1, source_target_pairs={{0,128},{1,129},{2,130},{3,131},{4,132},{5,133},{6,134},{7,135},{8... | collective-permute-start | bytes 184328 | tf_op jit(solution)/shard_map/ppermute | solution.py:31
  66.4 26.6 %copy-start.12 = (f32[4,6]{1,0:T(4,128)S(1)}, f32[4,6]{1,0:T(4,128)}, u32[]{:S(2)}) copy-start(f32[4,6]{1,0:T(4,128)} %param.31) | copy-start | bytes 292
  66.4 26.6 %copy-start.13 = (f32[4,6]{1,0:T(4,128)S(1)}, f32[4,6]{1,0:T(4,128)}, u32[]{:S(2)}) copy-start(f32[4,6]{1,0:T(4,128)} %param.27) | copy-start | bytes 292
  66.4 27.3 %copy-start.7 = (f32[64,384]{1,0:T(8,128)S(1)}, f32[64,384]{1,0:T(8,128)}, u32[]{:S(2)}) copy-start(f32[64,384]{1,0:T(8,128)} %param.28) | copy-start | bytes 294916
  66.4 27.3 %copy-start.8 = (f32[64,384]{1,0:T(8,128)S(1)}, f32[64,384]{1,0:T(8,128)}, u32[]{:S(2)}) copy-start(f32[64,384]{1,0:T(8,128)} %param.24) | copy-start | bytes 294916
  66.4 13.5 %collective-permute-start.9 = (f32[40,384]{1,0:T(8,128)S(1)}, f32[40,384]{1,0:T(8,128)S(1)}, u32[]{:S(2)}, u32[]{:S(2)}) collective-permute-start(f32[40,384]{1,0:T(8,128)S(1)} %add.181), channel_id=1, source_target_pairs={{0,384},{1,385},{2,386},{3,387},{4,388},{5,389},{6,390},{7,391},{8... | collective-permute-start | bytes 184328 | tf_op jit(solution)/shard_map/ppermute | solution.py:31
  80.0 5.1 %collective-permute-start.10 = (f32[40,384]{1,0:T(8,128)S(1)}, f32[40,384]{1,0:T(8,128)S(1)}, u32[]{:S(2)}, u32[]{:S(2)}) collective-permute-start(f32[40,384]{1,0:T(8,128)S(1)} %add.182), channel_id=1, source_target_pairs={{0,32},{1,33},{2,34},{3,35},{4,36},{5,37},{6,38},{7,39},{8,40},{9,... | collective-permute-start | bytes 184328 | tf_op jit(solution)/shard_map/ppermute | solution.py:31
  85.1 8.7 %copy-start.14 = (f32[64]{0:T(128)S(1)}, f32[64]{0:T(128)}, u32[]{:S(2)}) copy-start(f32[64]{0:T(128)} %param.30) | copy-start | bytes 772
  85.2 8.7 %copy-start.15 = (f32[64]{0:T(128)S(1)}, f32[64]{0:T(128)}, u32[]{:S(2)}) copy-start(f32[64]{0:T(128)} %param.26) | copy-start | bytes 772
  85.2 6.8 %collective-permute-start.11 = (f32[80,384]{1,0:T(8,128)S(1)}, f32[80,384]{1,0:T(8,128)S(1)}, u32[]{:S(2)}, u32[]{:S(2)}) collective-permute-start(f32[80,384]{1,0:T(8,128)S(1)} %pad_maximum_fusion.1), channel_id=1, source_target_pairs={{0,24},{1,25},{2,26},{3,27},{4,28},{5,29},{6,30},{7,31},{8,16},{9,... | collective-permute-start | bytes 368648 | tf_op jit(solution)/shard_map/ppermute | solution.py:31
  93.8 39.0 %copy-start.3 = (f32[64,384]{1,0:T(8,128)}, f32[64,384]{1,0:T(8,128)S(1)}, u32[]{:S(2)}) copy-start(f32[64,384]{1,0:T(8,128)S(1)} %get-tuple-element.35) | copy-start | bytes 294916
  93.8 39.0 %copy-start.4 = (f32[64,384]{1,0:T(8,128)}, f32[64,384]{1,0:T(8,128)S(1)}, u32[]{:S(2)}) copy-start(f32[64,384]{1,0:T(8,128)S(1)} %get-tuple-element.36) | copy-start | bytes 294916
  114.3 18.5 %copy-start.10 = (f32[4]{0:T(128)}, f32[4]{0:T(128)S(1)}, u32[]{:S(2)}) copy-start(f32[4]{0:T(128)S(1)} %get-tuple-element.51) | copy-start | bytes 52

commit v11 on v10

--- a/solution.py
+++ b/solution.py
@@ -154,18 +154,17 @@
     weight_sizes = jnp.sqrt(squares[:4])
     update_sizes = jnp.sqrt(squares[4:])
     trust_ratios = weight_sizes / (update_sizes + 1e-06)
-    updated = [
-        (weights[member] - 0.01 * trust_ratios[member] * results[member][2]).astype(jnp.bfloat16)
-        for member in range(4)
-    ]
-    rest = jnp.concatenate([updated[2].reshape(-1), updated[3].reshape(-1)])
+    members = len(weights)
+    ratios = (0.01 * trust_ratios).reshape(members, 1, 1)
+    updated = (stacked[:members] - ratios * stacked[members:]).astype(jnp.bfloat16)
+    norm_size = weight_norm.size
+    rest = jnp.concatenate([updated[2, 0, :norm_size], updated[3, 0, : weight_bias.size]])
     rest = jnp.pad(rest, (0, lanes - rest.shape[0])).reshape(1, lanes)
-    payload = jnp.concatenate([updated[0], updated[1].reshape(-1, lanes), rest], axis=0)
+    payload = jnp.concatenate([updated[0], updated[1], rest], axis=0)
     gather_rows = padded_width(payload.shape[0], 2 * ROW_TILE)
     payload = jnp.pad(payload, ((0, gather_rows - payload.shape[0]), (0, 0)))
     gathered = lax.all_gather(payload, "shard", axis=0, tiled=False)
     gathered_rest = gathered[:, query_rows + output_rows]
-    norm_size = weight_norm.size
     full = [
         gathered[:, :query_rows].reshape(-1, lanes),
         gathered[:, query_rows : query_rows + output_rows]

time: 137 us -> 134 us (0.978)
  between operations: 3.8 us -> 1.17 us
where the time goes in v11:
time: 134 us
  starting transfers between devices  52.1 us (39%)
  waiting for transfers between devices  34 us (25%)
  blocking collectives  33.4 us (25%)
  local copies, waits for them, and re-layouts  7.04 us (5%)
  other arithmetic  5.93 us (4%)
    ppermute x12, starting transfers between devices, exchange(): return lax.ppermute(value, AXES, [(d, d ^ mask) for d in range(devices)])  52.1 us
    ppermute x12, waiting for transfers between devices, exchange(): return lax.ppermute(value, AXES, [(d, d ^ mask) for d in range(devices)])  34 us
    psum x1, blocking collectives, on_device(): squares = lax.psum(jnp.sum(stacked * stacked, axis=(1, 2)), 'shard')  19.4 us
    all_gather x1, blocking collectives, on_device(): gathered = lax.all_gather(payload, 'shard', axis=0, tiled=False)  14.1 us
  transfers between devices with their start and end apart: 12, of which 11 were waited for; matrix products, arithmetic and copies ran while one was open for 0% of the time, Pallas kernels for 0%

profile of v11, /device:TPU:1, one launch (start us, length us, event | category | flops | bytes accessed | tf_op | source)
XLA Modules:
  0.0 133.6 jit_solution(14911650796117271489)
XLA Ops:
  0.7 1.4 %concatenate.28 = f32[4,2,64,384]{3,2,1,0:T(8,128)S(1)} reshape(f32[1,384,512]{2,1,0:T(8,128)} %param.17) | data formatting | bytes 1572864 | tf_op jit(solution)/shard_map/concatenate | solution.py:124
  2.1 0.8 copy.31
  2.9 0.5 broadcast.97
  3.4 1.3 %reduce.7 = f32[512]{0:T(512)S(1)} reduce(f32[1,512]{1,0:T(1,128)} %param.18, f32[]{:T(128)} %broadcast.97), dimensions={0}, to_apply=%param.18.reduce_sub_computation.3 | reduce | bytes 4100 | tf_op args[2]
  4.8 0.1 reshape_squeeze.8
  5.0 0.1 pad_maximum_fusion
  5.2 8.8 %collective-permute-start = (f32[4,136,384]{2,1,0:T(8,128)S(1)}, f32[4,136,384]{2,1,0:T(8,128)S(1)}, u32[]{:S(2)}, u32[]{:S(2)}) collective-permute-start(f32[4,136,384]{2,1,0:T(8,128)S(1)} %dynamic-slice_bitcast_fusion), channel_id=1, source_target_pairs={{0,1},{1,0},{2,3},{3,2},{4,5},{5,4},{6,7},{7,6},{8,9},{9,8},{10,11... | collective-permute-start | bytes 2506760 | tf_op jit(solution)/shard_map/ppermute | solution.py:31
  14.0 1.9 %collective-permute-done = f32[4,136,384]{2,1,0:T(8,128)S(1)} collective-permute-done((f32[4,136,384]{2,1,0:T(8,128)S(1)}, f32[4,136,384]{2,1,0:T(8,128)S(1)}, u32[]{:S(2)}, u32[]{:S(2)}) %collective-permute-start) | collective-permute-done | bytes 835616 | tf_op jit(solution)/shard_map/ppermute | solution.py:31
  15.9 0.1 bitcast_add_fusion
  16.1 2.1 %collective-permute-start.1 = (f32[136,384]{1,0:T(8,128)S(1)}, f32[136,384]{1,0:T(8,128)S(1)}, u32[]{:S(2)}, u32[]{:S(2)}) collective-permute-start(f32[136,384]{1,0:T(8,128)S(1)} %get-tuple-element.45), channel_id=1, source_target_pairs={{0,2},{1,3},{2,0},{3,1},{4,6},{5,7},{6,4},{7,5},{8,10},{9,11},{10,... | collective-permute-start | bytes 626696 | tf_op jit(solution)/shard_map/ppermute | solution.py:31
  18.2 1.9 %collective-permute-start.2 = (f32[136,384]{1,0:T(8,128)S(1)}, f32[136,384]{1,0:T(8,128)S(1)}, u32[]{:S(2)}, u32[]{:S(2)}) collective-permute-start(f32[136,384]{1,0:T(8,128)S(1)} %get-tuple-element.47), channel_id=1, source_target_pairs={{0,4},{1,5},{2,6},{3,7},{4,0},{5,1},{6,2},{7,3},{8,12},{9,13},{10,... | collective-permute-start | bytes 626696 | tf_op jit(solution)/shard_map/ppermute | solution.py:31
  20.1 5.7 %collective-permute-start.3 = (f32[136,384]{1,0:T(8,128)S(1)}, f32[136,384]{1,0:T(8,128)S(1)}, u32[]{:S(2)}, u32[]{:S(2)}) collective-permute-start(f32[136,384]{1,0:T(8,128)S(1)} %get-tuple-element.46), channel_id=1, source_target_pairs={{0,6},{1,7},{2,4},{3,5},{4,2},{5,3},{6,0},{7,1},{8,14},{9,15},{10,... | collective-permute-start | bytes 626696 | tf_op jit(solution)/shard_map/ppermute | solution.py:31
  25.9 2.1 %collective-permute-done.2 = f32[136,384]{1,0:T(8,128)S(1)} collective-permute-done((f32[136,384]{1,0:T(8,128)S(1)}, f32[136,384]{1,0:T(8,128)S(1)}, u32[]{:S(2)}, u32[]{:S(2)}) %collective-permute-start.2) | collective-permute-done | bytes 208928 | tf_op jit(solution)/shard_map/ppermute | solution.py:31
  28.0 5.2 %collective-permute-done.3 = f32[136,384]{1,0:T(8,128)S(1)} collective-permute-done((f32[136,384]{1,0:T(8,128)S(1)}, f32[136,384]{1,0:T(8,128)S(1)}, u32[]{:S(2)}, u32[]{:S(2)}) %collective-permute-start.3) | collective-permute-done | bytes 208928 | tf_op jit(solution)/shard_map/ppermute | solution.py:31
  33.3 2.5 %collective-permute-start.4 = (f32[80,384]{1,0:T(8,128)S(1)}, f32[80,384]{1,0:T(8,128)S(1)}, u32[]{:S(2)}, u32[]{:S(2)}) collective-permute-start(f32[80,384]{1,0:T(8,128)S(1)} %dynamic-slice_bitcast_fusion.4), channel_id=1, source_target_pairs={{0,24},{1,25},{2,26},{3,27},{4,28},{5,29},{6,30},{7,31},{8,16},{9,... | collective-permute-start | bytes 368648 | tf_op jit(solution)/shard_map/ppermute | solution.py:31
  35.8 5.0 %collective-permute-done.4 = f32[80,384]{1,0:T(8,128)S(1)} collective-permute-done((f32[80,384]{1,0:T(8,128)S(1)}, f32[80,384]{1,0:T(8,128)S(1)}, u32[]{:S(2)}, u32[]{:S(2)}) %collective-permute-start.4) | collective-permute-done | bytes 122912 | tf_op jit(solution)/shard_map/ppermute | solution.py:31
  40.8 1.9 %collective-permute-start.5 = (f32[40,384]{1,0:T(8,128)S(1)}, f32[40,384]{1,0:T(8,128)S(1)}, u32[]{:S(2)}, u32[]{:S(2)}) collective-permute-start(f32[40,384]{1,0:T(8,128)S(1)} %dynamic-slice_bitcast_fusion.5), channel_id=1, source_target_pairs={{0,32},{1,33},{2,34},{3,35},{4,36},{5,37},{6,38},{7,39},{8,40},{9,... | collective-permute-start | bytes 184328 | tf_op jit(solution)/shard_map/ppermute | solution.py:31
  42.8 3.0 %collective-permute-done.5 = f32[40,384]{1,0:T(8,128)S(1)} collective-permute-done((f32[40,384]{1,0:T(8,128)S(1)}, f32[40,384]{1,0:T(8,128)S(1)}, u32[]{:S(2)}, u32[]{:S(2)}) %collective-permute-start.5) | collective-permute-done | bytes 61472 | tf_op jit(solution)/shard_map/ppermute | solution.py:31
  45.8 2.1 %collective-permute-start.6 = (f32[40,384]{1,0:T(8,128)S(1)}, f32[40,384]{1,0:T(8,128)S(1)}, u32[]{:S(2)}, u32[]{:S(2)}) collective-permute-start(f32[40,384]{1,0:T(8,128)S(1)} %bitcast_add_fusion.3), channel_id=1, source_target_pairs={{0,8},{1,9},{2,10},{3,11},{4,12},{5,13},{6,14},{7,15},{8,0},{9,1},... | collective-permute-start | bytes 184328 | tf_op jit(solution)/shard_map/ppermute | solution.py:31
  47.9 3.0 %collective-permute-done.6 = f32[40,384]{1,0:T(8,128)S(1)} collective-permute-done((f32[40,384]{1,0:T(8,128)S(1)}, f32[40,384]{1,0:T(8,128)S(1)}, u32[]{:S(2)}, u32[]{:S(2)}) %collective-permute-start.6) | collective-permute-done | bytes 61472 | tf_op jit(solution)/shard_map/ppermute | solution.py:31
  51.0 3.2 %collective-permute-start.7 = (f32[40,384]{1,0:T(8,128)S(1)}, f32[40,384]{1,0:T(8,128)S(1)}, u32[]{:S(2)}, u32[]{:S(2)}) collective-permute-start(f32[40,384]{1,0:T(8,128)S(1)} %add.179), channel_id=1, source_target_pairs={{0,64},{1,65},{2,66},{3,67},{4,68},{5,69},{6,70},{7,71},{8,72},{9,... | collective-permute-start | bytes 184328 | tf_op jit(solution)/shard_map/ppermute | solution.py:31
  54.1 3.3 %collective-permute-done.7 = f32[40,384]{1,0:T(8,128)S(1)} collective-permute-done((f32[40,384]{1,0:T(8,128)S(1)}, f32[40,384]{1,0:T(8,128)S(1)}, u32[]{:S(2)}, u32[]{:S(2)}) %collective-permute-start.7) | collective-permute-done | bytes 61472 | tf_op jit(solution)/shard_map/ppermute | solution.py:31
  57.5 7.1 %collective-permute-start.8 = (f32[40,384]{1,0:T(8,128)S(1)}, f32[40,384]{1,0:T(8,128)S(1)}, u32[]{:S(2)}, u32[]{:S(2)}) collective-permute-start(f32[40,384]{1,0:T(8,128)S(1)} %add.180), channel_id=1, source_target_pairs={{0,128},{1,129},{2,130},{3,131},{4,132},{5,133},{6,134},{7,135},{8... | collective-permute-start | bytes 184328 | tf_op jit(solution)/shard_map/ppermute | solution.py:31
  64.7 0.1 reshape.76
  64.8 1.6 %collective-permute-done.8 = f32[40,384]{1,0:T(8,128)S(1)} collective-permute-done((f32[40,384]{1,0:T(8,128)S(1)}, f32[40,384]{1,0:T(8,128)S(1)}, u32[]{:S(2)}, u32[]{:S(2)}) %collective-permute-start.8) | collective-permute-done | bytes 61472 | tf_op jit(solution)/shard_map/ppermute | solution.py:31
  66.4 10.6 %collective-permute-start.9 = (f32[40,384]{1,0:T(8,128)S(1)}, f32[40,384]{1,0:T(8,128)S(1)}, u32[]{:S(2)}, u32[]{:S(2)}) collective-permute-start(f32[40,384]{1,0:T(8,128)S(1)} %add.181), channel_id=1, source_target_pairs={{0,384},{1,385},{2,386},{3,387},{4,388},{5,389},{6,390},{7,391},{8... | collective-permute-start | bytes 184328 | tf_op jit(solution)/shard_map/ppermute | solution.py:31
  76.9 3.0 %collective-permute-done.9 = f32[40,384]{1,0:T(8,128)S(1)} collective-permute-done((f32[40,384]{1,0:T(8,128)S(1)}, f32[40,384]{1,0:T(8,128)S(1)}, u32[]{:S(2)}, u32[]{:S(2)}) %collective-permute-start.9) | collective-permute-done | bytes 61472 | tf_op jit(solution)/shard_map/ppermute | solution.py:31
  80.0 1.9 %collective-permute-start.10 = (f32[40,384]{1,0:T(8,128)S(1)}, f32[40,384]{1,0:T(8,128)S(1)}, u32[]{:S(2)}, u32[]{:S(2)}) collective-permute-start(f32[40,384]{1,0:T(8,128)S(1)} %add.182), channel_id=1, source_target_pairs={{0,32},{1,33},{2,34},{3,35},{4,36},{5,37},{6,38},{7,39},{8,40},{9,... | collective-permute-start | bytes 184328 | tf_op jit(solution)/shard_map/ppermute | solution.py:31
  81.9 3.3 %collective-permute-done.10 = f32[40,384]{1,0:T(8,128)S(1)} collective-permute-done((f32[40,384]{1,0:T(8,128)S(1)}, f32[40,384]{1,0:T(8,128)S(1)}, u32[]{:S(2)}, u32[]{:S(2)}) %collective-permute-start.10) | collective-permute-done | bytes 61472 | tf_op jit(solution)/shard_map/ppermute | solution.py:31
  85.3 4.4 %collective-permute-start.11 = (f32[80,384]{1,0:T(8,128)S(1)}, f32[80,384]{1,0:T(8,128)S(1)}, u32[]{:S(2)}, u32[]{:S(2)}) collective-permute-start(f32[80,384]{1,0:T(8,128)S(1)} %pad_maximum_fusion.1), channel_id=1, source_target_pairs={{0,24},{1,25},{2,26},{3,27},{4,28},{5,29},{6,30},{7,31},{8,16},{9,... | collective-permute-start | bytes 368648 | tf_op jit(solution)/shard_map/ppermute | solution.py:31
  89.7 2.4 %collective-permute-done.11 = f32[80,384]{1,0:T(8,128)S(1)} collective-permute-done((f32[80,384]{1,0:T(8,128)S(1)}, f32[80,384]{1,0:T(8,128)S(1)}, u32[]{:S(2)}, u32[]{:S(2)}) %collective-permute-start.11) | collective-permute-done | bytes 122912 | tf_op jit(solution)/shard_map/ppermute | solution.py:31
  92.2 0.1 slice_reduce_fusion
  92.3 0.7 multiply_add_fusion.2
  93.1 0.1 reshape.82
  93.1 0.6 multiply_add_fusion.4
  93.7 0.1 reshape.83
  93.8 0.7 constant_dynamic-update-slice_fusion.1
  94.6 0.5 add_bitcast_fusion.1
  95.1 0.2 multiply_reduce_fusion
  95.3 19.4 %psum.7 = f32[8]{0:T(128)S(1)} all-reduce(f32[8]{0:T(128)S(1)} %multiply_reduce_fusion), channel_id=1, replica_groups=mesh['replica'=64,'shard'=8] {'shard'}, use_global_device_ids=true, to_apply=%region_1.2 | all-reduce | flops 8 | bytes 64 | tf_op jit(solution)/shard_map/psum | solution.py:153
  114.7 0.6 fusion.20
  115.3 0.1 fusion
  115.5 14.1 %all-gather = bf16[1152,384]{1,0:T(8,128)(2,1)S(1)} all-gather(bf16[144,384]{1,0:T(8,128)(2,1)S(1)} %fusion.7), channel_id=2, replica_groups=mesh['replica'=64,'shard'=8] {'shard'}, dimensions={0}, use_global_device_ids=true | all-gather | bytes 995328 | tf_op jit(solution)/shard_map/all_gather | solution.py:166
  129.6 0.9 fusion.26
  130.6 1.1 reshape_reshape.6
  131.7 0.7 copy.34
  132.4 0.6 reshape.86
  133.0 0.6 pad_maximum_fusion.3
  (70 shorter events, 1.1 us)
Async XLA Ops:
  0.6 4.3 %copy-start.1 = (f32[1,512,384]{2,1,0:T(8,128)S(1)}, f32[1,512,384]{2,1,0:T(8,128)}, u32[]{:S(2)}) copy-start(f32[1,512,384]{2,1,0:T(8,128)} %param.16) | copy-start | bytes 2359300
  5.2 10.8 %collective-permute-start = (f32[4,136,384]{2,1,0:T(8,128)S(1)}, f32[4,136,384]{2,1,0:T(8,128)S(1)}, u32[]{:S(2)}, u32[]{:S(2)}) collective-permute-start(f32[4,136,384]{2,1,0:T(8,128)S(1)} %dynamic-slice_bitcast_fusion), channel_id=1, source_target_pairs={{0,1},{1,0},{2,3},{3,2},{4,5},{5,4},{6,7},{7,6},{8,9},{9,8},{10,11... | collective-permute-start | bytes 2506760 | tf_op jit(solution)/shard_map/ppermute | solution.py:31
  16.1 48.5 %copy-start = (f32[64,384]{1,0:T(8,128)S(1)}, f32[64,384]{1,0:T(8,128)}, u32[]{:S(2)}) copy-start(f32[64,384]{1,0:T(8,128)} %param.20) | copy-start | bytes 294916
  16.1 48.5 %copy-start.2 = (f32[48,512]{1,0:T(8,128)S(1)}, f32[48,512]{1,0:T(8,128)}, u32[]{:S(2)}) copy-start(f32[48,512]{1,0:T(8,128)} %param.21) | copy-start | bytes 294916
  16.1 48.5 %copy-start.7 = (f32[4,6]{1,0:T(4,128)S(1)}, f32[4,6]{1,0:T(4,128)}, u32[]{:S(2)}) copy-start(f32[4,6]{1,0:T(4,128)} %param.23) | copy-start | bytes 292
  16.1 9.8 %collective-permute-start.1 = (f32[136,384]{1,0:T(8,128)S(1)}, f32[136,384]{1,0:T(8,128)S(1)}, u32[]{:S(2)}, u32[]{:S(2)}) collective-permute-start(f32[136,384]{1,0:T(8,128)S(1)} %get-tuple-element.45), channel_id=1, source_target_pairs={{0,2},{1,3},{2,0},{3,1},{4,6},{5,7},{6,4},{7,5},{8,10},{9,11},{10,... | collective-permute-start | bytes 626696 | tf_op jit(solution)/shard_map/ppermute | solution.py:31
  18.2 9.8 %collective-permute-start.2 = (f32[136,384]{1,0:T(8,128)S(1)}, f32[136,384]{1,0:T(8,128)S(1)}, u32[]{:S(2)}, u32[]{:S(2)}) collective-permute-start(f32[136,384]{1,0:T(8,128)S(1)} %get-tuple-element.47), channel_id=1, source_target_pairs={{0,4},{1,5},{2,6},{3,7},{4,0},{5,1},{6,2},{7,3},{8,12},{9,13},{10,... | collective-permute-start | bytes 626696 | tf_op jit(solution)/shard_map/ppermute | solution.py:31
  20.1 13.1 %collective-permute-start.3 = (f32[136,384]{1,0:T(8,128)S(1)}, f32[136,384]{1,0:T(8,128)S(1)}, u32[]{:S(2)}, u32[]{:S(2)}) collective-permute-start(f32[136,384]{1,0:T(8,128)S(1)} %get-tuple-element.46), channel_id=1, source_target_pairs={{0,6},{1,7},{2,4},{3,5},{4,2},{5,3},{6,0},{7,1},{8,14},{9,15},{10,... | collective-permute-start | bytes 626696 | tf_op jit(solution)/shard_map/ppermute | solution.py:31
  25.9 56.0 %copy-start.8 = (f32[64]{0:T(128)S(1)}, f32[64]{0:T(128)}, u32[]{:S(2)}) copy-start(f32[64]{0:T(128)} %param.22) | copy-start | bytes 772
  33.3 7.5 %collective-permute-start.4 = (f32[80,384]{1,0:T(8,128)S(1)}, f32[80,384]{1,0:T(8,128)S(1)}, u32[]{:S(2)}, u32[]{:S(2)}) collective-permute-start(f32[80,384]{1,0:T(8,128)S(1)} %dynamic-slice_bitcast_fusion.4), channel_id=1, source_target_pairs={{0,24},{1,25},{2,26},{3,27},{4,28},{5,29},{6,30},{7,31},{8,16},{9,... | collective-permute-start | bytes 368648 | tf_op jit(solution)/shard_map/ppermute | solution.py:31
  40.8 5.0 %collective-permute-start.5 = (f32[40,384]{1,0:T(8,128)S(1)}, f32[40,384]{1,0:T(8,128)S(1)}, u32[]{:S(2)}, u32[]{:S(2)}) collective-permute-start(f32[40,384]{1,0:T(8,128)S(1)} %dynamic-slice_bitcast_fusion.5), channel_id=1, source_target_pairs={{0,32},{1,33},{2,34},{3,35},{4,36},{5,37},{6,38},{7,39},{8,40},{9,... | collective-permute-start | bytes 184328 | tf_op jit(solution)/shard_map/ppermute | solution.py:31
  45.8 46.5 %copy-start.5 = (f32[48,512]{1,0:T(8,128)S(1)}, f32[48,512]{1,0:T(8,128)}, u32[]{:S(2)}) copy-start(f32[48,512]{1,0:T(8,128)} %param.29) | copy-start | bytes 294916
  45.8 46.5 %copy-start.6 = (f32[48,512]{1,0:T(8,128)S(1)}, f32[48,512]{1,0:T(8,128)}, u32[]{:S(2)}) copy-start(f32[48,512]{1,0:T(8,128)} %param.25) | copy-start | bytes 294916
  45.8 5.1 %collective-permute-start.6 = (f32[40,384]{1,0:T(8,128)S(1)}, f32[40,384]{1,0:T(8,128)S(1)}, u32[]{:S(2)}, u32[]{:S(2)}) collective-permute-start(f32[40,384]{1,0:T(8,128)S(1)} %bitcast_add_fusion.3), channel_id=1, source_target_pairs={{0,8},{1,9},{2,10},{3,11},{4,12},{5,13},{6,14},{7,15},{8,0},{9,1},... | collective-permute-start | bytes 184328 | tf_op jit(solution)/shard_map/ppermute | solution.py:31
  51.0 6.5 %collective-permute-start.7 = (f32[40,384]{1,0:T(8,128)S(1)}, f32[40,384]{1,0:T(8,128)S(1)}, u32[]{:S(2)}, u32[]{:S(2)}) collective-permute-start(f32[40,384]{1,0:T(8,128)S(1)} %add.179), channel_id=1, source_target_pairs={{0,64},{1,65},{2,66},{3,67},{4,68},{5,69},{6,70},{7,71},{8,72},{9,... | collective-permute-start | bytes 184328 | tf_op jit(solution)/shard_map/ppermute | solution.py:31
  57.5 8.9 %collective-permute-start.8 = (f32[40,384]{1,0:T(8,128)S(1)}, f32[40,384]{1,0:T(8,128)S(1)}, u32[]{:S(2)}, u32[]{:S(2)}) collective-permute-start(f32[40,384]{1,0:T(8,128)S(1)} %add.180), channel_id=1, source_target_pairs={{0,128},{1,129},{2,130},{3,131},{4,132},{5,133},{6,134},{7,135},{8... | collective-permute-start | bytes 184328 | tf_op jit(solution)/shard_map/ppermute | solution.py:31
  64.7 28.4 %copy-start.9 = (f32[4,6]{1,0:T(4,128)S(1)}, f32[4,6]{1,0:T(4,128)}, u32[]{:S(2)}) copy-start(f32[4,6]{1,0:T(4,128)} %param.31) | copy-start | bytes 292
  64.7 28.4 %copy-start.10 = (f32[4,6]{1,0:T(4,128)S(1)}, f32[4,6]{1,0:T(4,128)}, u32[]{:S(2)}) copy-start(f32[4,6]{1,0:T(4,128)} %param.27) | copy-start | bytes 292
  64.7 29.1 %copy-start.3 = (f32[64,384]{1,0:T(8,128)S(1)}, f32[64,384]{1,0:T(8,128)}, u32[]{:S(2)}) copy-start(f32[64,384]{1,0:T(8,128)} %param.28) | copy-start | bytes 294916
  64.7 29.1 %copy-start.4 = (f32[64,384]{1,0:T(8,128)S(1)}, f32[64,384]{1,0:T(8,128)}, u32[]{:S(2)}) copy-start(f32[64,384]{1,0:T(8,128)} %param.24) | copy-start | bytes 294916
  66.4 13.6 %collective-permute-start.9 = (f32[40,384]{1,0:T(8,128)S(1)}, f32[40,384]{1,0:T(8,128)S(1)}, u32[]{:S(2)}, u32[]{:S(2)}) collective-permute-start(f32[40,384]{1,0:T(8,128)S(1)} %add.181), channel_id=1, source_target_pairs={{0,384},{1,385},{2,386},{3,387},{4,388},{5,389},{6,390},{7,391},{8... | collective-permute-start | bytes 184328 | tf_op jit(solution)/shard_map/ppermute | solution.py:31
  80.0 5.3 %collective-permute-start.10 = (f32[40,384]{1,0:T(8,128)S(1)}, f32[40,384]{1,0:T(8,128)S(1)}, u32[]{:S(2)}, u32[]{:S(2)}) collective-permute-start(f32[40,384]{1,0:T(8,128)S(1)} %add.182), channel_id=1, source_target_pairs={{0,32},{1,33},{2,34},{3,35},{4,36},{5,37},{6,38},{7,39},{8,40},{9,... | collective-permute-start | bytes 184328 | tf_op jit(solution)/shard_map/ppermute | solution.py:31
  85.3 9.3 %copy-start.11 = (f32[64]{0:T(128)S(1)}, f32[64]{0:T(128)}, u32[]{:S(2)}) copy-start(f32[64]{0:T(128)} %param.30) | copy-start | bytes 772
  85.3 9.3 %copy-start.12 = (f32[64]{0:T(128)S(1)}, f32[64]{0:T(128)}, u32[]{:S(2)}) copy-start(f32[64]{0:T(128)} %param.26) | copy-start | bytes 772
  85.3 6.8 %collective-permute-start.11 = (f32[80,384]{1,0:T(8,128)S(1)}, f32[80,384]{1,0:T(8,128)S(1)}, u32[]{:S(2)}, u32[]{:S(2)}) collective-permute-start(f32[80,384]{1,0:T(8,128)S(1)} %pad_maximum_fusion.1), channel_id=1, source_target_pairs={{0,24},{1,25},{2,26},{3,27},{4,28},{5,29},{6,30},{7,31},{8,16},{9,... | collective-permute-start | bytes 368648 | tf_op jit(solution)/shard_map/ppermute | solution.py:31

commit v12 on v11

--- a/solution.py
+++ b/solution.py
@@ -131,25 +131,33 @@
     )
     block = reduce_blocks(packed, devices)
     summed_rest = block[query_rows + output_rows, :small_width]
-    summed_all = [
+    summed_tiles = [
         block[:query_rows],
-        block[query_rows : query_rows + output_rows].reshape(weight_output.shape),
-        summed_rest[: weight_norm.size].reshape(weight_norm.shape),
-        summed_rest[weight_norm.size :].reshape(weight_bias.shape),
+        block[query_rows : query_rows + output_rows],
+        as_tile(summed_rest[: weight_norm.size], query_rows, lanes),
+        as_tile(summed_rest[weight_norm.size :], query_rows, lanes),
     ]
-    results = [
-        step_math(
-            summed_all[member],
-            moments[member],
-            seconds[member],
-            weights[member],
-            decay_rates[member],
+    members = len(weights)
+    weight_tiles = jnp.stack([as_tile(weight, query_rows, lanes) for weight in weights])
+    decay = jnp.array(decay_rates, jnp.float32).reshape(members, 1, 1)
+    moment_tiles, second_tiles, update_tiles = step_math(
+        jnp.stack(summed_tiles),
+        jnp.stack([as_tile(moment, query_rows, lanes) for moment in moments]),
+        jnp.stack([as_tile(second, query_rows, lanes) for second in seconds]),
+        weight_tiles,
+        decay,
+    )
+
+    def untile(tiles):
+        return (
+            tiles[0],
+            tiles[1].reshape(weight_output.shape),
+            tiles[2, 0, : weight_norm.size],
+            tiles[3, 0, : weight_bias.size].reshape(weight_bias.shape),
         )
-        for member in range(4)
-    ]
-    terms = [as_tile(weight, query_rows, lanes) for weight in weights]
-    terms += [as_tile(result[2], query_rows, lanes) for result in results]
-    stacked = jnp.stack(terms)
+
+    results = list(zip(untile(moment_tiles), untile(second_tiles)))
+    stacked = jnp.concatenate([weight_tiles, update_tiles])
     squares = lax.psum(jnp.sum(stacked * stacked, axis=(1, 2)), "shard")
     weight_sizes = jnp.sqrt(squares[:4])
     update_sizes = jnp.sqrt(squares[4:])

time: 134 us -> 136 us (1.015)
  local copies, waits for them, and re-layouts: 7.04 us -> 10.9 us
  other arithmetic: 5.93 us -> 3.72 us
    another operation x5 -> x15, local copies, waits for them, and re-layouts: 0.09 us -> 2.79 us  [the longest x2 1.33 us: untile(): tiles[1].reshape(weight_output.shape)]
where the time goes in v12:
time: 136 us; the launch traced here: 135 us
  starting transfers between devices  52.2 us (38%)
  waiting for transfers between devices  33.6 us (25%)
  blocking collectives  33.4 us (25%)
  local copies, waits for them, and re-layouts  10.9 us (8%)
  other arithmetic  3.72 us (3%)
    ppermute x12, starting transfers between devices, exchange(): return lax.ppermute(value, AXES, [(d, d ^ mask) for d in range(devices)])  52.2 us
    ppermute x12, waiting for transfers between devices, exchange(): return lax.ppermute(value, AXES, [(d, d ^ mask) for d in range(devices)])  33.6 us
    psum x1, blocking collectives, on_device(): squares = lax.psum(jnp.sum(stacked * stacked, axis=(1, 2)), 'shard')  19.4 us
    all_gather x1, blocking collectives, on_device(): gathered = lax.all_gather(payload, 'shard', axis=0, tiled=False)  14.1 us
  transfers between devices with their start and end apart: 12, of which 11 were waited for; matrix products, arithmetic and copies ran while one was open for 0% of the time, Pallas kernels for 0%

profile of v12, /device:TPU:1, one launch (start us, length us, event | category | flops | bytes accessed | tf_op | source)
XLA Modules:
  0.0 135.2 jit_solution(13390499057033854890)
XLA Ops:
  0.7 1.4 %concatenate.30 = f32[4,2,64,384]{3,2,1,0:T(8,128)S(1)} reshape(f32[1,384,512]{2,1,0:T(8,128)} %param.18) | data formatting | bytes 1572864 | tf_op jit(solution)/shard_map/concatenate | solution.py:124
  2.1 0.8 copy.32
  2.9 0.5 broadcast.89
  3.4 1.3 reduce.11
  5.0 0.1 pad_maximum_fusion
  5.2 8.8 %collective-permute-start = (f32[4,136,384]{2,1,0:T(8,128)S(1)}, f32[4,136,384]{2,1,0:T(8,128)S(1)}, u32[]{:S(2)}, u32[]{:S(2)}) collective-permute-start(f32[4,136,384]{2,1,0:T(8,128)S(1)} %dynamic-slice_bitcast_fusion), channel_id=1, source_target_pairs={{0,1},{1,0},{2,3},{3,2},{4,5},{5,4},{6,7},{7,6},{8,9},{9,8},{10,11... | collective-permute-start | bytes 2506760 | tf_op jit(solution)/shard_map/ppermute | solution.py:31
  14.0 1.9 %collective-permute-done = f32[4,136,384]{2,1,0:T(8,128)S(1)} collective-permute-done((f32[4,136,384]{2,1,0:T(8,128)S(1)}, f32[4,136,384]{2,1,0:T(8,128)S(1)}, u32[]{:S(2)}, u32[]{:S(2)}) %collective-permute-start) | collective-permute-done | bytes 835616 | tf_op jit(solution)/shard_map/ppermute | solution.py:31
  15.9 0.1 bitcast_add_fusion
  16.2 2.1 %collective-permute-start.1 = (f32[136,384]{1,0:T(8,128)S(1)}, f32[136,384]{1,0:T(8,128)S(1)}, u32[]{:S(2)}, u32[]{:S(2)}) collective-permute-start(f32[136,384]{1,0:T(8,128)S(1)} %get-tuple-element.35), channel_id=1, source_target_pairs={{0,2},{1,3},{2,0},{3,1},{4,6},{5,7},{6,4},{7,5},{8,10},{9,11},{10,... | collective-permute-start | bytes 626696 | tf_op jit(solution)/shard_map/ppermute | solution.py:31
  18.2 1.9 %collective-permute-start.2 = (f32[136,384]{1,0:T(8,128)S(1)}, f32[136,384]{1,0:T(8,128)S(1)}, u32[]{:S(2)}, u32[]{:S(2)}) collective-permute-start(f32[136,384]{1,0:T(8,128)S(1)} %get-tuple-element.37), channel_id=1, source_target_pairs={{0,4},{1,5},{2,6},{3,7},{4,0},{5,1},{6,2},{7,3},{8,12},{9,13},{10,... | collective-permute-start | bytes 626696 | tf_op jit(solution)/shard_map/ppermute | solution.py:31
  20.2 5.7 %collective-permute-start.3 = (f32[136,384]{1,0:T(8,128)S(1)}, f32[136,384]{1,0:T(8,128)S(1)}, u32[]{:S(2)}, u32[]{:S(2)}) collective-permute-start(f32[136,384]{1,0:T(8,128)S(1)} %get-tuple-element.36), channel_id=1, source_target_pairs={{0,6},{1,7},{2,4},{3,5},{4,2},{5,3},{6,0},{7,1},{8,14},{9,15},{10,... | collective-permute-start | bytes 626696 | tf_op jit(solution)/shard_map/ppermute | solution.py:31
  25.9 2.1 %collective-permute-done.2 = f32[136,384]{1,0:T(8,128)S(1)} collective-permute-done((f32[136,384]{1,0:T(8,128)S(1)}, f32[136,384]{1,0:T(8,128)S(1)}, u32[]{:S(2)}, u32[]{:S(2)}) %collective-permute-start.2) | collective-permute-done | bytes 208928 | tf_op jit(solution)/shard_map/ppermute | solution.py:31
  28.0 5.2 %collective-permute-done.3 = f32[136,384]{1,0:T(8,128)S(1)} collective-permute-done((f32[136,384]{1,0:T(8,128)S(1)}, f32[136,384]{1,0:T(8,128)S(1)}, u32[]{:S(2)}, u32[]{:S(2)}) %collective-permute-start.3) | collective-permute-done | bytes 208928 | tf_op jit(solution)/shard_map/ppermute | solution.py:31
  33.4 2.6 %collective-permute-start.4 = (f32[80,384]{1,0:T(8,128)S(1)}, f32[80,384]{1,0:T(8,128)S(1)}, u32[]{:S(2)}, u32[]{:S(2)}) collective-permute-start(f32[80,384]{1,0:T(8,128)S(1)} %dynamic-slice_bitcast_fusion.4), channel_id=1, source_target_pairs={{0,24},{1,25},{2,26},{3,27},{4,28},{5,29},{6,30},{7,31},{8,16},{9,... | collective-permute-start | bytes 368648 | tf_op jit(solution)/shard_map/ppermute | solution.py:31
  36.1 0.1 reshape.81
  36.2 0.1 reshape.88
  36.4 4.6 %collective-permute-done.4 = f32[80,384]{1,0:T(8,128)S(1)} collective-permute-done((f32[80,384]{1,0:T(8,128)S(1)}, f32[80,384]{1,0:T(8,128)S(1)}, u32[]{:S(2)}, u32[]{:S(2)}) %collective-permute-start.4) | collective-permute-done | bytes 122912 | tf_op jit(solution)/shard_map/ppermute | solution.py:31
  41.0 1.9 %collective-permute-start.5 = (f32[40,384]{1,0:T(8,128)S(1)}, f32[40,384]{1,0:T(8,128)S(1)}, u32[]{:S(2)}, u32[]{:S(2)}) collective-permute-start(f32[40,384]{1,0:T(8,128)S(1)} %dynamic-slice_bitcast_fusion.5), channel_id=1, source_target_pairs={{0,32},{1,33},{2,34},{3,35},{4,36},{5,37},{6,38},{7,39},{8,40},{9,... | collective-permute-start | bytes 184328 | tf_op jit(solution)/shard_map/ppermute | solution.py:31
  43.0 3.0 %collective-permute-done.5 = f32[40,384]{1,0:T(8,128)S(1)} collective-permute-done((f32[40,384]{1,0:T(8,128)S(1)}, f32[40,384]{1,0:T(8,128)S(1)}, u32[]{:S(2)}, u32[]{:S(2)}) %collective-permute-start.5) | collective-permute-done | bytes 61472 | tf_op jit(solution)/shard_map/ppermute | solution.py:31
  46.0 1.9 %collective-permute-start.6 = (f32[40,384]{1,0:T(8,128)S(1)}, f32[40,384]{1,0:T(8,128)S(1)}, u32[]{:S(2)}, u32[]{:S(2)}) collective-permute-start(f32[40,384]{1,0:T(8,128)S(1)} %bitcast_add_fusion.3), channel_id=1, source_target_pairs={{0,8},{1,9},{2,10},{3,11},{4,12},{5,13},{6,14},{7,15},{8,0},{9,1},... | collective-permute-start | bytes 184328 | tf_op jit(solution)/shard_map/ppermute | solution.py:31
  48.0 3.0 %collective-permute-done.6 = f32[40,384]{1,0:T(8,128)S(1)} collective-permute-done((f32[40,384]{1,0:T(8,128)S(1)}, f32[40,384]{1,0:T(8,128)S(1)}, u32[]{:S(2)}, u32[]{:S(2)}) %collective-permute-start.6) | collective-permute-done | bytes 61472 | tf_op jit(solution)/shard_map/ppermute | solution.py:31
  51.0 3.3 %collective-permute-start.7 = (f32[40,384]{1,0:T(8,128)S(1)}, f32[40,384]{1,0:T(8,128)S(1)}, u32[]{:S(2)}, u32[]{:S(2)}) collective-permute-start(f32[40,384]{1,0:T(8,128)S(1)} %add.153), channel_id=1, source_target_pairs={{0,64},{1,65},{2,66},{3,67},{4,68},{5,69},{6,70},{7,71},{8,72},{9,... | collective-permute-start | bytes 184328 | tf_op jit(solution)/shard_map/ppermute | solution.py:31
  54.4 3.3 %collective-permute-done.7 = f32[40,384]{1,0:T(8,128)S(1)} collective-permute-done((f32[40,384]{1,0:T(8,128)S(1)}, f32[40,384]{1,0:T(8,128)S(1)}, u32[]{:S(2)}, u32[]{:S(2)}) %collective-permute-start.7) | collective-permute-done | bytes 61472 | tf_op jit(solution)/shard_map/ppermute | solution.py:31
  57.7 7.1 %collective-permute-start.8 = (f32[40,384]{1,0:T(8,128)S(1)}, f32[40,384]{1,0:T(8,128)S(1)}, u32[]{:S(2)}, u32[]{:S(2)}) collective-permute-start(f32[40,384]{1,0:T(8,128)S(1)} %add.154), channel_id=1, source_target_pairs={{0,128},{1,129},{2,130},{3,131},{4,132},{5,133},{6,134},{7,135},{8... | collective-permute-start | bytes 184328 | tf_op jit(solution)/shard_map/ppermute | solution.py:31
  64.8 1.8 %collective-permute-done.8 = f32[40,384]{1,0:T(8,128)S(1)} collective-permute-done((f32[40,384]{1,0:T(8,128)S(1)}, f32[40,384]{1,0:T(8,128)S(1)}, u32[]{:S(2)}, u32[]{:S(2)}) %collective-permute-start.8) | collective-permute-done | bytes 61472 | tf_op jit(solution)/shard_map/ppermute | solution.py:31
  66.6 10.6 %collective-permute-start.9 = (f32[40,384]{1,0:T(8,128)S(1)}, f32[40,384]{1,0:T(8,128)S(1)}, u32[]{:S(2)}, u32[]{:S(2)}) collective-permute-start(f32[40,384]{1,0:T(8,128)S(1)} %add.155), channel_id=1, source_target_pairs={{0,384},{1,385},{2,386},{3,387},{4,388},{5,389},{6,390},{7,391},{8... | collective-permute-start | bytes 184328 | tf_op jit(solution)/shard_map/ppermute | solution.py:31
  77.2 3.0 %collective-permute-done.9 = f32[40,384]{1,0:T(8,128)S(1)} collective-permute-done((f32[40,384]{1,0:T(8,128)S(1)}, f32[40,384]{1,0:T(8,128)S(1)}, u32[]{:S(2)}, u32[]{:S(2)}) %collective-permute-start.9) | collective-permute-done | bytes 61472 | tf_op jit(solution)/shard_map/ppermute | solution.py:31
  80.2 1.9 %collective-permute-start.10 = (f32[40,384]{1,0:T(8,128)S(1)}, f32[40,384]{1,0:T(8,128)S(1)}, u32[]{:S(2)}, u32[]{:S(2)}) collective-permute-start(f32[40,384]{1,0:T(8,128)S(1)} %add.156), channel_id=1, source_target_pairs={{0,32},{1,33},{2,34},{3,35},{4,36},{5,37},{6,38},{7,39},{8,40},{9,... | collective-permute-start | bytes 184328 | tf_op jit(solution)/shard_map/ppermute | solution.py:31
  82.1 3.3 %collective-permute-done.10 = f32[40,384]{1,0:T(8,128)S(1)} collective-permute-done((f32[40,384]{1,0:T(8,128)S(1)}, f32[40,384]{1,0:T(8,128)S(1)}, u32[]{:S(2)}, u32[]{:S(2)}) %collective-permute-start.10) | collective-permute-done | bytes 61472 | tf_op jit(solution)/shard_map/ppermute | solution.py:31
  85.5 4.4 %collective-permute-start.11 = (f32[80,384]{1,0:T(8,128)S(1)}, f32[80,384]{1,0:T(8,128)S(1)}, u32[]{:S(2)}, u32[]{:S(2)}) collective-permute-start(f32[80,384]{1,0:T(8,128)S(1)} %pad_maximum_fusion.3), channel_id=1, source_target_pairs={{0,24},{1,25},{2,26},{3,27},{4,28},{5,29},{6,30},{7,31},{8,16},{9,... | collective-permute-start | bytes 368648 | tf_op jit(solution)/shard_map/ppermute | solution.py:31
  90.0 2.3 %collective-permute-done.11 = f32[80,384]{1,0:T(8,128)S(1)} collective-permute-done((f32[80,384]{1,0:T(8,128)S(1)}, f32[80,384]{1,0:T(8,128)S(1)}, u32[]{:S(2)}, u32[]{:S(2)}) %collective-permute-start.11) | collective-permute-done | bytes 122912 | tf_op jit(solution)/shard_map/ppermute | solution.py:31
  92.5 0.2 constant_dynamic-update-slice_fusion
  92.8 0.5 slice_bitcast_fusion.5
  93.3 0.7 fusion.19
  94.0 0.2 multiply_reduce_fusion
  94.2 19.4 %psum.7 = f32[8]{0:T(128)S(1)} all-reduce(f32[8]{0:T(128)S(1)} %multiply_reduce_fusion), channel_id=1, replica_groups=mesh['replica'=64,'shard'=8] {'shard'}, use_global_device_ids=true, to_apply=%region_1.2 | all-reduce | flops 8 | bytes 64 | tf_op jit(solution)/shard_map/psum | solution.py:161
  113.5 0.6 fusion.15
  114.1 0.2 subtract_convert_fusion
  114.5 14.1 %all-gather = bf16[1152,384]{1,0:T(8,128)(2,1)S(1)} all-gather(bf16[144,384]{1,0:T(8,128)(2,1)S(1)} %fusion.7), channel_id=2, replica_groups=mesh['replica'=64,'shard'=8] {'shard'}, dimensions={0}, use_global_device_ids=true | all-gather | bytes 995328 | tf_op jit(solution)/shard_map/all_gather | solution.py:174
  128.5 0.9 fusion.18
  129.5 0.7 reshape_squeeze.23
  130.2 0.7 reshape_squeeze.25
  130.8 0.7 reshape_squeeze.22
  131.5 0.7 reshape_squeeze.24
  132.1 1.1 reshape_reshape.6
  133.3 0.7 copy.35
  134.0 0.6 reshape.91
  134.6 0.6 pad_maximum_fusion.5
  (80 shorter events, 1.4 us)
Async XLA Ops:
  0.6 4.3 %copy-start.1 = (f32[1,512,384]{2,1,0:T(8,128)S(1)}, f32[1,512,384]{2,1,0:T(8,128)}, u32[]{:S(2)}) copy-start(f32[1,512,384]{2,1,0:T(8,128)} %param.17) | copy-start | bytes 2359300
  5.2 10.8 %collective-permute-start = (f32[4,136,384]{2,1,0:T(8,128)S(1)}, f32[4,136,384]{2,1,0:T(8,128)S(1)}, u32[]{:S(2)}, u32[]{:S(2)}) collective-permute-start(f32[4,136,384]{2,1,0:T(8,128)S(1)} %dynamic-slice_bitcast_fusion), channel_id=1, source_target_pairs={{0,1},{1,0},{2,3},{3,2},{4,5},{5,4},{6,7},{7,6},{8,9},{9,8},{10,11... | collective-permute-start | bytes 2506760 | tf_op jit(solution)/shard_map/ppermute | solution.py:31
  16.0 20.0 %copy-start = (f32[64,384]{1,0:T(8,128)S(1)}, f32[64,384]{1,0:T(8,128)}, u32[]{:S(2)}) copy-start(f32[64,384]{1,0:T(8,128)} %param.21) | copy-start | bytes 294916
  16.0 20.0 %copy-start.4 = (f32[48,512]{1,0:T(8,128)S(1)}, f32[48,512]{1,0:T(8,128)}, u32[]{:S(2)}) copy-start(f32[48,512]{1,0:T(8,128)} %param.22) | copy-start | bytes 294916
  16.1 20.0 %copy-start.9 = (f32[4,6]{1,0:T(4,128)S(1)}, f32[4,6]{1,0:T(4,128)}, u32[]{:S(2)}) copy-start(f32[4,6]{1,0:T(4,128)} %param.24) | copy-start | bytes 292
  16.1 20.1 %copy-start.10 = (f32[4,6]{1,0:T(4,128)S(1)}, f32[4,6]{1,0:T(4,128)}, u32[]{:S(2)}) copy-start(f32[4,6]{1,0:T(4,128)} %param.32) | copy-start | bytes 292
  16.1 20.2 %copy-start.11 = (f32[4,6]{1,0:T(4,128)S(1)}, f32[4,6]{1,0:T(4,128)}, u32[]{:S(2)}) copy-start(f32[4,6]{1,0:T(4,128)} %param.28) | copy-start | bytes 292
  16.1 20.3 %copy-start.7 = (f32[64]{0:T(128)S(1)}, f32[64]{0:T(128)}, u32[]{:S(2)}) copy-start(f32[64]{0:T(128)} %param.23) | copy-start | bytes 772
  16.2 9.7 %collective-permute-start.1 = (f32[136,384]{1,0:T(8,128)S(1)}, f32[136,384]{1,0:T(8,128)S(1)}, u32[]{:S(2)}, u32[]{:S(2)}) collective-permute-start(f32[136,384]{1,0:T(8,128)S(1)} %get-tuple-element.35), channel_id=1, source_target_pairs={{0,2},{1,3},{2,0},{3,1},{4,6},{5,7},{6,4},{7,5},{8,10},{9,11},{10,... | collective-permute-start | bytes 626696 | tf_op jit(solution)/shard_map/ppermute | solution.py:31
  18.2 9.8 %collective-permute-start.2 = (f32[136,384]{1,0:T(8,128)S(1)}, f32[136,384]{1,0:T(8,128)S(1)}, u32[]{:S(2)}, u32[]{:S(2)}) collective-permute-start(f32[136,384]{1,0:T(8,128)S(1)} %get-tuple-element.37), channel_id=1, source_target_pairs={{0,4},{1,5},{2,6},{3,7},{4,0},{5,1},{6,2},{7,3},{8,12},{9,13},{10,... | collective-permute-start | bytes 626696 | tf_op jit(solution)/shard_map/ppermute | solution.py:31
  20.2 13.1 %collective-permute-start.3 = (f32[136,384]{1,0:T(8,128)S(1)}, f32[136,384]{1,0:T(8,128)S(1)}, u32[]{:S(2)}, u32[]{:S(2)}) collective-permute-start(f32[136,384]{1,0:T(8,128)S(1)} %get-tuple-element.36), channel_id=1, source_target_pairs={{0,6},{1,7},{2,4},{3,5},{4,2},{5,3},{6,0},{7,1},{8,14},{9,15},{10,... | collective-permute-start | bytes 626696 | tf_op jit(solution)/shard_map/ppermute | solution.py:31
  33.3 56.6 %copy-start.12 = (f32[64]{0:T(128)S(1)}, f32[64]{0:T(128)}, u32[]{:S(2)}) copy-start(f32[64]{0:T(128)} %param.31) | copy-start | bytes 772
  33.3 56.6 %copy-start.5 = (f32[48,512]{1,0:T(8,128)S(1)}, f32[48,512]{1,0:T(8,128)}, u32[]{:S(2)}) copy-start(f32[48,512]{1,0:T(8,128)} %param.26) | copy-start | bytes 294916
  33.4 56.6 %copy-start.6 = (f32[48,512]{1,0:T(8,128)S(1)}, f32[48,512]{1,0:T(8,128)}, u32[]{:S(2)}) copy-start(f32[48,512]{1,0:T(8,128)} %param.30) | copy-start | bytes 294916
  33.4 7.6 %collective-permute-start.4 = (f32[80,384]{1,0:T(8,128)S(1)}, f32[80,384]{1,0:T(8,128)S(1)}, u32[]{:S(2)}, u32[]{:S(2)}) collective-permute-start(f32[80,384]{1,0:T(8,128)S(1)} %dynamic-slice_bitcast_fusion.4), channel_id=1, source_target_pairs={{0,24},{1,25},{2,26},{3,27},{4,28},{5,29},{6,30},{7,31},{8,16},{9,... | collective-permute-start | bytes 368648 | tf_op jit(solution)/shard_map/ppermute | solution.py:31
  36.0 54.0 %copy-start.13 = (f32[64]{0:T(128)S(1)}, f32[64]{0:T(128)}, u32[]{:S(2)}) copy-start(f32[64]{0:T(128)} %param.27) | copy-start | bytes 772
  41.0 5.0 %collective-permute-start.5 = (f32[40,384]{1,0:T(8,128)S(1)}, f32[40,384]{1,0:T(8,128)S(1)}, u32[]{:S(2)}, u32[]{:S(2)}) collective-permute-start(f32[40,384]{1,0:T(8,128)S(1)} %dynamic-slice_bitcast_fusion.5), channel_id=1, source_target_pairs={{0,32},{1,33},{2,34},{3,35},{4,36},{5,37},{6,38},{7,39},{8,40},{9,... | collective-permute-start | bytes 184328 | tf_op jit(solution)/shard_map/ppermute | solution.py:31
  46.0 5.0 %collective-permute-start.6 = (f32[40,384]{1,0:T(8,128)S(1)}, f32[40,384]{1,0:T(8,128)S(1)}, u32[]{:S(2)}, u32[]{:S(2)}) collective-permute-start(f32[40,384]{1,0:T(8,128)S(1)} %bitcast_add_fusion.3), channel_id=1, source_target_pairs={{0,8},{1,9},{2,10},{3,11},{4,12},{5,13},{6,14},{7,15},{8,0},{9,1},... | collective-permute-start | bytes 184328 | tf_op jit(solution)/shard_map/ppermute | solution.py:31
  51.0 41.5 %copy-start.2 = (f32[64,384]{1,0:T(8,128)S(1)}, f32[64,384]{1,0:T(8,128)}, u32[]{:S(2)}) copy-start(f32[64,384]{1,0:T(8,128)} %param.29) | copy-start | bytes 294916
  51.0 41.5 %copy-start.3 = (f32[64,384]{1,0:T(8,128)S(1)}, f32[64,384]{1,0:T(8,128)}, u32[]{:S(2)}) copy-start(f32[64,384]{1,0:T(8,128)} %param.25) | copy-start | bytes 294916
  51.0 41.5 %copy-start.8 = (f32[4]{0:T(128)S(1)}, f32[4]{0:T(128)}, u32[]{:S(2)}) copy-start(f32[4]{0:T(128)} %constant.68.clone) | copy-start | bytes 52
  51.0 6.7 %collective-permute-start.7 = (f32[40,384]{1,0:T(8,128)S(1)}, f32[40,384]{1,0:T(8,128)S(1)}, u32[]{:S(2)}, u32[]{:S(2)}) collective-permute-start(f32[40,384]{1,0:T(8,128)S(1)} %add.153), channel_id=1, source_target_pairs={{0,64},{1,65},{2,66},{3,67},{4,68},{5,69},{6,70},{7,71},{8,72},{9,... | collective-permute-start | bytes 184328 | tf_op jit(solution)/shard_map/ppermute | solution.py:31
  57.7 8.9 %collective-permute-start.8 = (f32[40,384]{1,0:T(8,128)S(1)}, f32[40,384]{1,0:T(8,128)S(1)}, u32[]{:S(2)}, u32[]{:S(2)}) collective-permute-start(f32[40,384]{1,0:T(8,128)S(1)} %add.154), channel_id=1, source_target_pairs={{0,128},{1,129},{2,130},{3,131},{4,132},{5,133},{6,134},{7,135},{8... | collective-permute-start | bytes 184328 | tf_op jit(solution)/shard_map/ppermute | solution.py:31
  66.6 13.6 %collective-permute-start.9 = (f32[40,384]{1,0:T(8,128)S(1)}, f32[40,384]{1,0:T(8,128)S(1)}, u32[]{:S(2)}, u32[]{:S(2)}) collective-permute-start(f32[40,384]{1,0:T(8,128)S(1)} %add.155), channel_id=1, source_target_pairs={{0,384},{1,385},{2,386},{3,387},{4,388},{5,389},{6,390},{7,391},{8... | collective-permute-start | bytes 184328 | tf_op jit(solution)/shard_map/ppermute | solution.py:31
  80.2 5.3 %collective-permute-start.10 = (f32[40,384]{1,0:T(8,128)S(1)}, f32[40,384]{1,0:T(8,128)S(1)}, u32[]{:S(2)}, u32[]{:S(2)}) collective-permute-start(f32[40,384]{1,0:T(8,128)S(1)} %add.156), channel_id=1, source_target_pairs={{0,32},{1,33},{2,34},{3,35},{4,36},{5,37},{6,38},{7,39},{8,40},{9,... | collective-permute-start | bytes 184328 | tf_op jit(solution)/shard_map/ppermute | solution.py:31
  85.5 6.8 %collective-permute-start.11 = (f32[80,384]{1,0:T(8,128)S(1)}, f32[80,384]{1,0:T(8,128)S(1)}, u32[]{:S(2)}, u32[]{:S(2)}) collective-permute-start(f32[80,384]{1,0:T(8,128)S(1)} %pad_maximum_fusion.3), channel_id=1, source_target_pairs={{0,24},{1,25},{2,26},{3,27},{4,28},{5,29},{6,30},{7,31},{8,16},{9,... | collective-permute-start | bytes 368648 | tf_op jit(solution)/shard_map/ppermute | solution.py:31

commit v13 on v11

--- a/solution.py
+++ b/solution.py
@@ -151,8 +151,9 @@
     terms += [as_tile(result[2], query_rows, lanes) for result in results]
     stacked = jnp.stack(terms)
     squares = lax.psum(jnp.sum(stacked * stacked, axis=(1, 2)), "shard")
-    weight_sizes = jnp.sqrt(squares[:4])
-    update_sizes = jnp.sqrt(squares[4:])
+    norm_table = jnp.sqrt(squares.reshape(2, -1))
+    weight_sizes = norm_table[0]
+    update_sizes = norm_table[1]
     trust_ratios = weight_sizes / (update_sizes + 1e-06)
     members = len(weights)
     ratios = (0.01 * trust_ratios).reshape(members, 1, 1)
@@ -175,7 +176,6 @@
         .reshape((shards,) + weight_bias.shape)
         .reshape((-1,) + weight_bias.shape[1:]),
     ]
-    norm_table = jnp.stack([weight_sizes, update_sizes])
     return (
         full[0],
         full[1],

time: 134 us -> 134 us (level)
  no operation moved by 1% of the time
where the time goes in v13:
time: 134 us
  starting transfers between devices  52.1 us (39%)
  blocking collectives  33.7 us (25%)
  waiting for transfers between devices  33.6 us (25%)
  local copies, waits for them, and re-layouts  7.7 us (6%)
  other arithmetic  5.37 us (4%)
    ppermute x12, starting transfers between devices, exchange(): return lax.ppermute(value, AXES, [(d, d ^ mask) for d in range(devices)])  52.1 us
    ppermute x12, waiting for transfers between devices, exchange(): return lax.ppermute(value, AXES, [(d, d ^ mask) for d in range(devices)])  33.6 us
    psum x1, blocking collectives, on_device(): squares = lax.psum(jnp.sum(stacked * stacked, axis=(1, 2)), 'shard')  19.7 us
    all_gather x1, blocking collectives, on_device(): gathered = lax.all_gather(payload, 'shard', axis=0, tiled=False)  14.1 us
  transfers between devices with their start and end apart: 12, of which 11 were waited for; matrix products, arithmetic and copies ran while one was open for 0% of the time, Pallas kernels for 0%

profile of v13, /device:TPU:1, one launch (start us, length us, event | category | flops | bytes accessed | tf_op | source)
XLA Modules:
  0.0 133.7 jit_solution(8324150269122196192)
XLA Ops:
  0.7 1.4 %concatenate.28 = f32[4,2,64,384]{3,2,1,0:T(8,128)S(1)} reshape(f32[1,384,512]{2,1,0:T(8,128)} %param.17) | data formatting | bytes 1572864 | tf_op jit(solution)/shard_map/concatenate | solution.py:124
  2.1 0.8 copy.31
  2.9 0.5 broadcast.108
  3.4 1.3 %reduce.7 = f32[512]{0:T(512)S(1)} reduce(f32[1,512]{1,0:T(1,128)} %param.18, f32[]{:T(128)} %broadcast.108), dimensions={0}, to_apply=%param.18.reduce_sub_computation.3 | reduce | bytes 4100 | tf_op args[2]
  4.8 0.1 reshape_squeeze.8
  5.0 0.1 pad_maximum_fusion
  5.2 8.8 %collective-permute-start = (f32[4,136,384]{2,1,0:T(8,128)S(1)}, f32[4,136,384]{2,1,0:T(8,128)S(1)}, u32[]{:S(2)}, u32[]{:S(2)}) collective-permute-start(f32[4,136,384]{2,1,0:T(8,128)S(1)} %dynamic-slice_bitcast_fusion), channel_id=1, source_target_pairs={{0,1},{1,0},{2,3},{3,2},{4,5},{5,4},{6,7},{7,6},{8,9},{9,8},{10,11... | collective-permute-start | bytes 2506760 | tf_op jit(solution)/shard_map/ppermute | solution.py:31
  14.0 1.9 %collective-permute-done = f32[4,136,384]{2,1,0:T(8,128)S(1)} collective-permute-done((f32[4,136,384]{2,1,0:T(8,128)S(1)}, f32[4,136,384]{2,1,0:T(8,128)S(1)}, u32[]{:S(2)}, u32[]{:S(2)}) %collective-permute-start) | collective-permute-done | bytes 835616 | tf_op jit(solution)/shard_map/ppermute | solution.py:31
  15.9 0.1 bitcast_add_fusion
  16.1 2.1 %collective-permute-start.1 = (f32[136,384]{1,0:T(8,128)S(1)}, f32[136,384]{1,0:T(8,128)S(1)}, u32[]{:S(2)}, u32[]{:S(2)}) collective-permute-start(f32[136,384]{1,0:T(8,128)S(1)} %get-tuple-element.45), channel_id=1, source_target_pairs={{0,2},{1,3},{2,0},{3,1},{4,6},{5,7},{6,4},{7,5},{8,10},{9,11},{10,... | collective-permute-start | bytes 626696 | tf_op jit(solution)/shard_map/ppermute | solution.py:31
  18.2 1.9 %collective-permute-start.2 = (f32[136,384]{1,0:T(8,128)S(1)}, f32[136,384]{1,0:T(8,128)S(1)}, u32[]{:S(2)}, u32[]{:S(2)}) collective-permute-start(f32[136,384]{1,0:T(8,128)S(1)} %get-tuple-element.47), channel_id=1, source_target_pairs={{0,4},{1,5},{2,6},{3,7},{4,0},{5,1},{6,2},{7,3},{8,12},{9,13},{10,... | collective-permute-start | bytes 626696 | tf_op jit(solution)/shard_map/ppermute | solution.py:31
  20.1 5.7 %collective-permute-start.3 = (f32[136,384]{1,0:T(8,128)S(1)}, f32[136,384]{1,0:T(8,128)S(1)}, u32[]{:S(2)}, u32[]{:S(2)}) collective-permute-start(f32[136,384]{1,0:T(8,128)S(1)} %get-tuple-element.46), channel_id=1, source_target_pairs={{0,6},{1,7},{2,4},{3,5},{4,2},{5,3},{6,0},{7,1},{8,14},{9,15},{10,... | collective-permute-start | bytes 626696 | tf_op jit(solution)/shard_map/ppermute | solution.py:31
  25.9 2.1 %collective-permute-done.2 = f32[136,384]{1,0:T(8,128)S(1)} collective-permute-done((f32[136,384]{1,0:T(8,128)S(1)}, f32[136,384]{1,0:T(8,128)S(1)}, u32[]{:S(2)}, u32[]{:S(2)}) %collective-permute-start.2) | collective-permute-done | bytes 208928 | tf_op jit(solution)/shard_map/ppermute | solution.py:31
  28.0 5.2 %collective-permute-done.3 = f32[136,384]{1,0:T(8,128)S(1)} collective-permute-done((f32[136,384]{1,0:T(8,128)S(1)}, f32[136,384]{1,0:T(8,128)S(1)}, u32[]{:S(2)}, u32[]{:S(2)}) %collective-permute-start.3) | collective-permute-done | bytes 208928 | tf_op jit(solution)/shard_map/ppermute | solution.py:31
  33.3 2.5 %collective-permute-start.4 = (f32[80,384]{1,0:T(8,128)S(1)}, f32[80,384]{1,0:T(8,128)S(1)}, u32[]{:S(2)}, u32[]{:S(2)}) collective-permute-start(f32[80,384]{1,0:T(8,128)S(1)} %dynamic-slice_bitcast_fusion.4), channel_id=1, source_target_pairs={{0,24},{1,25},{2,26},{3,27},{4,28},{5,29},{6,30},{7,31},{8,16},{9,... | collective-permute-start | bytes 368648 | tf_op jit(solution)/shard_map/ppermute | solution.py:31
  35.8 5.0 %collective-permute-done.4 = f32[80,384]{1,0:T(8,128)S(1)} collective-permute-done((f32[80,384]{1,0:T(8,128)S(1)}, f32[80,384]{1,0:T(8,128)S(1)}, u32[]{:S(2)}, u32[]{:S(2)}) %collective-permute-start.4) | collective-permute-done | bytes 122912 | tf_op jit(solution)/shard_map/ppermute | solution.py:31
  40.8 1.9 %collective-permute-start.5 = (f32[40,384]{1,0:T(8,128)S(1)}, f32[40,384]{1,0:T(8,128)S(1)}, u32[]{:S(2)}, u32[]{:S(2)}) collective-permute-start(f32[40,384]{1,0:T(8,128)S(1)} %dynamic-slice_bitcast_fusion.5), channel_id=1, source_target_pairs={{0,32},{1,33},{2,34},{3,35},{4,36},{5,37},{6,38},{7,39},{8,40},{9,... | collective-permute-start | bytes 184328 | tf_op jit(solution)/shard_map/ppermute | solution.py:31
  42.8 3.0 %collective-permute-done.5 = f32[40,384]{1,0:T(8,128)S(1)} collective-permute-done((f32[40,384]{1,0:T(8,128)S(1)}, f32[40,384]{1,0:T(8,128)S(1)}, u32[]{:S(2)}, u32[]{:S(2)}) %collective-permute-start.5) | collective-permute-done | bytes 61472 | tf_op jit(solution)/shard_map/ppermute | solution.py:31
  45.8 1.9 %collective-permute-start.6 = (f32[40,384]{1,0:T(8,128)S(1)}, f32[40,384]{1,0:T(8,128)S(1)}, u32[]{:S(2)}, u32[]{:S(2)}) collective-permute-start(f32[40,384]{1,0:T(8,128)S(1)} %bitcast_add_fusion.3), channel_id=1, source_target_pairs={{0,8},{1,9},{2,10},{3,11},{4,12},{5,13},{6,14},{7,15},{8,0},{9,1},... | collective-permute-start | bytes 184328 | tf_op jit(solution)/shard_map/ppermute | solution.py:31
  47.8 3.0 %collective-permute-done.6 = f32[40,384]{1,0:T(8,128)S(1)} collective-permute-done((f32[40,384]{1,0:T(8,128)S(1)}, f32[40,384]{1,0:T(8,128)S(1)}, u32[]{:S(2)}, u32[]{:S(2)}) %collective-permute-start.6) | collective-permute-done | bytes 61472 | tf_op jit(solution)/shard_map/ppermute | solution.py:31
  50.8 3.2 %collective-permute-start.7 = (f32[40,384]{1,0:T(8,128)S(1)}, f32[40,384]{1,0:T(8,128)S(1)}, u32[]{:S(2)}, u32[]{:S(2)}) collective-permute-start(f32[40,384]{1,0:T(8,128)S(1)} %add.185), channel_id=1, source_target_pairs={{0,64},{1,65},{2,66},{3,67},{4,68},{5,69},{6,70},{7,71},{8,72},{9,... | collective-permute-start | bytes 184328 | tf_op jit(solution)/shard_map/ppermute | solution.py:31
  54.0 3.3 %collective-permute-done.7 = f32[40,384]{1,0:T(8,128)S(1)} collective-permute-done((f32[40,384]{1,0:T(8,128)S(1)}, f32[40,384]{1,0:T(8,128)S(1)}, u32[]{:S(2)}, u32[]{:S(2)}) %collective-permute-start.7) | collective-permute-done | bytes 61472 | tf_op jit(solution)/shard_map/ppermute | solution.py:31
  57.3 7.1 %collective-permute-start.8 = (f32[40,384]{1,0:T(8,128)S(1)}, f32[40,384]{1,0:T(8,128)S(1)}, u32[]{:S(2)}, u32[]{:S(2)}) collective-permute-start(f32[40,384]{1,0:T(8,128)S(1)} %add.186), channel_id=1, source_target_pairs={{0,128},{1,129},{2,130},{3,131},{4,132},{5,133},{6,134},{7,135},{8... | collective-permute-start | bytes 184328 | tf_op jit(solution)/shard_map/ppermute | solution.py:31
  64.5 1.7 %collective-permute-done.8 = f32[40,384]{1,0:T(8,128)S(1)} collective-permute-done((f32[40,384]{1,0:T(8,128)S(1)}, f32[40,384]{1,0:T(8,128)S(1)}, u32[]{:S(2)}, u32[]{:S(2)}) %collective-permute-start.8) | collective-permute-done | bytes 61472 | tf_op jit(solution)/shard_map/ppermute | solution.py:31
  66.2 10.7 %collective-permute-start.9 = (f32[40,384]{1,0:T(8,128)S(1)}, f32[40,384]{1,0:T(8,128)S(1)}, u32[]{:S(2)}, u32[]{:S(2)}) collective-permute-start(f32[40,384]{1,0:T(8,128)S(1)} %add.187), channel_id=1, source_target_pairs={{0,384},{1,385},{2,386},{3,387},{4,388},{5,389},{6,390},{7,391},{8... | collective-permute-start | bytes 184328 | tf_op jit(solution)/shard_map/ppermute | solution.py:31
  77.0 2.9 %collective-permute-done.9 = f32[40,384]{1,0:T(8,128)S(1)} collective-permute-done((f32[40,384]{1,0:T(8,128)S(1)}, f32[40,384]{1,0:T(8,128)S(1)}, u32[]{:S(2)}, u32[]{:S(2)}) %collective-permute-start.9) | collective-permute-done | bytes 61472 | tf_op jit(solution)/shard_map/ppermute | solution.py:31
  79.8 1.9 %collective-permute-start.10 = (f32[40,384]{1,0:T(8,128)S(1)}, f32[40,384]{1,0:T(8,128)S(1)}, u32[]{:S(2)}, u32[]{:S(2)}) collective-permute-start(f32[40,384]{1,0:T(8,128)S(1)} %add.188), channel_id=1, source_target_pairs={{0,32},{1,33},{2,34},{3,35},{4,36},{5,37},{6,38},{7,39},{8,40},{9,... | collective-permute-start | bytes 184328 | tf_op jit(solution)/shard_map/ppermute | solution.py:31
  81.8 3.2 %collective-permute-done.10 = f32[40,384]{1,0:T(8,128)S(1)} collective-permute-done((f32[40,384]{1,0:T(8,128)S(1)}, f32[40,384]{1,0:T(8,128)S(1)}, u32[]{:S(2)}, u32[]{:S(2)}) %collective-permute-start.10) | collective-permute-done | bytes 61472 | tf_op jit(solution)/shard_map/ppermute | solution.py:31
  85.0 4.4 %collective-permute-start.11 = (f32[80,384]{1,0:T(8,128)S(1)}, f32[80,384]{1,0:T(8,128)S(1)}, u32[]{:S(2)}, u32[]{:S(2)}) collective-permute-start(f32[80,384]{1,0:T(8,128)S(1)} %pad_maximum_fusion.1), channel_id=1, source_target_pairs={{0,24},{1,25},{2,26},{3,27},{4,28},{5,29},{6,30},{7,31},{8,16},{9,... | collective-permute-start | bytes 368648 | tf_op jit(solution)/shard_map/ppermute | solution.py:31
  89.4 0.1 reshape.96
  89.5 2.3 %collective-permute-done.11 = f32[80,384]{1,0:T(8,128)S(1)} collective-permute-done((f32[80,384]{1,0:T(8,128)S(1)}, f32[80,384]{1,0:T(8,128)S(1)}, u32[]{:S(2)}, u32[]{:S(2)}) %collective-permute-start.11) | collective-permute-done | bytes 122912 | tf_op jit(solution)/shard_map/ppermute | solution.py:31
  91.8 0.1 slice_reduce_fusion
  92.0 0.7 multiply_add_fusion.2
  92.8 0.5 add_bitcast_fusion.1
  93.3 0.7 constant_dynamic-update-slice_fusion.1
  94.1 0.1 reshape.102
  94.2 0.6 multiply_add_fusion.4
  94.8 0.1 reshape.103
  94.8 0.2 multiply_reduce_fusion
  95.0 19.7 %psum.7 = f32[8]{0:T(128)S(1)} all-reduce(f32[8]{0:T(128)S(1)} %multiply_reduce_fusion), channel_id=1, replica_groups=mesh['replica'=64,'shard'=8] {'shard'}, use_global_device_ids=true, to_apply=%region_1.2 | all-reduce | flops 8 | bytes 64 | tf_op jit(solution)/shard_map/psum | solution.py:153
  114.7 0.6 broadcast_multiply_fusion
  115.3 0.1 fusion
  115.6 14.1 %all-gather = bf16[1152,384]{1,0:T(8,128)(2,1)S(1)} all-gather(bf16[144,384]{1,0:T(8,128)(2,1)S(1)} %fusion.7), channel_id=2, replica_groups=mesh['replica'=64,'shard'=8] {'shard'}, dimensions={0}, use_global_device_ids=true | all-gather | bytes 995328 | tf_op jit(solution)/shard_map/all_gather | solution.py:167
  129.6 0.9 fusion.24
  130.6 0.6 sqrt.23
  131.2 1.1 reshape_reshape.6
  132.4 0.7 copy.34
  133.0 0.6 reshape.106
  (72 shorter events, 1.1 us)
Async XLA Ops:
  0.6 4.3 %copy-start.1 = (f32[1,512,384]{2,1,0:T(8,128)S(1)}, f32[1,512,384]{2,1,0:T(8,128)}, u32[]{:S(2)}) copy-start(f32[1,512,384]{2,1,0:T(8,128)} %param.16) | copy-start | bytes 2359300
  5.2 10.8 %collective-permute-start = (f32[4,136,384]{2,1,0:T(8,128)S(1)}, f32[4,136,384]{2,1,0:T(8,128)S(1)}, u32[]{:S(2)}, u32[]{:S(2)}) collective-permute-start(f32[4,136,384]{2,1,0:T(8,128)S(1)} %dynamic-slice_bitcast_fusion), channel_id=1, source_target_pairs={{0,1},{1,0},{2,3},{3,2},{4,5},{5,4},{6,7},{7,6},{8,9},{9,8},{10,11... | collective-permute-start | bytes 2506760 | tf_op jit(solution)/shard_map/ppermute | solution.py:31
  16.1 48.3 %copy-start = (f32[64,384]{1,0:T(8,128)S(1)}, f32[64,384]{1,0:T(8,128)}, u32[]{:S(2)}) copy-start(f32[64,384]{1,0:T(8,128)} %param.20) | copy-start | bytes 294916
  16.1 48.3 %copy-start.2 = (f32[48,512]{1,0:T(8,128)S(1)}, f32[48,512]{1,0:T(8,128)}, u32[]{:S(2)}) copy-start(f32[48,512]{1,0:T(8,128)} %param.21) | copy-start | bytes 294916
  16.1 9.8 %collective-permute-start.1 = (f32[136,384]{1,0:T(8,128)S(1)}, f32[136,384]{1,0:T(8,128)S(1)}, u32[]{:S(2)}, u32[]{:S(2)}) collective-permute-start(f32[136,384]{1,0:T(8,128)S(1)} %get-tuple-element.45), channel_id=1, source_target_pairs={{0,2},{1,3},{2,0},{3,1},{4,6},{5,7},{6,4},{7,5},{8,10},{9,11},{10,... | collective-permute-start | bytes 626696 | tf_op jit(solution)/shard_map/ppermute | solution.py:31
  18.2 9.8 %collective-permute-start.2 = (f32[136,384]{1,0:T(8,128)S(1)}, f32[136,384]{1,0:T(8,128)S(1)}, u32[]{:S(2)}, u32[]{:S(2)}) collective-permute-start(f32[136,384]{1,0:T(8,128)S(1)} %get-tuple-element.47), channel_id=1, source_target_pairs={{0,4},{1,5},{2,6},{3,7},{4,0},{5,1},{6,2},{7,3},{8,12},{9,13},{10,... | collective-permute-start | bytes 626696 | tf_op jit(solution)/shard_map/ppermute | solution.py:31
  20.1 13.1 %collective-permute-start.3 = (f32[136,384]{1,0:T(8,128)S(1)}, f32[136,384]{1,0:T(8,128)S(1)}, u32[]{:S(2)}, u32[]{:S(2)}) collective-permute-start(f32[136,384]{1,0:T(8,128)S(1)} %get-tuple-element.46), channel_id=1, source_target_pairs={{0,6},{1,7},{2,4},{3,5},{4,2},{5,3},{6,0},{7,1},{8,14},{9,15},{10,... | collective-permute-start | bytes 626696 | tf_op jit(solution)/shard_map/ppermute | solution.py:31
  25.9 51.1 %copy-start.8 = (f32[64]{0:T(128)S(1)}, f32[64]{0:T(128)}, u32[]{:S(2)}) copy-start(f32[64]{0:T(128)} %param.22) | copy-start | bytes 772
  33.2 56.2 %copy-start.7 = (f32[4,6]{1,0:T(4,128)S(1)}, f32[4,6]{1,0:T(4,128)}, u32[]{:S(2)}) copy-start(f32[4,6]{1,0:T(4,128)} %param.23) | copy-start | bytes 292
  33.3 7.5 %collective-permute-start.4 = (f32[80,384]{1,0:T(8,128)S(1)}, f32[80,384]{1,0:T(8,128)S(1)}, u32[]{:S(2)}, u32[]{:S(2)}) collective-permute-start(f32[80,384]{1,0:T(8,128)S(1)} %dynamic-slice_bitcast_fusion.4), channel_id=1, source_target_pairs={{0,24},{1,25},{2,26},{3,27},{4,28},{5,29},{6,30},{7,31},{8,16},{9,... | collective-permute-start | bytes 368648 | tf_op jit(solution)/shard_map/ppermute | solution.py:31
  40.8 5.0 %collective-permute-start.5 = (f32[40,384]{1,0:T(8,128)S(1)}, f32[40,384]{1,0:T(8,128)S(1)}, u32[]{:S(2)}, u32[]{:S(2)}) collective-permute-start(f32[40,384]{1,0:T(8,128)S(1)} %dynamic-slice_bitcast_fusion.5), channel_id=1, source_target_pairs={{0,32},{1,33},{2,34},{3,35},{4,36},{5,37},{6,38},{7,39},{8,40},{9,... | collective-permute-start | bytes 184328 | tf_op jit(solution)/shard_map/ppermute | solution.py:31
  42.8 49.2 %copy-start.5 = (f32[48,512]{1,0:T(8,128)S(1)}, f32[48,512]{1,0:T(8,128)}, u32[]{:S(2)}) copy-start(f32[48,512]{1,0:T(8,128)} %param.29) | copy-start | bytes 294916
  42.8 49.2 %copy-start.6 = (f32[48,512]{1,0:T(8,128)S(1)}, f32[48,512]{1,0:T(8,128)}, u32[]{:S(2)}) copy-start(f32[48,512]{1,0:T(8,128)} %param.25) | copy-start | bytes 294916
  45.8 5.0 %collective-permute-start.6 = (f32[40,384]{1,0:T(8,128)S(1)}, f32[40,384]{1,0:T(8,128)S(1)}, u32[]{:S(2)}, u32[]{:S(2)}) collective-permute-start(f32[40,384]{1,0:T(8,128)S(1)} %bitcast_add_fusion.3), channel_id=1, source_target_pairs={{0,8},{1,9},{2,10},{3,11},{4,12},{5,13},{6,14},{7,15},{8,0},{9,1},... | collective-permute-start | bytes 184328 | tf_op jit(solution)/shard_map/ppermute | solution.py:31
  50.8 6.5 %collective-permute-start.7 = (f32[40,384]{1,0:T(8,128)S(1)}, f32[40,384]{1,0:T(8,128)S(1)}, u32[]{:S(2)}, u32[]{:S(2)}) collective-permute-start(f32[40,384]{1,0:T(8,128)S(1)} %add.185), channel_id=1, source_target_pairs={{0,64},{1,65},{2,66},{3,67},{4,68},{5,69},{6,70},{7,71},{8,72},{9,... | collective-permute-start | bytes 184328 | tf_op jit(solution)/shard_map/ppermute | solution.py:31
  57.3 8.9 %collective-permute-start.8 = (f32[40,384]{1,0:T(8,128)S(1)}, f32[40,384]{1,0:T(8,128)S(1)}, u32[]{:S(2)}, u32[]{:S(2)}) collective-permute-start(f32[40,384]{1,0:T(8,128)S(1)} %add.186), channel_id=1, source_target_pairs={{0,128},{1,129},{2,130},{3,131},{4,132},{5,133},{6,134},{7,135},{8... | collective-permute-start | bytes 184328 | tf_op jit(solution)/shard_map/ppermute | solution.py:31
  64.5 28.2 %copy-start.11 = (f32[64]{0:T(128)S(1)}, f32[64]{0:T(128)}, u32[]{:S(2)}) copy-start(f32[64]{0:T(128)} %param.30) | copy-start | bytes 772
  64.5 28.2 %copy-start.12 = (f32[64]{0:T(128)S(1)}, f32[64]{0:T(128)}, u32[]{:S(2)}) copy-start(f32[64]{0:T(128)} %param.26) | copy-start | bytes 772
  66.2 27.1 %copy-start.3 = (f32[64,384]{1,0:T(8,128)S(1)}, f32[64,384]{1,0:T(8,128)}, u32[]{:S(2)}) copy-start(f32[64,384]{1,0:T(8,128)} %param.28) | copy-start | bytes 294916
  66.2 27.1 %copy-start.4 = (f32[64,384]{1,0:T(8,128)S(1)}, f32[64,384]{1,0:T(8,128)}, u32[]{:S(2)}) copy-start(f32[64,384]{1,0:T(8,128)} %param.24) | copy-start | bytes 294916
  66.2 13.6 %collective-permute-start.9 = (f32[40,384]{1,0:T(8,128)S(1)}, f32[40,384]{1,0:T(8,128)S(1)}, u32[]{:S(2)}, u32[]{:S(2)}) collective-permute-start(f32[40,384]{1,0:T(8,128)S(1)} %add.187), channel_id=1, source_target_pairs={{0,384},{1,385},{2,386},{3,387},{4,388},{5,389},{6,390},{7,391},{8... | collective-permute-start | bytes 184328 | tf_op jit(solution)/shard_map/ppermute | solution.py:31
  79.8 5.1 %collective-permute-start.10 = (f32[40,384]{1,0:T(8,128)S(1)}, f32[40,384]{1,0:T(8,128)S(1)}, u32[]{:S(2)}, u32[]{:S(2)}) collective-permute-start(f32[40,384]{1,0:T(8,128)S(1)} %add.188), channel_id=1, source_target_pairs={{0,32},{1,33},{2,34},{3,35},{4,36},{5,37},{6,38},{7,39},{8,40},{9,... | collective-permute-start | bytes 184328 | tf_op jit(solution)/shard_map/ppermute | solution.py:31
  85.0 6.8 %collective-permute-start.11 = (f32[80,384]{1,0:T(8,128)S(1)}, f32[80,384]{1,0:T(8,128)S(1)}, u32[]{:S(2)}, u32[]{:S(2)}) collective-permute-start(f32[80,384]{1,0:T(8,128)S(1)} %pad_maximum_fusion.1), channel_id=1, source_target_pairs={{0,24},{1,25},{2,26},{3,27},{4,28},{5,29},{6,30},{7,31},{8,16},{9,... | collective-permute-start | bytes 368648 | tf_op jit(solution)/shard_map/ppermute | solution.py:31
  89.4 4.8 %copy-start.9 = (f32[4,6]{1,0:T(4,128)S(1)}, f32[4,6]{1,0:T(4,128)}, u32[]{:S(2)}) copy-start(f32[4,6]{1,0:T(4,128)} %param.31) | copy-start | bytes 292
  89.4 4.8 %copy-start.10 = (f32[4,6]{1,0:T(4,128)S(1)}, f32[4,6]{1,0:T(4,128)}, u32[]{:S(2)}) copy-start(f32[4,6]{1,0:T(4,128)} %param.27) | copy-start | bytes 292
